TPU v7x, 32 devices: a whole 2x2x4 slice. The times are simulated.
32 devices in a mesh: ri: 4 (over z), ao: 8 (over y, x, core).
Axes of the slice: x: 2, y: 2, z: 4, core: 2. Of those that a mesh axis runs over, the one named last changes fastest.
Arguments:
- tensor: bfloat16 [512, 256, 256], P('ri', 'ao'), may hold values from -0.5 to 0.5
- live_blocks: int32 [8, 8, 8], P('ri', 'ao'), may hold values 0 or 1
- occ_density: bfloat16 [256, 256], P('ao'), may hold values from -0.375 to 0.375
- virt_density: bfloat16 [256, 256], P('ao'), may hold values from -0.375 to 0.375
- occ_mask: int32 [8, 8], P('ao'), may hold values 0 or 1
- virt_mask: int32 [8, 8], P('ao'), may hold values 0 or 1
- pair_slots: int32 [8, 8], P('ao'), may hold values from 0 to 7, as said below
Outputs:
- polar: float32 [512, 512], P('ri', 'ao')
Inputs may be any that keep to these rules, and one draw needn't show every extreme that they name: pair_slots[b, 0] = b, and the 8 entries of a row are different AO blocks.
All inputs are finite; a program needn't handle non-finite values. No bound on the sum of `live_blocks` or of `occ_mask` or of `virt_mask` on one device may be relied on, other than what follows from the above.
Results may differ from a plain program's by a relative error of at most 0.0041.
Values may be sent and summed in bfloat16 or wider, within the bound.
No kernel may reach another device: no remote copies, remote signals or barrier semaphores. Data moves between devices by JAX's collectives and lax.ppermute only.
A program may use at most 192 MiB of HBM per device.

v0:
```python
import jax
import jax.numpy as jnp
from jax import lax
from jax.sharding import PartitionSpec as P

BS = 32
KS = 8
RB = 64


def shifted(block, axis, distance):
    devices = range(lax.axis_size(axis))
    route = [((i - distance) % len(devices), i) for i in devices]
    return lax.ppermute(block, axis, route)


def screen_density(density, block_mask):
    own_blocks = block_mask.shape[0]
    all_blocks = block_mask.shape[1]
    shaped = density.reshape(own_blocks, BS, all_blocks, BS)
    keeper = block_mask.astype(density.dtype)[:, None, :, None]
    return (shaped * keeper).reshape(density.shape)


def pick_slots(pair_slots, stacked, first_block):
    own_blocks = stacked.shape[1] // BS
    block_ids = first_block + jnp.arange(own_blocks, dtype=jnp.int32)
    matches = (pair_slots[:, :, None] == block_ids[None, None, :]).astype(jnp.bfloat16)
    shaped = stacked.reshape(2, own_blocks, BS, stacked.shape[2])
    return jnp.einsum("bkc,tcjn->tbkjn", matches, shaped, preferred_element_type=jnp.float32)


def per_device(tensor, live_blocks, occ_density, virt_density, occ_mask, virt_mask, pair_slots):
    own_rows = tensor.shape[0]
    own_width = tensor.shape[1]
    own_blocks = own_width // BS
    groups = live_blocks.shape[0]
    keeper = live_blocks.astype(jnp.bfloat16)[:, None, :, None, :, None]
    tensor_eff = (tensor.reshape(groups, RB, own_blocks, BS, KS, BS) * keeper).reshape(tensor.shape)
    stacked = jnp.stack(
        [screen_density(occ_density, occ_mask), screen_density(virt_density, virt_mask)]
    )
    ao_total = stacked.shape[2]
    cycle_size = lax.axis_size("ao")
    position = lax.axis_index("ao")

    def visit(turn_index, state):
        current, gathered_rows = state
        current = shifted(current, "ao", 1)
        source = (position - turn_index + cycle_size) % cycle_size
        return (current, gathered_rows + pick_slots(pair_slots, current, source * own_blocks))

    start_pick = pick_slots(pair_slots, stacked, position * own_blocks)
    unused, picked = lax.fori_loop(1, cycle_size, visit, (stacked, start_pick))
    picked = picked.astype(jnp.bfloat16)
    occ_rows = picked[0]
    virt_rows = picked[1]
    span_cols = min(128, ao_total)
    piece_count = ao_total // span_cols
    tensor_five = tensor_eff.reshape(own_rows, own_blocks, BS, KS, BS)
    occ_pieces = occ_rows.reshape(own_blocks, KS, BS, piece_count, span_cols)

    def occ_piece(piece_index):
        columns = lax.dynamic_index_in_dim(occ_pieces, piece_index, 3, keepdims=False)
        product = jnp.einsum(
            "pbikj,bkjl->lbip", tensor_five, columns, preferred_element_type=jnp.float32
        )
        return product.astype(jnp.bfloat16).reshape(span_cols, own_width, own_rows)

    half_occ = lax.map(occ_piece, jnp.arange(piece_count, dtype=jnp.int32)).reshape(
        ao_total, own_width, own_rows
    )
    half_occ_local = lax.all_to_all(half_occ, "ao", split_axis=0, concat_axis=1, tiled=True)

    def virt_piece(source_rows, piece_index):
        columns = lax.dynamic_slice_in_dim(virt_rows, piece_index * span_cols, span_cols, 3)
        product = jnp.einsum(
            "qbikj,bkjn->qbin", source_rows, columns, preferred_element_type=jnp.float32
        )
        return product.astype(jnp.bfloat16).reshape(source_rows.shape[0], own_width, span_cols)

    all_tensor = lax.all_gather(tensor_eff, "ri", axis=0, tiled=True)
    kept_rows = all_tensor.shape[0] // cycle_size
    source_rows = all_tensor
    polar_source_rows = source_rows.reshape(kept_rows * lax.axis_size("ao"), own_blocks, BS, KS, BS)

    def add_piece(piece_index, running):
        virt_part = virt_piece(polar_source_rows, piece_index)
        occ_part = lax.dynamic_slice_in_dim(half_occ_local, piece_index * span_cols, span_cols, 1)
        return running + jnp.einsum(
            "qln,lnp->qp", virt_part, occ_part, preferred_element_type=jnp.float32
        )

    polar_block = lax.psum_scatter(
        lax.fori_loop(
            0,
            piece_count,
            add_piece,
            jnp.zeros((polar_source_rows.shape[0], own_rows), jnp.float32),
        ),
        "ao",
        scatter_dimension=0,
        tiled=True,
    )
    return polar_block.T


def solution(mesh):
    placed = (
        P("ri", "ao", None),
        P("ri", "ao", None),
        P("ao", None),
        P("ao", None),
        P("ao", None),
        P("ao", None),
        P("ao", None),
    )
    return jax.shard_map(
        per_device, mesh=mesh, in_specs=placed, out_specs=P("ri", "ao"), check_vma=False
    )
```

profile of v0, /device:TPU:0, one launch (start us, length us, event | category | flops | bytes accessed | tf_op | source)
XLA Modules:
  0.0 228.5 jit_solution(457382478721264577)
XLA Ops:
  6.5 0.7 convert_element_type.41
  7.7 3.1 %broadcast_multiply_fusion.1 = bf16[128,32,256]{2,1,0:T(8,128)(2,1)} fusion(bf16[128,32,256]{2,1,0:T(8,128)(2,1)} %param.13, bf16[128,256]{1,0:T(8,128)(2,1)S(1)} %copy.41), kind=kLoop, calls=%fused_computation.23 | loop fusion | flops 1048576 | bytes 4259840 | tf_op jit(solution)/shard_map/mul | solution.py:39
  10.9 1.6 copy-done.1
  12.5 3.1 %copy.43 = bf16[128,32,256]{0,2,1:T(8,128)(2,1)} copy(bf16[128,32,256]{2,1,0:T(8,128)(2,1)S(1)} %copy-done.1) | data formatting | bytes 4194304 | tf_op args[0]
  16.1 32.0 %while.41 = (s32[]{:T(128)}, bf16[2,32,256]{2,1,0:T(8,128)(2,1)S(1)}, f32[2,1,8,32,256]{4,3,2,1,0:T(8,128)S(1)}, s32[]{:T(128)}, s32[1,8]{1,0:T(1,128)S(1)}, /*index=5*/s32[]{:T(128)}, s32[]{:T(128)}, s32[]{:T(128)}, s32[]{:T(128)}) while((s32[]{:T(128)}, bf16[2,32,256]{2,1,0:T(8,128)(2,1)S(1)}, f32[2,1,8,32,256]{4,3,2,1,0:T(8,128)S(1)}, ...), condition=%wide.region_1.2_spmd, body=%wide.region_0.1_spmd.sunk | while | flops 278559 | bytes 1409390 | solution.py:54
  16.6 4.5 %collective-permute-done = bf16[2,32,256]{2,1,0:T(8,128)(2,1)S(1)} collective-permute-done((bf16[2,32,256]{2,1,0:T(8,128)(2,1)S(1)}, bf16[2,32,256]{2,1,0:T(8,128)(2,1)S(1)}, u32[]{:S(2)}, u32[]{:S(2)}) %collective-permute-start) | collective-permute-done | bytes 32800 | tf_op jit(solution)/shard_map/while/body/eval_jaxpr/ppermute | solution.py:14
  21.3 4.2 %collective-permute-done = bf16[2,32,256]{2,1,0:T(8,128)(2,1)S(1)} collective-permute-done((bf16[2,32,256]{2,1,0:T(8,128)(2,1)S(1)}, bf16[2,32,256]{2,1,0:T(8,128)(2,1)S(1)}, u32[]{:S(2)}, u32[]{:S(2)}) %collective-permute-start) | collective-permute-done | bytes 32800 | tf_op jit(solution)/shard_map/while/body/eval_jaxpr/ppermute | solution.py:14
  25.8 4.2 %collective-permute-done = bf16[2,32,256]{2,1,0:T(8,128)(2,1)S(1)} collective-permute-done((bf16[2,32,256]{2,1,0:T(8,128)(2,1)S(1)}, bf16[2,32,256]{2,1,0:T(8,128)(2,1)S(1)}, u32[]{:S(2)}, u32[]{:S(2)}) %collective-permute-start) | collective-permute-done | bytes 32800 | tf_op jit(solution)/shard_map/while/body/eval_jaxpr/ppermute | solution.py:14
  30.3 4.2 %collective-permute-done = bf16[2,32,256]{2,1,0:T(8,128)(2,1)S(1)} collective-permute-done((bf16[2,32,256]{2,1,0:T(8,128)(2,1)S(1)}, bf16[2,32,256]{2,1,0:T(8,128)(2,1)S(1)}, u32[]{:S(2)}, u32[]{:S(2)}) %collective-permute-start) | collective-permute-done | bytes 32800 | tf_op jit(solution)/shard_map/while/body/eval_jaxpr/ppermute | solution.py:14
  34.8 4.2 %collective-permute-done = bf16[2,32,256]{2,1,0:T(8,128)(2,1)S(1)} collective-permute-done((bf16[2,32,256]{2,1,0:T(8,128)(2,1)S(1)}, bf16[2,32,256]{2,1,0:T(8,128)(2,1)S(1)}, u32[]{:S(2)}, u32[]{:S(2)}) %collective-permute-start) | collective-permute-done | bytes 32800 | tf_op jit(solution)/shard_map/while/body/eval_jaxpr/ppermute | solution.py:14
  39.2 4.2 %collective-permute-done = bf16[2,32,256]{2,1,0:T(8,128)(2,1)S(1)} collective-permute-done((bf16[2,32,256]{2,1,0:T(8,128)(2,1)S(1)}, bf16[2,32,256]{2,1,0:T(8,128)(2,1)S(1)}, u32[]{:S(2)}, u32[]{:S(2)}) %collective-permute-start) | collective-permute-done | bytes 32800 | tf_op jit(solution)/shard_map/while/body/eval_jaxpr/ppermute | solution.py:14
  43.7 4.2 %collective-permute-done = bf16[2,32,256]{2,1,0:T(8,128)(2,1)S(1)} collective-permute-done((bf16[2,32,256]{2,1,0:T(8,128)(2,1)S(1)}, bf16[2,32,256]{2,1,0:T(8,128)(2,1)S(1)}, u32[]{:S(2)}, u32[]{:S(2)}) %collective-permute-start) | collective-permute-done | bytes 32800 | tf_op jit(solution)/shard_map/while/body/eval_jaxpr/ppermute | solution.py:14
  48.3 1.7 broadcast_multiply_fusion
  50.1 12.4 %while.42 = (s32[]{:T(128)}, bf16[2,128,32,128]{3,2,1,0:T(8,128)(2,1)}, s32[2]{0:T(128)S(1)}, bf16[1,8,32,2,128]{4,2,1,3,0:T(8,128)(2,1)S(1)}, bf16[128,1,32,8,3...) while((s32[]{:T(128)}, bf16[2,128,32,128]{3,2,1,0:T(8,128)(2,1)}, s32[2]{0:T(128)S(1)}, ...), condition=%wide.region_3.4_spmd, body=%wide.region_2.3_spmd.sunk | while | flops 268959744 | bytes 22085836 | solution.py:70
  50.1 0.6 dynamic_slice.40
  53.1 1.1 copy-done.3
  54.3 0.7 copy_dynamic-update-slice_fusion.2
  55.0 1.3 copy-done.4
  59.3 1.1 copy-done.3
  60.4 0.7 copy_dynamic-update-slice_fusion.2
  61.2 1.3 copy-done.4
  62.5 3.6 %all-to-all-start = ((bf16[256,32,128]{2,1,0:T(8,128)(2,1)}), bf16[256,32,128]{2,1,0:T(8,128)(2,1)S(1)}, u32[]{:S(2)}, u32[]{:S(2)}) async-start(bf16[256,32,128]{2,1,0:T(8,128)(2,1)} %bitcast.132), calls=%async_computation | async-start | bytes 4194304 | tf_op jit(solution)/shard_map/all_to_all | solution.py:73
  66.2 26.5 %all-to-all-done = bf16[256,32,128]{2,1,0:T(8,128)(2,1)S(1)} async-done(((bf16[256,32,128]{2,1,0:T(8,128)(2,1)}), bf16[256,32,128]{2,1,0:T(8,128)(2,1)S(1)}, u32[]{:S(2)}, u32[]{:S(2)}) %all-to-all-start) | async-done | bytes 2097184 | tf_op jit(solution)/shard_map/all_to_all | solution.py:73
  92.7 1.3 copy-done.2
  94.0 2.2 copy.47
  96.3 67.1 %all-gather.2.cloned.1.call-done = bf16[512,32,256]{2,1,0:T(8,128)(2,1)} async-done(((bf16[128,32,256]{2,1,0:T(8,128)(2,1)}), bf16[512,32,256]{2,1,0:T(8,128)(2,1)}) %all-gather.2.cloned.1.call-update) | async-done | bytes 8388624 | tf_op jit(solution)/shard_map/all_gather | solution.py:82
  163.4 13.8 %copy.42 = bf16[512,32,256]{0,2,1:T(8,128)(2,1)} copy(bf16[512,32,256]{2,1,0:T(8,128)(2,1)} %all-gather.2.cloned.1.call-done) | data formatting | bytes 16777216 | tf_op jit(solution)/shard_map/all_gather | solution.py:82
  177.2 11.8 %while.43 = (s32[]{:T(128)}, f32[512,128]{1,0:T(8,128)S(1)}, bf16[1,8,32,256]{3,2,1,0:T(8,128)(2,1)S(1)}, bf16[512,1,32,8,32]{0,4,3,2,1:T(8,128)(2,1)}, bf16[32,...) while((s32[]{:T(128)}, f32[512,128]{1,0:T(8,128)S(1)}, ...), condition=%wide.region_5.6_spmd.clone, body=%wide.region_4.5_spmd.clone.sunk | while | flops 1612840960 | bytes 10028700 | solution.py:95
  177.2 5.9 %fusion.57 = f32[512,128]{1,0:T(8,128)S(1)} fusion(bf16[512,1,32,8,32]{0,4,3,2,1:T(8,128)(2,1)} %get-tuple-element.511, bf16[32,256,128]{2,1,0:T(8,128)(2,1)S(1)} %get-tuple-element.512, s32[]{:T(128)S(6)} %select_n.38, f32[512,128]{1,0:T(8,128)S(1)} %get-tuple-element.500, pred[]{:T(512)S(6)} %compare.4, ...), kind=kOutput, calls=%fused_computation.17.clone.1 | convolution fusion | flops 1612840960 | bytes 10028544 | tf_op jit(solution)/shard_map/while/body/eval_jaxpr/qln,lnp->qp/dot_general | solution.py:90
  183.1 5.9 %fusion.57 = f32[512,128]{1,0:T(8,128)S(1)} fusion(bf16[512,1,32,8,32]{0,4,3,2,1:T(8,128)(2,1)} %get-tuple-element.511, bf16[32,256,128]{2,1,0:T(8,128)(2,1)S(1)} %get-tuple-element.512, s32[]{:T(128)S(6)} %select_n.38, f32[512,128]{1,0:T(8,128)S(1)} %get-tuple-element.500, pred[]{:T(512)S(6)} %compare.4, ...), kind=kOutput, calls=%fused_computation.17.clone.1 | convolution fusion | flops 1612840960 | bytes 10028544 | tf_op jit(solution)/shard_map/while/body/eval_jaxpr/qln,lnp->qp/dot_general | solution.py:90
  189.0 0.7 copy-done
  189.7 32.0 %reduce-scatter.2.cloned.1.call-done = f32[64,128]{1,0:T(8,128)} async-done(((f32[512,128]{1,0:T(8,128)}), f32[64,128]{1,0:T(8,128)}) %reduce-scatter.2.cloned.1.call-update) | async-done | bytes 32784 | tf_op jit(solution)/shard_map/reduce_scatter | solution.py:94
  (82 shorter events, 4.8 us)
Async XLA Ops:
  6.5 156.8 %all-gather.2.cloned.1.call-start = ((), (), s32[]{:S(2)}) async-start(), calls=%async_computation.2 | async-start | bytes 10485760 | tf_op jit(solution)/shard_map/all_gather | solution.py:82
  10.8 1.6 copy-start.1
  12.4 3.1 %copy-start.7 = (s32[1,8]{1,0:T(1,128)S(1)}, s32[1,8]{1,0:T(1,128)}, u32[]{:S(2)}) copy-start(s32[1,8]{1,0:T(1,128)} %param.18) | copy-start | bytes 100
  12.4 3.3 %copy-start.8 = (s32[1,8]{1,0:T(1,128)S(1)}, s32[1,8]{1,0:T(1,128)}, u32[]{:S(2)}) copy-start(s32[1,8]{1,0:T(1,128)} %param.17) | copy-start | bytes 100
  12.4 3.5 %copy-start.5 = (bf16[32,256]{1,0:T(8,128)(2,1)S(1)}, bf16[32,256]{1,0:T(8,128)(2,1)}, u32[]{:S(2)}) copy-start(bf16[32,256]{1,0:T(8,128)(2,1)} %param.16) | copy-start | bytes 49156
  12.4 3.5 %copy-start.6 = (bf16[32,256]{1,0:T(8,128)(2,1)S(1)}, bf16[32,256]{1,0:T(8,128)(2,1)}, u32[]{:S(2)}) copy-start(bf16[32,256]{1,0:T(8,128)(2,1)} %param.15) | copy-start | bytes 49156
  12.4 3.5 %copy-start.9 = (s32[1,8]{1,0:T(1,128)S(1)}, s32[1,8]{1,0:T(1,128)}, u32[]{:S(2)}) copy-start(s32[1,8]{1,0:T(1,128)} %param.19) | copy-start | bytes 100
  16.1 5.0 %collective-permute-start = (bf16[2,32,256]{2,1,0:T(8,128)(2,1)S(1)}, bf16[2,32,256]{2,1,0:T(8,128)(2,1)S(1)}, u32[]{:S(2)}, u32[]{:S(2)}) collective-permute-start(bf16[2,32,256]{2,1,0:T(8,128)(2,1)S(1)} %get-tuple-element.449), channel_id=1, source_target_pairs={{7,0},{0,1},{1,2},{2,3},{3,4},{4,5},{5,6},{6,7},{15,8},{8,9},{9,10... | collective-permute-start | bytes 98312 | tf_op jit(solution)/shard_map/while/body/eval_jaxpr/ppermute | solution.py:14
  21.2 4.3 %collective-permute-start = (bf16[2,32,256]{2,1,0:T(8,128)(2,1)S(1)}, bf16[2,32,256]{2,1,0:T(8,128)(2,1)S(1)}, u32[]{:S(2)}, u32[]{:S(2)}) collective-permute-start(bf16[2,32,256]{2,1,0:T(8,128)(2,1)S(1)} %get-tuple-element.449), channel_id=1, source_target_pairs={{7,0},{0,1},{1,2},{2,3},{3,4},{4,5},{5,6},{6,7},{15,8},{8,9},{9,10... | collective-permute-start | bytes 98312 | tf_op jit(solution)/shard_map/while/body/eval_jaxpr/ppermute | solution.py:14
  25.7 4.3 %collective-permute-start = (bf16[2,32,256]{2,1,0:T(8,128)(2,1)S(1)}, bf16[2,32,256]{2,1,0:T(8,128)(2,1)S(1)}, u32[]{:S(2)}, u32[]{:S(2)}) collective-permute-start(bf16[2,32,256]{2,1,0:T(8,128)(2,1)S(1)} %get-tuple-element.449), channel_id=1, source_target_pairs={{7,0},{0,1},{1,2},{2,3},{3,4},{4,5},{5,6},{6,7},{15,8},{8,9},{9,10... | collective-permute-start | bytes 98312 | tf_op jit(solution)/shard_map/while/body/eval_jaxpr/ppermute | solution.py:14
  30.2 4.3 %collective-permute-start = (bf16[2,32,256]{2,1,0:T(8,128)(2,1)S(1)}, bf16[2,32,256]{2,1,0:T(8,128)(2,1)S(1)}, u32[]{:S(2)}, u32[]{:S(2)}) collective-permute-start(bf16[2,32,256]{2,1,0:T(8,128)(2,1)S(1)} %get-tuple-element.449), channel_id=1, source_target_pairs={{7,0},{0,1},{1,2},{2,3},{3,4},{4,5},{5,6},{6,7},{15,8},{8,9},{9,10... | collective-permute-start | bytes 98312 | tf_op jit(solution)/shard_map/while/body/eval_jaxpr/ppermute | solution.py:14
  34.7 4.3 %collective-permute-start = (bf16[2,32,256]{2,1,0:T(8,128)(2,1)S(1)}, bf16[2,32,256]{2,1,0:T(8,128)(2,1)S(1)}, u32[]{:S(2)}, u32[]{:S(2)}) collective-permute-start(bf16[2,32,256]{2,1,0:T(8,128)(2,1)S(1)} %get-tuple-element.449), channel_id=1, source_target_pairs={{7,0},{0,1},{1,2},{2,3},{3,4},{4,5},{5,6},{6,7},{15,8},{8,9},{9,10... | collective-permute-start | bytes 98312 | tf_op jit(solution)/shard_map/while/body/eval_jaxpr/ppermute | solution.py:14
  39.1 4.3 %collective-permute-start = (bf16[2,32,256]{2,1,0:T(8,128)(2,1)S(1)}, bf16[2,32,256]{2,1,0:T(8,128)(2,1)S(1)}, u32[]{:S(2)}, u32[]{:S(2)}) collective-permute-start(bf16[2,32,256]{2,1,0:T(8,128)(2,1)S(1)} %get-tuple-element.449), channel_id=1, source_target_pairs={{7,0},{0,1},{1,2},{2,3},{3,4},{4,5},{5,6},{6,7},{15,8},{8,9},{9,10... | collective-permute-start | bytes 98312 | tf_op jit(solution)/shard_map/while/body/eval_jaxpr/ppermute | solution.py:14
  43.6 4.3 %collective-permute-start = (bf16[2,32,256]{2,1,0:T(8,128)(2,1)S(1)}, bf16[2,32,256]{2,1,0:T(8,128)(2,1)S(1)}, u32[]{:S(2)}, u32[]{:S(2)}) collective-permute-start(bf16[2,32,256]{2,1,0:T(8,128)(2,1)S(1)} %get-tuple-element.449), channel_id=1, source_target_pairs={{7,0},{0,1},{1,2},{2,3},{3,4},{4,5},{5,6},{6,7},{15,8},{8,9},{9,10... | collective-permute-start | bytes 98312 | tf_op jit(solution)/shard_map/while/body/eval_jaxpr/ppermute | solution.py:14
  52.6 1.6 copy-start.3
  55.0 1.3 copy-start.4
  58.9 1.6 copy-start.3
  61.2 1.3 copy-start.4
  62.5 30.2 %all-to-all-start = ((bf16[256,32,128]{2,1,0:T(8,128)(2,1)}), bf16[256,32,128]{2,1,0:T(8,128)(2,1)S(1)}, u32[]{:S(2)}, u32[]{:S(2)}) async-start(bf16[256,32,128]{2,1,0:T(8,128)(2,1)} %bitcast.132), calls=%async_computation | async-start | bytes 4194304 | tf_op jit(solution)/shard_map/all_to_all | solution.py:73
  66.1 155.6 %reduce-scatter.2.cloned.1.call-start = ((), (), s32[]{:S(2)}) async-start(), calls=%async_computation.3 | async-start | bytes 294912 | tf_op jit(solution)/shard_map/reduce_scatter | solution.py:94
  92.7 1.3 copy-start.2
  189.0 0.7 copy-start
Sparse Core Ops, SparseCore 0:
  11.0 152.3 all-gather.1
  189.8 31.8 reduce-scatter.1
where the time goes:
time: 229 us
  waiting for transfers between devices  155 us (68%)
  local copies, waits for them, and re-layouts  31.3 us (14%)
  between operations  13.6 us (6%)
  matrix products  12.7 us (6%)
  other arithmetic  6.8 us (3%)
  starting transfers between devices  4.5 us (2%)
  loops' own time  4.39 us (2%)
    all_gather x1, waiting for transfers between devices, per_device(): all_tensor = lax.all_gather(tensor_eff, 'ri', axis=0, tiled=True)  67.1 us
    reduce_scatter x1, waiting for transfers between devices, per_device(): lax.psum_scatter(lax.fori_loop(0, piece_count, add_piece, jnp.zeros((pola...  32 us
    ppermute x7, waiting for transfers between devices, shifted(): return lax.ppermute(block, axis, route)  29.6 us
    all_to_all x1, waiting for transfers between devices, per_device(): lax.all_to_all(half_occ, 'ao', split_axis=0, concat_axis=1, tiled=True)  26.5 us
    all_gather x1, local copies, waits for them, and re-layouts, per_device(): all_tensor = lax.all_gather(tensor_eff, 'ri', axis=0, tiled=True)  13.8 us
    dot_general x2, matrix products, add_piece(): jnp.einsum('qln,lnp->qp', virt_part, occ_part, preferred_element_type=jnp...  11.8 us
    unnamed x17, local copies, waits for them, and re-layouts  6.7 us
    while x15, local copies, waits for them, and re-layouts  4.9 us
  transfers between devices with their start and end apart: 10, of which 10 were waited for; matrix products, arithmetic and copies ran while one was open for 5% of the time, Pallas kernels for 0%

commit v1 on v0

v1 whole, which is shorter than its diff:
```python
import jax
import jax.numpy as jnp
from jax import lax
from jax.sharding import PartitionSpec as P

BS = 32
KS = 8
RB = 64


def screen_density(density, block_mask):
    own_blocks = block_mask.shape[0]
    all_blocks = block_mask.shape[1]
    shaped = density.reshape(own_blocks, BS, all_blocks, BS)
    keeper = block_mask.astype(density.dtype)[:, None, :, None]
    return (shaped * keeper).reshape(density.shape)


def pair_routes(size):
    routes = []
    for dist in range(1, size // 2 + 1):
        if 2 * dist < size:
            route = [(r, (r + dist) % size) for r in range(size)]
        else:
            route = []
            for i in range(size // 2):
                if i % 2 == 0:
                    route.append((i, i + dist))
                else:
                    route.append((i + dist, i))
        partner = list(range(size))
        for src, dst in route:
            partner[dst] = src
        routes.append((route, partner))
    return routes


def half_products(slab, live, rhs):
    rows = slab.shape[0]
    groups = rows // RB
    keep = jnp.repeat(live[:, 0, :].astype(jnp.bfloat16), BS, axis=1)
    rhs_masked = rhs[None] * keep[:, None, :, None]
    shaped = slab.reshape(groups, RB * BS, KS * BS)
    out = jnp.einsum(
        "gmk,gdkl->gdml", shaped, rhs_masked, preferred_element_type=jnp.float32
    ).astype(jnp.bfloat16)
    ao_total = rhs.shape[2]
    occ_half = out[:, 0].reshape(rows, BS, ao_total)
    virt_half = out[:, 1].reshape(rows, BS, ao_total)
    return occ_half, virt_half


def swap_local(block, cycle_size):
    rows = block.shape[0]
    ao_total = block.shape[2]
    sent = block.reshape(rows, BS, cycle_size, BS).transpose(2, 0, 3, 1)
    got = lax.all_to_all(sent, "ao", 0, 0, tiled=True)
    return got.transpose(1, 2, 0, 3).reshape(rows, BS, ao_total)


def add_block(total, part, plane, col_block):
    rows = part.shape[0]
    at = (plane, jnp.int32(0), col_block * rows)
    here = lax.dynamic_slice(total, at, (1, rows, part.shape[1]))
    return lax.dynamic_update_slice(total, here + part[None], at)


def per_device(tensor, live_blocks, occ_density, virt_density, occ_mask, virt_mask, pair_slots):
    rows = tensor.shape[0]
    own_width = tensor.shape[1]
    assert own_width == BS
    planes = lax.axis_size("ri")
    cycle_size = lax.axis_size("ao")
    plane = lax.axis_index("ri")

    routes = pair_routes(planes)
    received = [
        (lax.ppermute(tensor, "ri", route), lax.ppermute(live_blocks, "ri", route), partner)
        for route, partner in routes
    ]

    stacked = jnp.stack(
        [screen_density(occ_density, occ_mask), screen_density(virt_density, virt_mask)]
    )
    full = lax.all_gather(stacked, "ao", axis=1, tiled=True)
    ao_total = full.shape[2]
    all_blocks = ao_total // BS
    picked = full.reshape(2, all_blocks, BS, ao_total)[:, pair_slots[0]]
    rhs = picked.reshape(2, KS * BS, ao_total)

    occ_own, virt_own = half_products(tensor, live_blocks, rhs)
    occ_own_t = swap_local(occ_own, cycle_size)
    virt_own_t = swap_local(virt_own, cycle_size)

    total = jnp.zeros((planes, rows, planes * rows), jnp.float32)
    diag = jnp.einsum("pln,qln->pq", occ_own_t, virt_own, preferred_element_type=jnp.float32)
    total = add_block(total, diag, plane, plane)
    for slab, live, partner in received:
        other = jnp.array(partner, jnp.int32)[plane]
        occ_other, virt_other = half_products(slab, live, rhs)
        mine_theirs = jnp.einsum(
            "pln,qln->pq", occ_own_t, virt_other, preferred_element_type=jnp.float32
        )
        theirs_mine = jnp.einsum(
            "pnl,qnl->pq", occ_other, virt_own_t, preferred_element_type=jnp.float32
        )
        total = add_block(total, mine_theirs, plane, other)
        total = add_block(total, theirs_mine, other, plane)

    in_plane = lax.psum_scatter(total, "ao", scatter_dimension=2, tiled=True)
    return lax.psum_scatter(in_plane, "ri", scatter_dimension=0, tiled=True)[0]


def solution(mesh):
    placed = (
        P("ri", "ao", None),
        P("ri", "ao", None),
        P("ao", None),
        P("ao", None),
        P("ao", None),
        P("ao", None),
        P("ao", None),
    )
    return jax.shard_map(
        per_device, mesh=mesh, in_specs=placed, out_specs=P("ri", "ao"), check_vma=False
    )
```

time: 229 us -> 309 us (1.35)
  local copies, waits for them, and re-layouts: 31.3 us -> 77.9 us
  starting transfers between devices: 4.5 us -> 20.3 us
  blocking collectives: 0 us -> 10.8 us
  matrix products: 12.7 us -> 21.8 us
  between operations: 13.6 us -> 19.4 us
  loops' own time: 4.39 us -> 0 us
  other arithmetic: 6.8 us -> 3.43 us
    all_gather x1 -> x0, waiting for transfers between devices: 67.1 us -> none  [per_device(): all_tensor = lax.all_gather(tensor_eff, 'ri', axis=0, tiled=True)]
    unnamed x2 -> x3, waiting for transfers between devices: 0.03 us -> 54.1 us
    ppermute x7 -> x4, waiting for transfers between devices: 29.6 us -> 77.1 us  [the longest x2 77.1 us: per_device(): lax.ppermute(live_blocks, 'ri', route)]
    transpose x0 -> x2, local copies, waits for them, and re-layouts: none -> 26.3 us  [swap_local(): sent = block.reshape(rows, BS, cycle_size, BS).transpose(2, 0, 3, 1)]
    slice x1 -> x9, local copies, waits for them, and re-layouts: 0.02 us -> 24.8 us  [the longest x4 13.3 us: half_products(): virt_half = out[:, 1].reshape(rows, BS, ao_total)]
    all_to_all x1 -> x2, waiting for transfers between devices: 26.5 us -> 4.42 us  [swap_local(): got = lax.all_to_all(sent, 'ao', 0, 0, tiled=True)]
    all_gather x1 -> x0, local copies, waits for them, and re-layouts: 13.8 us -> none  [per_device(): all_tensor = lax.all_gather(tensor_eff, 'ri', axis=0, tiled=True)]
    reduce_scatter x1, waiting for transfers between devices: 32 us -> 18.9 us  [per_device(): return lax.psum_scatter(in_plane, 'ri', scatter_dimension=0, tiled=True)[0]]
  transfers between devices with their start and end apart: 10 -> 8, of which waited for: 10 -> 4; matrix products, arithmetic and copies ran while one was open for 5% -> 15% of each run, Pallas kernels for 0% -> 0%
where the time goes in v1:
time: 309 us; the launch traced here: 308 us
  waiting for transfers between devices  155 us (50%)
  local copies, waits for them, and re-layouts  77.9 us (25%)
  matrix products  21.8 us (7%)
  starting transfers between devices  20.3 us (7%)
  between operations  19.4 us (6%)
  blocking collectives  10.8 us (3%)
  other arithmetic  3.43 us (1%)
    ppermute x2, waiting for transfers between devices, per_device(): lax.ppermute(live_blocks, 'ri', route)  77.1 us
    unnamed x3, waiting for transfers between devices  54.1 us
    transpose x2, local copies, waits for them, and re-layouts, swap_local(): sent = block.reshape(rows, BS, cycle_size, BS).transpose(2, 0, 3, 1)  26.3 us
    reduce_scatter x1, waiting for transfers between devices, per_device(): return lax.psum_scatter(in_plane, 'ri', scatter_dimension=0, tiled=True)[0]  18.9 us
    slice x4, local copies, waits for them, and re-layouts, half_products(): virt_half = out[:, 1].reshape(rows, BS, ao_total)  13.3 us
    another operation x2, local copies, waits for them, and re-layouts, swap_local(): sent = block.reshape(rows, BS, cycle_size, BS).transpose(2, 0, 3, 1)  12.5 us
    slice x5, local copies, waits for them, and re-layouts, half_products(): occ_half = out[:, 0].reshape(rows, BS, ao_total)  11.5 us
    all_gather x1, blocking collectives, per_device(): full = lax.all_gather(stacked, 'ao', axis=1, tiled=True)  10.8 us
  transfers between devices with their start and end apart: 8, of which 4 were waited for; matrix products, arithmetic and copies ran while one was open for 15% of the time, Pallas kernels for 0%

profile of v1, /device:TPU:0, one launch (start us, length us, event | category | flops | bytes accessed | tf_op | source)
XLA Modules:
  0.0 308.2 jit_solution(7075712475799778831)
XLA Ops:
  8.9 10.8 %all_gather.3 = bf16[2,256,256]{2,1,0:T(8,128)(2,1)S(1)} all-gather(bf16[2,32,256]{2,1,0:T(8,128)(2,1)S(1)} %pad_maximum_fusion), channel_id=1, replica_groups=mesh['ri'=4,'ao'=8] {'ao'}, dimensions={1}, use_global_device_ids=true | all-gather | bytes 294912 | tf_op jit(solution)/shard_map/all_gather | solution.py:85
  22.0 2.9 convert_bitcast_fusion.2
  24.8 2.6 fusion.64
  27.4 2.8 copy.80
  30.3 6.2 %reshape_reshape_squeeze.6 = bf16[128,32,8,32]{3,2,1,0:T(8,128)(2,1)} reshape(bf16[2,1,2048,256]{3,2,0,1:T(8,128)(2,1)S(1)} %copy.80) | data formatting | bytes 4194304 | tf_op jit(solution)/shard_map/reshape;reshape;squeeze | solution.py:56
  36.5 13.1 %copy.81 = bf16[8,128,32,32]{1,3,2,0:T(8,128)(2,1)} copy(bf16[8,128,32,32]{2,0,3,1:T(8,128)(2,1)} %bitcast.111) | data formatting | bytes 4194304 | tf_op jit(solution)/shard_map/transpose | solution.py:56
  49.7 4.4 %all-to-all-start = ((bf16[8,128,32,32]{1,3,2,0:T(8,128)(2,1)}), bf16[8,128,32,32]{1,3,2,0:T(8,128)(2,1)}, u32[]{:S(2)}, u32[]{:S(2)}) async-start(bf16[8,128,32,32]{1,3,2,0:T(8,128)(2,1)} %copy.81), calls=%async_computation | async-start | bytes 4194304 | tf_op jit(solution)/shard_map/all_to_all | solution.py:57
  54.1 2.9 copy.83
  56.9 6.2 %reshape_reshape_squeeze.7 = bf16[128,32,8,32]{3,2,1,0:T(8,128)(2,1)} reshape(bf16[2,1,2048,256]{3,2,0,1:T(8,128)(2,1)S(1)} %copy.83) | data formatting | bytes 4194304 | tf_op jit(solution)/shard_map/reshape;reshape;squeeze | solution.py:56
  63.2 13.1 %copy.91 = bf16[8,128,32,32]{1,3,2,0:T(8,128)(2,1)} copy(bf16[8,128,32,32]{2,0,3,1:T(8,128)(2,1)} %bitcast.112) | data formatting | bytes 4194304 | tf_op jit(solution)/shard_map/transpose | solution.py:56
  76.3 4.4 %all-to-all-done = bf16[8,128,32,32]{1,3,2,0:T(8,128)(2,1)} async-done(((bf16[8,128,32,32]{1,3,2,0:T(8,128)(2,1)}), bf16[8,128,32,32]{1,3,2,0:T(8,128)(2,1)}, u32[]{:S(2)}, u32[]{:S(2)}) %all-to-all-start) | async-done | bytes 2097184 | tf_op jit(solution)/shard_map/all_to_all | solution.py:57
  80.7 4.4 %all-to-all-start.1 = ((bf16[8,128,32,32]{1,3,2,0:T(8,128)(2,1)}), bf16[8,128,32,32]{1,3,2,0:T(8,128)(2,1)}, u32[]{:S(2)}, u32[]{:S(2)}) async-start(bf16[8,128,32,32]{1,3,2,0:T(8,128)(2,1)} %copy.91), calls=%async_computation.1 | async-start | bytes 4194304 | tf_op jit(solution)/shard_map/all_to_all | solution.py:57
  85.1 1.6 collective-permute-start.1
  86.8 5.8 %collective-permute-start.3 = (bf16[128,32,256]{2,1,0:T(8,128)(2,1)}, bf16[128,32,256]{2,1,0:T(8,128)(2,1)}, u32[]{:S(2)}, u32[]{:S(2)}) collective-permute-start(bf16[128,32,256]{2,1,0:T(8,128)(2,1)} %param.9), channel_id=1, source_target_pairs={{0,16},{24,8},{1,17},{25,9},{2,18},{26,10},{3,19},{27,11},{4,20},{... | collective-permute-start | bytes 6291464 | tf_op jit(solution)/shard_map/ppermute | solution.py:78
  92.6 4.0 %collective-permute-start.2 = (s32[2,1,8]{2,1,0:T(1,128)S(1)}, s32[2,1,8]{2,1,0:T(1,128)S(1)}, u32[]{:S(2)}, u32[]{:S(2)}) collective-permute-start(s32[2,1,8]{2,1,0:T(1,128)S(1)} %copy-done.6), channel_id=1, source_target_pairs={{0,16},{24,8},{1,17},{25,9},{2,18},{26,10},{3,19},{27,11},{4,20},{... | collective-permute-start | bytes 200 | tf_op jit(solution)/shard_map/ppermute | solution.py:78
  103.0 77.1 %collective-permute-done = s32[2,1,8]{2,1,0:T(1,128)S(1)} collective-permute-done((s32[2,1,8]{2,1,0:T(1,128)S(1)}, s32[2,1,8]{2,1,0:T(1,128)S(1)}, u32[]{:S(2)}, u32[]{:S(2)}) %collective-permute-start) | collective-permute-done | bytes 96 | tf_op jit(solution)/shard_map/ppermute | solution.py:78
  180.4 3.6 %copy.82 = bf16[8,128,32,32]{1,3,0,2:T(8,128)(2,1)} copy(bf16[8,128,32,32]{1,3,2,0:T(8,128)(2,1)} %all-to-all-done) | data formatting | bytes 4194304 | tf_op jit(solution)/shard_map/all_to_all | solution.py:57
  183.9 3.7 %copy.92 = bf16[8,128,32,32]{1,3,0,2:T(8,128)(2,1)} copy(bf16[8,128,32,32]{1,3,2,0:T(8,128)(2,1)} %all-to-all-done.1) | data formatting | bytes 4194304 | tf_op jit(solution)/shard_map/all_to_all | solution.py:57
  187.8 2.8 fusion.13
  190.6 2.9 convert_bitcast_fusion.1
  193.5 1.8 fusion.63
  195.3 3.9 %copy.86 = bf16[2,1,2048,256]{3,2,0,1:T(8,128)(2,1)} copy(bf16[2,1,2048,256]{2,3,1,0:T(8,128)(2,1)} %get-tuple-element.8) | data formatting | bytes 4194304 | tf_op jit(solution)/shard_map/slice | solution.py:49
  199.3 2.5 copy.89
  201.8 2.9 convert_bitcast_fusion
  204.7 1.8 fusion.62
  206.4 3.9 %copy.95 = bf16[2,1,2048,256]{3,2,0,1:T(8,128)(2,1)} copy(bf16[2,1,2048,256]{2,3,1,0:T(8,128)(2,1)} %get-tuple-element.6) | data formatting | bytes 4194304 | tf_op jit(solution)/shard_map/slice | solution.py:49
  210.4 2.5 copy.98
  212.9 5.0 %fusion.22 = f32[4,128,512]{2,1,0:T(8,128)S(1)} fusion(f32[4,128,512]{2,1,0:T(8,128)S(1)} %fusion.13, s32[]{:T(128)S(6)} %select_n.43, s32[]{:T(128)S(6)} %select_n.45, bf16[128,32,256]{0,2,1:T(8,128)(2,1)} %bitcast.115, bf16[128,32,256]{2,1,0:T(8,128)(2,1)} %bitcast.120), kind=kOutput, calls=%fused_computation.18 | convolution fusion | flops 268451840 | bytes 4325384 | tf_op jit(solution)/shard_map/pln,qln->pq/dot_general | solution.py:101
  217.9 1.4 fusion.31
  220.1 2.6 fusion.40
  226.8 54.1 %all-reduce.3.cloned.1.call-done = f32[4,128,512]{1,0,2:T(4,128)} async-done(((f32[4,128,512]{1,0,2:T(4,128)}), f32[4,128,512]{1,0,2:T(4,128)}) %all-reduce.3.cloned.1.call-update) | async-done | bytes 1048592
  282.5 18.9 %reduce-scatter.2.cloned.1.call-done = f32[1,128,64]{1,2,0:T(8,128)} async-done(((f32[4,128,64]{1,2,0:T(8,128)}), f32[1,128,64]{1,2,0:T(8,128)}) %reduce-scatter.2.cloned.1.call-update) | async-done | bytes 32784 | tf_op jit(solution)/shard_map/reduce_scatter | solution.py:111
  (62 shorter events, 12.1 us)
Async XLA Ops:
  49.7 31.0 %all-to-all-start = ((bf16[8,128,32,32]{1,3,2,0:T(8,128)(2,1)}), bf16[8,128,32,32]{1,3,2,0:T(8,128)(2,1)}, u32[]{:S(2)}, u32[]{:S(2)}) async-start(bf16[8,128,32,32]{1,3,2,0:T(8,128)(2,1)} %copy.81), calls=%async_computation | async-start | bytes 4194304 | tf_op jit(solution)/shard_map/all_to_all | solution.py:57
  76.3 16.3 %copy-start.6 = (s32[2,1,8]{2,1,0:T(1,128)S(1)}, s32[2,1,8]{2,1,0:T(1,128)}, u32[]{:S(2)}) copy-start(s32[2,1,8]{2,1,0:T(1,128)} %param.10) | copy-start | bytes 196
  76.3 20.3 %copy-start.9 = (s32[4]{0:T(128)S(1)}, s32[4]{0:T(128)}, u32[]{:S(2)}) copy-start(s32[4]{0:T(128)} %constant.22.clone) | copy-start | bytes 52
  76.3 22.9 %copy-start.8 = (s32[4]{0:T(128)S(1)}, s32[4]{0:T(128)}, u32[]{:S(2)}) copy-start(s32[4]{0:T(128)} %constant.23.clone) | copy-start | bytes 52
  80.7 103.2 %all-to-all-start.1 = ((bf16[8,128,32,32]{1,3,2,0:T(8,128)(2,1)}), bf16[8,128,32,32]{1,3,2,0:T(8,128)(2,1)}, u32[]{:S(2)}, u32[]{:S(2)}) async-start(bf16[8,128,32,32]{1,3,2,0:T(8,128)(2,1)} %copy.91), calls=%async_computation.1 | async-start | bytes 4194304 | tf_op jit(solution)/shard_map/all_to_all | solution.py:57
  85.1 195.8 %all-reduce.3.cloned.1.call-start = ((), (), s32[]{:S(2)}) async-start(), calls=%async_computation.4 | async-start | bytes 2097152
  85.1 105.5 %collective-permute-start.1 = (bf16[128,32,256]{2,1,0:T(8,128)(2,1)}, bf16[128,32,256]{2,1,0:T(8,128)(2,1)}, u32[]{:S(2)}, u32[]{:S(2)}) collective-permute-start(bf16[128,32,256]{2,1,0:T(8,128)(2,1)} %param.9), channel_id=1, source_target_pairs={{0,8},{8,16},{16,24},{24,0},{1,9},{9,17},{17,25},{25,1},{2,10},{10... | collective-permute-start | bytes 6291464 | tf_op jit(solution)/shard_map/ppermute | solution.py:78
  86.8 115.0 %collective-permute-start.3 = (bf16[128,32,256]{2,1,0:T(8,128)(2,1)}, bf16[128,32,256]{2,1,0:T(8,128)(2,1)}, u32[]{:S(2)}, u32[]{:S(2)}) collective-permute-start(bf16[128,32,256]{2,1,0:T(8,128)(2,1)} %param.9), channel_id=1, source_target_pairs={{0,16},{24,8},{1,17},{25,9},{2,18},{26,10},{3,19},{27,11},{4,20},{... | collective-permute-start | bytes 6291464 | tf_op jit(solution)/shard_map/ppermute | solution.py:78
  92.6 87.4 %collective-permute-start = (s32[2,1,8]{2,1,0:T(1,128)S(1)}, s32[2,1,8]{2,1,0:T(1,128)S(1)}, u32[]{:S(2)}, u32[]{:S(2)}) collective-permute-start(s32[2,1,8]{2,1,0:T(1,128)S(1)} %copy-done.6), channel_id=1, source_target_pairs={{0,8},{8,16},{16,24},{24,0},{1,9},{9,17},{17,25},{25,1},{2,10},{10... | collective-permute-start | bytes 200 | tf_op jit(solution)/shard_map/ppermute | solution.py:78
  92.6 87.6 %collective-permute-start.2 = (s32[2,1,8]{2,1,0:T(1,128)S(1)}, s32[2,1,8]{2,1,0:T(1,128)S(1)}, u32[]{:S(2)}, u32[]{:S(2)}) collective-permute-start(s32[2,1,8]{2,1,0:T(1,128)S(1)} %copy-done.6), channel_id=1, source_target_pairs={{0,16},{24,8},{1,17},{25,9},{2,18},{26,10},{3,19},{27,11},{4,20},{... | collective-permute-start | bytes 200 | tf_op jit(solution)/shard_map/ppermute | solution.py:78
  183.9 3.8 %copy-start = (bf16[8,128,32,32]{1,3,0,2:T(8,128)(2,1)S(1)}, bf16[8,128,32,32]{1,3,0,2:T(8,128)(2,1)}, u32[]{:S(2)}) copy-start(bf16[8,128,32,32]{1,3,0,2:T(8,128)(2,1)} %copy.82) | copy-start | bytes 6291460
  212.9 5.0 %copy-start.2 = (bf16[8,128,32,32]{1,3,0,2:T(8,128)(2,1)S(1)}, bf16[8,128,32,32]{1,3,0,2:T(8,128)(2,1)}, u32[]{:S(2)}) copy-start(bf16[8,128,32,32]{1,3,0,2:T(8,128)(2,1)} %copy.92) | copy-start | bytes 6291460
  212.9 5.0 %copy-start.3 = (bf16[2,1,2048,256]{3,2,0,1:T(8,128)(2,1)S(1)}, bf16[2,1,2048,256]{3,2,0,1:T(8,128)(2,1)}, u32[]{:S(2)}) copy-start(bf16[2,1,2048,256]{3,2,0,1:T(8,128)(2,1)} %copy.89) | copy-start | bytes 6291460
  217.9 1.6 copy-start.1
  217.9 2.2 copy-start.5
  220.1 2.6 copy-start.4
  224.1 1.4 copy-start.7
  225.5 75.9 %reduce-scatter.2.cloned.1.call-start = ((), (), s32[]{:S(2)}) async-start(), calls=%async_computation.3 | async-start | bytes 163840 | tf_op jit(solution)/shard_map/reduce_scatter | solution.py:111
Sparse Core Ops, SparseCore 0:
  225.6 55.2 all-reduce.2
  283.1 18.2 reduce-scatter.1

commit v2 on v1

v2 whole, which is shorter than its diff:
```python
import jax
import jax.numpy as jnp
from jax import lax
from jax.sharding import PartitionSpec as P

BS = 32
KS = 8
RB = 64


def screen_density(density, block_mask):
    own_blocks = block_mask.shape[0]
    all_blocks = block_mask.shape[1]
    shaped = density.reshape(own_blocks, BS, all_blocks, BS)
    keeper = block_mask.astype(density.dtype)[:, None, :, None]
    return (shaped * keeper).reshape(density.shape)


def pair_routes(size):
    routes = []
    for dist in range(1, size // 2 + 1):
        if 2 * dist < size:
            route = [(r, (r + dist) % size) for r in range(size)]
        else:
            route = []
            for i in range(size // 2):
                if i % 2 == 0:
                    route.append((i, i + dist))
                else:
                    route.append((i + dist, i))
        recv_from = list(range(size))
        send_to = list(range(size))
        for src, dst in route:
            recv_from[dst] = src
            send_to[src] = dst
        routes.append((route, recv_from, send_to))
    return routes


def mask_slab(slab, live):
    rows = slab.shape[0]
    groups = rows // RB
    keeper = live.astype(slab.dtype)[:, None, :, :, None]
    shaped = slab.reshape(groups, RB, slab.shape[1], KS, BS) * keeper
    return shaped.reshape(slab.shape)


def split_hi_lo(values):
    hi = values.astype(jnp.bfloat16)
    lo = (values - hi.astype(jnp.float32)).astype(jnp.bfloat16)
    return hi, lo


def slab_product(slab, hi, lo):
    flat = slab.reshape(slab.shape[0], -1)
    return jnp.dot(flat, hi, preferred_element_type=jnp.float32) + jnp.dot(
        flat, lo, preferred_element_type=jnp.float32
    )


def add_cols(total, part, col_block):
    rows = part.shape[0]
    at = (jnp.int32(0), col_block * rows)
    here = lax.dynamic_slice(total, at, part.shape)
    return lax.dynamic_update_slice(total, here + part, at)


def per_device(tensor, live_blocks, occ_density, virt_density, occ_mask, virt_mask, pair_slots):
    rows = tensor.shape[0]
    assert tensor.shape[1] == BS
    planes = lax.axis_size("ri")
    cycle_size = lax.axis_size("ao")
    plane = lax.axis_index("ri")

    routes = pair_routes(planes)
    received = [
        (lax.ppermute(tensor, "ri", route), lax.ppermute(live_blocks, "ri", route))
        for route, _, _ in routes
    ]

    stacked = jnp.stack(
        [screen_density(occ_density, occ_mask), screen_density(virt_density, virt_mask)]
    )
    full = lax.all_gather(stacked, "ao", axis=1, tiled=True)
    ao_total = full.shape[2]
    all_blocks = ao_total // BS
    picked = full.reshape(2, all_blocks, BS, ao_total)[:, pair_slots[0]]
    occ_rows = picked[0].reshape(KS * BS, ao_total)
    virt_rows = picked[1].reshape(KS * BS, ao_total)

    own = mask_slab(tensor, live_blocks)
    halves = jnp.einsum(
        "prk,dkc->dcrp",
        own,
        jnp.stack([occ_rows, virt_rows]),
        preferred_element_type=jnp.float32,
    ).astype(jnp.bfloat16)
    swapped = lax.all_to_all(halves, "ao", 1, 2, tiled=True)
    occ_t = swapped[0]
    virt_t = swapped[1]
    v_part = jnp.einsum("mn,lnp->lmp", virt_rows, occ_t, preferred_element_type=jnp.float32)
    w_part = jnp.einsum("kl,nlq->nkq", occ_rows, virt_t, preferred_element_type=jnp.float32)
    v_hi, v_lo = split_hi_lo(v_part.reshape(-1, rows))
    w_hi, w_lo = split_hi_lo(w_part.reshape(-1, rows))
    vw_hi = jnp.concatenate([v_hi, w_hi], axis=1)
    vw_lo = jnp.concatenate([v_lo, w_lo], axis=1)

    vw_hi, vw_lo, received = lax.optimization_barrier((vw_hi, vw_lo, received))
    total = jnp.zeros((rows, planes * rows), jnp.float32)
    total = add_cols(total, slab_product(own, w_hi, w_lo), plane)
    for (slab, live), (route, recv_from, send_to) in zip(received, routes):
        product = slab_product(mask_slab(slab, live), vw_hi, vw_lo)
        source = jnp.array(recv_from, jnp.int32)[plane]
        target = jnp.array(send_to, jnp.int32)[plane]
        total = add_cols(total, product[:, :rows].T, source)
        back = lax.ppermute(product[:, rows:], "ri", [(d, s) for s, d in route])
        total = add_cols(total, back, target)

    width = total.shape[1] // cycle_size
    sent = total.reshape(rows, cycle_size, width).transpose(1, 0, 2)
    got = lax.all_to_all(sent, "ao", 0, 0, tiled=True)
    return jnp.sum(got, axis=0)


def solution(mesh):
    placed = (
        P("ri", "ao", None),
        P("ri", "ao", None),
        P("ao", None),
        P("ao", None),
        P("ao", None),
        P("ao", None),
        P("ao", None),
    )
    return jax.shard_map(
        per_device, mesh=mesh, in_specs=placed, out_specs=P("ri", "ao"), check_vma=False
    )
```

time: 309 us -> 192 us (0.62)
  waiting for transfers between devices: 155 us -> 42.5 us
  other arithmetic: 3.43 us -> 22.4 us
  between operations: 19.4 us -> 3.07 us
  blocking collectives: 10.8 us -> 21.4 us
  local copies, waits for them, and re-layouts: 77.9 us -> 69.1 us
  matrix products: 21.8 us -> 14.5 us
    ppermute x2, waiting for transfers between devices: 77.1 us -> 2.42 us  [per_device(): lax.ppermute(live_blocks, 'ri', route)]
    unnamed x3 -> x0, waiting for transfers between devices: 54.1 us -> none
    all_to_all x2 -> x1, waiting for transfers between devices: 4.42 us -> 34.7 us  [per_device(): swapped = lax.all_to_all(halves, 'ao', 1, 2, tiled=True)]
    mul x4 -> x10, local copies, waits for them, and re-layouts: 0.4 us -> 26.4 us  [mask_slab(): shaped = slab.reshape(groups, RB, slab.shape[1], KS, BS) * keeper]
    slice x9 -> x6, local copies, waits for them, and re-layouts: 24.8 us -> 3.28 us  [the longest x2 2.68 us: per_device(): occ_t = swapped[0]]
    reduce_scatter x1 -> x0, waiting for transfers between devices: 18.9 us -> none  [per_device(): return lax.psum_scatter(in_plane, 'ri', scatter_dimension=0, tiled=True)[0]]
    transpose x2, local copies, waits for them, and re-layouts: 26.3 us -> 11.5 us  [the longest x1 5.88 us: per_device(): jnp.einsum('kl,nlq->nkq', occ_rows, virt_t, preferred_element_type=jnp.fl...]
    another operation x2, local copies, waits for them, and re-layouts: 12.5 us -> 0.2 us  [per_device(): jnp.stack([occ_rows, virt_rows])]
  transfers between devices with their start and end apart: 8 -> 7, of which waited for: 4 -> 3; matrix products, arithmetic and copies ran while one was open for 15% -> 33% of each run, Pallas kernels for 0% -> 0%
where the time goes in v2:
time: 192 us; the launch traced here: 191 us
  local copies, waits for them, and re-layouts  69.1 us (36%)
  waiting for transfers between devices  42.5 us (22%)
  other arithmetic  22.4 us (12%)
  blocking collectives  21.4 us (11%)
  starting transfers between devices  17.7 us (9%)
  matrix products  14.5 us (8%)
  between operations  3.07 us (2%)
    all_to_all x1, waiting for transfers between devices, per_device(): swapped = lax.all_to_all(halves, 'ao', 1, 2, tiled=True)  34.7 us
    mul x10, local copies, waits for them, and re-layouts, mask_slab(): shaped = slab.reshape(groups, RB, slab.shape[1], KS, BS) * keeper  26.4 us
    all_gather x1, blocking collectives, per_device(): full = lax.all_gather(stacked, 'ao', axis=1, tiled=True)  10.8 us
    all_to_all x1, blocking collectives, per_device(): got = lax.all_to_all(sent, 'ao', 0, 0, tiled=True)  10.6 us
    optimization_barrier x2, local copies, waits for them, and re-layouts, per_device(): vw_hi, vw_lo, received = lax.optimization_barrier((vw_hi, vw_lo, received))  9.21 us
    convert_element_type x2, other arithmetic, split_hi_lo(): lo = (values - hi.astype(jnp.float32)).astype(jnp.bfloat16)  7.73 us
    unnamed x30, local copies, waits for them, and re-layouts  7.09 us
    ppermute x2, starting transfers between devices, per_device(): lax.ppermute(tensor, 'ri', route)  6.08 us
  transfers between devices with their start and end apart: 7, of which 3 were waited for; matrix products, arithmetic and copies ran while one was open for 33% of the time, Pallas kernels for 0%

profile of v2, /device:TPU:0, one launch (start us, length us, event | category | flops | bytes accessed | tf_op | source)
XLA Modules:
  0.0 190.7 jit_solution(473279201870852127)
XLA Ops:
  3.6 10.8 %all_gather.3 = bf16[2,256,256]{2,1,0:T(8,128)(2,1)S(1)} all-gather(bf16[2,32,256]{2,1,0:T(8,128)(2,1)S(1)} %pad_maximum_fusion.2), channel_id=1, replica_groups=mesh['ri'=4,'ao'=8] {'ao'}, dimensions={1}, use_global_device_ids=true | all-gather | bytes 294912 | tf_op jit(solution)/shard_map/all_gather | solution.py:84
  15.8 1.8 broadcast_multiply_fusion
  17.6 3.2 %convert_bitcast_fusion = bf16[2,256,32,128]{3,1,2,0:T(8,128)(2,1)S(1)} fusion(bf16[128,32,256]{2,1,0:T(8,128)(2,1)S(1)} %broadcast_multiply_fusion, bf16[1,256,256]{1,2,0:T(8,128)(2,1)S(1)} %copy.68, bf16[1,256,256]{1,2,0:T(8,128)(2,1)S(1)} %copy.67), kind=kOutput, calls=%fused_computation.10 | convolution fusion | flops 1076363264 | bytes 6553600 | tf_op jit(solution)/shard_map/prk,dkc->dcrp/dot_general | solution.py:92
  20.7 4.7 %copy.70 = bf16[2,256,32,128]{3,2,0,1:T(8,128)(2,1)} copy(bf16[2,256,32,128]{3,1,2,0:T(8,128)(2,1)S(1)} %convert_bitcast_fusion) | data formatting | bytes 8388608 | tf_op jit(solution)/shard_map/convert_element_type | solution.py:97
  25.5 4.7 %all-to-all-start = ((bf16[2,256,32,128]{3,2,0,1:T(8,128)(2,1)}), bf16[2,256,32,128]{3,2,0,1:T(8,128)(2,1)}, u32[]{:S(2)}, u32[]{:S(2)}) async-start(bf16[2,256,32,128]{3,2,0,1:T(8,128)(2,1)} %copy.70), calls=%async_computation | async-start | bytes 8388608 | tf_op jit(solution)/shard_map/all_to_all | solution.py:98
  30.2 1.6 collective-permute-start
  33.4 4.4 %collective-permute-start.2 = (bf16[128,32,256]{2,1,0:T(8,128)(2,1)}, bf16[128,32,256]{2,1,0:T(8,128)(2,1)}, u32[]{:S(2)}, u32[]{:S(2)}) collective-permute-start(bf16[128,32,256]{2,1,0:T(8,128)(2,1)} %param.11), channel_id=1, source_target_pairs={{0,16},{24,8},{1,17},{25,9},{2,18},{26,10},{3,19},{27,11},{4,20},{... | collective-permute-start | bytes 6291464 | tf_op jit(solution)/shard_map/ppermute | solution.py:77
  44.5 34.7 %all-to-all-done = bf16[2,256,32,128]{3,2,0,1:T(8,128)(2,1)} async-done(((bf16[2,256,32,128]{3,2,0,1:T(8,128)(2,1)}), bf16[2,256,32,128]{3,2,0,1:T(8,128)(2,1)}, u32[]{:S(2)}, u32[]{:S(2)}) %all-to-all-start) | async-done | bytes 4194336 | tf_op jit(solution)/shard_map/all_to_all | solution.py:98
  79.3 2.9 %copy.71 = bf16[2,256,32,128]{3,2,1,0:T(8,128)(2,1)S(1)} copy(bf16[2,256,32,128]{3,2,0,1:T(8,128)(2,1)} %all-to-all-done) | data formatting | bytes 8388608 | tf_op jit(solution)/shard_map/all_to_all | solution.py:98
  82.2 2.1 %fusion.25 = (bf16[1,32,8,32,128]{4,3,1,2,0:T(8,128)(2,1)}, bf16[1,32,8,32,128]{4,3,1,2,0:T(8,128)(2,1)S(1)}) fusion(bf16[2,32,8,32,128]{4,3,1,2,0:T(8,128)(2,1)S(1)} %bitcast.99), kind=kLoop, calls=%fused_computation.50 | loop fusion | bytes 8388608 | tf_op jit(solution)/shard_map/slice | solution.py:99
  85.7 1.9 %copy-done = f32[32,256,128]{1,2,0:T(8,128)} copy-done((f32[32,256,128]{1,2,0:T(8,128)}, f32[32,256,128]{1,2,0:T(8,128)S(1)}, u32[]{:S(2)}) %copy-start) | copy-done | bytes 4194328
  87.6 2.7 %fusion.11 = f32[128,128]{0,1:T(8,128)S(1)} fusion(f32[32,256,128]{1,2,0:T(8,128)S(1)} %convolution_bitcast_fusion.1, bf16[128,32,256]{2,1,0:T(8,128)(2,1)S(1)} %broadcast_multiply_fusion), kind=kOutput, calls=%fused_computation.24 | convolution fusion | flops 272629760 | bytes 6356992 | tf_op jit(solution)/shard_map/dot_general | solution.py:56
  90.3 5.9 %copy.80 = f32[32,256,128]{2,1,0:T(8,128)} copy(f32[32,256,128]{1,2,0:T(8,128)} %copy-done) | data formatting | bytes 8388608 | tf_op jit(solution)/shard_map/kl,nlq->nkq/transpose | solution.py:102
  96.2 4.9 %fusion = (bf16[8192,128]{1,0:T(8,128)(2,1)}, bf16[8192,128]{1,0:T(8,128)(2,1)}) fusion(f32[32,256,128]{2,1,0:T(8,128)} %copy.80), kind=kLoop, calls=%fused_computation.5 | loop fusion | flops 4194304 | bytes 8388608 | tf_op jit(solution)/shard_map/convert_element_type | solution.py:50
  101.6 2.8 %convolution_bitcast_fusion = f32[32,256,128]{1,2,0:T(8,128)} fusion(bf16[32,256,128]{2,1,0:T(8,128)(2,1)S(1)} %bitcast.101, bf16[256,256,1]{1,0,2:T(8,128)(2,1)S(1)} %bitcast.103), kind=kOutput, calls=%fused_computation.11 | convolution fusion | flops 536870912 | bytes 6422528 | tf_op jit(solution)/shard_map/mn,lnp->lmp/dot_general | solution.py:101
  104.4 5.6 %copy.79 = f32[32,256,128]{2,1,0:T(8,128)} copy(f32[32,256,128]{1,2,0:T(8,128)} %convolution_bitcast_fusion) | data formatting | bytes 8388608 | tf_op jit(solution)/shard_map/mn,lnp->lmp/transpose | solution.py:101
  110.0 2.9 %fusion.1 = (bf16[8192,128]{1,0:T(8,128)(2,1)S(1)}, bf16[8192,128]{1,0:T(8,128)(2,1)S(1)}) fusion(f32[32,256,128]{2,1,0:T(8,128)} %copy.79), kind=kLoop, calls=%fused_computation.8 | loop fusion | flops 4194304 | bytes 8388608 | tf_op jit(solution)/shard_map/convert_element_type | solution.py:50
  113.5 1.6 fusion.14
  115.1 2.4 %pad_maximum_fusion = bf16[8192,256]{1,0:T(8,128)(2,1)} fusion(bf16[8192,128]{1,0:T(8,128)(2,1)S(1)} %copy-done.8, bf16[8192,128]{1,0:T(8,128)(2,1)S(1)} %get-tuple-element.18), kind=kLoop, calls=%fused_computation.1 | loop fusion | flops 8388608 | bytes 8388608 | tf_op jit(solution)/shard_map/concatenate | solution.py:105
  117.5 2.5 %pad_maximum_fusion.1 = bf16[8192,256]{1,0:T(8,128)(2,1)} fusion(bf16[8192,128]{1,0:T(8,128)(2,1)S(1)} %copy-done.7, bf16[8192,128]{1,0:T(8,128)(2,1)S(1)} %get-tuple-element.17), kind=kLoop, calls=%fused_computation.2 | loop fusion | flops 8388608 | bytes 8388608 | tf_op jit(solution)/shard_map/concatenate | solution.py:106
  120.1 2.4 %collective-permute-done.3 = s32[2,1,8]{2,1,0:T(1,128)S(1)} collective-permute-done((s32[2,1,8]{2,1,0:T(1,128)S(1)}, s32[2,1,8]{2,1,0:T(1,128)S(1)}, u32[]{:S(2)}, u32[]{:S(2)}) %collective-permute-start.3) | collective-permute-done | bytes 96 | tf_op jit(solution)/shard_map/ppermute | solution.py:77
  122.6 6.1 %mul.132 = bf16[2,64,32,8,32]{1,0,4,3,2:T(2,128)(2,1)} broadcast(bf16[2,8]{0,1:T(8,128)(2,1)S(1)} %bitcast.110), dimensions={0,3} | broadcast | bytes 2097184 | tf_op jit(solution)/shard_map/mul | solution.py:44
  128.7 6.8 %mul.133 = bf16[128,8192]{0,1:T(8,128)(2,1)S(1)} reshape(bf16[2,64,32,8,32]{1,0,4,3,2:T(2,128)(2,1)} %mul.132) | data formatting | bytes 4194304 | tf_op jit(solution)/shard_map/mul | solution.py:44
  135.5 4.6 %copy.81 = bf16[128,32,256]{0,2,1:T(8,128)(2,1)} copy(bf16[128,32,256]{2,1,0:T(8,128)(2,1)} %collective-permute-done) | data formatting | bytes 4194304 | tf_op jit(solution)/shard_map/optimization_barrier | solution.py:108
  140.1 2.0 %bitcast_multiply_fusion.1 = bf16[128,8192]{0,1:T(8,128)(2,1)S(1)} fusion(bf16[128,8192]{0,1:T(8,128)(2,1)S(1)} %mul.133, bf16[128,32,256]{0,2,1:T(8,128)(2,1)} %copy.81), kind=kLoop, calls=%fused_computation.15 | loop fusion | flops 1048576 | bytes 6291456 | tf_op jit(solution)/shard_map/mul | solution.py:44
  146.1 2.6 %collective-permute-start.4 = (f32[128,128]{1,0:T(8,128)S(1)}, f32[128,128]{1,0:T(8,128)S(1)}, u32[]{:S(2)}, u32[]{:S(2)}) collective-permute-start(f32[128,128]{1,0:T(8,128)S(1)} %get-tuple-element.25), channel_id=1, source_target_pairs={{8,0},{16,8},{24,16},{0,24},{9,1},{17,9},{25,17},{1,25},{10,2},{18... | collective-permute-start | bytes 196616 | tf_op jit(solution)/shard_map/ppermute | solution.py:116
  148.8 6.1 %mul.140 = bf16[2,64,32,8,32]{1,0,4,3,2:T(2,128)(2,1)} broadcast(bf16[2,8]{0,1:T(8,128)(2,1)S(1)} %bitcast.111), dimensions={0,3} | broadcast | bytes 2097184 | tf_op jit(solution)/shard_map/mul | solution.py:44
  154.9 6.8 %mul.141 = bf16[128,8192]{0,1:T(8,128)(2,1)S(1)} reshape(bf16[2,64,32,8,32]{1,0,4,3,2:T(2,128)(2,1)} %mul.140) | data formatting | bytes 4194304 | tf_op jit(solution)/shard_map/mul | solution.py:44
  161.7 4.6 %copy.85 = bf16[128,32,256]{0,2,1:T(8,128)(2,1)} copy(bf16[128,32,256]{2,1,0:T(8,128)(2,1)} %collective-permute-done.2) | data formatting | bytes 4194304 | tf_op jit(solution)/shard_map/optimization_barrier | solution.py:108
  166.3 2.0 %bitcast_multiply_fusion = bf16[128,8192]{0,1:T(8,128)(2,1)S(1)} fusion(bf16[128,8192]{0,1:T(8,128)(2,1)S(1)} %mul.141, bf16[128,32,256]{0,2,1:T(8,128)(2,1)} %copy.85), kind=kLoop, calls=%fused_computation.14 | loop fusion | flops 1048576 | bytes 6291456 | tf_op jit(solution)/shard_map/mul | solution.py:44
  173.9 5.4 %collective-permute-done.5 = f32[128,128]{1,0:T(8,128)S(1)} collective-permute-done((f32[128,128]{1,0:T(8,128)S(1)}, f32[128,128]{1,0:T(8,128)S(1)}, u32[]{:S(2)}, u32[]{:S(2)}) %collective-permute-start.5) | collective-permute-done | bytes 65568 | tf_op jit(solution)/shard_map/ppermute | solution.py:116
  179.5 10.6 %all_to_all.20 = f32[8,128,64]{1,2,0:T(8,128)S(1)} all-to-all(f32[8,128,64]{1,2,0:T(8,128)S(1)} %bitcast.108), channel_id=1, replica_groups=mesh['ri'=4,'ao'=8] {'ao'}, dimensions={0} | all-to-all | bytes 524288 | tf_op jit(solution)/shard_map/all_to_all | solution.py:121
  (84 shorter events, 23.7 us)
Async XLA Ops:
  25.4 6.4 %copy-start.9 = (s32[2,1,8]{2,1,0:T(1,128)S(1)}, s32[2,1,8]{2,1,0:T(1,128)}, u32[]{:S(2)}) copy-start(s32[2,1,8]{2,1,0:T(1,128)} %param.12) | copy-start | bytes 196
  25.4 13.9 %copy-start.13 = (s32[4]{0:T(128)S(1)}, s32[4]{0:T(128)}, u32[]{:S(2)}) copy-start(s32[4]{0:T(128)} %constant.32.clone) | copy-start | bytes 52
  25.4 15.1 %copy-start.12 = (s32[4]{0:T(128)S(1)}, s32[4]{0:T(128)}, u32[]{:S(2)}) copy-start(s32[4]{0:T(128)} %constant.33.clone) | copy-start | bytes 52
  25.4 16.4 %copy-start.11 = (s32[4]{0:T(128)S(1)}, s32[4]{0:T(128)}, u32[]{:S(2)}) copy-start(s32[4]{0:T(128)} %constant.34.clone) | copy-start | bytes 52
  25.4 17.8 %copy-start.10 = (s32[4]{0:T(128)S(1)}, s32[4]{0:T(128)}, u32[]{:S(2)}) copy-start(s32[4]{0:T(128)} %constant.35.clone) | copy-start | bytes 52
  25.5 53.8 %all-to-all-start = ((bf16[2,256,32,128]{3,2,0,1:T(8,128)(2,1)}), bf16[2,256,32,128]{3,2,0,1:T(8,128)(2,1)}, u32[]{:S(2)}, u32[]{:S(2)}) async-start(bf16[2,256,32,128]{3,2,0,1:T(8,128)(2,1)} %copy.70), calls=%async_computation | async-start | bytes 8388608 | tf_op jit(solution)/shard_map/all_to_all | solution.py:98
  30.2 92.3 %collective-permute-start = (bf16[128,32,256]{2,1,0:T(8,128)(2,1)}, bf16[128,32,256]{2,1,0:T(8,128)(2,1)}, u32[]{:S(2)}, u32[]{:S(2)}) collective-permute-start(bf16[128,32,256]{2,1,0:T(8,128)(2,1)} %param.11), channel_id=1, source_target_pairs={{0,8},{8,16},{16,24},{24,0},{1,9},{9,17},{17,25},{25,1},{2,10},{10... | collective-permute-start | bytes 6291464 | tf_op jit(solution)/shard_map/ppermute | solution.py:77
  31.8 88.3 %collective-permute-start.1 = (s32[2,1,8]{2,1,0:T(1,128)S(1)}, s32[2,1,8]{2,1,0:T(1,128)S(1)}, u32[]{:S(2)}, u32[]{:S(2)}) collective-permute-start(s32[2,1,8]{2,1,0:T(1,128)S(1)} %copy-done.9), channel_id=1, source_target_pairs={{0,8},{8,16},{16,24},{24,0},{1,9},{9,17},{17,25},{25,1},{2,10},{10... | collective-permute-start | bytes 200 | tf_op jit(solution)/shard_map/ppermute | solution.py:77
  33.4 89.1 %collective-permute-start.2 = (bf16[128,32,256]{2,1,0:T(8,128)(2,1)}, bf16[128,32,256]{2,1,0:T(8,128)(2,1)}, u32[]{:S(2)}, u32[]{:S(2)}) collective-permute-start(bf16[128,32,256]{2,1,0:T(8,128)(2,1)} %param.11), channel_id=1, source_target_pairs={{0,16},{24,8},{1,17},{25,9},{2,18},{26,10},{3,19},{27,11},{4,20},{... | collective-permute-start | bytes 6291464 | tf_op jit(solution)/shard_map/ppermute | solution.py:77
  37.8 84.7 %collective-permute-start.3 = (s32[2,1,8]{2,1,0:T(1,128)S(1)}, s32[2,1,8]{2,1,0:T(1,128)S(1)}, u32[]{:S(2)}, u32[]{:S(2)}) collective-permute-start(s32[2,1,8]{2,1,0:T(1,128)S(1)} %copy-done.9), channel_id=1, source_target_pairs={{0,16},{24,8},{1,17},{25,9},{2,18},{26,10},{3,19},{27,11},{4,20},{... | collective-permute-start | bytes 200 | tf_op jit(solution)/shard_map/ppermute | solution.py:77
  85.7 1.9 %copy-start = (f32[32,256,128]{1,2,0:T(8,128)}, f32[32,256,128]{1,2,0:T(8,128)S(1)}, u32[]{:S(2)}) copy-start(f32[32,256,128]{1,2,0:T(8,128)S(1)} %convolution_bitcast_fusion.1) | copy-start | bytes 12582916
  96.2 4.9 %copy-start.6 = (bf16[1,32,8,32,128]{4,3,1,2,0:T(8,128)(2,1)S(1)}, bf16[1,32,8,32,128]{4,3,1,2,0:T(8,128)(2,1)}, u32[]{:S(2)}) copy-start(bf16[1,32,8,32,128]{4,3,1,2,0:T(8,128)(2,1)} %get-tuple-element.21) | copy-start | bytes 6291460
  110.0 3.4 %copy-start.1 = (f32[32,256,128]{1,2,0:T(8,128)S(1)}, f32[32,256,128]{1,2,0:T(8,128)}, u32[]{:S(2)}) copy-start(f32[32,256,128]{1,2,0:T(8,128)} %copy-done) | copy-start | bytes 12582916
  113.5 1.6 copy-start.8
  115.1 2.4 %copy-start.7 = (bf16[8192,128]{1,0:T(8,128)(2,1)S(1)}, bf16[8192,128]{1,0:T(8,128)(2,1)}, u32[]{:S(2)}) copy-start(bf16[8192,128]{1,0:T(8,128)(2,1)} %get-tuple-element.19) | copy-start | bytes 6291460
  140.1 2.8 %copy-start.4 = (bf16[8192,256]{1,0:T(8,128)(2,1)S(1)}, bf16[8192,256]{1,0:T(8,128)(2,1)}, u32[]{:S(2)}) copy-start(bf16[8192,256]{1,0:T(8,128)(2,1)} %pad_maximum_fusion.1) | copy-start | bytes 12582916
  142.9 2.2 %copy-start.2 = (bf16[8192,256]{1,0:T(8,128)(2,1)S(1)}, bf16[8192,256]{1,0:T(8,128)(2,1)}, u32[]{:S(2)}) copy-start(bf16[8192,256]{1,0:T(8,128)(2,1)} %pad_maximum_fusion) | copy-start | bytes 12582916
  146.1 27.5 %collective-permute-start.4 = (f32[128,128]{1,0:T(8,128)S(1)}, f32[128,128]{1,0:T(8,128)S(1)}, u32[]{:S(2)}, u32[]{:S(2)}) collective-permute-start(f32[128,128]{1,0:T(8,128)S(1)} %get-tuple-element.25), channel_id=1, source_target_pairs={{8,0},{16,8},{24,16},{0,24},{9,1},{17,9},{25,17},{1,25},{10,2},{18... | collective-permute-start | bytes 196616 | tf_op jit(solution)/shard_map/ppermute | solution.py:116
  166.3 2.8 %copy-start.5 = (bf16[8192,256]{1,0:T(8,128)(2,1)S(1)}, bf16[8192,256]{1,0:T(8,128)(2,1)}, u32[]{:S(2)}) copy-start(bf16[8192,256]{1,0:T(8,128)(2,1)} %pad_maximum_fusion.1) | copy-start | bytes 12582916
  169.1 2.2 %copy-start.3 = (bf16[8192,256]{1,0:T(8,128)(2,1)S(1)}, bf16[8192,256]{1,0:T(8,128)(2,1)}, u32[]{:S(2)}) copy-start(bf16[8192,256]{1,0:T(8,128)(2,1)} %pad_maximum_fusion) | copy-start | bytes 12582916
  172.2 7.1 %collective-permute-start.5 = (f32[128,128]{1,0:T(8,128)S(1)}, f32[128,128]{1,0:T(8,128)S(1)}, u32[]{:S(2)}, u32[]{:S(2)}) collective-permute-start(f32[128,128]{1,0:T(8,128)S(1)} %slice.43), channel_id=1, source_target_pairs={{16,0},{8,24},{17,1},{9,25},{18,2},{10,26},{19,3},{11,27},{20,4},{... | collective-permute-start | bytes 196616 | tf_op jit(solution)/shard_map/ppermute | solution.py:116

commit v3 on v2

--- a/solution.py
+++ b/solution.py
@@ -38,17 +38,13 @@
 
 
 def mask_slab(slab, live):
-    rows = slab.shape[0]
-    groups = rows // RB
-    keeper = live.astype(slab.dtype)[:, None, :, :, None]
-    shaped = slab.reshape(groups, RB, slab.shape[1], KS, BS) * keeper
-    return shaped.reshape(slab.shape)
+    keeper = jnp.repeat(jnp.repeat(live[:, 0, :].astype(slab.dtype), RB, axis=0), BS, axis=1)
+    return slab * keeper[:, None, :]
 
 
 def split_hi_lo(values):
-    hi = values.astype(jnp.bfloat16)
-    lo = (values - hi.astype(jnp.float32)).astype(jnp.bfloat16)
-    return hi, lo
+    rounded = lax.reduce_precision(values, exponent_bits=8, mantissa_bits=7)
+    return rounded.astype(jnp.bfloat16), (values - rounded).astype(jnp.bfloat16)
 
 
 def slab_product(slab, hi, lo):
@@ -73,10 +69,8 @@
     plane = lax.axis_index("ri")
 
     routes = pair_routes(planes)
-    received = [
-        (lax.ppermute(tensor, "ri", route), lax.ppermute(live_blocks, "ri", route))
-        for route, _, _ in routes
-    ]
+    own = mask_slab(tensor, live_blocks)
+    received = [lax.ppermute(own, "ri", route) for route, _, _ in routes]
 
     stacked = jnp.stack(
         [screen_density(occ_density, occ_mask), screen_density(virt_density, virt_mask)]
@@ -88,7 +82,6 @@
     occ_rows = picked[0].reshape(KS * BS, ao_total)
     virt_rows = picked[1].reshape(KS * BS, ao_total)
 
-    own = mask_slab(tensor, live_blocks)
     halves = jnp.einsum(
         "prk,dkc->dcrp",
         own,
@@ -102,18 +95,17 @@
     w_part = jnp.einsum("kl,nlq->nkq", occ_rows, virt_t, preferred_element_type=jnp.float32)
     v_hi, v_lo = split_hi_lo(v_part.reshape(-1, rows))
     w_hi, w_lo = split_hi_lo(w_part.reshape(-1, rows))
-    vw_hi = jnp.concatenate([v_hi, w_hi], axis=1)
-    vw_lo = jnp.concatenate([v_lo, w_lo], axis=1)
 
-    vw_hi, vw_lo, received = lax.optimization_barrier((vw_hi, vw_lo, received))
+    v_hi, v_lo, w_hi, w_lo, received = lax.optimization_barrier(
+        (v_hi, v_lo, w_hi, w_lo, received)
+    )
     total = jnp.zeros((rows, planes * rows), jnp.float32)
     total = add_cols(total, slab_product(own, w_hi, w_lo), plane)
-    for (slab, live), (route, recv_from, send_to) in zip(received, routes):
-        product = slab_product(mask_slab(slab, live), vw_hi, vw_lo)
+    for slab, (route, recv_from, send_to) in zip(received, routes):
         source = jnp.array(recv_from, jnp.int32)[plane]
         target = jnp.array(send_to, jnp.int32)[plane]
-        total = add_cols(total, product[:, :rows].T, source)
-        back = lax.ppermute(product[:, rows:], "ri", [(d, s) for s, d in route])
+        total = add_cols(total, slab_product(slab, v_hi, v_lo).T, source)
+        back = lax.ppermute(slab_product(slab, w_hi, w_lo), "ri", [(d, s) for s, d in route])
         total = add_cols(total, back, target)
 
     width = total.shape[1] // cycle_size

time: 192 us -> 156 us (0.81)
  local copies, waits for them, and re-layouts: 69.1 us -> 36.5 us
  other arithmetic: 22.4 us -> 12.9 us
  matrix products: 14.5 us -> 18.8 us
  waiting for transfers between devices: 42.5 us -> 46.3 us
    mul x10 -> x1, local copies, waits for them, and re-layouts: 26.4 us -> 0.11 us  [mask_slab(): return slab * keeper[:, None, :]]
    optimization_barrier x2 -> x0, local copies, waits for them, and re-layouts: 9.21 us -> none  [per_device(): vw_hi, vw_lo, received = lax.optimization_barrier((vw_hi, vw_lo, received))]
    ppermute x6 -> x4, waiting for transfers between devices: 7.81 us -> 14 us  [the longest x2 13.2 us: per_device(): received = [lax.ppermute(own, 'ri', route) for route, _, _ in routes]]
    concatenate x2 -> x0, other arithmetic: 4.86 us -> none  [the longest x1 2.46 us: per_device(): vw_lo = jnp.concatenate([v_lo, w_lo], axis=1)]
    mul x3 -> x1, other arithmetic: 5.66 us -> 1.53 us  [mask_slab(): return slab * keeper[:, None, :]]
    unnamed x30 -> x19, local copies, waits for them, and re-layouts: 7.09 us -> 10.5 us
    all_to_all x1, waiting for transfers between devices: 34.7 us -> 32.3 us  [per_device(): swapped = lax.all_to_all(halves, 'ao', 1, 2, tiled=True)]
    slice x2 -> x1, local copies, waits for them, and re-layouts: 2.68 us -> 0.56 us  [per_device(): occ_t = swapped[0]]
  transfers between devices with their start and end apart: 7 -> 5, of which waited for: 3 -> 3; matrix products, arithmetic and copies ran while one was open for 33% -> 27% of each run, Pallas kernels for 0% -> 0%
where the time goes in v3:
time: 156 us; the launch traced here: 155 us
  waiting for transfers between devices  46.3 us (30%)
  local copies, waits for them, and re-layouts  36.5 us (23%)
  blocking collectives  21.2 us (14%)
  matrix products  18.8 us (12%)
  starting transfers between devices  16.1 us (10%)
  other arithmetic  12.9 us (8%)
  between operations  2.8 us (2%)
    all_to_all x1, waiting for transfers between devices, per_device(): swapped = lax.all_to_all(halves, 'ao', 1, 2, tiled=True)  32.3 us
    ppermute x2, waiting for transfers between devices, per_device(): received = [lax.ppermute(own, 'ri', route) for route, _, _ in routes]  13.2 us
    all_gather x1, blocking collectives, per_device(): full = lax.all_gather(stacked, 'ao', axis=1, tiled=True)  10.8 us
    unnamed x19, local copies, waits for them, and re-layouts  10.5 us
    all_to_all x1, blocking collectives, per_device(): got = lax.all_to_all(sent, 'ao', 0, 0, tiled=True)  10.5 us
    ppermute x2, starting transfers between devices, per_device(): received = [lax.ppermute(own, 'ri', route) for route, _, _ in routes]  7.47 us
    convert_element_type x2, other arithmetic, split_hi_lo(): (values - rounded).astype(jnp.bfloat16)  7.16 us
    transpose x1, local copies, waits for them, and re-layouts, per_device(): jnp.einsum('mn,lnp->lmp', virt_rows, occ_t, preferred_element_type=jnp.fl...  5.63 us
  transfers between devices with their start and end apart: 5, of which 3 were waited for; matrix products, arithmetic and copies ran while one was open for 27% of the time, Pallas kernels for 0%

profile of v3, /device:TPU:0, one launch (start us, length us, event | category | flops | bytes accessed | tf_op | source)
XLA Modules:
  0.0 154.7 jit_solution(15814281544155135362)
XLA Ops:
  0.0 0.8 convert_bitcast_fusion.2
  2.5 10.8 %all_gather.3 = bf16[2,256,256]{2,1,0:T(8,128)(2,1)S(1)} all-gather(bf16[2,32,256]{2,1,0:T(8,128)(2,1)S(1)} %pad_maximum_fusion), channel_id=1, replica_groups=mesh['ri'=4,'ao'=8] {'ao'}, dimensions={1}, use_global_device_ids=true | all-gather | bytes 294912 | tf_op jit(solution)/shard_map/all_gather | solution.py:78
  15.9 1.5 broadcast_multiply_fusion
  17.4 4.7 %convert_bitcast_fusion = bf16[2,256,32,128]{3,1,2,0:T(8,128)(2,1)S(1)} fusion(bf16[128,32,256]{2,1,0:T(8,128)(2,1)} %broadcast_multiply_fusion, bf16[1,256,256]{1,2,0:T(8,128)(2,1)S(1)} %copy.52, bf16[1,256,256]{1,2,0:T(8,128)(2,1)S(1)} %copy.51), kind=kOutput, calls=%fused_computation.7 | convolution fusion | flops 1076363264 | bytes 6553600 | tf_op jit(solution)/shard_map/prk,dkc->dcrp/dot_general | solution.py:85
  22.2 4.7 %copy.54 = bf16[2,256,32,128]{3,2,0,1:T(8,128)(2,1)} copy(bf16[2,256,32,128]{3,1,2,0:T(8,128)(2,1)S(1)} %convert_bitcast_fusion) | data formatting | bytes 8388608 | tf_op jit(solution)/shard_map/convert_element_type | solution.py:90
  26.9 4.7 %all-to-all-start = ((bf16[2,256,32,128]{3,2,0,1:T(8,128)(2,1)}), bf16[2,256,32,128]{3,2,0,1:T(8,128)(2,1)}, u32[]{:S(2)}, u32[]{:S(2)}) async-start(bf16[2,256,32,128]{3,2,0,1:T(8,128)(2,1)} %copy.54), calls=%async_computation | async-start | bytes 8388608 | tf_op jit(solution)/shard_map/all_to_all | solution.py:91
  31.6 1.6 %collective-permute-start = (bf16[128,32,256]{2,1,0:T(8,128)(2,1)}, bf16[128,32,256]{2,1,0:T(8,128)(2,1)}, u32[]{:S(2)}, u32[]{:S(2)}) collective-permute-start(bf16[128,32,256]{2,1,0:T(8,128)(2,1)} %broadcast_multiply_fusion), channel_id=1, source_target_pairs={{0,8},{8,16},{16,24},{24,0},{1,9},{9,17},{17,25},{25,1},{2,10},{10... | collective-permute-start | bytes 6291464 | tf_op jit(solution)/shard_map/ppermute | solution.py:73
  33.2 5.8 %collective-permute-start.1 = (bf16[128,32,256]{2,1,0:T(8,128)(2,1)}, bf16[128,32,256]{2,1,0:T(8,128)(2,1)}, u32[]{:S(2)}, u32[]{:S(2)}) collective-permute-start(bf16[128,32,256]{2,1,0:T(8,128)(2,1)} %broadcast_multiply_fusion), channel_id=1, source_target_pairs={{0,16},{24,8},{1,17},{25,9},{2,18},{26,10},{3,19},{27,11},{4,20},{... | collective-permute-start | bytes 6291464 | tf_op jit(solution)/shard_map/ppermute | solution.py:73
  44.0 4.3 %copy.74 = bf16[16,8,32,256]{3,1,2,0:T(8,128)(2,1)} copy(bf16[16,8,32,256]{3,2,1,0:T(8,128)(2,1)} %bitcast.40) | data formatting | bytes 4194304
  48.4 32.3 %all-to-all-done = bf16[2,256,32,128]{3,2,0,1:T(8,128)(2,1)} async-done(((bf16[2,256,32,128]{3,2,0,1:T(8,128)(2,1)}), bf16[2,256,32,128]{3,2,0,1:T(8,128)(2,1)}, u32[]{:S(2)}, u32[]{:S(2)}) %all-to-all-start) | async-done | bytes 4194336 | tf_op jit(solution)/shard_map/all_to_all | solution.py:91
  80.7 2.9 %copy.55 = bf16[2,256,32,128]{3,2,1,0:T(8,128)(2,1)S(1)} copy(bf16[2,256,32,128]{3,2,0,1:T(8,128)(2,1)} %all-to-all-done) | data formatting | bytes 8388608 | tf_op jit(solution)/shard_map/all_to_all | solution.py:91
  83.6 2.1 %fusion.9 = (bf16[1,32,8,32,128]{4,3,1,2,0:T(8,128)(2,1)S(1)}, bf16[1,32,8,32,128]{4,3,1,2,0:T(8,128)(2,1)}) fusion(bf16[2,32,8,32,128]{4,3,1,2,0:T(8,128)(2,1)S(1)} %bitcast.98), kind=kLoop, calls=%fused_computation.35 | loop fusion | bytes 8388608 | tf_op jit(solution)/shard_map/slice | solution.py:93
  86.3 2.8 %convolution_bitcast_fusion = f32[32,256,128]{1,2,0:T(8,128)} fusion(bf16[32,256,128]{2,1,0:T(8,128)(2,1)S(1)} %bitcast.99, bf16[256,256,1]{1,0,2:T(8,128)(2,1)S(1)} %bitcast.105), kind=kOutput, calls=%fused_computation.8 | convolution fusion | flops 536870912 | bytes 6422528 | tf_op jit(solution)/shard_map/kl,nlq->nkq/dot_general | solution.py:95
  89.0 5.6 %copy.61 = f32[32,256,128]{2,1,0:T(8,128)} copy(f32[32,256,128]{1,2,0:T(8,128)} %convolution_bitcast_fusion) | data formatting | bytes 8388608 | tf_op jit(solution)/shard_map/kl,nlq->nkq/transpose | solution.py:95
  94.6 4.3 %fusion.1 = (bf16[8192,128]{1,0:T(8,128)(2,1)}, bf16[8192,128]{1,0:T(8,128)(2,1)S(1)}) fusion(f32[32,256,128]{2,1,0:T(8,128)} %copy.61), kind=kLoop, calls=%fused_computation.6 | loop fusion | flops 4194304 | bytes 8388608 | tf_op jit(solution)/shard_map/convert_element_type | solution.py:47
  99.5 2.7 %convolution_bitcast_fusion.1 = f32[32,256,128]{1,2,0:T(8,128)} fusion(bf16[32,256,128]{2,1,0:T(8,128)(2,1)S(1)} %bitcast.100, bf16[256,256,1]{1,0,2:T(8,128)(2,1)S(1)} %bitcast.103), kind=kOutput, calls=%fused_computation.9 | convolution fusion | flops 536870912 | bytes 6422528 | tf_op jit(solution)/shard_map/mn,lnp->lmp/dot_general | solution.py:94
  102.2 5.6 %copy.58 = f32[32,256,128]{2,1,0:T(8,128)} copy(f32[32,256,128]{1,2,0:T(8,128)} %convolution_bitcast_fusion.1) | data formatting | bytes 8388608 | tf_op jit(solution)/shard_map/mn,lnp->lmp/transpose | solution.py:94
  107.9 2.8 %fusion = (bf16[8192,128]{1,0:T(8,128)(2,1)S(1)}, bf16[8192,128]{1,0:T(8,128)(2,1)S(1)}) fusion(f32[32,256,128]{2,1,0:T(8,128)} %copy.58), kind=kLoop, calls=%fused_computation.5 | loop fusion | flops 4194304 | bytes 8388608 | tf_op jit(solution)/shard_map/convert_element_type | solution.py:47
  110.7 13.2 %collective-permute-done.1 = bf16[128,32,256]{2,1,0:T(8,128)(2,1)} collective-permute-done((bf16[128,32,256]{2,1,0:T(8,128)(2,1)}, bf16[128,32,256]{2,1,0:T(8,128)(2,1)}, u32[]{:S(2)}, u32[]{:S(2)}) %collective-permute-start.1) | collective-permute-done | bytes 2097184 | tf_op jit(solution)/shard_map/ppermute | solution.py:73
  123.9 3.2 %copy.76 = bf16[16,8,32,256]{3,1,2,0:T(8,128)(2,1)S(1)} copy(bf16[16,8,32,256]{3,2,1,0:T(8,128)(2,1)} %bitcast.44) | data formatting | bytes 4194304
  127.0 0.9 fusion.13
  128.7 3.0 %copy.75 = bf16[16,8,32,256]{3,1,2,0:T(8,128)(2,1)S(1)} copy(bf16[16,8,32,256]{3,2,1,0:T(8,128)(2,1)} %bitcast.42) | data formatting | bytes 4194304
  131.8 0.9 fusion.12
  133.4 0.9 convolution_add_fusion.2
  134.4 1.4 collective-permute-start.3
  135.8 0.9 convolution_add_fusion.3
  136.7 2.5 %collective-permute-start.2 = (f32[128,128]{0,1:T(8,128)S(1)}, f32[128,128]{0,1:T(8,128)S(1)}, u32[]{:S(2)}, u32[]{:S(2)}) collective-permute-start(f32[128,128]{0,1:T(8,128)S(1)} %convolution_add_fusion.3), channel_id=1, source_target_pairs={{8,0},{16,8},{24,16},{0,24},{9,1},{17,9},{25,17},{1,25},{10,2},{18... | collective-permute-start | bytes 196616 | tf_op jit(solution)/shard_map/ppermute | solution.py:108
  139.3 1.0 fusion.11
  140.3 0.9 fusion.4
  141.2 0.8 add_dynamic-update-slice_fusion.3
  142.0 0.9 collective-permute-done.2
  143.6 10.5 %all_to_all.20 = f32[8,128,64]{1,2,0:T(8,128)S(1)} all-to-all(f32[8,128,64]{1,2,0:T(8,128)S(1)} %bitcast.101), channel_id=1, replica_groups=mesh['ri'=4,'ao'=8] {'ao'}, dimensions={0} | all-to-all | bytes 524288 | tf_op jit(solution)/shard_map/all_to_all | solution.py:113
  (50 shorter events, 10.7 us)
Async XLA Ops:
  0.0 15.9 %copy-start.3 = (bf16[128,32,256]{2,1,0:T(8,128)(2,1)S(1)}, bf16[128,32,256]{2,1,0:T(8,128)(2,1)}, u32[]{:S(2)}) copy-start(bf16[128,32,256]{2,1,0:T(8,128)(2,1)} %param.11) | copy-start | bytes 6291460
  26.8 12.2 %copy-start.7 = (s32[4]{0:T(128)S(1)}, s32[4]{0:T(128)}, u32[]{:S(2)}) copy-start(s32[4]{0:T(128)} %constant.32.clone) | copy-start | bytes 52
  26.8 13.4 %copy-start.6 = (s32[4]{0:T(128)S(1)}, s32[4]{0:T(128)}, u32[]{:S(2)}) copy-start(s32[4]{0:T(128)} %constant.33.clone) | copy-start | bytes 52
  26.9 14.7 %copy-start.5 = (s32[4]{0:T(128)S(1)}, s32[4]{0:T(128)}, u32[]{:S(2)}) copy-start(s32[4]{0:T(128)} %constant.34.clone) | copy-start | bytes 52
  26.9 16.1 %copy-start.4 = (s32[4]{0:T(128)S(1)}, s32[4]{0:T(128)}, u32[]{:S(2)}) copy-start(s32[4]{0:T(128)} %constant.35.clone) | copy-start | bytes 52
  26.9 53.8 %all-to-all-start = ((bf16[2,256,32,128]{3,2,0,1:T(8,128)(2,1)}), bf16[2,256,32,128]{3,2,0,1:T(8,128)(2,1)}, u32[]{:S(2)}, u32[]{:S(2)}) async-start(bf16[2,256,32,128]{3,2,0,1:T(8,128)(2,1)} %copy.54), calls=%async_computation | async-start | bytes 8388608 | tf_op jit(solution)/shard_map/all_to_all | solution.py:91
  31.6 79.1 %collective-permute-start = (bf16[128,32,256]{2,1,0:T(8,128)(2,1)}, bf16[128,32,256]{2,1,0:T(8,128)(2,1)}, u32[]{:S(2)}, u32[]{:S(2)}) collective-permute-start(bf16[128,32,256]{2,1,0:T(8,128)(2,1)} %broadcast_multiply_fusion), channel_id=1, source_target_pairs={{0,8},{8,16},{16,24},{24,0},{1,9},{9,17},{17,25},{25,1},{2,10},{10... | collective-permute-start | bytes 6291464 | tf_op jit(solution)/shard_map/ppermute | solution.py:73
  33.2 90.7 %collective-permute-start.1 = (bf16[128,32,256]{2,1,0:T(8,128)(2,1)}, bf16[128,32,256]{2,1,0:T(8,128)(2,1)}, u32[]{:S(2)}, u32[]{:S(2)}) collective-permute-start(bf16[128,32,256]{2,1,0:T(8,128)(2,1)} %broadcast_multiply_fusion), channel_id=1, source_target_pairs={{0,16},{24,8},{1,17},{25,9},{2,18},{26,10},{3,19},{27,11},{4,20},{... | collective-permute-start | bytes 6291464 | tf_op jit(solution)/shard_map/ppermute | solution.py:73
  94.6 4.3 %copy-start.2 = (bf16[1,32,8,32,128]{4,3,1,2,0:T(8,128)(2,1)S(1)}, bf16[1,32,8,32,128]{4,3,1,2,0:T(8,128)(2,1)}, u32[]{:S(2)}) copy-start(bf16[1,32,8,32,128]{4,3,1,2,0:T(8,128)(2,1)} %get-tuple-element.20) | copy-start | bytes 6291460
  123.9 3.2 %copy-start = (bf16[8192,128]{1,0:T(8,128)(2,1)S(1)}, bf16[8192,128]{1,0:T(8,128)(2,1)}, u32[]{:S(2)}) copy-start(bf16[8192,128]{1,0:T(8,128)(2,1)} %get-tuple-element.12) | copy-start | bytes 6291460
  134.4 4.9 %copy-start.1 = (bf16[16,8,32,256]{3,1,2,0:T(8,128)(2,1)S(1)}, bf16[16,8,32,256]{3,1,2,0:T(8,128)(2,1)}, u32[]{:S(2)}) copy-start(bf16[16,8,32,256]{3,1,2,0:T(8,128)(2,1)} %copy.74) | copy-start | bytes 6291460
  134.4 9.2 %collective-permute-start.3 = (f32[128,128]{0,1:T(8,128)S(1)}, f32[128,128]{0,1:T(8,128)S(1)}, u32[]{:S(2)}, u32[]{:S(2)}) collective-permute-start(f32[128,128]{0,1:T(8,128)S(1)} %convolution_add_fusion.2), channel_id=1, source_target_pairs={{16,0},{8,24},{17,1},{9,25},{18,2},{10,26},{19,3},{11,27},{20,4},{... | collective-permute-start | bytes 196616 | tf_op jit(solution)/shard_map/ppermute | solution.py:108
  136.7 6.1 %collective-permute-start.2 = (f32[128,128]{0,1:T(8,128)S(1)}, f32[128,128]{0,1:T(8,128)S(1)}, u32[]{:S(2)}, u32[]{:S(2)}) collective-permute-start(f32[128,128]{0,1:T(8,128)S(1)} %convolution_add_fusion.3), channel_id=1, source_target_pairs={{8,0},{16,8},{24,16},{0,24},{9,1},{17,9},{25,17},{1,25},{10,2},{18... | collective-permute-start | bytes 196616 | tf_op jit(solution)/shard_map/ppermute | solution.py:108

commit v4 on v3

--- a/solution.py
+++ b/solution.py
@@ -48,9 +48,8 @@
 
 
 def slab_product(slab, hi, lo):
-    flat = slab.reshape(slab.shape[0], -1)
-    return jnp.dot(flat, hi, preferred_element_type=jnp.float32) + jnp.dot(
-        flat, lo, preferred_element_type=jnp.float32
+    return jnp.einsum("srk,prk->sp", slab, hi, preferred_element_type=jnp.float32) + jnp.einsum(
+        "srk,prk->sp", slab, lo, preferred_element_type=jnp.float32
     )
 
 
@@ -91,10 +90,10 @@
     swapped = lax.all_to_all(halves, "ao", 1, 2, tiled=True)
     occ_t = swapped[0]
     virt_t = swapped[1]
-    v_part = jnp.einsum("mn,lnp->lmp", virt_rows, occ_t, preferred_element_type=jnp.float32)
-    w_part = jnp.einsum("kl,nlq->nkq", occ_rows, virt_t, preferred_element_type=jnp.float32)
-    v_hi, v_lo = split_hi_lo(v_part.reshape(-1, rows))
-    w_hi, w_lo = split_hi_lo(w_part.reshape(-1, rows))
+    v_part = jnp.einsum("mn,lnp->plm", virt_rows, occ_t, preferred_element_type=jnp.float32)
+    w_part = jnp.einsum("kl,nlq->qnk", occ_rows, virt_t, preferred_element_type=jnp.float32)
+    v_hi, v_lo = split_hi_lo(v_part)
+    w_hi, w_lo = split_hi_lo(w_part)
 
     v_hi, v_lo, w_hi, w_lo, received = lax.optimization_barrier(
         (v_hi, v_lo, w_hi, w_lo, received)

time: 156 us -> 171 us (1.096)
  waiting for transfers between devices: 46.3 us -> 72.8 us
  local copies, waits for them, and re-layouts: 36.5 us -> 13.7 us
  matrix products: 18.8 us -> 37.5 us
  other arithmetic: 12.9 us -> 5.84 us
    ppermute x2, waiting for transfers between devices: 13.2 us -> 36.1 us  [per_device(): received = [lax.ppermute(own, 'ri', route) for route, _, _ in routes]]
    dot_general x12, matrix products: 14.1 us -> 34.3 us  [the longest x5 19.1 us: slab_product(): jnp.einsum('srk,prk->sp', slab, lo, preferred_element_type=jnp.float32)]
    transpose x2 -> x0, local copies, waits for them, and re-layouts: 11.2 us -> none  [the longest x1 5.63 us: per_device(): jnp.einsum('mn,lnp->lmp', virt_rows, occ_t, preferred_element_type=jnp.fl...]
    unnamed x19 -> x8, local copies, waits for them, and re-layouts: 10.5 us -> 0.01 us
    convert_element_type x2 -> x0, other arithmetic: 7.16 us -> none  [split_hi_lo(): (values - rounded).astype(jnp.bfloat16)]
    all_to_all x1, waiting for transfers between devices: 32.3 us -> 36.7 us  [per_device(): swapped = lax.all_to_all(halves, 'ao', 1, 2, tiled=True)]
  transfers between devices with their start and end apart: 5 -> 5, of which waited for: 3 -> 2; matrix products, arithmetic and copies ran while one was open for 27% -> 12% of each run, Pallas kernels for 0% -> 0%
where the time goes in v4:
time: 171 us; the launch traced here: 170 us
  waiting for transfers between devices  72.8 us (43%)
  matrix products  37.5 us (22%)
  blocking collectives  21.4 us (13%)
  starting transfers between devices  15.7 us (9%)
  local copies, waits for them, and re-layouts  13.7 us (8%)
  other arithmetic  5.84 us (3%)
  between operations  2.83 us (2%)
    all_to_all x1, waiting for transfers between devices, per_device(): swapped = lax.all_to_all(halves, 'ao', 1, 2, tiled=True)  36.7 us
    ppermute x2, waiting for transfers between devices, per_device(): received = [lax.ppermute(own, 'ri', route) for route, _, _ in routes]  36.1 us
    dot_general x5, matrix products, slab_product(): jnp.einsum('srk,prk->sp', slab, lo, preferred_element_type=jnp.float32)  19.1 us
    dot_general x5, matrix products, slab_product(): jnp.einsum('srk,prk->sp', slab, hi, preferred_element_type=jnp.float32)  13.7 us
    all_gather x1, blocking collectives, per_device(): full = lax.all_gather(stacked, 'ao', axis=1, tiled=True)  10.8 us
    all_to_all x1, blocking collectives, per_device(): got = lax.all_to_all(sent, 'ao', 0, 0, tiled=True)  10.6 us
    ppermute x2, starting transfers between devices, per_device(): received = [lax.ppermute(own, 'ri', route) for route, _, _ in routes]  7.44 us
    all_to_all x1, starting transfers between devices, per_device(): swapped = lax.all_to_all(halves, 'ao', 1, 2, tiled=True)  4.7 us
  transfers between devices with their start and end apart: 5, of which 2 were waited for; matrix products, arithmetic and copies ran while one was open for 12% of the time, Pallas kernels for 0%

profile of v4, /device:TPU:0, one launch (start us, length us, event | category | flops | bytes accessed | tf_op | source)
XLA Modules:
  0.0 169.8 jit_solution(6342562631553279702)
XLA Ops:
  0.0 0.7 convert_element_type.30
  1.1 0.7 convert_bitcast_fusion.2
  1.9 0.7 convert_bitcast_fusion.1
  2.7 0.7 multiply_bitcast_fusion
  3.5 10.8 %all_gather.3 = bf16[2,256,256]{2,1,0:T(8,128)(2,1)S(1)} all-gather(bf16[2,32,256]{2,1,0:T(8,128)(2,1)S(1)} %pad_maximum_fusion), channel_id=1, replica_groups=mesh['ri'=4,'ao'=8] {'ao'}, dimensions={1}, use_global_device_ids=true | all-gather | bytes 294912 | tf_op jit(solution)/shard_map/all_gather | solution.py:77
  14.2 0.7 fusion.74
  15.7 1.8 %broadcast_multiply_fusion = bf16[128,32,256]{2,1,0:T(8,128)(2,1)S(1)} fusion(bf16[128,32,256]{2,1,0:T(8,128)(2,1)} %param.11, bf16[128,256]{1,0:T(8,128)(2,1)S(1)} %copy.76), kind=kLoop, calls=%fused_computation.46 | loop fusion | flops 1048576 | bytes 4259840 | tf_op jit(solution)/shard_map/mul | solution.py:42
  17.5 3.2 %convert_bitcast_fusion = bf16[2,256,32,128]{3,1,2,0:T(8,128)(2,1)S(1)} fusion(bf16[128,32,256]{2,1,0:T(8,128)(2,1)S(1)} %broadcast_multiply_fusion, bf16[1,256,256]{1,2,0:T(8,128)(2,1)S(1)} %copy.78, bf16[1,256,256]{1,2,0:T(8,128)(2,1)S(1)} %copy.77), kind=kOutput, calls=%fused_computation.7 | convolution fusion | flops 1076363264 | bytes 6553600 | tf_op jit(solution)/shard_map/prk,dkc->dcrp/dot_general | solution.py:84
  20.6 4.7 %copy.80 = bf16[2,256,32,128]{3,2,0,1:T(8,128)(2,1)} copy(bf16[2,256,32,128]{3,1,2,0:T(8,128)(2,1)S(1)} %convert_bitcast_fusion) | data formatting | bytes 8388608 | tf_op jit(solution)/shard_map/convert_element_type | solution.py:89
  25.3 4.7 %all-to-all-start = ((bf16[2,256,32,128]{3,2,0,1:T(8,128)(2,1)}), bf16[2,256,32,128]{3,2,0,1:T(8,128)(2,1)}, u32[]{:S(2)}, u32[]{:S(2)}) async-start(bf16[2,256,32,128]{3,2,0,1:T(8,128)(2,1)} %copy.80), calls=%async_computation | async-start | bytes 8388608 | tf_op jit(solution)/shard_map/all_to_all | solution.py:90
  30.0 1.6 collective-permute-start
  31.7 5.8 %collective-permute-start.1 = (bf16[128,32,256]{2,1,0:T(8,128)(2,1)S(1)}, bf16[128,32,256]{2,1,0:T(8,128)(2,1)}, u32[]{:S(2)}, u32[]{:S(2)}) collective-permute-start(bf16[128,32,256]{2,1,0:T(8,128)(2,1)S(1)} %broadcast_multiply_fusion), channel_id=1, source_target_pairs={{0,16},{24,8},{1,17},{25,9},{2,18},{26,10},{3,19},{27,11},{4,20},{... | collective-permute-start | bytes 6291464 | tf_op jit(solution)/shard_map/ppermute | solution.py:72
  42.5 36.7 %all-to-all-done = bf16[2,256,32,128]{3,2,0,1:T(8,128)(2,1)} async-done(((bf16[2,256,32,128]{3,2,0,1:T(8,128)(2,1)}), bf16[2,256,32,128]{3,2,0,1:T(8,128)(2,1)}, u32[]{:S(2)}, u32[]{:S(2)}) %all-to-all-start) | async-done | bytes 4194336 | tf_op jit(solution)/shard_map/all_to_all | solution.py:90
  79.1 2.9 %copy.81 = bf16[2,256,32,128]{3,2,1,0:T(8,128)(2,1)S(1)} copy(bf16[2,256,32,128]{3,2,0,1:T(8,128)(2,1)} %all-to-all-done) | data formatting | bytes 8388608 | tf_op jit(solution)/shard_map/all_to_all | solution.py:90
  82.1 1.0 fusion.76
  84.3 0.8 fusion.1
  85.1 0.8 fusion
  85.9 36.1 %collective-permute-done.1 = bf16[128,32,256]{2,1,0:T(8,128)(2,1)} collective-permute-done((bf16[128,32,256]{2,1,0:T(8,128)(2,1)S(1)}, bf16[128,32,256]{2,1,0:T(8,128)(2,1)}, u32[]{:S(2)}, u32[]{:S(2)}) %collective-permute-start.1) | collective-permute-done | bytes 2097184 | tf_op jit(solution)/shard_map/ppermute | solution.py:72
  122.0 4.1 %fusion.45 = f32[128,128]{0,1:T(8,128)S(1)} fusion(bf16[128,32,256]{2,0,1:T(8,128)(2,1)S(1)} %get-tuple-element.12, bf16[128,32,256]{2,1,0:T(8,128)(2,1)} %collective-permute-done.1), kind=kOutput, calls=%fused_computation.37 | convolution fusion | flops 268435456 | bytes 4259840 | tf_op jit(solution)/shard_map/srk,prk->sp/dot_general | solution.py:51
  126.1 4.0 %fusion.39 = f32[128,128]{0,1:T(8,128)S(1)} fusion(bf16[128,32,256]{2,0,1:T(8,128)(2,1)S(1)} %get-tuple-element.15, bf16[128,32,256]{2,1,0:T(8,128)(2,1)} %collective-permute-done.1), kind=kOutput, calls=%fused_computation.35 | convolution fusion | flops 268435456 | bytes 4259840 | tf_op jit(solution)/shard_map/srk,prk->sp/dot_general | solution.py:51
  130.2 4.1 %fusion.33 = f32[128,128]{0,1:T(8,128)S(1)} fusion(bf16[128,32,256]{2,0,1:T(8,128)(2,1)S(1)} %get-tuple-element.12, bf16[128,32,256]{2,1,0:T(8,128)(2,1)} %collective-permute-done), kind=kOutput, calls=%fused_computation.33 | convolution fusion | flops 268435456 | bytes 4259840 | tf_op jit(solution)/shard_map/srk,prk->sp/dot_general | solution.py:51
  134.3 4.3 %fusion.27 = f32[128,128]{0,1:T(8,128)S(1)} fusion(bf16[128,32,256]{2,0,1:T(8,128)(2,1)S(1)} %get-tuple-element.15, bf16[128,32,256]{2,1,0:T(8,128)(2,1)} %collective-permute-done), kind=kOutput, calls=%fused_computation.31 | convolution fusion | flops 268435456 | bytes 4259840 | tf_op jit(solution)/shard_map/srk,prk->sp/dot_general | solution.py:51
  138.6 2.5 %fusion.51 = f32[128,128]{0,1:T(8,128)S(1)} fusion(bf16[128,32,256]{2,0,1:T(8,128)(2,1)S(1)} %get-tuple-element.12, bf16[128,32,256]{2,1,0:T(8,128)(2,1)S(1)} %broadcast_multiply_fusion), kind=kOutput, calls=%fused_computation.39 | convolution fusion | flops 268435456 | bytes 4259840 | tf_op jit(solution)/shard_map/srk,prk->sp/dot_general | solution.py:51
  141.1 3.1 %fusion.60 = f32[128,128]{0,1:T(8,128)S(1)} fusion(f32[128,128]{0,1:T(8,128)S(1)} %fusion.45, bf16[128,32,256]{2,0,1:T(8,128)(2,1)S(1)} %get-tuple-element.11, bf16[128,32,256]{2,1,0:T(8,128)(2,1)} %collective-permute-done.1), kind=kOutput, calls=%fused_computation.42 | convolution fusion | flops 268451840 | bytes 4325376 | tf_op jit(solution)/shard_map/srk,prk->sp/dot_general | solution.py:51
  144.2 1.3 collective-permute-start.3
  145.5 3.1 %fusion.66 = f32[128,128]{0,1:T(8,128)S(1)} fusion(f32[128,128]{0,1:T(8,128)S(1)} %fusion.33, bf16[128,32,256]{2,0,1:T(8,128)(2,1)S(1)} %get-tuple-element.11, bf16[128,32,256]{2,1,0:T(8,128)(2,1)} %collective-permute-done), kind=kOutput, calls=%fused_computation.44 | convolution fusion | flops 268451840 | bytes 4325376 | tf_op jit(solution)/shard_map/srk,prk->sp/dot_general | solution.py:51
  148.6 2.3 %collective-permute-start.2 = (f32[128,128]{0,1:T(8,128)S(1)}, f32[128,128]{0,1:T(8,128)S(1)}, u32[]{:S(2)}, u32[]{:S(2)}) collective-permute-start(f32[128,128]{0,1:T(8,128)S(1)} %fusion.66), channel_id=1, source_target_pairs={{8,0},{16,8},{24,16},{0,24},{9,1},{17,9},{25,17},{1,25},{10,2},{18... | collective-permute-start | bytes 196616 | tf_op jit(solution)/shard_map/ppermute | solution.py:107
  150.9 1.5 fusion.57
  152.4 3.0 %add_dynamic-update-slice_fusion.3 = f32[128,512]{0,1:T(8,128)S(1)} fusion(f32[128,512]{0,1:T(8,128)S(1)} %fusion.57, s32[]{:T(128)S(6)} %select_n.38, f32[128,128]{0,1:T(8,128)S(1)} %fusion.27, bf16[128,32,256]{2,0,1:T(8,128)(2,1)S(1)} %get-tuple-element.13, bf16[128,32,256]{2,1,0:T(8,128)(2,1)} %collective-permute-done), kind=kOutput, calls=%fused_computation.53 | convolution fusion | flops 268468224 | bytes 4390916 | tf_op jit(solution)/shard_map/srk,prk->sp/dot_general | solution.py:51
  155.5 3.0 %add_dynamic-update-slice_fusion.1 = f32[128,512]{0,1:T(8,128)S(1)} fusion(f32[128,512]{0,1:T(8,128)S(1)} %add_dynamic-update-slice_fusion.2, s32[]{:T(128)S(6)} %select_n.40, f32[128,128]{0,1:T(8,128)S(1)} %fusion.39, bf16[128,32,256]{2,0,1:T(8,128)(2,1)S(1)} %get-tuple-element.13, bf16[128,32,256]{2,1,0:T(8,128)(2,1)} %collective-permute-done.1), kind=kOutput, calls=%fused_computation.51 | convolution fusion | flops 268468224 | bytes 4390916 | tf_op jit(solution)/shard_map/srk,prk->sp/dot_general | solution.py:51
  158.6 10.6 %all_to_all.20 = f32[8,128,64]{1,2,0:T(8,128)S(1)} all-to-all(f32[8,128,64]{1,2,0:T(8,128)S(1)} %bitcast.103), channel_id=1, replica_groups=mesh['ri'=4,'ao'=8] {'ao'}, dimensions={0} | all-to-all | bytes 524288 | tf_op jit(solution)/shard_map/all_to_all | solution.py:112
  169.2 0.6 reduce_sum.9
  (35 shorter events, 5.2 us)
Async XLA Ops:
  25.3 12.2 %copy-start.3 = (s32[4]{0:T(128)S(1)}, s32[4]{0:T(128)}, u32[]{:S(2)}) copy-start(s32[4]{0:T(128)} %constant.32.clone) | copy-start | bytes 52
  25.3 13.4 %copy-start.2 = (s32[4]{0:T(128)S(1)}, s32[4]{0:T(128)}, u32[]{:S(2)}) copy-start(s32[4]{0:T(128)} %constant.33.clone) | copy-start | bytes 52
  25.3 14.7 %copy-start.1 = (s32[4]{0:T(128)S(1)}, s32[4]{0:T(128)}, u32[]{:S(2)}) copy-start(s32[4]{0:T(128)} %constant.34.clone) | copy-start | bytes 52
  25.3 15.9 %copy-start = (s32[4]{0:T(128)S(1)}, s32[4]{0:T(128)}, u32[]{:S(2)}) copy-start(s32[4]{0:T(128)} %constant.35.clone) | copy-start | bytes 52
  25.3 53.8 %all-to-all-start = ((bf16[2,256,32,128]{3,2,0,1:T(8,128)(2,1)}), bf16[2,256,32,128]{3,2,0,1:T(8,128)(2,1)}, u32[]{:S(2)}, u32[]{:S(2)}) async-start(bf16[2,256,32,128]{3,2,0,1:T(8,128)(2,1)} %copy.80), calls=%async_computation | async-start | bytes 8388608 | tf_op jit(solution)/shard_map/all_to_all | solution.py:90
  30.0 55.9 %collective-permute-start = (bf16[128,32,256]{2,1,0:T(8,128)(2,1)S(1)}, bf16[128,32,256]{2,1,0:T(8,128)(2,1)}, u32[]{:S(2)}, u32[]{:S(2)}) collective-permute-start(bf16[128,32,256]{2,1,0:T(8,128)(2,1)S(1)} %broadcast_multiply_fusion), channel_id=1, source_target_pairs={{0,8},{8,16},{16,24},{24,0},{1,9},{9,17},{17,25},{25,1},{2,10},{10... | collective-permute-start | bytes 6291464 | tf_op jit(solution)/shard_map/ppermute | solution.py:72
  31.7 90.4 %collective-permute-start.1 = (bf16[128,32,256]{2,1,0:T(8,128)(2,1)S(1)}, bf16[128,32,256]{2,1,0:T(8,128)(2,1)}, u32[]{:S(2)}, u32[]{:S(2)}) collective-permute-start(bf16[128,32,256]{2,1,0:T(8,128)(2,1)S(1)} %broadcast_multiply_fusion), channel_id=1, source_target_pairs={{0,16},{24,8},{1,17},{25,9},{2,18},{26,10},{3,19},{27,11},{4,20},{... | collective-permute-start | bytes 6291464 | tf_op jit(solution)/shard_map/ppermute | solution.py:72
  144.2 14.3 %collective-permute-start.3 = (f32[128,128]{0,1:T(8,128)S(1)}, f32[128,128]{0,1:T(8,128)S(1)}, u32[]{:S(2)}, u32[]{:S(2)}) collective-permute-start(f32[128,128]{0,1:T(8,128)S(1)} %fusion.60), channel_id=1, source_target_pairs={{16,0},{8,24},{17,1},{9,25},{18,2},{10,26},{19,3},{11,27},{20,4},{... | collective-permute-start | bytes 196616 | tf_op jit(solution)/shard_map/ppermute | solution.py:107
  148.6 6.9 %collective-permute-start.2 = (f32[128,128]{0,1:T(8,128)S(1)}, f32[128,128]{0,1:T(8,128)S(1)}, u32[]{:S(2)}, u32[]{:S(2)}) collective-permute-start(f32[128,128]{0,1:T(8,128)S(1)} %fusion.66), channel_id=1, source_target_pairs={{8,0},{16,8},{24,16},{0,24},{9,1},{17,9},{25,17},{1,25},{10,2},{18... | collective-permute-start | bytes 196616 | tf_op jit(solution)/shard_map/ppermute | solution.py:107

commit v5 on v4

--- a/solution.py
+++ b/solution.py
@@ -47,10 +47,10 @@
     return rounded.astype(jnp.bfloat16), (values - rounded).astype(jnp.bfloat16)
 
 
-def slab_product(slab, hi, lo):
-    return jnp.einsum("srk,prk->sp", slab, hi, preferred_element_type=jnp.float32) + jnp.einsum(
-        "srk,prk->sp", slab, lo, preferred_element_type=jnp.float32
-    )
+def slab_product(flat, weights):
+    out = jnp.dot(flat, weights, preferred_element_type=jnp.float32)
+    half = weights.shape[1] // 2
+    return out[:, :half] + out[:, half:]
 
 
 def add_cols(total, part, col_block):
@@ -69,7 +69,8 @@
 
     routes = pair_routes(planes)
     own = mask_slab(tensor, live_blocks)
-    received = [lax.ppermute(own, "ri", route) for route, _, _ in routes]
+    own_flat = own.reshape(rows, -1)
+    received = [lax.ppermute(own_flat, "ri", route) for route, _, _ in routes]
 
     stacked = jnp.stack(
         [screen_density(occ_density, occ_mask), screen_density(virt_density, virt_mask)]
@@ -92,19 +93,22 @@
     virt_t = swapped[1]
     v_part = jnp.einsum("mn,lnp->plm", virt_rows, occ_t, preferred_element_type=jnp.float32)
     w_part = jnp.einsum("kl,nlq->qnk", occ_rows, virt_t, preferred_element_type=jnp.float32)
-    v_hi, v_lo = split_hi_lo(v_part)
-    w_hi, w_lo = split_hi_lo(w_part)
+    v_hi, v_lo = split_hi_lo(v_part.reshape(rows, -1))
+    w_hi, w_lo = split_hi_lo(w_part.reshape(rows, -1))
+    v_weights = jnp.concatenate([v_hi, v_lo]).T
+    w_weights = jnp.concatenate([w_hi, w_lo]).T
+    diag = slab_product(own_flat, w_weights)
 
-    v_hi, v_lo, w_hi, w_lo, received = lax.optimization_barrier(
-        (v_hi, v_lo, w_hi, w_lo, received)
+    v_weights, w_weights, diag, received = lax.optimization_barrier(
+        (v_weights, w_weights, diag, received)
     )
     total = jnp.zeros((rows, planes * rows), jnp.float32)
-    total = add_cols(total, slab_product(own, w_hi, w_lo), plane)
+    total = add_cols(total, diag, plane)
     for slab, (route, recv_from, send_to) in zip(received, routes):
         source = jnp.array(recv_from, jnp.int32)[plane]
         target = jnp.array(send_to, jnp.int32)[plane]
-        total = add_cols(total, slab_product(slab, v_hi, v_lo).T, source)
-        back = lax.ppermute(slab_product(slab, w_hi, w_lo), "ri", [(d, s) for s, d in route])
+        total = add_cols(total, slab_product(slab, v_weights).T, source)
+        back = lax.ppermute(slab_product(slab, w_weights), "ri", [(d, s) for s, d in route])
         total = add_cols(total, back, target)
 
     width = total.shape[1] // cycle_size

time: 171 us -> 153 us (0.89)
  waiting for transfers between devices: 72.8 us -> 49.1 us
  matrix products: 37.5 us -> 19.4 us
  local copies, waits for them, and re-layouts: 13.7 us -> 29.4 us
  other arithmetic: 5.84 us -> 14.8 us
    dot_general x10 -> x5, matrix products: 32.8 us -> 10.8 us  [slab_product(): out = jnp.dot(flat, weights, preferred_element_type=jnp.float32)]
    ppermute x4, waiting for transfers between devices: 36.1 us -> 15.5 us  [the longest x2 11.4 us: per_device(): received = [lax.ppermute(own_flat, 'ri', route) for route, _, _ in routes]]
    transpose x0 -> x2, local copies, waits for them, and re-layouts: none -> 11.1 us  [the longest x1 5.56 us: per_device(): jnp.einsum('mn,lnp->plm', virt_rows, occ_t, preferred_element_type=jnp.fl...]
    convert_element_type x0 -> x2, other arithmetic: none -> 7.95 us  [split_hi_lo(): rounded.astype(jnp.bfloat16)]
    unnamed x8 -> x15, local copies, waits for them, and re-layouts: 0.01 us -> 3.26 us
    all_to_all x1, waiting for transfers between devices: 36.7 us -> 33.6 us  [per_device(): swapped = lax.all_to_all(halves, 'ao', 1, 2, tiled=True)]
    dot_general x1, matrix products: 0.78 us -> 2.74 us  [per_device(): jnp.einsum('kl,nlq->qnk', occ_rows, virt_t, preferred_element_type=jnp.fl...]
    dot_general x1, matrix products: 0.77 us -> 2.73 us  [per_device(): jnp.einsum('mn,lnp->plm', virt_rows, occ_t, preferred_element_type=jnp.fl...]
  transfers between devices with their start and end apart: 5 -> 5, of which waited for: 2 -> 3; matrix products, arithmetic and copies ran while one was open for 12% -> 26% of each run, Pallas kernels for 0% -> 0%
where the time goes in v5:
time: 153 us; the launch traced here: 152 us
  waiting for transfers between devices  49.1 us (32%)
  local copies, waits for them, and re-layouts  29.4 us (19%)
  blocking collectives  21.3 us (14%)
  matrix products  19.4 us (13%)
  starting transfers between devices  15.5 us (10%)
  other arithmetic  14.8 us (10%)
  between operations  3.04 us (2%)
    all_to_all x1, waiting for transfers between devices, per_device(): swapped = lax.all_to_all(halves, 'ao', 1, 2, tiled=True)  33.6 us
    ppermute x2, waiting for transfers between devices, per_device(): received = [lax.ppermute(own_flat, 'ri', route) for route, _, _ in routes]  11.4 us
    dot_general x5, matrix products, slab_product(): out = jnp.dot(flat, weights, preferred_element_type=jnp.float32)  10.8 us
    all_gather x1, blocking collectives, per_device(): full = lax.all_gather(stacked, 'ao', axis=1, tiled=True)  10.8 us
    all_to_all x1, blocking collectives, per_device(): got = lax.all_to_all(sent, 'ao', 0, 0, tiled=True)  10.5 us
    convert_element_type x2, other arithmetic, split_hi_lo(): rounded.astype(jnp.bfloat16)  7.95 us
    ppermute x2, starting transfers between devices, per_device(): received = [lax.ppermute(own_flat, 'ri', route) for route, _, _ in routes]  7.39 us
    transpose x1, local copies, waits for them, and re-layouts, per_device(): jnp.einsum('mn,lnp->plm', virt_rows, occ_t, preferred_element_type=jnp.fl...  5.56 us
  transfers between devices with their start and end apart: 5, of which 3 were waited for; matrix products, arithmetic and copies ran while one was open for 26% of the time, Pallas kernels for 0%

profile of v5, /device:TPU:0, one launch (start us, length us, event | category | flops | bytes accessed | tf_op | source)
XLA Modules:
  0.0 152.5 jit_solution(15009313593799279018)
XLA Ops:
  0.8 0.7 convert_bitcast_fusion.1
  1.6 0.7 multiply_bitcast_fusion
  2.4 10.8 %all_gather.3 = bf16[2,256,256]{2,1,0:T(8,128)(2,1)S(1)} all-gather(bf16[2,32,256]{2,1,0:T(8,128)(2,1)S(1)} %pad_maximum_fusion.2), channel_id=1, replica_groups=mesh['ri'=4,'ao'=8] {'ao'}, dimensions={1}, use_global_device_ids=true | all-gather | bytes 294912 | tf_op jit(solution)/shard_map/all_gather | solution.py:78
  14.6 0.7 convert_element_type.32
  15.7 1.8 %broadcast_multiply_fusion = bf16[128,32,256]{2,1,0:T(8,128)(2,1)S(1)} fusion(bf16[128,32,256]{2,1,0:T(8,128)(2,1)} %param.11, bf16[128,256]{1,0:T(8,128)(2,1)S(1)} %copy.55), kind=kLoop, calls=%fused_computation.16 | loop fusion | flops 1048576 | bytes 4259840 | tf_op jit(solution)/shard_map/mul | solution.py:42
  17.5 3.2 %convert_bitcast_fusion = bf16[2,256,32,128]{3,1,2,0:T(8,128)(2,1)S(1)} fusion(bf16[128,32,256]{2,1,0:T(8,128)(2,1)S(1)} %broadcast_multiply_fusion, bf16[1,256,256]{1,2,0:T(8,128)(2,1)S(1)} %copy.53, bf16[1,256,256]{1,2,0:T(8,128)(2,1)S(1)} %copy.52), kind=kOutput, calls=%fused_computation.9 | convolution fusion | flops 1076363264 | bytes 6553600 | tf_op jit(solution)/shard_map/prk,dkc->dcrp/dot_general | solution.py:85
  20.6 4.7 %copy.57 = bf16[2,256,32,128]{3,2,0,1:T(8,128)(2,1)} copy(bf16[2,256,32,128]{3,1,2,0:T(8,128)(2,1)S(1)} %convert_bitcast_fusion) | data formatting | bytes 8388608 | tf_op jit(solution)/shard_map/convert_element_type | solution.py:90
  25.3 4.5 %all-to-all-start = ((bf16[2,256,32,128]{3,2,0,1:T(8,128)(2,1)}), bf16[2,256,32,128]{3,2,0,1:T(8,128)(2,1)}, u32[]{:S(2)}, u32[]{:S(2)}) async-start(bf16[2,256,32,128]{3,2,0,1:T(8,128)(2,1)} %copy.57), calls=%async_computation | async-start | bytes 8388608 | tf_op jit(solution)/shard_map/all_to_all | solution.py:91
  29.9 2.8 %copy.76 = bf16[16,8,32,256]{3,1,2,0:T(8,128)(2,1)} copy(bf16[16,8,32,256]{3,2,1,0:T(8,128)(2,1)S(1)} %bitcast.89) | data formatting | bytes 4194304
  32.7 1.6 %collective-permute-start = (bf16[128,8192]{1,0:T(8,128)(2,1)}, bf16[128,8192]{1,0:T(8,128)(2,1)S(1)}, u32[]{:S(2)}, u32[]{:S(2)}) collective-permute-start(bf16[128,8192]{1,0:T(8,128)(2,1)} %bitcast.45), channel_id=1, source_target_pairs={{0,8},{8,16},{16,24},{24,0},{1,9},{9,17},{17,25},{25,1},{2,10},{10... | collective-permute-start | bytes 6291464 | tf_op jit(solution)/shard_map/ppermute | solution.py:73
  34.2 5.8 %collective-permute-start.1 = (bf16[128,8192]{1,0:T(8,128)(2,1)}, bf16[128,8192]{1,0:T(8,128)(2,1)}, u32[]{:S(2)}, u32[]{:S(2)}) collective-permute-start(bf16[128,8192]{1,0:T(8,128)(2,1)} %bitcast.45), channel_id=1, source_target_pairs={{0,16},{24,8},{1,17},{25,9},{2,18},{26,10},{3,19},{27,11},{4,20},{... | collective-permute-start | bytes 6291464 | tf_op jit(solution)/shard_map/ppermute | solution.py:73
  41.3 0.7 dynamic_slice.26
  44.0 0.7 dynamic_slice.30
  45.4 33.6 %all-to-all-done = bf16[2,256,32,128]{3,2,0,1:T(8,128)(2,1)} async-done(((bf16[2,256,32,128]{3,2,0,1:T(8,128)(2,1)}), bf16[2,256,32,128]{3,2,0,1:T(8,128)(2,1)}, u32[]{:S(2)}, u32[]{:S(2)}) %all-to-all-start) | async-done | bytes 4194336 | tf_op jit(solution)/shard_map/all_to_all | solution.py:91
  79.0 2.9 %copy.58 = bf16[2,256,32,128]{3,2,1,0:T(8,128)(2,1)S(1)} copy(bf16[2,256,32,128]{3,2,0,1:T(8,128)(2,1)} %all-to-all-done) | data formatting | bytes 8388608 | tf_op jit(solution)/shard_map/all_to_all | solution.py:91
  81.9 2.1 %fusion.17 = (bf16[1,32,8,32,128]{4,3,1,2,0:T(8,128)(2,1)S(1)}, bf16[1,32,8,32,128]{4,3,1,2,0:T(8,128)(2,1)}) fusion(bf16[2,32,8,32,128]{4,3,1,2,0:T(8,128)(2,1)S(1)} %bitcast.90), kind=kLoop, calls=%fused_computation.44 | loop fusion | bytes 8388608 | tf_op jit(solution)/shard_map/slice | solution.py:93
  84.6 2.7 %convolution_bitcast_fusion = f32[128,32,256]{2,0,1:T(8,128)} fusion(bf16[32,256,128]{2,1,0:T(8,128)(2,1)S(1)} %bitcast.91, bf16[256,256,1]{1,0,2:T(8,128)(2,1)S(1)} %bitcast.97), kind=kOutput, calls=%fused_computation.12 | convolution fusion | flops 536870912 | bytes 6422528 | tf_op jit(solution)/shard_map/kl,nlq->qnk/dot_general | solution.py:95
  87.3 5.6 %copy.64 = f32[128,32,256]{0,2,1:T(8,128)} copy(f32[128,32,256]{2,0,1:T(8,128)} %convolution_bitcast_fusion) | data formatting | bytes 8388608 | tf_op jit(solution)/shard_map/kl,nlq->qnk/transpose | solution.py:95
  92.9 5.0 %reduce-precision_convert_fusion = (bf16[128,8192]{0,1:T(8,128)(2,1)}, bf16[128,8192]{0,1:T(8,128)(2,1)}) fusion(f32[128,32,256]{0,2,1:T(8,128)} %copy.64), kind=kLoop, calls=%fused_computation.2 | loop fusion | flops 4194304 | bytes 8388608 | tf_op jit(solution)/shard_map/convert_element_type | solution.py:47
  98.4 2.7 %convolution_bitcast_fusion.1 = f32[128,32,256]{2,0,1:T(8,128)} fusion(bf16[32,256,128]{2,1,0:T(8,128)(2,1)S(1)} %bitcast.92, bf16[256,256,1]{1,0,2:T(8,128)(2,1)S(1)} %bitcast.95), kind=kOutput, calls=%fused_computation.13 | convolution fusion | flops 536870912 | bytes 6422528 | tf_op jit(solution)/shard_map/mn,lnp->plm/dot_general | solution.py:94
  101.1 5.6 %copy.61 = f32[128,32,256]{0,2,1:T(8,128)} copy(f32[128,32,256]{2,0,1:T(8,128)} %convolution_bitcast_fusion.1) | data formatting | bytes 8388608 | tf_op jit(solution)/shard_map/mn,lnp->plm/transpose | solution.py:94
  106.7 3.0 %reduce-precision_convert_fusion.1 = (bf16[128,8192]{0,1:T(8,128)(2,1)S(1)}, bf16[128,8192]{0,1:T(8,128)(2,1)S(1)}) fusion(f32[128,32,256]{0,2,1:T(8,128)} %copy.61), kind=kLoop, calls=%fused_computation.4 | loop fusion | flops 4194304 | bytes 8388608 | tf_op jit(solution)/shard_map/convert_element_type | solution.py:47
  110.2 2.4 %fusion.2 = f32[128,256]{1,0:T(8,128)S(1)} fusion(bf16[128,8192]{1,0:T(8,128)(2,1)} %bitcast.45, bf16[128,8192]{0,1:T(8,128)(2,1)S(1)} %copy-done.2, bf16[128,8192]{0,1:T(8,128)(2,1)S(1)} %copy-done.1), kind=kOutput, calls=%fused_computation.10 | convolution fusion | flops 545259520 | bytes 6422528 | tf_op jit(solution)/shard_map/dot_general | solution.py:51
  113.6 11.4 %collective-permute-done.1 = bf16[128,8192]{1,0:T(8,128)(2,1)} collective-permute-done((bf16[128,8192]{1,0:T(8,128)(2,1)}, bf16[128,8192]{1,0:T(8,128)(2,1)}, u32[]{:S(2)}, u32[]{:S(2)}) %collective-permute-start.1) | collective-permute-done | bytes 2097184 | tf_op jit(solution)/shard_map/ppermute | solution.py:73
  124.9 3.4 %fusion.22 = f32[128,256]{0,1:T(8,128)S(1)} fusion(bf16[128,8192]{1,0:T(8,128)(2,1)} %collective-permute-done.1, bf16[8192,256]{1,0:T(8,128)(2,1)S(1)} %fusion.3), kind=kOutput, calls=%fused_computation.49 | convolution fusion | flops 536870912 | bytes 6422528 | tf_op jit(solution)/shard_map/dot_general | solution.py:51
  128.3 2.4 %fusion.21 = f32[128,256]{1,0:T(8,128)S(1)} fusion(bf16[128,8192]{1,0:T(8,128)(2,1)} %collective-permute-done.1, bf16[8192,256]{1,0:T(8,128)(2,1)S(1)} %maximum_bitcast_fusion), kind=kOutput, calls=%fused_computation.48 | convolution fusion | flops 536870912 | bytes 6422528 | tf_op jit(solution)/shard_map/dot_general | solution.py:51
  130.7 1.8 %fusion.20 = f32[128,256]{0,1:T(8,128)S(1)} fusion(bf16[128,8192]{1,0:T(8,128)(2,1)S(1)} %collective-permute-done, bf16[8192,256]{1,0:T(8,128)(2,1)S(1)} %fusion.3), kind=kOutput, calls=%fused_computation.47 | convolution fusion | flops 536870912 | bytes 6422528 | tf_op jit(solution)/shard_map/dot_general | solution.py:51
  132.6 0.8 fusion.19
  133.4 1.3 collective-permute-start.3
  134.7 2.3 %collective-permute-start.2 = (f32[128,128]{0,1:T(8,128)S(1)}, f32[128,128]{0,1:T(8,128)S(1)}, u32[]{:S(2)}, u32[]{:S(2)}) collective-permute-start(f32[128,128]{0,1:T(8,128)S(1)} %slice_add_fusion.2), channel_id=1, source_target_pairs={{8,0},{16,8},{24,16},{0,24},{9,1},{17,9},{25,17},{1,25},{10,2},{18... | collective-permute-start | bytes 196616 | tf_op jit(solution)/shard_map/ppermute | solution.py:111
  137.2 4.1 %collective-permute-done.2 = f32[128,128]{0,1:T(8,128)S(1)} collective-permute-done((f32[128,128]{0,1:T(8,128)S(1)}, f32[128,128]{0,1:T(8,128)S(1)}, u32[]{:S(2)}, u32[]{:S(2)}) %collective-permute-start.2) | collective-permute-done | bytes 65568 | tf_op jit(solution)/shard_map/ppermute | solution.py:111
  141.3 10.5 %all_to_all.20 = f32[8,128,64]{1,2,0:T(8,128)S(1)} all-to-all(f32[8,128,64]{1,2,0:T(8,128)S(1)} %bitcast.93), channel_id=1, replica_groups=mesh['ri'=4,'ao'=8] {'ao'}, dimensions={0} | all-to-all | bytes 524288 | tf_op jit(solution)/shard_map/all_to_all | solution.py:116
  (50 shorter events, 7.4 us)
Async XLA Ops:
  25.3 53.7 %all-to-all-start = ((bf16[2,256,32,128]{3,2,0,1:T(8,128)(2,1)}), bf16[2,256,32,128]{3,2,0,1:T(8,128)(2,1)}, u32[]{:S(2)}, u32[]{:S(2)}) async-start(bf16[2,256,32,128]{3,2,0,1:T(8,128)(2,1)} %copy.57), calls=%async_computation | async-start | bytes 8388608 | tf_op jit(solution)/shard_map/all_to_all | solution.py:91
  29.9 10.2 %copy-start.6 = (s32[4]{0:T(128)S(1)}, s32[4]{0:T(128)}, u32[]{:S(2)}) copy-start(s32[4]{0:T(128)} %constant.32.clone) | copy-start | bytes 52
  29.9 11.4 %copy-start.5 = (s32[4]{0:T(128)S(1)}, s32[4]{0:T(128)}, u32[]{:S(2)}) copy-start(s32[4]{0:T(128)} %constant.33.clone) | copy-start | bytes 52
  29.9 12.8 %copy-start.4 = (s32[4]{0:T(128)S(1)}, s32[4]{0:T(128)}, u32[]{:S(2)}) copy-start(s32[4]{0:T(128)} %constant.34.clone) | copy-start | bytes 52
  29.9 14.1 %copy-start.3 = (s32[4]{0:T(128)S(1)}, s32[4]{0:T(128)}, u32[]{:S(2)}) copy-start(s32[4]{0:T(128)} %constant.35.clone) | copy-start | bytes 52
  32.7 80.9 %collective-permute-start = (bf16[128,8192]{1,0:T(8,128)(2,1)}, bf16[128,8192]{1,0:T(8,128)(2,1)S(1)}, u32[]{:S(2)}, u32[]{:S(2)}) collective-permute-start(bf16[128,8192]{1,0:T(8,128)(2,1)} %bitcast.45), channel_id=1, source_target_pairs={{0,8},{8,16},{16,24},{24,0},{1,9},{9,17},{17,25},{25,1},{2,10},{10... | collective-permute-start | bytes 6291464 | tf_op jit(solution)/shard_map/ppermute | solution.py:73
  34.2 90.7 %collective-permute-start.1 = (bf16[128,8192]{1,0:T(8,128)(2,1)}, bf16[128,8192]{1,0:T(8,128)(2,1)}, u32[]{:S(2)}, u32[]{:S(2)}) collective-permute-start(bf16[128,8192]{1,0:T(8,128)(2,1)} %bitcast.45), channel_id=1, source_target_pairs={{0,16},{24,8},{1,17},{25,9},{2,18},{26,10},{3,19},{27,11},{4,20},{... | collective-permute-start | bytes 6291464 | tf_op jit(solution)/shard_map/ppermute | solution.py:73
  92.9 5.0 %copy-start = (bf16[1,32,8,32,128]{4,3,1,2,0:T(8,128)(2,1)S(1)}, bf16[1,32,8,32,128]{4,3,1,2,0:T(8,128)(2,1)}, u32[]{:S(2)}) copy-start(bf16[1,32,8,32,128]{4,3,1,2,0:T(8,128)(2,1)} %get-tuple-element.18) | copy-start | bytes 6291460
  106.7 3.0 %copy-start.1 = (bf16[128,8192]{0,1:T(8,128)(2,1)S(1)}, bf16[128,8192]{0,1:T(8,128)(2,1)}, u32[]{:S(2)}) copy-start(bf16[128,8192]{0,1:T(8,128)(2,1)} %get-tuple-element.15) | copy-start | bytes 6291460
  106.7 3.5 %copy-start.2 = (bf16[128,8192]{0,1:T(8,128)(2,1)S(1)}, bf16[128,8192]{0,1:T(8,128)(2,1)}, u32[]{:S(2)}) copy-start(bf16[128,8192]{0,1:T(8,128)(2,1)} %get-tuple-element.16) | copy-start | bytes 6291460
  133.4 7.9 %collective-permute-start.3 = (f32[128,128]{0,1:T(8,128)S(1)}, f32[128,128]{0,1:T(8,128)S(1)}, u32[]{:S(2)}, u32[]{:S(2)}) collective-permute-start(f32[128,128]{0,1:T(8,128)S(1)} %slice_add_fusion), channel_id=1, source_target_pairs={{16,0},{8,24},{17,1},{9,25},{18,2},{10,26},{19,3},{11,27},{20,4},{... | collective-permute-start | bytes 196616 | tf_op jit(solution)/shard_map/ppermute | solution.py:111
  134.7 6.5 %collective-permute-start.2 = (f32[128,128]{0,1:T(8,128)S(1)}, f32[128,128]{0,1:T(8,128)S(1)}, u32[]{:S(2)}, u32[]{:S(2)}) collective-permute-start(f32[128,128]{0,1:T(8,128)S(1)} %slice_add_fusion.2), channel_id=1, source_target_pairs={{8,0},{16,8},{24,16},{0,24},{9,1},{17,9},{25,17},{1,25},{10,2},{18... | collective-permute-start | bytes 196616 | tf_op jit(solution)/shard_map/ppermute | solution.py:111

commit v6 on v5

--- a/solution.py
+++ b/solution.py
@@ -53,6 +53,39 @@
     return out[:, :half] + out[:, half:]
 
 
+def gather_rows(block, cycle_size):
+    me = lax.axis_index("ao")
+    pieces = [block]
+    for dist in range(1, cycle_size):
+        route = [(i, (i + dist) % cycle_size) for i in range(cycle_size)]
+        pieces.append(lax.ppermute(block, "ao", route))
+    stacked = jnp.stack(pieces)
+    order = (me - jnp.arange(cycle_size, dtype=jnp.int32)) % cycle_size
+    got = jnp.take(stacked, order, axis=0)
+    return jnp.moveaxis(got, 0, 1).reshape(
+        block.shape[0], cycle_size * block.shape[1], block.shape[2]
+    )
+
+
+def swap_blocks(halves, cycle_size):
+    me = lax.axis_index("ao")
+    width = halves.shape[1] // cycle_size
+    pieces = []
+    for dist in range(cycle_size):
+        start = ((me + dist) % cycle_size) * width
+        piece = lax.dynamic_slice_in_dim(halves, start, width, axis=1)
+        if dist:
+            route = [(i, (i + dist) % cycle_size) for i in range(cycle_size)]
+            piece = lax.ppermute(piece, "ao", route)
+        pieces.append(piece)
+    stacked = jnp.stack(pieces)
+    order = (me - jnp.arange(cycle_size, dtype=jnp.int32)) % cycle_size
+    got = jnp.take(stacked, order, axis=0)
+    return jnp.moveaxis(got, 0, 2).reshape(
+        halves.shape[0], width, cycle_size * halves.shape[2], halves.shape[3]
+    )
+
+
 def add_cols(total, part, col_block):
     rows = part.shape[0]
     at = (jnp.int32(0), col_block * rows)
@@ -75,7 +108,7 @@
     stacked = jnp.stack(
         [screen_density(occ_density, occ_mask), screen_density(virt_density, virt_mask)]
     )
-    full = lax.all_gather(stacked, "ao", axis=1, tiled=True)
+    full = gather_rows(stacked, cycle_size)
     ao_total = full.shape[2]
     all_blocks = ao_total // BS
     picked = full.reshape(2, all_blocks, BS, ao_total)[:, pair_slots[0]]
@@ -88,7 +121,7 @@
         jnp.stack([occ_rows, virt_rows]),
         preferred_element_type=jnp.float32,
     ).astype(jnp.bfloat16)
-    swapped = lax.all_to_all(halves, "ao", 1, 2, tiled=True)
+    swapped = swap_blocks(halves, cycle_size)
     occ_t = swapped[0]
     virt_t = swapped[1]
     v_part = jnp.einsum("mn,lnp->plm", virt_rows, occ_t, preferred_element_type=jnp.float32)

time: 153 us -> 157 us (1.026)
  starting transfers between devices: 15.5 us -> 44.6 us
  waiting for transfers between devices: 49.1 us -> 21.5 us
  blocking collectives: 21.3 us -> 9.66 us
  local copies, waits for them, and re-layouts: 29.4 us -> 38.3 us
  other arithmetic: 14.8 us -> 17.6 us
  matrix products: 19.4 us -> 21.3 us
    ppermute x0 -> x14, starting transfers between devices: none -> 34.4 us  [the longest x7 24.5 us: swap_blocks(): piece = lax.ppermute(piece, 'ao', route)]
    all_to_all x1 -> x0, waiting for transfers between devices: 33.6 us -> none  [per_device(): swapped = lax.all_to_all(halves, 'ao', 1, 2, tiled=True)]
    ppermute x0 -> x14, waiting for transfers between devices: none -> 17.3 us  [the longest x7 15.8 us: swap_blocks(): piece = lax.ppermute(piece, 'ao', route)]
    ppermute x2, waiting for transfers between devices: 11.4 us -> 0.01 us  [per_device(): received = [lax.ppermute(own_flat, 'ri', route) for route, _, _ in routes]]
    all_gather x1 -> x0, blocking collectives: 10.8 us -> none  [per_device(): full = lax.all_gather(stacked, 'ao', axis=1, tiled=True)]
    unnamed x15 -> x30, local copies, waits for them, and re-layouts: 3.26 us -> 12.4 us
    gather x0 -> x2, local copies, waits for them, and re-layouts: none -> 5.88 us  [the longest x1 5.32 us: swap_blocks(): got = jnp.take(stacked, order, axis=0)]
    convert_element_type x1 -> x0, local copies, waits for them, and re-layouts: 4.66 us -> none  [per_device(): halves = jnp.einsum('prk,dkc->dcrp', own, jnp.stack([occ_rows, virt_rows]...]
  transfers between devices with their start and end apart: 5 -> 18, of which waited for: 3 -> 6; matrix products, arithmetic and copies ran while one was open for 26% -> 38% of each run, Pallas kernels for 0% -> 0%
where the time goes in v6:
time: 157 us; the launch traced here: 156 us
  starting transfers between devices  44.6 us (28%)
  local copies, waits for them, and re-layouts  38.3 us (24%)
  waiting for transfers between devices  21.5 us (14%)
  matrix products  21.3 us (14%)
  other arithmetic  17.6 us (11%)
  blocking collectives  9.66 us (6%)
  between operations  3.15 us (2%)
    ppermute x7, starting transfers between devices, swap_blocks(): piece = lax.ppermute(piece, 'ao', route)  24.5 us
    ppermute x7, waiting for transfers between devices, swap_blocks(): piece = lax.ppermute(piece, 'ao', route)  15.8 us
    unnamed x30, local copies, waits for them, and re-layouts  12.4 us
    dot_general x5, matrix products, slab_product(): out = jnp.dot(flat, weights, preferred_element_type=jnp.float32)  10.8 us
    ppermute x7, starting transfers between devices, gather_rows(): pieces.append(lax.ppermute(block, 'ao', route))  9.83 us
    all_to_all x1, blocking collectives, per_device(): got = lax.all_to_all(sent, 'ao', 0, 0, tiled=True)  9.66 us
    convert_element_type x2, other arithmetic, split_hi_lo(): rounded.astype(jnp.bfloat16)  8.01 us
    ppermute x2, starting transfers between devices, per_device(): received = [lax.ppermute(own_flat, 'ri', route) for route, _, _ in routes]  7.54 us
  transfers between devices with their start and end apart: 18, of which 6 were waited for; matrix products, arithmetic and copies ran while one was open for 38% of the time, Pallas kernels for 0%

profile of v6, /device:TPU:0, one launch (start us, length us, event | category | flops | bytes accessed | tf_op | source)
XLA Modules:
  0.0 156.1 jit_solution(13244979914046434025)
XLA Ops:
  2.9 2.6 %collective-permute-start.1 = (bf16[2,32,256]{2,1,0:T(8,128)(2,1)S(1)}, bf16[2,32,256]{2,1,0:T(8,128)(2,1)S(1)}, u32[]{:S(2)}, u32[]{:S(2)}) collective-permute-start(bf16[2,32,256]{2,1,0:T(8,128)(2,1)S(1)} %pad_maximum_fusion.2), channel_id=1, source_target_pairs={{0,2},{1,3},{2,4},{3,5},{4,6},{5,7},{6,0},{7,1},{8,10},{9,11},{10,... | collective-permute-start | bytes 98312 | tf_op jit(solution)/shard_map/ppermute | solution.py:61
  5.5 2.4 %collective-permute-start.2 = (bf16[2,32,256]{2,1,0:T(8,128)(2,1)S(1)}, bf16[2,32,256]{2,1,0:T(8,128)(2,1)S(1)}, u32[]{:S(2)}, u32[]{:S(2)}) collective-permute-start(bf16[2,32,256]{2,1,0:T(8,128)(2,1)S(1)} %pad_maximum_fusion.2), channel_id=1, source_target_pairs={{0,3},{1,4},{2,5},{3,6},{4,7},{5,0},{6,1},{7,2},{8,11},{9,12},{10,... | collective-permute-start | bytes 98312 | tf_op jit(solution)/shard_map/ppermute | solution.py:61
  10.2 1.8 %broadcast_multiply_fusion = bf16[128,32,256]{2,1,0:T(8,128)(2,1)S(1)} fusion(bf16[128,32,256]{2,1,0:T(8,128)(2,1)} %param.11, bf16[128,256]{1,0:T(8,128)(2,1)S(1)} %copy.54), kind=kLoop, calls=%fused_computation.21 | loop fusion | flops 1048576 | bytes 4259840 | tf_op jit(solution)/shard_map/mul | solution.py:42
  12.1 1.5 collective-permute-start.5
  13.6 2.3 %collective-permute-start.6 = (bf16[2,32,256]{2,1,0:T(8,128)(2,1)S(1)}, bf16[2,32,256]{2,1,0:T(8,128)(2,1)S(1)}, u32[]{:S(2)}, u32[]{:S(2)}) collective-permute-start(bf16[2,32,256]{2,1,0:T(8,128)(2,1)S(1)} %pad_maximum_fusion.2), channel_id=1, source_target_pairs={{0,7},{1,0},{2,1},{3,2},{4,3},{5,4},{6,5},{7,6},{8,15},{9,8},{10,9... | collective-permute-start | bytes 98312 | tf_op jit(solution)/shard_map/ppermute | solution.py:61
  19.0 3.2 %convolution_convert_fusion = bf16[2,256,128,32]{2,1,3,0:T(8,128)(2,1)S(1)} fusion(bf16[128,32,256]{2,1,0:T(8,128)(2,1)S(1)} %broadcast_multiply_fusion, bf16[1,256,256]{1,2,0:T(8,128)(2,1)S(1)} %copy.52, bf16[1,256,256]{1,2,0:T(8,128)(2,1)S(1)} %copy.51), kind=kOutput, calls=%fused_computation.14 | convolution fusion | flops 1076363264 | bytes 6553600 | tf_op jit(solution)/shard_map/prk,dkc->dcrp/dot_general | solution.py:118
  22.2 1.8 %dynamic-slice_bitcast_fusion = (bf16[2,32,32,128]{3,1,2,0:T(8,128)(2,1)S(1)}, bf16[2,32,32,128]{3,1,2,0:T(8,128)(2,1)S(1)}, bf16[2,32,32,128]{3,1,2,0:T(8,128)(...) fusion(bf16[2,256,128,32]{2,1,3,0:T(8,128)(2,1)S(1)} %convoluti, ...), kind=kLoop, calls=%fused_computation.30 | loop fusion | bytes 7340060 | tf_op jit(solution)/shard_map/dynamic_slice | solution.py:76
  26.0 2.8 %copy.69 = bf16[16,8,32,256]{3,1,2,0:T(8,128)(2,1)} copy(bf16[16,8,32,256]{3,2,1,0:T(8,128)(2,1)S(1)} %bitcast.135) | data formatting | bytes 4194304
  28.7 1.7 %collective-permute-start.14 = (bf16[128,8192]{1,0:T(8,128)(2,1)}, bf16[128,8192]{1,0:T(8,128)(2,1)S(1)}, u32[]{:S(2)}, u32[]{:S(2)}) collective-permute-start(bf16[128,8192]{1,0:T(8,128)(2,1)} %bitcast.68), channel_id=1, source_target_pairs={{0,8},{8,16},{16,24},{24,0},{1,9},{9,17},{17,25},{25,1},{2,10},{10... | collective-permute-start | bytes 6291464 | tf_op jit(solution)/shard_map/ppermute | solution.py:106
  30.5 5.8 %collective-permute-start.15 = (bf16[128,8192]{1,0:T(8,128)(2,1)}, bf16[128,8192]{1,0:T(8,128)(2,1)}, u32[]{:S(2)}, u32[]{:S(2)}) collective-permute-start(bf16[128,8192]{1,0:T(8,128)(2,1)} %bitcast.68), channel_id=1, source_target_pairs={{0,16},{24,8},{1,17},{25,9},{2,18},{26,10},{3,19},{27,11},{4,20},{... | collective-permute-start | bytes 6291464 | tf_op jit(solution)/shard_map/ppermute | solution.py:106
  41.5 1.9 %bitcast_dynamic-update-slice_fusion = bf16[8,2,32,32,128]{4,2,3,1,0:T(8,128)(2,1)} fusion(bf16[2,256,128,32]{2,1,3,0:T(8,128)(2,1)} %copy-done, s32[]{:T(128)S(6)} %select_n.155), kind=kLoop, calls=%fused_computation.22 | loop fusion | bytes 1048580
  43.4 1.5 collective-permute-start.10
  44.9 1.9 %bitcast_dynamic-update-slice_fusion.7 = bf16[8,2,32,32,128]{4,2,3,1,0:T(8,128)(2,1)} fusion(bf16[8,2,32,32,128]{4,2,3,1,0:T(8,128)(2,1)} %bitcast_dynamic-update-slice_fusion, bf16[2,32,32,128]{3,1,2,0:T(8,128)(2,1)} %collective-permute-done.7), kind=kLoop, calls=%fused_computation.29 | loop fusion | bytes 1048576
  48.3 1.9 %bitcast_dynamic-update-slice_fusion.6 = bf16[8,2,32,32,128]{4,2,3,1,0:T(8,128)(2,1)} fusion(bf16[8,2,32,32,128]{4,2,3,1,0:T(8,128)(2,1)} %bitcast_dynamic-update-slice_fusion.7, bf16[2,32,32,128]{3,1,2,0:T(8,128)(2,1)} %collective-permute-done.8), kind=kLoop, calls=%fused_computation.28 | loop fusion | bytes 1048576
  50.1 11.7 %collective-permute-done.9 = bf16[2,32,32,128]{3,1,2,0:T(8,128)(2,1)S(1)} collective-permute-done((bf16[2,32,32,128]{3,1,2,0:T(8,128)(2,1)}, bf16[2,32,32,128]{3,1,2,0:T(8,128)(2,1)S(1)}, u32[]{:S(2)}, u32[]{:S(2)}) %collective-permute-start.9) | collective-permute-done | bytes 524320 | tf_op jit(solution)/shard_map/ppermute | solution.py:79
  62.7 19.6 %collective-permute-start.13 = (bf16[2,32,32,128]{3,1,2,0:T(8,128)(2,1)S(1)}, bf16[2,32,32,128]{3,1,2,0:T(8,128)(2,1)S(1)}, u32[]{:S(2)}, u32[]{:S(2)}) collective-permute-start(bf16[2,32,32,128]{3,1,2,0:T(8,128)(2,1)S(1)} %get-tuple-element.21), channel_id=1, source_target_pairs={{0,7},{1,0},{2,1},{3,2},{4,3},{5,4},{6,5},{7,6},{8,15},{9,8},{10,9... | collective-permute-start | bytes 1572872 | tf_op jit(solution)/shard_map/ppermute | solution.py:79
  84.9 4.1 %collective-permute-done.13 = bf16[2,32,32,128]{3,1,2,0:T(8,128)(2,1)S(1)} collective-permute-done((bf16[2,32,32,128]{3,1,2,0:T(8,128)(2,1)S(1)}, bf16[2,32,32,128]{3,1,2,0:T(8,128)(2,1)S(1)}, u32[]{:S(2)}, u32[]{:S(2)}) %collective-permute-start.13) | collective-permute-done | bytes 524320 | tf_op jit(solution)/shard_map/ppermute | solution.py:79
  89.9 5.3 %gather_fusion.2 = bf16[8,2,32,32,128]{4,2,3,1,0:T(8,128)(2,1)} fusion(bf16[8,2,32,32,128]{4,2,3,1,0:T(8,128)(2,1)} %bitcast_dynamic-update-slice_fusion.1, s32[1024]{0:T(1024)S(1)} %pad_clamp_fusion.1), kind=kCustom, calls=%fused_computation.2 | custom fusion | bytes 8388640 | tf_op jit(solution)/shard_map/jit(_take)/gather | solution.py:83
  95.2 2.7 %select_bitcast_fusion = bf16[2,32,8,32,128]{4,1,3,0,2:T(8,128)(2,1)S(1)} fusion(bf16[8,2,32,32,128]{4,2,3,1,0:T(8,128)(2,1)} %gather_fusion.2, pred[8]{0:T(512)(128)(4,1)S(1)} %compare_and_fusion), kind=kLoop, calls=%fused_computation.11 | loop fusion | flops 2097152 | bytes 8388616 | tf_op jit(solution)/shard_map/jit(_take)/select_n | solution.py:83
  97.8 2.1 %fusion.22 = (bf16[1,32,8,32,128]{4,1,3,0,2:T(8,128)(2,1)S(1)}, bf16[1,32,8,32,128]{4,1,3,0,2:T(8,128)(2,1)}) fusion(bf16[2,32,8,32,128]{4,1,3,0,2:T(8,128)(2,1)S(1)} %select_bitcast_fusion), kind=kLoop, calls=%fused_computation.86 | loop fusion | bytes 8388608 | tf_op jit(solution)/shard_map/slice | solution.py:126
  99.9 3.7 %convolution_bitcast_fusion = f32[128,32,256]{2,0,1:T(8,128)} fusion(bf16[256,256,1]{1,0,2:T(8,128)(2,1)S(1)} %bitcast.142, bf16[32,256,128]{2,0,1:T(8,128)(2,1)S(1)} %bitcast.137), kind=kOutput, calls=%fused_computation.15 | convolution fusion | flops 536870912 | bytes 6422528 | tf_op jit(solution)/shard_map/kl,nlq->qnk/dot_general | solution.py:128
  103.6 5.6 %copy.59 = f32[128,32,256]{0,2,1:T(8,128)} copy(f32[128,32,256]{2,0,1:T(8,128)} %convolution_bitcast_fusion) | data formatting | bytes 8388608 | tf_op jit(solution)/shard_map/kl,nlq->qnk/transpose | solution.py:128
  109.2 5.0 %reduce-precision_convert_fusion = (bf16[128,8192]{0,1:T(8,128)(2,1)}, bf16[128,8192]{0,1:T(8,128)(2,1)}) fusion(f32[128,32,256]{0,2,1:T(8,128)} %copy.59), kind=kLoop, calls=%fused_computation.4 | loop fusion | flops 4194304 | bytes 8388608 | tf_op jit(solution)/shard_map/convert_element_type | solution.py:47
  114.2 3.7 %convolution_bitcast_fusion.1 = f32[128,32,256]{2,0,1:T(8,128)} fusion(bf16[256,256,1]{1,0,2:T(8,128)(2,1)S(1)} %bitcast.140, bf16[32,256,128]{2,0,1:T(8,128)(2,1)S(1)} %bitcast.136), kind=kOutput, calls=%fused_computation.16 | convolution fusion | flops 536870912 | bytes 6422528 | tf_op jit(solution)/shard_map/mn,lnp->plm/dot_general | solution.py:127
  117.9 5.6 %copy.57 = f32[128,32,256]{0,2,1:T(8,128)} copy(f32[128,32,256]{2,0,1:T(8,128)} %convolution_bitcast_fusion.1) | data formatting | bytes 8388608 | tf_op jit(solution)/shard_map/mn,lnp->plm/transpose | solution.py:127
  123.4 3.0 %reduce-precision_convert_fusion.1 = (bf16[128,8192]{0,1:T(8,128)(2,1)S(1)}, bf16[128,8192]{0,1:T(8,128)(2,1)S(1)}) fusion(f32[128,32,256]{0,2,1:T(8,128)} %copy.57), kind=kLoop, calls=%fused_computation.6 | loop fusion | flops 4194304 | bytes 8388608 | tf_op jit(solution)/shard_map/convert_element_type | solution.py:47
  126.9 2.4 %fusion.2 = f32[128,256]{1,0:T(8,128)S(1)} fusion(bf16[128,8192]{1,0:T(8,128)(2,1)} %bitcast.68, bf16[128,8192]{0,1:T(8,128)(2,1)S(1)} %copy-done.3, bf16[128,8192]{0,1:T(8,128)(2,1)S(1)} %copy-done.2), kind=kOutput, calls=%fused_computation.12 | convolution fusion | flops 545259520 | bytes 6422528 | tf_op jit(solution)/shard_map/dot_general | solution.py:51
  130.3 3.4 %fusion.27 = f32[128,256]{0,1:T(8,128)S(1)} fusion(bf16[128,8192]{1,0:T(8,128)(2,1)} %collective-permute-done.15, bf16[8192,256]{1,0:T(8,128)(2,1)S(1)} %fusion.3), kind=kOutput, calls=%fused_computation.91 | convolution fusion | flops 536870912 | bytes 6422528 | tf_op jit(solution)/shard_map/dot_general | solution.py:51
  133.7 2.4 %fusion.26 = f32[128,256]{1,0:T(8,128)S(1)} fusion(bf16[128,8192]{1,0:T(8,128)(2,1)} %collective-permute-done.15, bf16[8192,256]{1,0:T(8,128)(2,1)S(1)} %maximum_bitcast_fusion), kind=kOutput, calls=%fused_computation.90 | convolution fusion | flops 536870912 | bytes 6422528 | tf_op jit(solution)/shard_map/dot_general | solution.py:51
  136.1 1.8 %fusion.25 = f32[128,256]{0,1:T(8,128)S(1)} fusion(bf16[128,8192]{1,0:T(8,128)(2,1)S(1)} %collective-permute-done.14, bf16[8192,256]{1,0:T(8,128)(2,1)S(1)} %fusion.3), kind=kOutput, calls=%fused_computation.89 | convolution fusion | flops 536870912 | bytes 6422528 | tf_op jit(solution)/shard_map/dot_general | solution.py:51
  141.6 3.3 %collective-permute-done.16 = f32[128,128]{0,1:T(8,128)S(1)} collective-permute-done((f32[128,128]{0,1:T(8,128)S(1)}, f32[128,128]{0,1:T(8,128)S(1)}, u32[]{:S(2)}, u32[]{:S(2)}) %collective-permute-start.16) | collective-permute-done | bytes 65568 | tf_op jit(solution)/shard_map/ppermute | solution.py:144
  145.8 9.7 %all_to_all.5 = f32[8,128,64]{1,2,0:T(8,128)S(1)} all-to-all(f32[8,128,64]{1,2,0:T(8,128)S(1)} %bitcast.138), channel_id=1, replica_groups=mesh['ri'=4,'ao'=8] {'ao'}, dimensions={0} | all-to-all | bytes 524288 | tf_op jit(solution)/shard_map/all_to_all | solution.py:149
  (98 shorter events, 25.2 us)
Async XLA Ops:
  2.4 9.7 %collective-permute-start = (bf16[2,32,256]{2,1,0:T(8,128)(2,1)S(1)}, bf16[2,32,256]{2,1,0:T(8,128)(2,1)S(1)}, u32[]{:S(2)}, u32[]{:S(2)}) collective-permute-start(bf16[2,32,256]{2,1,0:T(8,128)(2,1)S(1)} %pad_maximum_fusion.2), channel_id=1, source_target_pairs={{0,1},{1,2},{2,3},{3,4},{4,5},{5,6},{6,7},{7,0},{8,9},{9,10},{10,1... | collective-permute-start | bytes 98312 | tf_op jit(solution)/shard_map/ppermute | solution.py:61
  2.9 10.7 %collective-permute-start.1 = (bf16[2,32,256]{2,1,0:T(8,128)(2,1)S(1)}, bf16[2,32,256]{2,1,0:T(8,128)(2,1)S(1)}, u32[]{:S(2)}, u32[]{:S(2)}) collective-permute-start(bf16[2,32,256]{2,1,0:T(8,128)(2,1)S(1)} %pad_maximum_fusion.2), channel_id=1, source_target_pairs={{0,2},{1,3},{2,4},{3,5},{4,6},{5,7},{6,0},{7,1},{8,10},{9,11},{10,... | collective-permute-start | bytes 98312 | tf_op jit(solution)/shard_map/ppermute | solution.py:61
  5.5 10.5 %collective-permute-start.2 = (bf16[2,32,256]{2,1,0:T(8,128)(2,1)S(1)}, bf16[2,32,256]{2,1,0:T(8,128)(2,1)S(1)}, u32[]{:S(2)}, u32[]{:S(2)}) collective-permute-start(bf16[2,32,256]{2,1,0:T(8,128)(2,1)S(1)} %pad_maximum_fusion.2), channel_id=1, source_target_pairs={{0,3},{1,4},{2,5},{3,6},{4,7},{5,0},{6,1},{7,2},{8,11},{9,12},{10,... | collective-permute-start | bytes 98312 | tf_op jit(solution)/shard_map/ppermute | solution.py:61
  7.8 8.1 %collective-permute-start.3 = (bf16[2,32,256]{2,1,0:T(8,128)(2,1)S(1)}, bf16[2,32,256]{2,1,0:T(8,128)(2,1)S(1)}, u32[]{:S(2)}, u32[]{:S(2)}) collective-permute-start(bf16[2,32,256]{2,1,0:T(8,128)(2,1)S(1)} %pad_maximum_fusion.2), channel_id=1, source_target_pairs={{0,4},{1,5},{2,6},{3,7},{4,0},{5,1},{6,2},{7,3},{8,12},{9,13},{10,... | collective-permute-start | bytes 98312 | tf_op jit(solution)/shard_map/ppermute | solution.py:61
  8.3 7.6 %collective-permute-start.4 = (bf16[2,32,256]{2,1,0:T(8,128)(2,1)S(1)}, bf16[2,32,256]{2,1,0:T(8,128)(2,1)S(1)}, u32[]{:S(2)}, u32[]{:S(2)}) collective-permute-start(bf16[2,32,256]{2,1,0:T(8,128)(2,1)S(1)} %pad_maximum_fusion.2), channel_id=1, source_target_pairs={{0,5},{1,6},{2,7},{3,0},{4,1},{5,2},{6,3},{7,4},{8,13},{9,14},{10,... | collective-permute-start | bytes 98312 | tf_op jit(solution)/shard_map/ppermute | solution.py:61
  12.1 4.0 %collective-permute-start.5 = (bf16[2,32,256]{2,1,0:T(8,128)(2,1)S(1)}, bf16[2,32,256]{2,1,0:T(8,128)(2,1)S(1)}, u32[]{:S(2)}, u32[]{:S(2)}) collective-permute-start(bf16[2,32,256]{2,1,0:T(8,128)(2,1)S(1)} %pad_maximum_fusion.2), channel_id=1, source_target_pairs={{0,6},{1,7},{2,0},{3,1},{4,2},{5,3},{6,4},{7,5},{8,14},{9,15},{10,... | collective-permute-start | bytes 98312 | tf_op jit(solution)/shard_map/ppermute | solution.py:61
  13.6 3.9 %collective-permute-start.6 = (bf16[2,32,256]{2,1,0:T(8,128)(2,1)S(1)}, bf16[2,32,256]{2,1,0:T(8,128)(2,1)S(1)}, u32[]{:S(2)}, u32[]{:S(2)}) collective-permute-start(bf16[2,32,256]{2,1,0:T(8,128)(2,1)S(1)} %pad_maximum_fusion.2), channel_id=1, source_target_pairs={{0,7},{1,0},{2,1},{3,2},{4,3},{5,4},{6,5},{7,6},{8,15},{9,8},{10,9... | collective-permute-start | bytes 98312 | tf_op jit(solution)/shard_map/ppermute | solution.py:61
  22.2 6.6 %copy-start = (bf16[2,256,128,32]{2,1,3,0:T(8,128)(2,1)}, bf16[2,256,128,32]{2,1,3,0:T(8,128)(2,1)S(1)}, u32[]{:S(2)}) copy-start(bf16[2,256,128,32]{2,1,3,0:T(8,128)(2,1)S(1)} %convolution_convert_fusion) | copy-start | bytes 12582916
  22.2 14.1 %copy-start.7 = (s32[4]{0:T(128)S(1)}, s32[4]{0:T(128)}, u32[]{:S(2)}) copy-start(s32[4]{0:T(128)} %constant.127.clone) | copy-start | bytes 52
  22.2 15.3 %copy-start.6 = (s32[4]{0:T(128)S(1)}, s32[4]{0:T(128)}, u32[]{:S(2)}) copy-start(s32[4]{0:T(128)} %constant.128.clone) | copy-start | bytes 52
  22.2 16.6 %copy-start.5 = (s32[4]{0:T(128)S(1)}, s32[4]{0:T(128)}, u32[]{:S(2)}) copy-start(s32[4]{0:T(128)} %constant.129.clone) | copy-start | bytes 52
  22.2 17.8 %copy-start.4 = (s32[4]{0:T(128)S(1)}, s32[4]{0:T(128)}, u32[]{:S(2)}) copy-start(s32[4]{0:T(128)} %constant.130.clone) | copy-start | bytes 52
  24.1 19.3 %collective-permute-start.7 = (bf16[2,32,32,128]{3,1,2,0:T(8,128)(2,1)}, bf16[2,32,32,128]{3,1,2,0:T(8,128)(2,1)}, u32[]{:S(2)}, u32[]{:S(2)}) collective-permute-start(bf16[2,32,32,128]{3,1,2,0:T(8,128)(2,1)} %get-tuple-element.27), channel_id=1, source_target_pairs={{0,1},{1,2},{2,3},{3,4},{4,5},{5,6},{6,7},{7,0},{8,9},{9,10},{10,1... | collective-permute-start | bytes 1572872 | tf_op jit(solution)/shard_map/ppermute | solution.py:79
  24.8 22.0 %collective-permute-start.8 = (bf16[2,32,32,128]{3,1,2,0:T(8,128)(2,1)}, bf16[2,32,32,128]{3,1,2,0:T(8,128)(2,1)}, u32[]{:S(2)}, u32[]{:S(2)}) collective-permute-start(bf16[2,32,32,128]{3,1,2,0:T(8,128)(2,1)} %get-tuple-element.26), channel_id=1, source_target_pairs={{0,2},{1,3},{2,4},{3,5},{4,6},{5,7},{6,0},{7,1},{8,10},{9,11},{10,... | collective-permute-start | bytes 1572872 | tf_op jit(solution)/shard_map/ppermute | solution.py:79
  28.7 101.5 %collective-permute-start.14 = (bf16[128,8192]{1,0:T(8,128)(2,1)}, bf16[128,8192]{1,0:T(8,128)(2,1)S(1)}, u32[]{:S(2)}, u32[]{:S(2)}) collective-permute-start(bf16[128,8192]{1,0:T(8,128)(2,1)} %bitcast.68), channel_id=1, source_target_pairs={{0,8},{8,16},{16,24},{24,0},{1,9},{9,17},{17,25},{25,1},{2,10},{10... | collective-permute-start | bytes 6291464 | tf_op jit(solution)/shard_map/ppermute | solution.py:106
  30.5 99.8 %collective-permute-start.15 = (bf16[128,8192]{1,0:T(8,128)(2,1)}, bf16[128,8192]{1,0:T(8,128)(2,1)}, u32[]{:S(2)}, u32[]{:S(2)}) collective-permute-start(bf16[128,8192]{1,0:T(8,128)(2,1)} %bitcast.68), channel_id=1, source_target_pairs={{0,16},{24,8},{1,17},{25,9},{2,18},{26,10},{3,19},{27,11},{4,20},{... | collective-permute-start | bytes 6291464 | tf_op jit(solution)/shard_map/ppermute | solution.py:106
  41.4 20.3 %collective-permute-start.9 = (bf16[2,32,32,128]{3,1,2,0:T(8,128)(2,1)}, bf16[2,32,32,128]{3,1,2,0:T(8,128)(2,1)S(1)}, u32[]{:S(2)}, u32[]{:S(2)}) collective-permute-start(bf16[2,32,32,128]{3,1,2,0:T(8,128)(2,1)} %get-tuple-element.25), channel_id=1, source_target_pairs={{0,3},{1,4},{2,5},{3,6},{4,7},{5,0},{6,1},{7,2},{8,11},{9,12},{10,... | collective-permute-start | bytes 1572872 | tf_op jit(solution)/shard_map/ppermute | solution.py:79
  43.4 19.3 %collective-permute-start.10 = (bf16[2,32,32,128]{3,1,2,0:T(8,128)(2,1)}, bf16[2,32,32,128]{3,1,2,0:T(8,128)(2,1)S(1)}, u32[]{:S(2)}, u32[]{:S(2)}) collective-permute-start(bf16[2,32,32,128]{3,1,2,0:T(8,128)(2,1)} %get-tuple-element.24), channel_id=1, source_target_pairs={{0,4},{1,5},{2,6},{3,7},{4,0},{5,1},{6,2},{7,3},{8,12},{9,13},{10,... | collective-permute-start | bytes 1572872 | tf_op jit(solution)/shard_map/ppermute | solution.py:79
  46.8 36.4 %collective-permute-start.11 = (bf16[2,32,32,128]{3,1,2,0:T(8,128)(2,1)}, bf16[2,32,32,128]{3,1,2,0:T(8,128)(2,1)S(1)}, u32[]{:S(2)}, u32[]{:S(2)}) collective-permute-start(bf16[2,32,32,128]{3,1,2,0:T(8,128)(2,1)} %get-tuple-element.23), channel_id=1, source_target_pairs={{0,5},{1,6},{2,7},{3,0},{4,1},{5,2},{6,3},{7,4},{8,13},{9,14},{10,... | collective-permute-start | bytes 1572872 | tf_op jit(solution)/shard_map/ppermute | solution.py:79
  61.8 22.2 %collective-permute-start.12 = (bf16[2,32,32,128]{3,1,2,0:T(8,128)(2,1)S(1)}, bf16[2,32,32,128]{3,1,2,0:T(8,128)(2,1)S(1)}, u32[]{:S(2)}, u32[]{:S(2)}) collective-permute-start(bf16[2,32,32,128]{3,1,2,0:T(8,128)(2,1)S(1)} %get-tuple-element.22), channel_id=1, source_target_pairs={{0,6},{1,7},{2,0},{3,1},{4,2},{5,3},{6,4},{7,5},{8,14},{9,15},{10,... | collective-permute-start | bytes 1572872 | tf_op jit(solution)/shard_map/ppermute | solution.py:79
  62.7 26.3 %collective-permute-start.13 = (bf16[2,32,32,128]{3,1,2,0:T(8,128)(2,1)S(1)}, bf16[2,32,32,128]{3,1,2,0:T(8,128)(2,1)S(1)}, u32[]{:S(2)}, u32[]{:S(2)}) collective-permute-start(bf16[2,32,32,128]{3,1,2,0:T(8,128)(2,1)S(1)} %get-tuple-element.21), channel_id=1, source_target_pairs={{0,7},{1,0},{2,1},{3,2},{4,3},{5,4},{6,5},{7,6},{8,15},{9,8},{10,9... | collective-permute-start | bytes 1572872 | tf_op jit(solution)/shard_map/ppermute | solution.py:79
  109.2 5.0 %copy-start.1 = (bf16[1,32,8,32,128]{4,1,3,0,2:T(8,128)(2,1)S(1)}, bf16[1,32,8,32,128]{4,1,3,0,2:T(8,128)(2,1)}, u32[]{:S(2)}) copy-start(bf16[1,32,8,32,128]{4,1,3,0,2:T(8,128)(2,1)} %get-tuple-element.18) | copy-start | bytes 6291460
  123.4 3.0 %copy-start.2 = (bf16[128,8192]{0,1:T(8,128)(2,1)S(1)}, bf16[128,8192]{0,1:T(8,128)(2,1)}, u32[]{:S(2)}) copy-start(bf16[128,8192]{0,1:T(8,128)(2,1)} %get-tuple-element.15) | copy-start | bytes 6291460
  123.4 3.5 %copy-start.3 = (bf16[128,8192]{0,1:T(8,128)(2,1)S(1)}, bf16[128,8192]{0,1:T(8,128)(2,1)}, u32[]{:S(2)}) copy-start(bf16[128,8192]{0,1:T(8,128)(2,1)} %get-tuple-element.16) | copy-start | bytes 6291460
  138.7 7.1 %collective-permute-start.17 = (f32[128,128]{0,1:T(8,128)S(1)}, f32[128,128]{0,1:T(8,128)S(1)}, u32[]{:S(2)}, u32[]{:S(2)}) collective-permute-start(f32[128,128]{0,1:T(8,128)S(1)} %slice_add_fusion), channel_id=1, source_target_pairs={{16,0},{8,24},{17,1},{9,25},{18,2},{10,26},{19,3},{11,27},{20,4},{... | collective-permute-start | bytes 196616 | tf_op jit(solution)/shard_map/ppermute | solution.py:144
  140.0 4.8 %collective-permute-start.16 = (f32[128,128]{0,1:T(8,128)S(1)}, f32[128,128]{0,1:T(8,128)S(1)}, u32[]{:S(2)}, u32[]{:S(2)}) collective-permute-start(f32[128,128]{0,1:T(8,128)S(1)} %slice_add_fusion.2), channel_id=1, source_target_pairs={{8,0},{16,8},{24,16},{0,24},{9,1},{17,9},{25,17},{1,25},{10,2},{18... | collective-permute-start | bytes 196616 | tf_op jit(solution)/shard_map/ppermute | solution.py:144

commit v7 on v5

--- a/solution.py
+++ b/solution.py
@@ -47,6 +47,11 @@
     return rounded.astype(jnp.bfloat16), (values - rounded).astype(jnp.bfloat16)
 
 
+def weight_pair(values):
+    hi, lo = split_hi_lo(values)
+    return jnp.stack([hi, lo], axis=1).reshape(values.shape[0], -1)
+
+
 def slab_product(flat, weights):
     out = jnp.dot(flat, weights, preferred_element_type=jnp.float32)
     half = weights.shape[1] // 2
@@ -69,7 +74,7 @@
 
     routes = pair_routes(planes)
     own = mask_slab(tensor, live_blocks)
-    own_flat = own.reshape(rows, -1)
+    own_flat = own.transpose(0, 2, 1).reshape(rows, -1)
     received = [lax.ppermute(own_flat, "ri", route) for route, _, _ in routes]
 
     stacked = jnp.stack(
@@ -83,20 +88,18 @@
     virt_rows = picked[1].reshape(KS * BS, ao_total)
 
     halves = jnp.einsum(
-        "prk,dkc->dcrp",
+        "dkc,prk->dcpr",
+        jnp.stack([occ_rows, virt_rows]),
         own,
-        jnp.stack([occ_rows, virt_rows]),
         preferred_element_type=jnp.float32,
     ).astype(jnp.bfloat16)
-    swapped = lax.all_to_all(halves, "ao", 1, 2, tiled=True)
+    swapped = lax.all_to_all(halves, "ao", 1, 3, tiled=True)
     occ_t = swapped[0]
     virt_t = swapped[1]
-    v_part = jnp.einsum("mn,lnp->plm", virt_rows, occ_t, preferred_element_type=jnp.float32)
-    w_part = jnp.einsum("kl,nlq->qnk", occ_rows, virt_t, preferred_element_type=jnp.float32)
-    v_hi, v_lo = split_hi_lo(v_part.reshape(rows, -1))
-    w_hi, w_lo = split_hi_lo(w_part.reshape(rows, -1))
-    v_weights = jnp.concatenate([v_hi, v_lo]).T
-    w_weights = jnp.concatenate([w_hi, w_lo]).T
+    v_part = jnp.einsum("mn,lpn->mlp", virt_rows, occ_t, preferred_element_type=jnp.float32)
+    w_part = jnp.einsum("kl,nql->knq", occ_rows, virt_t, preferred_element_type=jnp.float32)
+    v_weights = weight_pair(v_part.reshape(-1, rows))
+    w_weights = weight_pair(w_part.reshape(-1, rows))
     diag = slab_product(own_flat, w_weights)
 
     v_weights, w_weights, diag, received = lax.optimization_barrier(

time: 153 us -> 161 us (1.052)
  local copies, waits for them, and re-layouts: 29.4 us -> 38.9 us
  waiting for transfers between devices: 49.1 us -> 45.8 us
    another operation x0 -> x2, local copies, waits for them, and re-layouts: none -> 12.7 us  [weight_pair(): return jnp.stack([hi, lo], axis=1).reshape(values.shape[0], -1)]
    transpose x2 -> x0, local copies, waits for them, and re-layouts: 11.1 us -> none  [the longest x1 5.56 us: per_device(): jnp.einsum('mn,lnp->plm', virt_rows, occ_t, preferred_element_type=jnp.fl...]
    another operation x0 -> x2, other arithmetic: none -> 6.9 us  [weight_pair(): return jnp.stack([hi, lo], axis=1).reshape(values.shape[0], -1)]
    ppermute x2, waiting for transfers between devices: 11.4 us -> 4.86 us  [per_device(): received = [lax.ppermute(own_flat, 'ri', route) for route, _, _ in routes]]
    dot_general x5, matrix products: 10.8 us -> 16.1 us  [slab_product(): out = jnp.dot(flat, weights, preferred_element_type=jnp.float32)]
    dot_general x0 -> x2, local copies, waits for them, and re-layouts: none -> 4.86 us  [the longest x1 2.43 us: per_device(): jnp.einsum('kl,nql->knq', occ_rows, virt_t, preferred_element_type=jnp.fl...]
    convert_element_type x2, other arithmetic: 7.95 us -> 3.26 us  [split_hi_lo(): rounded.astype(jnp.bfloat16)]
    dot_general x3, matrix products: 8.62 us -> 4.33 us  [the longest x1 2.88 us: per_device(): jnp.einsum('dkc,prk->dcpr', jnp.stack([occ_rows, virt_rows]), own, prefer...]
  transfers between devices with their start and end apart: 5 -> 5, of which waited for: 3 -> 3; matrix products, arithmetic and copies ran while one was open for 26% -> 25% of each run, Pallas kernels for 0% -> 0%
where the time goes in v7:
time: 161 us; the launch traced here: 160 us
  waiting for transfers between devices  45.8 us (28%)
  local copies, waits for them, and re-layouts  38.9 us (24%)
  blocking collectives  21.2 us (13%)
  matrix products  20.5 us (13%)
  starting transfers between devices  15.7 us (10%)
  other arithmetic  15.4 us (10%)
  between operations  2.82 us (2%)
    all_to_all x1, waiting for transfers between devices, per_device(): swapped = lax.all_to_all(halves, 'ao', 1, 3, tiled=True)  36.8 us
    dot_general x5, matrix products, slab_product(): out = jnp.dot(flat, weights, preferred_element_type=jnp.float32)  16.1 us
    another operation x2, local copies, waits for them, and re-layouts, weight_pair(): return jnp.stack([hi, lo], axis=1).reshape(values.shape[0], -1)  12.7 us
    all_gather x1, blocking collectives, per_device(): full = lax.all_gather(stacked, 'ao', axis=1, tiled=True)  10.8 us
    all_to_all x1, blocking collectives, per_device(): got = lax.all_to_all(sent, 'ao', 0, 0, tiled=True)  10.4 us
    ppermute x2, starting transfers between devices, per_device(): received = [lax.ppermute(own_flat, 'ri', route) for route, _, _ in routes]  7.42 us
    another operation x2, other arithmetic, weight_pair(): return jnp.stack([hi, lo], axis=1).reshape(values.shape[0], -1)  6.9 us
    unnamed x15, local copies, waits for them, and re-layouts  5.21 us
  transfers between devices with their start and end apart: 5, of which 3 were waited for; matrix products, arithmetic and copies ran while one was open for 25% of the time, Pallas kernels for 0%

profile of v7, /device:TPU:0, one launch (start us, length us, event | category | flops | bytes accessed | tf_op | source)
XLA Modules:
  0.0 160.3 jit_solution(14748895319146093442)
XLA Ops:
  1.6 0.7 multiply_bitcast_fusion
  2.4 10.8 %all_gather.3 = bf16[2,256,256]{2,1,0:T(8,128)(2,1)S(1)} all-gather(bf16[2,32,256]{2,1,0:T(8,128)(2,1)S(1)} %pad_maximum_fusion.2), channel_id=1, replica_groups=mesh['ri'=4,'ao'=8] {'ao'}, dimensions={1}, use_global_device_ids=true | all-gather | bytes 294912 | tf_op jit(solution)/shard_map/all_gather | solution.py:83
  14.7 5.2 %copy.74 = bf16[128,32,256]{0,1,2:T(8,128)(2,1)} copy(bf16[128,32,256]{2,1,0:T(8,128)(2,1)} %param.11) | data formatting | bytes 4194304 | tf_op args[0]
  20.1 1.8 %broadcast_multiply_fusion = bf16[128,32,256]{0,1,2:T(8,128)(2,1)S(1)} fusion(bf16[128,32,256]{0,1,2:T(8,128)(2,1)} %copy.74, bf16[128,256]{0,1:T(8,128)(2,1)S(1)} %bitcast.101), kind=kLoop, calls=%fused_computation.11 | loop fusion | flops 1048576 | bytes 4259840 | tf_op jit(solution)/shard_map/mul | solution.py:42
  21.9 2.8 %copy.75 = bf16[128,32,256]{2,0,1:T(8,128)(2,1)} copy(bf16[128,32,256]{0,1,2:T(8,128)(2,1)S(1)} %broadcast_multiply_fusion) | data formatting | bytes 4194304 | tf_op jit(solution)/shard_map/mul | solution.py:42
  24.7 2.9 %convolution_convert_fusion = bf16[2,256,128,32]{2,1,3,0:T(8,128)(2,1)S(1)} fusion(bf16[128,32,256]{2,0,1:T(8,128)(2,1)} %copy.75, bf16[1,256,256]{1,2,0:T(8,128)(2,1)S(1)} %copy.72, bf16[1,256,256]{1,2,0:T(8,128)(2,1)S(1)} %copy.71), kind=kOutput, calls=%fused_computation.9 | convolution fusion | flops 1076363264 | bytes 6553600 | tf_op jit(solution)/shard_map/dkc,prk->dcpr/dot_general | solution.py:90
  27.5 4.7 %copy.76 = bf16[2,256,128,32]{2,3,0,1:T(8,128)(2,1)} copy(bf16[2,256,128,32]{2,1,3,0:T(8,128)(2,1)S(1)} %convolution_convert_fusion) | data formatting | bytes 8388608 | tf_op jit(solution)/shard_map/convert_element_type | solution.py:95
  32.2 4.7 %all-to-all-start = ((bf16[2,256,128,32]{2,3,0,1:T(8,128)(2,1)}), bf16[2,256,128,32]{2,3,0,1:T(8,128)(2,1)}, u32[]{:S(2)}, u32[]{:S(2)}) async-start(bf16[2,256,128,32]{2,3,0,1:T(8,128)(2,1)} %copy.76), calls=%async_computation | async-start | bytes 8388608 | tf_op jit(solution)/shard_map/all_to_all | solution.py:96
  36.9 1.6 %collective-permute-start = (bf16[128,8192]{0,1:T(8,128)(2,1)S(1)}, bf16[128,8192]{0,1:T(8,128)(2,1)}, u32[]{:S(2)}, u32[]{:S(2)}) collective-permute-start(bf16[128,8192]{0,1:T(8,128)(2,1)S(1)} %bitcast.88), channel_id=1, source_target_pairs={{0,8},{8,16},{16,24},{24,0},{1,9},{9,17},{17,25},{25,1},{2,10},{10... | collective-permute-start | bytes 6291464 | tf_op jit(solution)/shard_map/ppermute | solution.py:78
  38.5 5.8 %collective-permute-start.1 = (bf16[128,8192]{0,1:T(8,128)(2,1)S(1)}, bf16[128,8192]{0,1:T(8,128)(2,1)}, u32[]{:S(2)}, u32[]{:S(2)}) collective-permute-start(bf16[128,8192]{0,1:T(8,128)(2,1)S(1)} %bitcast.89), channel_id=1, source_target_pairs={{0,16},{24,8},{1,17},{25,9},{2,18},{26,10},{3,19},{27,11},{4,20},{... | collective-permute-start | bytes 6291464 | tf_op jit(solution)/shard_map/ppermute | solution.py:78
  49.2 36.8 %all-to-all-done = bf16[2,256,128,32]{2,3,0,1:T(8,128)(2,1)} async-done(((bf16[2,256,128,32]{2,3,0,1:T(8,128)(2,1)}), bf16[2,256,128,32]{2,3,0,1:T(8,128)(2,1)}, u32[]{:S(2)}, u32[]{:S(2)}) %all-to-all-start) | async-done | bytes 4194336 | tf_op jit(solution)/shard_map/all_to_all | solution.py:96
  86.0 2.9 %copy.77 = bf16[2,256,128,32]{2,3,1,0:T(8,128)(2,1)S(1)} copy(bf16[2,256,128,32]{2,3,0,1:T(8,128)(2,1)} %all-to-all-done) | data formatting | bytes 8388608 | tf_op jit(solution)/shard_map/all_to_all | solution.py:96
  89.0 0.7 fusion.13
  90.3 0.7 fusion.16
  91.0 2.4 %copy.84 = f32[256,32,128]{2,1,0:T(8,128)S(1)} copy(f32[256,32,128]{2,0,1:T(8,128)S(1)} %fusion.16) | data formatting | bytes 8388608 | tf_op jit(solution)/shard_map/kl,nql->knq/dot_general | solution.py:100
  94.7 0.7 fusion.15
  95.5 2.4 %copy.80 = f32[256,32,128]{2,1,0:T(8,128)S(1)} copy(f32[256,32,128]{2,0,1:T(8,128)S(1)} %fusion.15) | data formatting | bytes 8388608 | tf_op jit(solution)/shard_map/mn,lpn->mlp/dot_general | solution.py:99
  97.9 2.6 %reduce-precision_convert_fusion.1 = (bf16[8192,1,128]{2,0,1:T(8,128)(2,1)}, bf16[8192,1,128]{2,0,1:T(8,128)(2,1)}) fusion(f32[256,32,128]{2,1,0:T(8,128)S(1)} %copy.80), kind=kLoop, calls=%fused_computation.4 | loop fusion | flops 4194304 | bytes 8388608 | tf_op jit(solution)/shard_map/convert_element_type | solution.py:47
  100.5 2.3 %pad_maximum_fusion.1 = bf16[8192,2,128]{2,0,1:T(8,128)(2,1)} fusion(bf16[8192,1,128]{2,0,1:T(8,128)(2,1)S(1)} %get-tuple-element.16, bf16[8192,1,128]{2,0,1:T(8,128)(2,1)S(1)} %get-tuple-element.15), kind=kLoop, calls=%fused_computation.8 | loop fusion | flops 2097152 | bytes 8388608 | tf_op jit(solution)/shard_map/stack | solution.py:52
  102.8 6.4 %copy.85 = bf16[8192,2,128]{0,2,1:T(8,128)(2,1)} copy(bf16[8192,2,128]{2,0,1:T(8,128)(2,1)} %pad_maximum_fusion.1) | data formatting | bytes 8388608 | tf_op jit(solution)/shard_map/stack | solution.py:52
  109.2 4.6 %pad_maximum_fusion = bf16[8192,2,128]{2,0,1:T(8,128)(2,1)} fusion(bf16[8192,1,128]{2,0,1:T(8,128)(2,1)} %get-tuple-element.20, bf16[8192,1,128]{2,0,1:T(8,128)(2,1)} %get-tuple-element.19), kind=kLoop, calls=%fused_computation.7 | loop fusion | flops 2097152 | bytes 8388608 | tf_op jit(solution)/shard_map/stack | solution.py:52
  113.8 6.3 %copy.81 = bf16[8192,2,128]{0,2,1:T(8,128)(2,1)} copy(bf16[8192,2,128]{2,0,1:T(8,128)(2,1)} %pad_maximum_fusion) | data formatting | bytes 8388608 | tf_op jit(solution)/shard_map/stack | solution.py:52
  120.2 3.8 %fusion.17 = f32[128,256]{1,0:T(8,128)S(1)} fusion(bf16[128,8192]{0,1:T(8,128)(2,1)S(1)} %bitcast.90, bf16[8192,256]{0,1:T(8,128)(2,1)} %bitcast.83), kind=kOutput, calls=%fused_computation.42 | convolution fusion | flops 536870912 | bytes 6422528 | tf_op jit(solution)/shard_map/dot_general | solution.py:56
  124.0 4.9 %collective-permute-done.1 = bf16[128,8192]{0,1:T(8,128)(2,1)} collective-permute-done((bf16[128,8192]{0,1:T(8,128)(2,1)S(1)}, bf16[128,8192]{0,1:T(8,128)(2,1)}, u32[]{:S(2)}, u32[]{:S(2)}) %collective-permute-start.1) | collective-permute-done | bytes 2097184 | tf_op jit(solution)/shard_map/ppermute | solution.py:78
  128.9 3.1 %fusion.21 = f32[128,256]{0,1:T(8,128)S(1)} fusion(bf16[8192,256]{0,1:T(8,128)(2,1)S(1)} %bitcast.84, bf16[128,8192]{0,1:T(8,128)(2,1)} %collective-permute-done.1), kind=kOutput, calls=%fused_computation.46 | convolution fusion | flops 536870912 | bytes 6422528 | tf_op jit(solution)/shard_map/dot_general | solution.py:56
  132.0 3.1 %fusion.19 = f32[128,256]{1,0:T(8,128)S(1)} fusion(bf16[128,8192]{0,1:T(8,128)(2,1)} %collective-permute-done.1, bf16[8192,256]{0,1:T(8,128)(2,1)S(1)} %bitcast.86), kind=kOutput, calls=%fused_computation.44 | convolution fusion | flops 536870912 | bytes 6422528 | tf_op jit(solution)/shard_map/dot_general | solution.py:56
  135.2 2.9 %fusion.20 = f32[128,256]{0,1:T(8,128)S(1)} fusion(bf16[8192,256]{0,1:T(8,128)(2,1)S(1)} %bitcast.85, bf16[128,8192]{0,1:T(8,128)(2,1)} %collective-permute-done), kind=kOutput, calls=%fused_computation.45 | convolution fusion | flops 536870912 | bytes 6422528 | tf_op jit(solution)/shard_map/dot_general | solution.py:56
  138.1 3.1 %fusion.18 = f32[128,256]{1,0:T(8,128)S(1)} fusion(bf16[128,8192]{0,1:T(8,128)(2,1)} %collective-permute-done, bf16[8192,256]{0,1:T(8,128)(2,1)S(1)} %bitcast.87), kind=kOutput, calls=%fused_computation.43 | convolution fusion | flops 536870912 | bytes 6422528 | tf_op jit(solution)/shard_map/dot_general | solution.py:56
  141.3 1.3 collective-permute-start.3
  142.6 2.3 %collective-permute-start.2 = (f32[128,128]{0,1:T(8,128)S(1)}, f32[128,128]{0,1:T(8,128)S(1)}, u32[]{:S(2)}, u32[]{:S(2)}) collective-permute-start(f32[128,128]{0,1:T(8,128)S(1)} %slice_add_fusion.2), channel_id=1, source_target_pairs={{8,0},{16,8},{24,16},{0,24},{9,1},{17,9},{25,17},{1,25},{10,2},{18... | collective-permute-start | bytes 196616 | tf_op jit(solution)/shard_map/ppermute | solution.py:114
  145.1 4.1 %collective-permute-done.2 = f32[128,128]{0,1:T(8,128)S(1)} collective-permute-done((f32[128,128]{0,1:T(8,128)S(1)}, f32[128,128]{0,1:T(8,128)S(1)}, u32[]{:S(2)}, u32[]{:S(2)}) %collective-permute-start.2) | collective-permute-done | bytes 65568 | tf_op jit(solution)/shard_map/ppermute | solution.py:114
  149.3 10.4 %all_to_all.20 = f32[8,128,64]{1,2,0:T(8,128)S(1)} all-to-all(f32[8,128,64]{1,2,0:T(8,128)S(1)} %bitcast.94), channel_id=1, replica_groups=mesh['ri'=4,'ao'=8] {'ao'}, dimensions={0} | all-to-all | bytes 524288 | tf_op jit(solution)/shard_map/all_to_all | solution.py:119
  (52 shorter events, 8.4 us)
Async XLA Ops:
  14.6 5.2 %copy-start.2 = (s32[2,1,8]{2,1,0:T(1,128)S(1)}, s32[2,1,8]{2,1,0:T(1,128)}, u32[]{:S(2)}) copy-start(s32[2,1,8]{2,1,0:T(1,128)} %param.12) | copy-start | bytes 196
  32.2 12.1 %copy-start.6 = (s32[4]{0:T(128)S(1)}, s32[4]{0:T(128)}, u32[]{:S(2)}) copy-start(s32[4]{0:T(128)} %constant.32.clone) | copy-start | bytes 52
  32.2 13.4 %copy-start.5 = (s32[4]{0:T(128)S(1)}, s32[4]{0:T(128)}, u32[]{:S(2)}) copy-start(s32[4]{0:T(128)} %constant.33.clone) | copy-start | bytes 52
  32.2 14.6 %copy-start.4 = (s32[4]{0:T(128)S(1)}, s32[4]{0:T(128)}, u32[]{:S(2)}) copy-start(s32[4]{0:T(128)} %constant.34.clone) | copy-start | bytes 52
  32.2 15.8 %copy-start.3 = (s32[4]{0:T(128)S(1)}, s32[4]{0:T(128)}, u32[]{:S(2)}) copy-start(s32[4]{0:T(128)} %constant.35.clone) | copy-start | bytes 52
  32.2 53.8 %all-to-all-start = ((bf16[2,256,128,32]{2,3,0,1:T(8,128)(2,1)}), bf16[2,256,128,32]{2,3,0,1:T(8,128)(2,1)}, u32[]{:S(2)}, u32[]{:S(2)}) async-start(bf16[2,256,128,32]{2,3,0,1:T(8,128)(2,1)} %copy.76), calls=%async_computation | async-start | bytes 8388608 | tf_op jit(solution)/shard_map/all_to_all | solution.py:96
  36.9 87.1 %collective-permute-start = (bf16[128,8192]{0,1:T(8,128)(2,1)S(1)}, bf16[128,8192]{0,1:T(8,128)(2,1)}, u32[]{:S(2)}, u32[]{:S(2)}) collective-permute-start(bf16[128,8192]{0,1:T(8,128)(2,1)S(1)} %bitcast.88), channel_id=1, source_target_pairs={{0,8},{8,16},{16,24},{24,0},{1,9},{9,17},{17,25},{25,1},{2,10},{10... | collective-permute-start | bytes 6291464 | tf_op jit(solution)/shard_map/ppermute | solution.py:78
  38.5 90.4 %collective-permute-start.1 = (bf16[128,8192]{0,1:T(8,128)(2,1)S(1)}, bf16[128,8192]{0,1:T(8,128)(2,1)}, u32[]{:S(2)}, u32[]{:S(2)}) collective-permute-start(bf16[128,8192]{0,1:T(8,128)(2,1)S(1)} %bitcast.89), channel_id=1, source_target_pairs={{0,16},{24,8},{1,17},{25,9},{2,18},{26,10},{3,19},{27,11},{4,20},{... | collective-permute-start | bytes 6291464 | tf_op jit(solution)/shard_map/ppermute | solution.py:78
  120.2 8.7 %copy-start = (bf16[8192,2,128]{0,2,1:T(8,128)(2,1)S(1)}, bf16[8192,2,128]{0,2,1:T(8,128)(2,1)}, u32[]{:S(2)}) copy-start(bf16[8192,2,128]{0,2,1:T(8,128)(2,1)} %copy.85) | copy-start | bytes 12582916
  128.9 3.1 %copy-start.1 = (bf16[8192,2,128]{0,2,1:T(8,128)(2,1)S(1)}, bf16[8192,2,128]{0,2,1:T(8,128)(2,1)}, u32[]{:S(2)}) copy-start(bf16[8192,2,128]{0,2,1:T(8,128)(2,1)} %copy.81) | copy-start | bytes 12582916
  141.3 8.0 %collective-permute-start.3 = (f32[128,128]{0,1:T(8,128)S(1)}, f32[128,128]{0,1:T(8,128)S(1)}, u32[]{:S(2)}, u32[]{:S(2)}) collective-permute-start(f32[128,128]{0,1:T(8,128)S(1)} %slice_add_fusion), channel_id=1, source_target_pairs={{16,0},{8,24},{17,1},{9,25},{18,2},{10,26},{19,3},{11,27},{20,4},{... | collective-permute-start | bytes 196616 | tf_op jit(solution)/shard_map/ppermute | solution.py:114
  142.6 6.6 %collective-permute-start.2 = (f32[128,128]{0,1:T(8,128)S(1)}, f32[128,128]{0,1:T(8,128)S(1)}, u32[]{:S(2)}, u32[]{:S(2)}) collective-permute-start(f32[128,128]{0,1:T(8,128)S(1)} %slice_add_fusion.2), channel_id=1, source_target_pairs={{8,0},{16,8},{24,16},{0,24},{9,1},{17,9},{25,17},{1,25},{10,2},{18... | collective-permute-start | bytes 196616 | tf_op jit(solution)/shard_map/ppermute | solution.py:114

commit v8 on v5

--- a/solution.py
+++ b/solution.py
@@ -70,7 +70,9 @@
     routes = pair_routes(planes)
     own = mask_slab(tensor, live_blocks)
     own_flat = own.reshape(rows, -1)
-    received = [lax.ppermute(own_flat, "ri", route) for route, _, _ in routes]
+    lead = rows // 4
+    early = [lax.ppermute(own_flat[:lead], "ri", route) for route, _, _ in routes]
+    late = [lax.ppermute(own_flat[lead:], "ri", route) for route, _, _ in routes]
 
     stacked = jnp.stack(
         [screen_density(occ_density, occ_mask), screen_density(virt_density, virt_mask)]
@@ -88,6 +90,7 @@
         jnp.stack([occ_rows, virt_rows]),
         preferred_element_type=jnp.float32,
     ).astype(jnp.bfloat16)
+    halves, early = lax.optimization_barrier((halves, early))
     swapped = lax.all_to_all(halves, "ao", 1, 2, tiled=True)
     occ_t = swapped[0]
     virt_t = swapped[1]
@@ -99,9 +102,10 @@
     w_weights = jnp.concatenate([w_hi, w_lo]).T
     diag = slab_product(own_flat, w_weights)
 
-    v_weights, w_weights, diag, received = lax.optimization_barrier(
-        (v_weights, w_weights, diag, received)
+    v_weights, w_weights, diag, late = lax.optimization_barrier(
+        (v_weights, w_weights, diag, late)
     )
+    received = [jnp.concatenate([a, b]) for a, b in zip(early, late)]
     total = jnp.zeros((rows, planes * rows), jnp.float32)
     total = add_cols(total, diag, plane)
     for slab, (route, recv_from, send_to) in zip(received, routes):

time: 153 us -> 151 us (0.987)
  waiting for transfers between devices: 49.1 us -> 38.3 us
  local copies, waits for them, and re-layouts: 29.4 us -> 40 us
  starting transfers between devices: 15.5 us -> 23 us
  matrix products: 19.4 us -> 14.7 us
  other arithmetic: 14.8 us -> 12.2 us
  blocking collectives: 21.3 us -> 18.7 us
    ppermute x2 -> x4, waiting for transfers between devices: 11.4 us -> 3.81 us  [the longest x2 3.81 us: per_device(): lax.ppermute(own_flat[:lead], 'ri', route)]
    unnamed x15 -> x33, local copies, waits for them, and re-layouts: 3.26 us -> 10.7 us
    ppermute x2 -> x4, starting transfers between devices: 7.39 us -> 14.8 us  [the longest x2 8.3 us: per_device(): lax.ppermute(own_flat[:lead], 'ri', route)]
    dot_general x5, matrix products: 10.8 us -> 5.83 us  [slab_product(): out = jnp.dot(flat, weights, preferred_element_type=jnp.float32)]
    optimization_barrier x1 -> x2, local copies, waits for them, and re-layouts: 0.09 us -> 4.8 us  [the longest x1 4.71 us: per_device(): halves, early = lax.optimization_barrier((halves, early))]
    convert_element_type x1 -> x0, local copies, waits for them, and re-layouts: 4.66 us -> none  [per_device(): halves = jnp.einsum('prk,dkc->dcrp', own, jnp.stack([occ_rows, virt_rows]...]
    all_to_all x1, waiting for transfers between devices: 33.6 us -> 30.5 us  [per_device(): swapped = lax.all_to_all(halves, 'ao', 1, 2, tiled=True)]
    concatenate x0 -> x2, local copies, waits for them, and re-layouts: none -> 3.02 us  [per_device(): received = [jnp.concatenate([a, b]) for a, b in zip(early, late)]]
  transfers between devices with their start and end apart: 5 -> 7, of which waited for: 3 -> 3; matrix products, arithmetic and copies ran while one was open for 26% -> 31% of each run, Pallas kernels for 0% -> 0%
where the time goes in v8:
time: 151 us; the launch traced here: 150 us
  local copies, waits for them, and re-layouts  40 us (26%)
  waiting for transfers between devices  38.3 us (25%)
  starting transfers between devices  23 us (15%)
  blocking collectives  18.7 us (12%)
  matrix products  14.7 us (10%)
  other arithmetic  12.2 us (8%)
  between operations  2.99 us (2%)
    all_to_all x1, waiting for transfers between devices, per_device(): swapped = lax.all_to_all(halves, 'ao', 1, 2, tiled=True)  30.5 us
    unnamed x33, local copies, waits for them, and re-layouts  10.7 us
    all_to_all x1, blocking collectives, per_device(): got = lax.all_to_all(sent, 'ao', 0, 0, tiled=True)  9.35 us
    all_gather x1, blocking collectives, per_device(): full = lax.all_gather(stacked, 'ao', axis=1, tiled=True)  9.32 us
    ppermute x2, starting transfers between devices, per_device(): lax.ppermute(own_flat[:lead], 'ri', route)  8.3 us
    convert_element_type x2, other arithmetic, split_hi_lo(): rounded.astype(jnp.bfloat16)  8.07 us
    ppermute x2, starting transfers between devices, per_device(): lax.ppermute(own_flat[lead:], 'ri', route)  6.52 us
    dot_general x5, matrix products, slab_product(): out = jnp.dot(flat, weights, preferred_element_type=jnp.float32)  5.83 us
  transfers between devices with their start and end apart: 7, of which 3 were waited for; matrix products, arithmetic and copies ran while one was open for 31% of the time, Pallas kernels for 0%

profile of v8, /device:TPU:0, one launch (start us, length us, event | category | flops | bytes accessed | tf_op | source)
XLA Modules:
  0.0 149.8 jit_solution(2286924347125920327)
XLA Ops:
  1.1 1.8 %broadcast_multiply_fusion = bf16[128,32,256]{2,1,0:T(8,128)(2,1)S(1)} fusion(bf16[128,32,256]{2,1,0:T(8,128)(2,1)} %param.11, bf16[128,256]{1,0:T(8,128)(2,1)S(1)} %copy.55), kind=kLoop, calls=%fused_computation.16 | loop fusion | flops 1048576 | bytes 4259840 | tf_op jit(solution)/shard_map/mul | solution.py:42
  2.9 1.1 copy.76
  4.0 3.0 %collective-permute-start = (bf16[32,8192]{1,0:T(8,128)(2,1)}, bf16[32,8192]{1,0:T(8,128)(2,1)S(1)}, u32[]{:S(2)}, u32[]{:S(2)}) collective-permute-start(bf16[32,8192]{1,0:T(8,128)(2,1)} %bitcast.45), channel_id=1, source_target_pairs={{0,8},{8,16},{16,24},{24,0},{1,9},{9,17},{17,25},{25,1},{2,10},{10... | collective-permute-start | bytes 1572872 | tf_op jit(solution)/shard_map/ppermute | solution.py:74
  7.1 5.3 %collective-permute-start.1 = (bf16[32,8192]{1,0:T(8,128)(2,1)}, bf16[32,8192]{1,0:T(8,128)(2,1)}, u32[]{:S(2)}, u32[]{:S(2)}) collective-permute-start(bf16[32,8192]{1,0:T(8,128)(2,1)} %bitcast.45), channel_id=1, source_target_pairs={{0,16},{24,8},{1,17},{25,9},{2,18},{26,10},{3,19},{27,11},{4,20},{... | collective-permute-start | bytes 1572872 | tf_op jit(solution)/shard_map/ppermute | solution.py:74
  12.7 9.3 %all_gather.3 = bf16[2,256,256]{2,1,0:T(8,128)(2,1)S(1)} all-gather(bf16[2,32,256]{2,1,0:T(8,128)(2,1)S(1)} %pad_maximum_fusion.2), channel_id=1, replica_groups=mesh['ri'=4,'ao'=8] {'ao'}, dimensions={1}, use_global_device_ids=true | all-gather | bytes 294912 | tf_op jit(solution)/shard_map/all_gather | solution.py:80
  22.9 3.2 %convert_bitcast_fusion = bf16[2,256,32,128]{3,1,2,0:T(8,128)(2,1)S(1)} fusion(bf16[128,32,256]{2,1,0:T(8,128)(2,1)S(1)} %broadcast_multiply_fusion, bf16[1,256,256]{1,2,0:T(8,128)(2,1)S(1)} %copy.53, bf16[1,256,256]{1,2,0:T(8,128)(2,1)S(1)} %copy.52), kind=kOutput, calls=%fused_computation.9 | convolution fusion | flops 1076363264 | bytes 6553600 | tf_op jit(solution)/shard_map/prk,dkc->dcrp/dot_general | solution.py:87
  26.0 3.8 %collective-permute-done.1 = bf16[32,8192]{1,0:T(8,128)(2,1)} collective-permute-done((bf16[32,8192]{1,0:T(8,128)(2,1)}, bf16[32,8192]{1,0:T(8,128)(2,1)}, u32[]{:S(2)}, u32[]{:S(2)}) %collective-permute-start.1) | collective-permute-done | bytes 524320 | tf_op jit(solution)/shard_map/ppermute | solution.py:74
  29.9 4.7 %copy.57 = bf16[2,256,32,128]{3,2,0,1:T(8,128)(2,1)} copy(bf16[2,256,32,128]{3,1,2,0:T(8,128)(2,1)S(1)} %convert_bitcast_fusion) | data formatting | bytes 8388608 | tf_op jit(solution)/shard_map/optimization_barrier | solution.py:93
  34.6 4.5 %all-to-all-start = ((bf16[2,256,32,128]{3,2,0,1:T(8,128)(2,1)}), bf16[2,256,32,128]{3,2,0,1:T(8,128)(2,1)}, u32[]{:S(2)}, u32[]{:S(2)}) async-start(bf16[2,256,32,128]{3,2,0,1:T(8,128)(2,1)} %copy.57), calls=%async_computation | async-start | bytes 8388608 | tf_op jit(solution)/shard_map/all_to_all | solution.py:94
  39.3 2.2 %copy.78 = bf16[12,8,32,256]{3,1,2,0:T(8,128)(2,1)} copy(bf16[12,8,32,256]{3,2,1,0:T(8,128)(2,1)S(1)} %bitcast.97) | data formatting | bytes 3145728
  41.5 3.3 %collective-permute-start.2 = (bf16[96,8192]{1,0:T(8,128)(2,1)}, bf16[96,8192]{1,0:T(8,128)(2,1)}, u32[]{:S(2)}, u32[]{:S(2)}) collective-permute-start(bf16[96,8192]{1,0:T(8,128)(2,1)} %bitcast.49), channel_id=1, source_target_pairs={{0,8},{8,16},{16,24},{24,0},{1,9},{9,17},{17,25},{25,1},{2,10},{10... | collective-permute-start | bytes 4718600 | tf_op jit(solution)/shard_map/ppermute | solution.py:75
  44.8 3.2 %collective-permute-start.3 = (bf16[96,8192]{1,0:T(8,128)(2,1)}, bf16[96,8192]{1,0:T(8,128)(2,1)}, u32[]{:S(2)}, u32[]{:S(2)}) collective-permute-start(bf16[96,8192]{1,0:T(8,128)(2,1)} %bitcast.49), channel_id=1, source_target_pairs={{0,16},{24,8},{1,17},{25,9},{2,18},{26,10},{3,19},{27,11},{4,20},{... | collective-permute-start | bytes 4718600 | tf_op jit(solution)/shard_map/ppermute | solution.py:75
  53.0 2.8 %copy.77 = bf16[16,8,32,256]{3,1,2,0:T(8,128)(2,1)} copy(bf16[16,8,32,256]{3,2,1,0:T(8,128)(2,1)S(1)} %bitcast.93) | data formatting | bytes 4194304
  55.8 1.9 %constant_dynamic-update-slice_fusion.3 = bf16[128,8192]{1,0:T(8,128)(2,1)} fusion(bf16[32,8192]{1,0:T(8,128)(2,1)} %collective-permute-done.1), kind=kLoop, calls=%fused_computation.39 | loop fusion | bytes 1048576
  57.7 30.5 %all-to-all-done = bf16[2,256,32,128]{3,2,0,1:T(8,128)(2,1)} async-done(((bf16[2,256,32,128]{3,2,0,1:T(8,128)(2,1)}), bf16[2,256,32,128]{3,2,0,1:T(8,128)(2,1)}, u32[]{:S(2)}, u32[]{:S(2)}) %all-to-all-start) | async-done | bytes 4194336 | tf_op jit(solution)/shard_map/all_to_all | solution.py:94
  88.2 2.9 %copy.58 = bf16[2,256,32,128]{3,2,1,0:T(8,128)(2,1)S(1)} copy(bf16[2,256,32,128]{3,2,0,1:T(8,128)(2,1)} %all-to-all-done) | data formatting | bytes 8388608 | tf_op jit(solution)/shard_map/all_to_all | solution.py:94
  91.2 2.1 %fusion.17 = (bf16[1,32,8,32,128]{4,3,1,2,0:T(8,128)(2,1)S(1)}, bf16[1,32,8,32,128]{4,3,1,2,0:T(8,128)(2,1)}) fusion(bf16[2,32,8,32,128]{4,3,1,2,0:T(8,128)(2,1)S(1)} %bitcast.94), kind=kLoop, calls=%fused_computation.48 | loop fusion | bytes 8388608 | tf_op jit(solution)/shard_map/slice | solution.py:96
  93.9 2.9 %convolution_bitcast_fusion = f32[128,32,256]{2,0,1:T(8,128)} fusion(bf16[32,256,128]{2,1,0:T(8,128)(2,1)S(1)} %bitcast.95, bf16[256,256,1]{1,0,2:T(8,128)(2,1)S(1)} %bitcast.104), kind=kOutput, calls=%fused_computation.12 | convolution fusion | flops 536870912 | bytes 6422528 | tf_op jit(solution)/shard_map/kl,nlq->qnk/dot_general | solution.py:98
  96.8 5.6 %copy.64 = f32[128,32,256]{0,2,1:T(8,128)} copy(f32[128,32,256]{2,0,1:T(8,128)} %convolution_bitcast_fusion) | data formatting | bytes 8388608 | tf_op jit(solution)/shard_map/kl,nlq->qnk/transpose | solution.py:98
  102.4 5.1 %reduce-precision_convert_fusion = (bf16[128,8192]{0,1:T(8,128)(2,1)}, bf16[128,8192]{0,1:T(8,128)(2,1)}) fusion(f32[128,32,256]{0,2,1:T(8,128)} %copy.64), kind=kLoop, calls=%fused_computation.2 | loop fusion | flops 4194304 | bytes 8388608 | tf_op jit(solution)/shard_map/convert_element_type | solution.py:47
  108.0 2.8 %convolution_bitcast_fusion.1 = f32[128,32,256]{2,0,1:T(8,128)} fusion(bf16[32,256,128]{2,1,0:T(8,128)(2,1)S(1)} %bitcast.96, bf16[256,256,1]{1,0,2:T(8,128)(2,1)S(1)} %bitcast.102), kind=kOutput, calls=%fused_computation.13 | convolution fusion | flops 536870912 | bytes 6422528 | tf_op jit(solution)/shard_map/mn,lnp->plm/dot_general | solution.py:97
  110.8 5.6 %copy.61 = f32[128,32,256]{0,2,1:T(8,128)} copy(f32[128,32,256]{2,0,1:T(8,128)} %convolution_bitcast_fusion.1) | data formatting | bytes 8388608 | tf_op jit(solution)/shard_map/mn,lnp->plm/transpose | solution.py:97
  116.4 3.0 %reduce-precision_convert_fusion.1 = (bf16[128,8192]{0,1:T(8,128)(2,1)S(1)}, bf16[128,8192]{0,1:T(8,128)(2,1)S(1)}) fusion(f32[128,32,256]{0,2,1:T(8,128)} %copy.61), kind=kLoop, calls=%fused_computation.4 | loop fusion | flops 4194304 | bytes 8388608 | tf_op jit(solution)/shard_map/convert_element_type | solution.py:47
  120.3 1.1 copy-done.4
  123.8 1.5 %constant_dynamic-update-slice_fusion.2 = bf16[128,8192]{1,0:T(8,128)(2,1)S(1)} fusion(bf16[128,8192]{1,0:T(8,128)(2,1)S(1)} %copy-done, bf16[96,8192]{1,0:T(8,128)(2,1)} %collective-permute-done.3), kind=kLoop, calls=%fused_computation.38 | loop fusion | bytes 3145728 | tf_op jit(solution)/shard_map/concatenate | solution.py:108
  125.3 1.8 %fusion.22 = f32[128,256]{0,1:T(8,128)S(1)} fusion(bf16[128,8192]{1,0:T(8,128)(2,1)S(1)} %constant_dynamic-update-slice_fusion.2, bf16[8192,256]{1,0:T(8,128)(2,1)S(1)} %fusion.3), kind=kOutput, calls=%fused_computation.53 | convolution fusion | flops 536870912 | bytes 6422528 | tf_op jit(solution)/shard_map/dot_general | solution.py:51
  127.9 1.5 %constant_dynamic-update-slice_fusion = bf16[128,8192]{1,0:T(8,128)(2,1)S(1)} fusion(bf16[128,8192]{1,0:T(8,128)(2,1)S(1)} %constant_dynamic-update-slice_fusion.1, bf16[96,8192]{1,0:T(8,128)(2,1)} %collective-permute-done.2), kind=kLoop, calls=%fused_computation.36 | loop fusion | bytes 3145728 | tf_op jit(solution)/shard_map/concatenate | solution.py:108
  129.4 1.8 %fusion.20 = f32[128,256]{0,1:T(8,128)S(1)} fusion(bf16[128,8192]{1,0:T(8,128)(2,1)S(1)} %constant_dynamic-update-slice_fusion, bf16[8192,256]{1,0:T(8,128)(2,1)S(1)} %fusion.3), kind=kOutput, calls=%fused_computation.51 | convolution fusion | flops 536870912 | bytes 6422528 | tf_op jit(solution)/shard_map/dot_general | solution.py:51
  132.0 1.3 collective-permute-start.5
  133.3 2.3 %collective-permute-start.4 = (f32[128,128]{0,1:T(8,128)S(1)}, f32[128,128]{0,1:T(8,128)S(1)}, u32[]{:S(2)}, u32[]{:S(2)}) collective-permute-start(f32[128,128]{0,1:T(8,128)S(1)} %slice_add_fusion.2), channel_id=1, source_target_pairs={{8,0},{16,8},{24,16},{0,24},{9,1},{17,9},{25,17},{1,25},{10,2},{18... | collective-permute-start | bytes 196616 | tf_op jit(solution)/shard_map/ppermute | solution.py:115
  135.8 4.0 %collective-permute-done.4 = f32[128,128]{0,1:T(8,128)S(1)} collective-permute-done((f32[128,128]{0,1:T(8,128)S(1)}, f32[128,128]{0,1:T(8,128)S(1)}, u32[]{:S(2)}, u32[]{:S(2)}) %collective-permute-start.4) | collective-permute-done | bytes 65568 | tf_op jit(solution)/shard_map/ppermute | solution.py:115
  139.8 9.3 %all_to_all.20 = f32[8,128,64]{1,2,0:T(8,128)S(1)} all-to-all(f32[8,128,64]{1,2,0:T(8,128)S(1)} %bitcast.98), channel_id=1, replica_groups=mesh['ri'=4,'ao'=8] {'ao'}, dimensions={0} | all-to-all | bytes 524288 | tf_op jit(solution)/shard_map/all_to_all | solution.py:120
  (76 shorter events, 11.6 us)
Async XLA Ops:
  2.8 9.5 %copy-start.7 = (s32[1,8]{1,0:T(1,128)S(1)}, s32[1,8]{1,0:T(1,128)}, u32[]{:S(2)}) copy-start(s32[1,8]{1,0:T(1,128)} %param.15) | copy-start | bytes 100
  2.9 9.7 %copy-start.8 = (s32[1,8]{1,0:T(1,128)S(1)}, s32[1,8]{1,0:T(1,128)}, u32[]{:S(2)}) copy-start(s32[1,8]{1,0:T(1,128)} %param.16) | copy-start | bytes 100
  2.9 9.8 %copy-start.5 = (bf16[32,256]{1,0:T(8,128)(2,1)S(1)}, bf16[32,256]{1,0:T(8,128)(2,1)}, u32[]{:S(2)}) copy-start(bf16[32,256]{1,0:T(8,128)(2,1)} %param.14) | copy-start | bytes 49156
  2.9 9.8 %copy-start.6 = (bf16[32,256]{1,0:T(8,128)(2,1)S(1)}, bf16[32,256]{1,0:T(8,128)(2,1)}, u32[]{:S(2)}) copy-start(bf16[32,256]{1,0:T(8,128)(2,1)} %param.13) | copy-start | bytes 49156
  2.9 19.2 %copy-start.9 = (s32[1,8]{1,0:T(1,128)S(1)}, s32[1,8]{1,0:T(1,128)}, u32[]{:S(2)}) copy-start(s32[1,8]{1,0:T(1,128)} %param.17) | copy-start | bytes 100
  4.0 22.0 %collective-permute-start = (bf16[32,8192]{1,0:T(8,128)(2,1)}, bf16[32,8192]{1,0:T(8,128)(2,1)S(1)}, u32[]{:S(2)}, u32[]{:S(2)}) collective-permute-start(bf16[32,8192]{1,0:T(8,128)(2,1)} %bitcast.45), channel_id=1, source_target_pairs={{0,8},{8,16},{16,24},{24,0},{1,9},{9,17},{17,25},{25,1},{2,10},{10... | collective-permute-start | bytes 1572872 | tf_op jit(solution)/shard_map/ppermute | solution.py:74
  7.1 22.8 %collective-permute-start.1 = (bf16[32,8192]{1,0:T(8,128)(2,1)}, bf16[32,8192]{1,0:T(8,128)(2,1)}, u32[]{:S(2)}, u32[]{:S(2)}) collective-permute-start(bf16[32,8192]{1,0:T(8,128)(2,1)} %bitcast.45), channel_id=1, source_target_pairs={{0,16},{24,8},{1,17},{25,9},{2,18},{26,10},{3,19},{27,11},{4,20},{... | collective-permute-start | bytes 1572872 | tf_op jit(solution)/shard_map/ppermute | solution.py:74
  34.6 53.7 %all-to-all-start = ((bf16[2,256,32,128]{3,2,0,1:T(8,128)(2,1)}), bf16[2,256,32,128]{3,2,0,1:T(8,128)(2,1)}, u32[]{:S(2)}, u32[]{:S(2)}) async-start(bf16[2,256,32,128]{3,2,0,1:T(8,128)(2,1)} %copy.57), calls=%async_computation | async-start | bytes 8388608 | tf_op jit(solution)/shard_map/all_to_all | solution.py:94
  39.2 8.7 %copy-start.13 = (s32[4]{0:T(128)S(1)}, s32[4]{0:T(128)}, u32[]{:S(2)}) copy-start(s32[4]{0:T(128)} %constant.32.clone) | copy-start | bytes 52
  39.3 10.0 %copy-start.12 = (s32[4]{0:T(128)S(1)}, s32[4]{0:T(128)}, u32[]{:S(2)}) copy-start(s32[4]{0:T(128)} %constant.33.clone) | copy-start | bytes 52
  39.3 11.1 %copy-start.11 = (s32[4]{0:T(128)S(1)}, s32[4]{0:T(128)}, u32[]{:S(2)}) copy-start(s32[4]{0:T(128)} %constant.34.clone) | copy-start | bytes 52
  39.3 12.5 %copy-start.10 = (s32[4]{0:T(128)S(1)}, s32[4]{0:T(128)}, u32[]{:S(2)}) copy-start(s32[4]{0:T(128)} %constant.35.clone) | copy-start | bytes 52
  41.5 81.2 %collective-permute-start.2 = (bf16[96,8192]{1,0:T(8,128)(2,1)}, bf16[96,8192]{1,0:T(8,128)(2,1)}, u32[]{:S(2)}, u32[]{:S(2)}) collective-permute-start(bf16[96,8192]{1,0:T(8,128)(2,1)} %bitcast.49), channel_id=1, source_target_pairs={{0,8},{8,16},{16,24},{24,0},{1,9},{9,17},{17,25},{25,1},{2,10},{10... | collective-permute-start | bytes 4718600 | tf_op jit(solution)/shard_map/ppermute | solution.py:75
  44.8 77.9 %collective-permute-start.3 = (bf16[96,8192]{1,0:T(8,128)(2,1)}, bf16[96,8192]{1,0:T(8,128)(2,1)}, u32[]{:S(2)}, u32[]{:S(2)}) collective-permute-start(bf16[96,8192]{1,0:T(8,128)(2,1)} %bitcast.49), channel_id=1, source_target_pairs={{0,16},{24,8},{1,17},{25,9},{2,18},{26,10},{3,19},{27,11},{4,20},{... | collective-permute-start | bytes 4718600 | tf_op jit(solution)/shard_map/ppermute | solution.py:75
  102.4 5.1 %copy-start.1 = (bf16[1,32,8,32,128]{4,3,1,2,0:T(8,128)(2,1)S(1)}, bf16[1,32,8,32,128]{4,3,1,2,0:T(8,128)(2,1)}, u32[]{:S(2)}) copy-start(bf16[1,32,8,32,128]{4,3,1,2,0:T(8,128)(2,1)} %get-tuple-element.24) | copy-start | bytes 6291460
  116.4 3.0 %copy-start.2 = (bf16[128,8192]{0,1:T(8,128)(2,1)S(1)}, bf16[128,8192]{0,1:T(8,128)(2,1)}, u32[]{:S(2)}) copy-start(bf16[128,8192]{0,1:T(8,128)(2,1)} %get-tuple-element.21) | copy-start | bytes 6291460
  116.4 3.5 %copy-start.3 = (bf16[128,8192]{0,1:T(8,128)(2,1)S(1)}, bf16[128,8192]{0,1:T(8,128)(2,1)}, u32[]{:S(2)}) copy-start(bf16[128,8192]{0,1:T(8,128)(2,1)} %get-tuple-element.22) | copy-start | bytes 6291460
  119.9 1.6 %copy-start.4 = (bf16[16,8,32,256]{3,1,2,0:T(8,128)(2,1)S(1)}, bf16[16,8,32,256]{3,1,2,0:T(8,128)(2,1)}, u32[]{:S(2)}) copy-start(bf16[16,8,32,256]{3,1,2,0:T(8,128)(2,1)} %copy.77) | copy-start | bytes 6291460
  122.2 1.6 %copy-start = (bf16[128,8192]{1,0:T(8,128)(2,1)S(1)}, bf16[128,8192]{1,0:T(8,128)(2,1)}, u32[]{:S(2)}) copy-start(bf16[128,8192]{1,0:T(8,128)(2,1)} %constant_dynamic-update-slice_fusion.3) | copy-start | bytes 6291460
  132.0 7.8 %collective-permute-start.5 = (f32[128,128]{0,1:T(8,128)S(1)}, f32[128,128]{0,1:T(8,128)S(1)}, u32[]{:S(2)}, u32[]{:S(2)}) collective-permute-start(f32[128,128]{0,1:T(8,128)S(1)} %slice_add_fusion), channel_id=1, source_target_pairs={{16,0},{8,24},{17,1},{9,25},{18,2},{10,26},{19,3},{11,27},{20,4},{... | collective-permute-start | bytes 196616 | tf_op jit(solution)/shard_map/ppermute | solution.py:115
  133.3 6.4 %collective-permute-start.4 = (f32[128,128]{0,1:T(8,128)S(1)}, f32[128,128]{0,1:T(8,128)S(1)}, u32[]{:S(2)}, u32[]{:S(2)}) collective-permute-start(f32[128,128]{0,1:T(8,128)S(1)} %slice_add_fusion.2), channel_id=1, source_target_pairs={{8,0},{16,8},{24,16},{0,24},{9,1},{17,9},{25,17},{1,25},{10,2},{18... | collective-permute-start | bytes 196616 | tf_op jit(solution)/shard_map/ppermute | solution.py:115

commit v9 on v8

--- a/solution.py
+++ b/solution.py
@@ -45,6 +45,12 @@
 def split_hi_lo(values):
     rounded = lax.reduce_precision(values, exponent_bits=8, mantissa_bits=7)
     return rounded.astype(jnp.bfloat16), (values - rounded).astype(jnp.bfloat16)
+
+
+def weight_pair(values):
+    hi, lo = split_hi_lo(values)
+    both = jnp.stack([hi, lo])
+    return both.transpose(2, 3, 0, 1).reshape(values.shape[1] * values.shape[2], -1)
 
 
 def slab_product(flat, weights):
@@ -96,10 +102,8 @@
     virt_t = swapped[1]
     v_part = jnp.einsum("mn,lnp->plm", virt_rows, occ_t, preferred_element_type=jnp.float32)
     w_part = jnp.einsum("kl,nlq->qnk", occ_rows, virt_t, preferred_element_type=jnp.float32)
-    v_hi, v_lo = split_hi_lo(v_part.reshape(rows, -1))
-    w_hi, w_lo = split_hi_lo(w_part.reshape(rows, -1))
-    v_weights = jnp.concatenate([v_hi, v_lo]).T
-    w_weights = jnp.concatenate([w_hi, w_lo]).T
+    v_weights = weight_pair(v_part)
+    w_weights = weight_pair(w_part)
     diag = slab_product(own_flat, w_weights)
 
     v_weights, w_weights, diag, late = lax.optimization_barrier(

time: 151 us -> 141 us (0.934)
  other arithmetic: 12.2 us -> 3.96 us
  waiting for transfers between devices: 38.3 us -> 41.5 us
  matrix products: 14.7 us -> 11.9 us
  starting transfers between devices: 23 us -> 21.3 us
    convert_element_type x2 -> x0, other arithmetic: 8.07 us -> none  [split_hi_lo(): rounded.astype(jnp.bfloat16)]
    transpose x2, local copies, waits for them, and re-layouts: 11.2 us -> 4.86 us  [weight_pair(): both.transpose(2, 3, 0, 1).reshape(values.shape[1] * values.shape[2], -1)]
    unnamed x33 -> x29, local copies, waits for them, and re-layouts: 10.7 us -> 16.7 us
    ppermute x2, waiting for transfers between devices: 0.01 us -> 2.21 us  [per_device(): lax.ppermute(own_flat[lead:], 'ri', route)]
    dot_general x1, matrix products: 2.86 us -> 0.78 us  [per_device(): jnp.einsum('kl,nlq->qnk', occ_rows, virt_t, preferred_element_type=jnp.fl...]
    dot_general x1, matrix products: 2.81 us -> 0.78 us  [per_device(): jnp.einsum('mn,lnp->plm', virt_rows, occ_t, preferred_element_type=jnp.fl...]
    ppermute x2, starting transfers between devices: 3.6 us -> 1.88 us  [per_device(): lax.ppermute(slab_product(slab, w_weights), 'ri', [(d, s) for s, d in rou...]
  transfers between devices with their start and end apart: 7 -> 7, of which waited for: 3 -> 5; matrix products, arithmetic and copies ran while one was open for 31% -> 26% of each run, Pallas kernels for 0% -> 0%
where the time goes in v9:
time: 141 us; the launch traced here: 140 us
  waiting for transfers between devices  41.5 us (29%)
  local copies, waits for them, and re-layouts  38.5 us (27%)
  starting transfers between devices  21.3 us (15%)
  blocking collectives  19.8 us (14%)
  matrix products  11.9 us (8%)
  other arithmetic  3.96 us (3%)
  between operations  3.01 us (2%)
    all_to_all x1, waiting for transfers between devices, per_device(): swapped = lax.all_to_all(halves, 'ao', 1, 2, tiled=True)  30.5 us
    unnamed x29, local copies, waits for them, and re-layouts  16.7 us
    all_to_all x1, blocking collectives, per_device(): got = lax.all_to_all(sent, 'ao', 0, 0, tiled=True)  10.5 us
    all_gather x1, blocking collectives, per_device(): full = lax.all_gather(stacked, 'ao', axis=1, tiled=True)  9.32 us
    ppermute x2, starting transfers between devices, per_device(): lax.ppermute(own_flat[:lead], 'ri', route)  8.3 us
    dot_general x5, matrix products, slab_product(): out = jnp.dot(flat, weights, preferred_element_type=jnp.float32)  7.23 us
    ppermute x2, starting transfers between devices, per_device(): lax.ppermute(own_flat[lead:], 'ri', route)  6.51 us
    ppermute x2, waiting for transfers between devices, per_device(): lax.ppermute(slab_product(slab, w_weights), 'ri', [(d, s) for s, d in rou...  5.05 us
  transfers between devices with their start and end apart: 7, of which 5 were waited for; matrix products, arithmetic and copies ran while one was open for 26% of the time, Pallas kernels for 0%

profile of v9, /device:TPU:0, one launch (start us, length us, event | category | flops | bytes accessed | tf_op | source)
XLA Modules:
  0.0 140.1 jit_solution(12680412703638906)
XLA Ops:
  1.1 1.8 %broadcast_multiply_fusion = bf16[128,32,256]{2,1,0:T(8,128)(2,1)S(1)} fusion(bf16[128,32,256]{2,1,0:T(8,128)(2,1)} %param.11, bf16[128,256]{1,0:T(8,128)(2,1)S(1)} %copy.55), kind=kLoop, calls=%fused_computation.16 | loop fusion | flops 1048576 | bytes 4259840 | tf_op jit(solution)/shard_map/mul | solution.py:42
  2.9 1.1 copy.76
  4.0 3.0 %collective-permute-start = (bf16[32,8192]{1,0:T(8,128)(2,1)}, bf16[32,8192]{1,0:T(8,128)(2,1)S(1)}, u32[]{:S(2)}, u32[]{:S(2)}) collective-permute-start(bf16[32,8192]{1,0:T(8,128)(2,1)} %bitcast.47), channel_id=1, source_target_pairs={{0,8},{8,16},{16,24},{24,0},{1,9},{9,17},{17,25},{25,1},{2,10},{10... | collective-permute-start | bytes 1572872 | tf_op jit(solution)/shard_map/ppermute | solution.py:80
  7.1 5.3 %collective-permute-start.1 = (bf16[32,8192]{1,0:T(8,128)(2,1)}, bf16[32,8192]{1,0:T(8,128)(2,1)}, u32[]{:S(2)}, u32[]{:S(2)}) collective-permute-start(bf16[32,8192]{1,0:T(8,128)(2,1)} %bitcast.47), channel_id=1, source_target_pairs={{0,16},{24,8},{1,17},{25,9},{2,18},{26,10},{3,19},{27,11},{4,20},{... | collective-permute-start | bytes 1572872 | tf_op jit(solution)/shard_map/ppermute | solution.py:80
  12.7 9.3 %all_gather.3 = bf16[2,256,256]{2,1,0:T(8,128)(2,1)S(1)} all-gather(bf16[2,32,256]{2,1,0:T(8,128)(2,1)S(1)} %pad_maximum_fusion), channel_id=1, replica_groups=mesh['ri'=4,'ao'=8] {'ao'}, dimensions={1}, use_global_device_ids=true | all-gather | bytes 294912 | tf_op jit(solution)/shard_map/all_gather | solution.py:86
  22.9 3.2 %convert_bitcast_fusion = bf16[2,256,32,128]{3,1,2,0:T(8,128)(2,1)S(1)} fusion(bf16[128,32,256]{2,1,0:T(8,128)(2,1)S(1)} %broadcast_multiply_fusion, bf16[1,256,256]{1,2,0:T(8,128)(2,1)S(1)} %copy.53, bf16[1,256,256]{1,2,0:T(8,128)(2,1)S(1)} %copy.52), kind=kOutput, calls=%fused_computation.9 | convolution fusion | flops 1076363264 | bytes 6553600 | tf_op jit(solution)/shard_map/prk,dkc->dcrp/dot_general | solution.py:93
  26.0 3.8 %collective-permute-done.1 = bf16[32,8192]{1,0:T(8,128)(2,1)} collective-permute-done((bf16[32,8192]{1,0:T(8,128)(2,1)}, bf16[32,8192]{1,0:T(8,128)(2,1)}, u32[]{:S(2)}, u32[]{:S(2)}) %collective-permute-start.1) | collective-permute-done | bytes 524320 | tf_op jit(solution)/shard_map/ppermute | solution.py:80
  29.8 4.7 %copy.57 = bf16[2,256,32,128]{3,2,0,1:T(8,128)(2,1)} copy(bf16[2,256,32,128]{3,1,2,0:T(8,128)(2,1)S(1)} %convert_bitcast_fusion) | data formatting | bytes 8388608 | tf_op jit(solution)/shard_map/optimization_barrier | solution.py:99
  34.5 4.6 %all-to-all-start = ((bf16[2,256,32,128]{3,2,0,1:T(8,128)(2,1)}), bf16[2,256,32,128]{3,2,0,1:T(8,128)(2,1)}, u32[]{:S(2)}, u32[]{:S(2)}) async-start(bf16[2,256,32,128]{3,2,0,1:T(8,128)(2,1)} %copy.57), calls=%async_computation | async-start | bytes 8388608 | tf_op jit(solution)/shard_map/all_to_all | solution.py:100
  39.3 2.2 %copy.80 = bf16[12,8,32,256]{3,1,2,0:T(8,128)(2,1)} copy(bf16[12,8,32,256]{3,2,1,0:T(8,128)(2,1)S(1)} %bitcast.128) | data formatting | bytes 3145728
  41.5 3.3 %collective-permute-start.2 = (bf16[96,8192]{1,0:T(8,128)(2,1)}, bf16[96,8192]{1,0:T(8,128)(2,1)}, u32[]{:S(2)}, u32[]{:S(2)}) collective-permute-start(bf16[96,8192]{1,0:T(8,128)(2,1)} %bitcast.61), channel_id=1, source_target_pairs={{0,8},{8,16},{16,24},{24,0},{1,9},{9,17},{17,25},{25,1},{2,10},{10... | collective-permute-start | bytes 4718600 | tf_op jit(solution)/shard_map/ppermute | solution.py:81
  44.8 3.2 %collective-permute-start.3 = (bf16[96,8192]{1,0:T(8,128)(2,1)}, bf16[96,8192]{1,0:T(8,128)(2,1)}, u32[]{:S(2)}, u32[]{:S(2)}) collective-permute-start(bf16[96,8192]{1,0:T(8,128)(2,1)} %bitcast.61), channel_id=1, source_target_pairs={{0,16},{24,8},{1,17},{25,9},{2,18},{26,10},{3,19},{27,11},{4,20},{... | collective-permute-start | bytes 4718600 | tf_op jit(solution)/shard_map/ppermute | solution.py:81
  53.0 2.8 %copy.79 = bf16[16,8,32,256]{3,1,2,0:T(8,128)(2,1)} copy(bf16[16,8,32,256]{3,2,1,0:T(8,128)(2,1)S(1)} %bitcast.119) | data formatting | bytes 4194304
  55.8 1.9 %constant_dynamic-update-slice_fusion.3 = bf16[128,8192]{1,0:T(8,128)(2,1)} fusion(bf16[32,8192]{1,0:T(8,128)(2,1)} %collective-permute-done.1), kind=kLoop, calls=%fused_computation.39 | loop fusion | bytes 1048576
  57.8 30.5 %all-to-all-done = bf16[2,256,32,128]{3,2,0,1:T(8,128)(2,1)} async-done(((bf16[2,256,32,128]{3,2,0,1:T(8,128)(2,1)}), bf16[2,256,32,128]{3,2,0,1:T(8,128)(2,1)}, u32[]{:S(2)}, u32[]{:S(2)}) %all-to-all-start) | async-done | bytes 4194336 | tf_op jit(solution)/shard_map/all_to_all | solution.py:100
  88.2 2.9 %copy.58 = bf16[2,256,32,128]{3,2,1,0:T(8,128)(2,1)S(1)} copy(bf16[2,256,32,128]{3,2,0,1:T(8,128)(2,1)} %all-to-all-done) | data formatting | bytes 8388608 | tf_op jit(solution)/shard_map/all_to_all | solution.py:100
  93.7 2.4 %copy.64 = bf16[32,256,2,128]{1,0,3,2:T(8,128)(2,1)S(1)} copy(bf16[32,256,2,128]{1,3,0,2:T(8,128)(2,1)S(1)} %maximum_bitcast_fusion.1) | data formatting | bytes 8388608 | tf_op jit(solution)/shard_map/transpose | solution.py:53
  96.1 4.3 %copy.78 = bf16[32,8,32,256]{3,1,2,0:T(8,128)(2,1)S(1)} copy(bf16[32,8,32,256]{3,2,1,0:T(8,128)(2,1)S(1)} %bitcast.123) | data formatting | bytes 8388608
  100.4 0.8 copy.59
  102.4 2.4 %copy.61 = bf16[32,256,2,128]{1,0,3,2:T(8,128)(2,1)S(1)} copy(bf16[32,256,2,128]{1,3,0,2:T(8,128)(2,1)S(1)} %maximum_bitcast_fusion) | data formatting | bytes 8388608 | tf_op jit(solution)/shard_map/transpose | solution.py:53
  104.8 4.3 %copy.77 = bf16[32,8,32,256]{3,1,2,0:T(8,128)(2,1)S(1)} copy(bf16[32,8,32,256]{3,2,1,0:T(8,128)(2,1)S(1)} %bitcast.124) | data formatting | bytes 8388608
  109.2 1.5 %fusion.20 = f32[128,256]{1,0:T(8,128)S(1)} fusion(bf16[128,8192]{1,0:T(8,128)(2,1)S(1)} %bitcast.125, bf16[8192,256]{0,1:T(8,128)(2,1)S(1)} %bitcast.116), kind=kOutput, calls=%fused_computation.49 | convolution fusion | flops 536870912 | bytes 6422528 | tf_op jit(solution)/shard_map/dot_general | solution.py:57
  110.8 2.2 %collective-permute-done.3 = bf16[96,8192]{1,0:T(8,128)(2,1)} collective-permute-done((bf16[96,8192]{1,0:T(8,128)(2,1)}, bf16[96,8192]{1,0:T(8,128)(2,1)}, u32[]{:S(2)}, u32[]{:S(2)}) %collective-permute-start.3) | collective-permute-done | bytes 1572896 | tf_op jit(solution)/shard_map/ppermute | solution.py:81
  113.0 1.5 %constant_dynamic-update-slice_fusion.2 = bf16[128,8192]{1,0:T(8,128)(2,1)S(1)} fusion(bf16[128,8192]{1,0:T(8,128)(2,1)S(1)} %copy-done, bf16[96,8192]{1,0:T(8,128)(2,1)} %collective-permute-done.3), kind=kLoop, calls=%fused_computation.38 | loop fusion | bytes 3145728 | tf_op jit(solution)/shard_map/concatenate | solution.py:112
  114.5 1.4 fusion.24
  115.8 1.5 %fusion.23 = f32[128,256]{1,0:T(8,128)S(1)} fusion(bf16[128,8192]{1,0:T(8,128)(2,1)S(1)} %constant_dynamic-update-slice_fusion.2, bf16[8192,256]{0,1:T(8,128)(2,1)S(1)} %bitcast.120), kind=kOutput, calls=%fused_computation.52 | convolution fusion | flops 536870912 | bytes 6422528 | tf_op jit(solution)/shard_map/dot_general | solution.py:57
  117.4 1.5 %constant_dynamic-update-slice_fusion = bf16[128,8192]{1,0:T(8,128)(2,1)S(1)} fusion(bf16[128,8192]{1,0:T(8,128)(2,1)S(1)} %constant_dynamic-update-slice_fusion.1, bf16[96,8192]{1,0:T(8,128)(2,1)} %collective-permute-done.2), kind=kLoop, calls=%fused_computation.36 | loop fusion | bytes 3145728 | tf_op jit(solution)/shard_map/concatenate | solution.py:112
  118.9 1.3 fusion.22
  120.2 1.5 %fusion.21 = f32[128,256]{1,0:T(8,128)S(1)} fusion(bf16[128,8192]{1,0:T(8,128)(2,1)S(1)} %constant_dynamic-update-slice_fusion, bf16[8192,256]{0,1:T(8,128)(2,1)S(1)} %bitcast.121), kind=kOutput, calls=%fused_computation.50 | convolution fusion | flops 536870912 | bytes 6422528 | tf_op jit(solution)/shard_map/dot_general | solution.py:57
  121.7 1.3 collective-permute-start.5
  123.8 4.3 %collective-permute-done.4 = f32[128,128]{0,1:T(8,128)S(1)} collective-permute-done((f32[128,128]{0,1:T(8,128)S(1)}, f32[128,128]{0,1:T(8,128)S(1)}, u32[]{:S(2)}, u32[]{:S(2)}) %collective-permute-start.4) | collective-permute-done | bytes 65568 | tf_op jit(solution)/shard_map/ppermute | solution.py:119
  128.9 10.5 %all_to_all.20 = f32[8,128,64]{1,2,0:T(8,128)S(1)} all-to-all(f32[8,128,64]{1,2,0:T(8,128)S(1)} %bitcast.129), channel_id=1, replica_groups=mesh['ri'=4,'ao'=8] {'ao'}, dimensions={0} | all-to-all | bytes 524288 | tf_op jit(solution)/shard_map/all_to_all | solution.py:124
  (70 shorter events, 10.8 us)
Async XLA Ops:
  2.8 9.5 %copy-start.4 = (s32[1,8]{1,0:T(1,128)S(1)}, s32[1,8]{1,0:T(1,128)}, u32[]{:S(2)}) copy-start(s32[1,8]{1,0:T(1,128)} %param.15) | copy-start | bytes 100
  2.9 9.7 %copy-start.5 = (s32[1,8]{1,0:T(1,128)S(1)}, s32[1,8]{1,0:T(1,128)}, u32[]{:S(2)}) copy-start(s32[1,8]{1,0:T(1,128)} %param.16) | copy-start | bytes 100
  2.9 9.8 %copy-start.2 = (bf16[32,256]{1,0:T(8,128)(2,1)S(1)}, bf16[32,256]{1,0:T(8,128)(2,1)}, u32[]{:S(2)}) copy-start(bf16[32,256]{1,0:T(8,128)(2,1)} %param.14) | copy-start | bytes 49156
  2.9 9.8 %copy-start.3 = (bf16[32,256]{1,0:T(8,128)(2,1)S(1)}, bf16[32,256]{1,0:T(8,128)(2,1)}, u32[]{:S(2)}) copy-start(bf16[32,256]{1,0:T(8,128)(2,1)} %param.13) | copy-start | bytes 49156
  2.9 19.2 %copy-start.6 = (s32[1,8]{1,0:T(1,128)S(1)}, s32[1,8]{1,0:T(1,128)}, u32[]{:S(2)}) copy-start(s32[1,8]{1,0:T(1,128)} %param.17) | copy-start | bytes 100
  4.0 22.0 %collective-permute-start = (bf16[32,8192]{1,0:T(8,128)(2,1)}, bf16[32,8192]{1,0:T(8,128)(2,1)S(1)}, u32[]{:S(2)}, u32[]{:S(2)}) collective-permute-start(bf16[32,8192]{1,0:T(8,128)(2,1)} %bitcast.47), channel_id=1, source_target_pairs={{0,8},{8,16},{16,24},{24,0},{1,9},{9,17},{17,25},{25,1},{2,10},{10... | collective-permute-start | bytes 1572872 | tf_op jit(solution)/shard_map/ppermute | solution.py:80
  7.1 22.8 %collective-permute-start.1 = (bf16[32,8192]{1,0:T(8,128)(2,1)}, bf16[32,8192]{1,0:T(8,128)(2,1)}, u32[]{:S(2)}, u32[]{:S(2)}) collective-permute-start(bf16[32,8192]{1,0:T(8,128)(2,1)} %bitcast.47), channel_id=1, source_target_pairs={{0,16},{24,8},{1,17},{25,9},{2,18},{26,10},{3,19},{27,11},{4,20},{... | collective-permute-start | bytes 1572872 | tf_op jit(solution)/shard_map/ppermute | solution.py:80
  34.5 53.7 %all-to-all-start = ((bf16[2,256,32,128]{3,2,0,1:T(8,128)(2,1)}), bf16[2,256,32,128]{3,2,0,1:T(8,128)(2,1)}, u32[]{:S(2)}, u32[]{:S(2)}) async-start(bf16[2,256,32,128]{3,2,0,1:T(8,128)(2,1)} %copy.57), calls=%async_computation | async-start | bytes 8388608 | tf_op jit(solution)/shard_map/all_to_all | solution.py:100
  39.2 8.7 %copy-start.10 = (s32[4]{0:T(128)S(1)}, s32[4]{0:T(128)}, u32[]{:S(2)}) copy-start(s32[4]{0:T(128)} %constant.32.clone) | copy-start | bytes 52
  39.2 10.0 %copy-start.9 = (s32[4]{0:T(128)S(1)}, s32[4]{0:T(128)}, u32[]{:S(2)}) copy-start(s32[4]{0:T(128)} %constant.33.clone) | copy-start | bytes 52
  39.3 11.3 %copy-start.8 = (s32[4]{0:T(128)S(1)}, s32[4]{0:T(128)}, u32[]{:S(2)}) copy-start(s32[4]{0:T(128)} %constant.34.clone) | copy-start | bytes 52
  39.3 12.6 %copy-start.7 = (s32[4]{0:T(128)S(1)}, s32[4]{0:T(128)}, u32[]{:S(2)}) copy-start(s32[4]{0:T(128)} %constant.35.clone) | copy-start | bytes 52
  41.5 69.3 %collective-permute-start.2 = (bf16[96,8192]{1,0:T(8,128)(2,1)}, bf16[96,8192]{1,0:T(8,128)(2,1)}, u32[]{:S(2)}, u32[]{:S(2)}) collective-permute-start(bf16[96,8192]{1,0:T(8,128)(2,1)} %bitcast.61), channel_id=1, source_target_pairs={{0,8},{8,16},{16,24},{24,0},{1,9},{9,17},{17,25},{25,1},{2,10},{10... | collective-permute-start | bytes 4718600 | tf_op jit(solution)/shard_map/ppermute | solution.py:81
  44.8 68.2 %collective-permute-start.3 = (bf16[96,8192]{1,0:T(8,128)(2,1)}, bf16[96,8192]{1,0:T(8,128)(2,1)}, u32[]{:S(2)}, u32[]{:S(2)}) collective-permute-start(bf16[96,8192]{1,0:T(8,128)(2,1)} %bitcast.61), channel_id=1, source_target_pairs={{0,16},{24,8},{1,17},{25,9},{2,18},{26,10},{3,19},{27,11},{4,20},{... | collective-permute-start | bytes 4718600 | tf_op jit(solution)/shard_map/ppermute | solution.py:81
  104.8 4.3 %copy-start.1 = (bf16[16,8,32,256]{3,1,2,0:T(8,128)(2,1)S(1)}, bf16[16,8,32,256]{3,1,2,0:T(8,128)(2,1)}, u32[]{:S(2)}) copy-start(bf16[16,8,32,256]{3,1,2,0:T(8,128)(2,1)} %copy.79) | copy-start | bytes 6291460
  109.2 3.8 %copy-start = (bf16[128,8192]{1,0:T(8,128)(2,1)S(1)}, bf16[128,8192]{1,0:T(8,128)(2,1)}, u32[]{:S(2)}) copy-start(bf16[128,8192]{1,0:T(8,128)(2,1)} %constant_dynamic-update-slice_fusion.3) | copy-start | bytes 6291460
  121.7 7.2 %collective-permute-start.5 = (f32[128,128]{0,1:T(8,128)S(1)}, f32[128,128]{0,1:T(8,128)S(1)}, u32[]{:S(2)}, u32[]{:S(2)}) collective-permute-start(f32[128,128]{0,1:T(8,128)S(1)} %slice_add_fusion), channel_id=1, source_target_pairs={{16,0},{8,24},{17,1},{9,25},{18,2},{10,26},{19,3},{11,27},{20,4},{... | collective-permute-start | bytes 196616 | tf_op jit(solution)/shard_map/ppermute | solution.py:119
  123.1 5.0 %collective-permute-start.4 = (f32[128,128]{0,1:T(8,128)S(1)}, f32[128,128]{0,1:T(8,128)S(1)}, u32[]{:S(2)}, u32[]{:S(2)}) collective-permute-start(f32[128,128]{0,1:T(8,128)S(1)} %slice_add_fusion.2), channel_id=1, source_target_pairs={{8,0},{16,8},{24,16},{0,24},{9,1},{17,9},{25,17},{1,25},{10,2},{18... | collective-permute-start | bytes 196616 | tf_op jit(solution)/shard_map/ppermute | solution.py:119

commit v10 on v9

--- a/solution.py
+++ b/solution.py
@@ -109,14 +109,18 @@
     v_weights, w_weights, diag, late = lax.optimization_barrier(
         (v_weights, w_weights, diag, late)
     )
-    received = [jnp.concatenate([a, b]) for a, b in zip(early, late)]
+    stacked_slabs = jnp.concatenate([part for pair in zip(early, late) for part in pair])
+    mine_all = slab_product(stacked_slabs, v_weights)
+    theirs_all = slab_product(stacked_slabs, w_weights)
     total = jnp.zeros((rows, planes * rows), jnp.float32)
     total = add_cols(total, diag, plane)
-    for slab, (route, recv_from, send_to) in zip(received, routes):
+    for index, (route, recv_from, send_to) in enumerate(routes):
         source = jnp.array(recv_from, jnp.int32)[plane]
         target = jnp.array(send_to, jnp.int32)[plane]
-        total = add_cols(total, slab_product(slab, v_weights).T, source)
-        back = lax.ppermute(slab_product(slab, w_weights), "ri", [(d, s) for s, d in route])
+        mine = mine_all[index * rows:(index + 1) * rows]
+        theirs = theirs_all[index * rows:(index + 1) * rows]
+        total = add_cols(total, mine.T, source)
+        back = lax.ppermute(theirs, "ri", [(d, s) for s, d in route])
         total = add_cols(total, back, target)
 
     width = total.shape[1] // cycle_size

time: 141 us -> 138 us (0.979)
  matrix products: 11.9 us -> 8.8 us
  waiting for transfers between devices: 41.5 us -> 43 us
    dot_general x5 -> x3, matrix products: 7.23 us -> 4.08 us  [slab_product(): out = jnp.dot(flat, weights, preferred_element_type=jnp.float32)]
    concatenate x2 -> x1, local copies, waits for them, and re-layouts: 3.02 us -> 1.51 us  [per_device(): jnp.concatenate([part for pair in zip(early, late) for part in pair])]
    unnamed x29 -> x30, local copies, waits for them, and re-layouts: 16.7 us -> 18.1 us
  transfers between devices with their start and end apart: 7 -> 7, of which waited for: 5 -> 5; matrix products, arithmetic and copies ran while one was open for 26% -> 27% of each run, Pallas kernels for 0% -> 0%
where the time goes in v10:
time: 138 us
  waiting for transfers between devices  43 us (31%)
  local copies, waits for them, and re-layouts  38.4 us (28%)
  starting transfers between devices  20.8 us (15%)
  blocking collectives  19.8 us (14%)
  matrix products  8.8 us (6%)
  other arithmetic  4.04 us (3%)
  between operations  2.87 us (2%)
    all_to_all x1, waiting for transfers between devices, per_device(): swapped = lax.all_to_all(halves, 'ao', 1, 2, tiled=True)  30.8 us
    unnamed x30, local copies, waits for them, and re-layouts  18.1 us
    all_to_all x1, blocking collectives, per_device(): got = lax.all_to_all(sent, 'ao', 0, 0, tiled=True)  10.5 us
    all_gather x1, blocking collectives, per_device(): full = lax.all_gather(stacked, 'ao', axis=1, tiled=True)  9.32 us
    ppermute x2, starting transfers between devices, per_device(): lax.ppermute(own_flat[:lead], 'ri', route)  7.54 us
    ppermute x2, starting transfers between devices, per_device(): lax.ppermute(own_flat[lead:], 'ri', route)  6.52 us
    ppermute x2, waiting for transfers between devices, per_device(): back = lax.ppermute(theirs, 'ri', [(d, s) for s, d in route])  5.64 us
    transpose x2, local copies, waits for them, and re-layouts, weight_pair(): both.transpose(2, 3, 0, 1).reshape(values.shape[1] * values.shape[2], -1)  4.86 us
  transfers between devices with their start and end apart: 7, of which 5 were waited for; matrix products, arithmetic and copies ran while one was open for 27% of the time, Pallas kernels for 0%

profile of v10, /device:TPU:0, one launch (start us, length us, event | category | flops | bytes accessed | tf_op | source)
XLA Modules:
  0.0 137.7 jit_solution(5658044548612533409)
XLA Ops:
  1.2 1.8 %broadcast_multiply_fusion = bf16[128,32,256]{2,1,0:T(8,128)(2,1)S(1)} fusion(bf16[128,32,256]{2,1,0:T(8,128)(2,1)} %param.11, bf16[128,256]{1,0:T(8,128)(2,1)S(1)} %copy.49), kind=kLoop, calls=%fused_computation.16 | loop fusion | flops 1048576 | bytes 4259840 | tf_op jit(solution)/shard_map/mul | solution.py:42
  3.0 1.1 copy.67
  4.1 3.0 %collective-permute-start = (bf16[32,8192]{1,0:T(8,128)(2,1)}, bf16[32,8192]{1,0:T(8,128)(2,1)}, u32[]{:S(2)}, u32[]{:S(2)}) collective-permute-start(bf16[32,8192]{1,0:T(8,128)(2,1)} %bitcast.47), channel_id=1, source_target_pairs={{0,8},{8,16},{16,24},{24,0},{1,9},{9,17},{17,25},{25,1},{2,10},{10... | collective-permute-start | bytes 1572872 | tf_op jit(solution)/shard_map/ppermute | solution.py:80
  7.1 4.5 %collective-permute-start.1 = (bf16[32,8192]{1,0:T(8,128)(2,1)}, bf16[32,8192]{1,0:T(8,128)(2,1)S(1)}, u32[]{:S(2)}, u32[]{:S(2)}) collective-permute-start(bf16[32,8192]{1,0:T(8,128)(2,1)} %bitcast.47), channel_id=1, source_target_pairs={{0,16},{24,8},{1,17},{25,9},{2,18},{26,10},{3,19},{27,11},{4,20},{... | collective-permute-start | bytes 1572872 | tf_op jit(solution)/shard_map/ppermute | solution.py:80
  12.0 9.3 %all_gather.3 = bf16[2,256,256]{2,1,0:T(8,128)(2,1)S(1)} all-gather(bf16[2,32,256]{2,1,0:T(8,128)(2,1)S(1)} %pad_maximum_fusion), channel_id=1, replica_groups=mesh['ri'=4,'ao'=8] {'ao'}, dimensions={1}, use_global_device_ids=true | all-gather | bytes 294912 | tf_op jit(solution)/shard_map/all_gather | solution.py:86
  22.1 3.2 %convert_bitcast_fusion = bf16[2,256,32,128]{3,1,2,0:T(8,128)(2,1)S(1)} fusion(bf16[128,32,256]{2,1,0:T(8,128)(2,1)S(1)} %broadcast_multiply_fusion, bf16[1,256,256]{1,2,0:T(8,128)(2,1)S(1)} %copy.47, bf16[1,256,256]{1,2,0:T(8,128)(2,1)S(1)} %copy.46), kind=kOutput, calls=%fused_computation.9 | convolution fusion | flops 1076363264 | bytes 6553600 | tf_op jit(solution)/shard_map/prk,dkc->dcrp/dot_general | solution.py:93
  25.3 4.6 %collective-permute-done.1 = bf16[32,8192]{1,0:T(8,128)(2,1)S(1)} collective-permute-done((bf16[32,8192]{1,0:T(8,128)(2,1)}, bf16[32,8192]{1,0:T(8,128)(2,1)S(1)}, u32[]{:S(2)}, u32[]{:S(2)}) %collective-permute-start.1) | collective-permute-done | bytes 524320 | tf_op jit(solution)/shard_map/ppermute | solution.py:80
  29.9 4.7 %copy.51 = bf16[2,256,32,128]{3,2,0,1:T(8,128)(2,1)} copy(bf16[2,256,32,128]{3,1,2,0:T(8,128)(2,1)S(1)} %convert_bitcast_fusion) | data formatting | bytes 8388608 | tf_op jit(solution)/shard_map/optimization_barrier | solution.py:99
  34.6 4.6 %all-to-all-start = ((bf16[2,256,32,128]{3,2,0,1:T(8,128)(2,1)}), bf16[2,256,32,128]{3,2,0,1:T(8,128)(2,1)}, u32[]{:S(2)}, u32[]{:S(2)}) async-start(bf16[2,256,32,128]{3,2,0,1:T(8,128)(2,1)} %copy.51), calls=%async_computation | async-start | bytes 8388608 | tf_op jit(solution)/shard_map/all_to_all | solution.py:100
  39.3 2.2 %copy.71 = bf16[12,8,32,256]{3,1,2,0:T(8,128)(2,1)} copy(bf16[12,8,32,256]{3,2,1,0:T(8,128)(2,1)S(1)} %bitcast.121) | data formatting | bytes 3145728
  41.5 3.2 %collective-permute-start.2 = (bf16[96,8192]{1,0:T(8,128)(2,1)}, bf16[96,8192]{1,0:T(8,128)(2,1)}, u32[]{:S(2)}, u32[]{:S(2)}) collective-permute-start(bf16[96,8192]{1,0:T(8,128)(2,1)} %bitcast.61), channel_id=1, source_target_pairs={{0,8},{8,16},{16,24},{24,0},{1,9},{9,17},{17,25},{25,1},{2,10},{10... | collective-permute-start | bytes 4718600 | tf_op jit(solution)/shard_map/ppermute | solution.py:81
  44.7 3.3 %collective-permute-start.3 = (bf16[96,8192]{1,0:T(8,128)(2,1)}, bf16[96,8192]{1,0:T(8,128)(2,1)}, u32[]{:S(2)}, u32[]{:S(2)}) collective-permute-start(bf16[96,8192]{1,0:T(8,128)(2,1)} %bitcast.61), channel_id=1, source_target_pairs={{0,16},{24,8},{1,17},{25,9},{2,18},{26,10},{3,19},{27,11},{4,20},{... | collective-permute-start | bytes 4718600 | tf_op jit(solution)/shard_map/ppermute | solution.py:81
  52.8 2.7 %copy.70 = bf16[16,8,32,256]{3,1,2,0:T(8,128)(2,1)} copy(bf16[16,8,32,256]{3,2,1,0:T(8,128)(2,1)S(1)} %bitcast.112) | data formatting | bytes 4194304
  55.6 1.9 %constant_dynamic-update-slice_fusion.3 = bf16[256,8192]{1,0:T(8,128)(2,1)} fusion(bf16[32,8192]{1,0:T(8,128)(2,1)} %collective-permute-done), kind=kLoop, calls=%fused_computation.37 | loop fusion | bytes 1048576
  57.5 30.8 %all-to-all-done = bf16[2,256,32,128]{3,2,0,1:T(8,128)(2,1)} async-done(((bf16[2,256,32,128]{3,2,0,1:T(8,128)(2,1)}), bf16[2,256,32,128]{3,2,0,1:T(8,128)(2,1)}, u32[]{:S(2)}, u32[]{:S(2)}) %all-to-all-start) | async-done | bytes 4194336 | tf_op jit(solution)/shard_map/all_to_all | solution.py:100
  88.3 2.9 %copy.52 = bf16[2,256,32,128]{3,2,1,0:T(8,128)(2,1)S(1)} copy(bf16[2,256,32,128]{3,2,0,1:T(8,128)(2,1)} %all-to-all-done) | data formatting | bytes 8388608 | tf_op jit(solution)/shard_map/all_to_all | solution.py:100
  93.7 2.4 %copy.58 = bf16[32,256,2,128]{1,0,3,2:T(8,128)(2,1)S(1)} copy(bf16[32,256,2,128]{1,3,0,2:T(8,128)(2,1)S(1)} %maximum_bitcast_fusion.1) | data formatting | bytes 8388608 | tf_op jit(solution)/shard_map/transpose | solution.py:53
  96.1 4.3 %copy.69 = bf16[32,8,32,256]{3,1,2,0:T(8,128)(2,1)S(1)} copy(bf16[32,8,32,256]{3,2,1,0:T(8,128)(2,1)S(1)} %bitcast.116) | data formatting | bytes 8388608
  100.4 0.8 copy.53
  101.3 0.8 fusion.4
  102.4 2.4 %copy.55 = bf16[32,256,2,128]{1,0,3,2:T(8,128)(2,1)S(1)} copy(bf16[32,256,2,128]{1,3,0,2:T(8,128)(2,1)S(1)} %maximum_bitcast_fusion) | data formatting | bytes 8388608 | tf_op jit(solution)/shard_map/transpose | solution.py:53
  104.9 4.3 %copy.68 = bf16[32,8,32,256]{3,1,2,0:T(8,128)(2,1)S(1)} copy(bf16[32,8,32,256]{3,2,1,0:T(8,128)(2,1)S(1)} %bitcast.117) | data formatting | bytes 8388608
  109.2 1.5 %fusion.19 = f32[128,256]{1,0:T(8,128)S(1)} fusion(bf16[128,8192]{1,0:T(8,128)(2,1)S(1)} %bitcast.118, bf16[8192,256]{0,1:T(8,128)(2,1)S(1)} %bitcast.113), kind=kOutput, calls=%fused_computation.48 | convolution fusion | flops 536870912 | bytes 6422528 | tf_op jit(solution)/shard_map/dot_general | solution.py:57
  110.8 2.1 %collective-permute-done.3 = bf16[96,8192]{1,0:T(8,128)(2,1)} collective-permute-done((bf16[96,8192]{1,0:T(8,128)(2,1)}, bf16[96,8192]{1,0:T(8,128)(2,1)}, u32[]{:S(2)}, u32[]{:S(2)}) %collective-permute-start.3) | collective-permute-done | bytes 1572896 | tf_op jit(solution)/shard_map/ppermute | solution.py:81
  112.8 1.5 %constant_dynamic-update-slice_fusion.2 = bf16[256,8192]{1,0:T(8,128)(2,1)S(1)} fusion(bf16[256,8192]{1,0:T(8,128)(2,1)S(1)} %copy-done.1, bf16[96,8192]{1,0:T(8,128)(2,1)} %collective-permute-done.2), kind=kLoop, calls=%fused_computation.36 | loop fusion | bytes 3145728
  114.4 1.5 %constant_dynamic-update-slice_fusion = bf16[256,8192]{1,0:T(8,128)(2,1)S(1)} fusion(bf16[256,8192]{1,0:T(8,128)(2,1)S(1)} %constant_dynamic-update-slice_fusion.1, bf16[96,8192]{1,0:T(8,128)(2,1)} %collective-permute-done.3), kind=kLoop, calls=%fused_computation.34 | loop fusion | bytes 3145728 | tf_op jit(solution)/shard_map/concatenate | solution.py:112
  115.9 1.3 fusion.21
  117.2 0.9 collective-permute-start.4
  118.1 1.3 fusion.20
  119.5 1.3 collective-permute-start.5
  121.6 5.0 %collective-permute-done.5 = f32[128,128]{0,1:T(8,128)S(1)} collective-permute-done((f32[128,128]{0,1:T(8,128)S(1)}, f32[128,128]{0,1:T(8,128)S(1)}, u32[]{:S(2)}, u32[]{:S(2)}) %collective-permute-start.5) | collective-permute-done | bytes 65568 | tf_op jit(solution)/shard_map/ppermute | solution.py:123
  126.6 10.5 %all_to_all.20 = f32[8,128,64]{1,2,0:T(8,128)S(1)} all-to-all(f32[8,128,64]{1,2,0:T(8,128)S(1)} %bitcast.123), channel_id=1, replica_groups=mesh['ri'=4,'ao'=8] {'ao'}, dimensions={0} | all-to-all | bytes 524288 | tf_op jit(solution)/shard_map/all_to_all | solution.py:128
  (69 shorter events, 9.3 us)
Async XLA Ops:
  0.0 11.6 %copy-start.4 = (s32[1,8]{1,0:T(1,128)S(1)}, s32[1,8]{1,0:T(1,128)}, u32[]{:S(2)}) copy-start(s32[1,8]{1,0:T(1,128)} %param.15) | copy-start | bytes 100
  0.0 11.8 %copy-start.5 = (s32[1,8]{1,0:T(1,128)S(1)}, s32[1,8]{1,0:T(1,128)}, u32[]{:S(2)}) copy-start(s32[1,8]{1,0:T(1,128)} %param.16) | copy-start | bytes 100
  0.0 12.0 %copy-start.3 = (bf16[32,256]{1,0:T(8,128)(2,1)S(1)}, bf16[32,256]{1,0:T(8,128)(2,1)}, u32[]{:S(2)}) copy-start(bf16[32,256]{1,0:T(8,128)(2,1)} %param.13) | copy-start | bytes 49156
  0.0 12.0 %copy-start.2 = (bf16[32,256]{1,0:T(8,128)(2,1)S(1)}, bf16[32,256]{1,0:T(8,128)(2,1)}, u32[]{:S(2)}) copy-start(bf16[32,256]{1,0:T(8,128)(2,1)} %param.14) | copy-start | bytes 49156
  0.0 21.3 %copy-start.6 = (s32[1,8]{1,0:T(1,128)S(1)}, s32[1,8]{1,0:T(1,128)}, u32[]{:S(2)}) copy-start(s32[1,8]{1,0:T(1,128)} %param.17) | copy-start | bytes 100
  4.1 21.2 %collective-permute-start = (bf16[32,8192]{1,0:T(8,128)(2,1)}, bf16[32,8192]{1,0:T(8,128)(2,1)}, u32[]{:S(2)}, u32[]{:S(2)}) collective-permute-start(bf16[32,8192]{1,0:T(8,128)(2,1)} %bitcast.47), channel_id=1, source_target_pairs={{0,8},{8,16},{16,24},{24,0},{1,9},{9,17},{17,25},{25,1},{2,10},{10... | collective-permute-start | bytes 1572872 | tf_op jit(solution)/shard_map/ppermute | solution.py:80
  7.1 22.8 %collective-permute-start.1 = (bf16[32,8192]{1,0:T(8,128)(2,1)}, bf16[32,8192]{1,0:T(8,128)(2,1)S(1)}, u32[]{:S(2)}, u32[]{:S(2)}) collective-permute-start(bf16[32,8192]{1,0:T(8,128)(2,1)} %bitcast.47), channel_id=1, source_target_pairs={{0,16},{24,8},{1,17},{25,9},{2,18},{26,10},{3,19},{27,11},{4,20},{... | collective-permute-start | bytes 1572872 | tf_op jit(solution)/shard_map/ppermute | solution.py:80
  34.6 53.7 %all-to-all-start = ((bf16[2,256,32,128]{3,2,0,1:T(8,128)(2,1)}), bf16[2,256,32,128]{3,2,0,1:T(8,128)(2,1)}, u32[]{:S(2)}, u32[]{:S(2)}) async-start(bf16[2,256,32,128]{3,2,0,1:T(8,128)(2,1)} %copy.51), calls=%async_computation | async-start | bytes 8388608 | tf_op jit(solution)/shard_map/all_to_all | solution.py:100
  39.1 8.9 %copy-start.10 = (s32[4]{0:T(128)S(1)}, s32[4]{0:T(128)}, u32[]{:S(2)}) copy-start(s32[4]{0:T(128)} %constant.32.clone) | copy-start | bytes 52
  39.2 10.1 %copy-start.9 = (s32[4]{0:T(128)S(1)}, s32[4]{0:T(128)}, u32[]{:S(2)}) copy-start(s32[4]{0:T(128)} %constant.33.clone) | copy-start | bytes 52
  39.2 11.2 %copy-start.8 = (s32[4]{0:T(128)S(1)}, s32[4]{0:T(128)}, u32[]{:S(2)}) copy-start(s32[4]{0:T(128)} %constant.34.clone) | copy-start | bytes 52
  39.2 12.5 %copy-start.7 = (s32[4]{0:T(128)S(1)}, s32[4]{0:T(128)}, u32[]{:S(2)}) copy-start(s32[4]{0:T(128)} %constant.35.clone) | copy-start | bytes 52
  41.5 69.3 %collective-permute-start.2 = (bf16[96,8192]{1,0:T(8,128)(2,1)}, bf16[96,8192]{1,0:T(8,128)(2,1)}, u32[]{:S(2)}, u32[]{:S(2)}) collective-permute-start(bf16[96,8192]{1,0:T(8,128)(2,1)} %bitcast.61), channel_id=1, source_target_pairs={{0,8},{8,16},{16,24},{24,0},{1,9},{9,17},{17,25},{25,1},{2,10},{10... | collective-permute-start | bytes 4718600 | tf_op jit(solution)/shard_map/ppermute | solution.py:81
  44.7 68.2 %collective-permute-start.3 = (bf16[96,8192]{1,0:T(8,128)(2,1)}, bf16[96,8192]{1,0:T(8,128)(2,1)}, u32[]{:S(2)}, u32[]{:S(2)}) collective-permute-start(bf16[96,8192]{1,0:T(8,128)(2,1)} %bitcast.61), channel_id=1, source_target_pairs={{0,16},{24,8},{1,17},{25,9},{2,18},{26,10},{3,19},{27,11},{4,20},{... | collective-permute-start | bytes 4718600 | tf_op jit(solution)/shard_map/ppermute | solution.py:81
  104.9 4.3 %copy-start = (bf16[16,8,32,256]{3,1,2,0:T(8,128)(2,1)S(1)}, bf16[16,8,32,256]{3,1,2,0:T(8,128)(2,1)}, u32[]{:S(2)}) copy-start(bf16[16,8,32,256]{3,1,2,0:T(8,128)(2,1)} %copy.70) | copy-start | bytes 6291460
  109.2 3.6 %copy-start.1 = (bf16[256,8192]{1,0:T(8,128)(2,1)S(1)}, bf16[256,8192]{1,0:T(8,128)(2,1)}, u32[]{:S(2)}) copy-start(bf16[256,8192]{1,0:T(8,128)(2,1)} %constant_dynamic-update-slice_fusion.3) | copy-start | bytes 12582916
  117.2 4.3 %collective-permute-start.4 = (f32[128,128]{0,1:T(8,128)S(1)}, f32[128,128]{0,1:T(8,128)S(1)}, u32[]{:S(2)}, u32[]{:S(2)}) collective-permute-start(f32[128,128]{0,1:T(8,128)S(1)} %get-tuple-element.30), channel_id=1, source_target_pairs={{8,0},{16,8},{24,16},{0,24},{9,1},{17,9},{25,17},{1,25},{10,2},{18... | collective-permute-start | bytes 196616 | tf_op jit(solution)/shard_map/ppermute | solution.py:123
  119.5 7.1 %collective-permute-start.5 = (f32[128,128]{0,1:T(8,128)S(1)}, f32[128,128]{0,1:T(8,128)S(1)}, u32[]{:S(2)}, u32[]{:S(2)}) collective-permute-start(f32[128,128]{0,1:T(8,128)S(1)} %get-tuple-element.29), channel_id=1, source_target_pairs={{16,0},{8,24},{17,1},{9,25},{18,2},{10,26},{19,3},{11,27},{20,4},{... | collective-permute-start | bytes 196616 | tf_op jit(solution)/shard_map/ppermute | solution.py:123

commit v11 on v10

--- a/solution.py
+++ b/solution.py
@@ -91,15 +91,15 @@
     virt_rows = picked[1].reshape(KS * BS, ao_total)
 
     halves = jnp.einsum(
-        "prk,dkc->dcrp",
+        "prk,dkc->cdrp",
         own,
         jnp.stack([occ_rows, virt_rows]),
         preferred_element_type=jnp.float32,
     ).astype(jnp.bfloat16)
     halves, early = lax.optimization_barrier((halves, early))
-    swapped = lax.all_to_all(halves, "ao", 1, 2, tiled=True)
-    occ_t = swapped[0]
-    virt_t = swapped[1]
+    swapped = lax.all_to_all(halves, "ao", 0, 2, tiled=True)
+    occ_t = swapped[:, 0]
+    virt_t = swapped[:, 1]
     v_part = jnp.einsum("mn,lnp->plm", virt_rows, occ_t, preferred_element_type=jnp.float32)
     w_part = jnp.einsum("kl,nlq->qnk", occ_rows, virt_t, preferred_element_type=jnp.float32)
     v_weights = weight_pair(v_part)

time: 138 us -> 138 us (level)
  local copies, waits for them, and re-layouts: 38.4 us -> 36.9 us
  waiting for transfers between devices: 43 us -> 44.4 us
    slice x3 -> x0, local copies, waits for them, and re-layouts: 2.11 us -> none  [the longest x2 1.28 us: per_device(): virt_t = swapped[1]]
    ppermute x2, waiting for transfers between devices: 2.06 us -> 3.66 us  [per_device(): lax.ppermute(own_flat[lead:], 'ri', route)]
  transfers between devices with their start and end apart: 7 -> 7, of which waited for: 5 -> 5; matrix products, arithmetic and copies ran while one was open for 27% -> 26% of each run, Pallas kernels for 0% -> 0%
where the time goes in v11:
time: 138 us
  waiting for transfers between devices  44.4 us (32%)
  local copies, waits for them, and re-layouts  36.9 us (27%)
  starting transfers between devices  20.6 us (15%)
  blocking collectives  19.9 us (14%)
  matrix products  8.78 us (6%)
  other arithmetic  4.04 us (3%)
  between operations  2.97 us (2%)
    all_to_all x1, waiting for transfers between devices, per_device(): swapped = lax.all_to_all(halves, 'ao', 0, 2, tiled=True)  30.6 us
    unnamed x30, local copies, waits for them, and re-layouts  18.1 us
    all_to_all x1, blocking collectives, per_device(): got = lax.all_to_all(sent, 'ao', 0, 0, tiled=True)  10.6 us
    all_gather x1, blocking collectives, per_device(): full = lax.all_gather(stacked, 'ao', axis=1, tiled=True)  9.32 us
    ppermute x2, starting transfers between devices, per_device(): lax.ppermute(own_flat[:lead], 'ri', route)  7.54 us
    ppermute x2, starting transfers between devices, per_device(): lax.ppermute(own_flat[lead:], 'ri', route)  6.51 us
    ppermute x2, waiting for transfers between devices, per_device(): back = lax.ppermute(theirs, 'ri', [(d, s) for s, d in route])  5.64 us
    transpose x2, local copies, waits for them, and re-layouts, weight_pair(): both.transpose(2, 3, 0, 1).reshape(values.shape[1] * values.shape[2], -1)  5.08 us
  transfers between devices with their start and end apart: 7, of which 5 were waited for; matrix products, arithmetic and copies ran while one was open for 26% of the time, Pallas kernels for 0%

profile of v11, /device:TPU:0, one launch (start us, length us, event | category | flops | bytes accessed | tf_op | source)
XLA Modules:
  0.0 137.7 jit_solution(5308742793465820730)
XLA Ops:
  1.2 1.8 %broadcast_multiply_fusion = bf16[128,32,256]{2,1,0:T(8,128)(2,1)S(1)} fusion(bf16[128,32,256]{2,1,0:T(8,128)(2,1)} %param.11, bf16[128,256]{1,0:T(8,128)(2,1)S(1)} %copy.48), kind=kLoop, calls=%fused_computation.20 | loop fusion | flops 1048576 | bytes 4259840 | tf_op jit(solution)/shard_map/mul | solution.py:42
  3.0 1.1 copy.64
  4.1 3.0 %collective-permute-start = (bf16[32,8192]{1,0:T(8,128)(2,1)}, bf16[32,8192]{1,0:T(8,128)(2,1)}, u32[]{:S(2)}, u32[]{:S(2)}) collective-permute-start(bf16[32,8192]{1,0:T(8,128)(2,1)} %bitcast.50), channel_id=1, source_target_pairs={{0,8},{8,16},{16,24},{24,0},{1,9},{9,17},{17,25},{25,1},{2,10},{10... | collective-permute-start | bytes 1572872 | tf_op jit(solution)/shard_map/ppermute | solution.py:80
  7.1 4.5 %collective-permute-start.1 = (bf16[32,8192]{1,0:T(8,128)(2,1)}, bf16[32,8192]{1,0:T(8,128)(2,1)S(1)}, u32[]{:S(2)}, u32[]{:S(2)}) collective-permute-start(bf16[32,8192]{1,0:T(8,128)(2,1)} %bitcast.50), channel_id=1, source_target_pairs={{0,16},{24,8},{1,17},{25,9},{2,18},{26,10},{3,19},{27,11},{4,20},{... | collective-permute-start | bytes 1572872 | tf_op jit(solution)/shard_map/ppermute | solution.py:80
  12.0 9.3 %all_gather.3 = bf16[2,256,256]{2,1,0:T(8,128)(2,1)S(1)} all-gather(bf16[2,32,256]{2,1,0:T(8,128)(2,1)S(1)} %pad_maximum_fusion), channel_id=1, replica_groups=mesh['ri'=4,'ao'=8] {'ao'}, dimensions={1}, use_global_device_ids=true | all-gather | bytes 294912 | tf_op jit(solution)/shard_map/all_gather | solution.py:86
  22.1 3.1 %convert_bitcast_fusion = bf16[256,2,32,128]{3,0,2,1:T(8,128)(2,1)S(1)} fusion(bf16[128,32,256]{2,1,0:T(8,128)(2,1)S(1)} %broadcast_multiply_fusion, bf16[1,256,256]{1,2,0:T(8,128)(2,1)S(1)} %copy.46, bf16[1,256,256]{1,2,0:T(8,128)(2,1)S(1)} %copy.45), kind=kOutput, calls=%fused_computation.9 | convolution fusion | flops 1076363264 | bytes 6553600 | tf_op jit(solution)/shard_map/prk,dkc->cdrp/dot_general | solution.py:93
  25.3 4.6 %collective-permute-done.1 = bf16[32,8192]{1,0:T(8,128)(2,1)S(1)} collective-permute-done((bf16[32,8192]{1,0:T(8,128)(2,1)}, bf16[32,8192]{1,0:T(8,128)(2,1)S(1)}, u32[]{:S(2)}, u32[]{:S(2)}) %collective-permute-start.1) | collective-permute-done | bytes 524320 | tf_op jit(solution)/shard_map/ppermute | solution.py:80
  29.9 4.7 %copy.50 = bf16[256,2,32,128]{3,2,1,0:T(8,128)(2,1)} copy(bf16[256,2,32,128]{3,0,2,1:T(8,128)(2,1)S(1)} %convert_bitcast_fusion) | data formatting | bytes 8388608 | tf_op jit(solution)/shard_map/optimization_barrier | solution.py:99
  34.6 4.6 %all-to-all-start = ((bf16[256,2,32,128]{3,2,1,0:T(8,128)(2,1)}), bf16[256,2,32,128]{3,2,1,0:T(8,128)(2,1)}, u32[]{:S(2)}, u32[]{:S(2)}) async-start(bf16[256,2,32,128]{3,2,1,0:T(8,128)(2,1)} %copy.50), calls=%async_computation | async-start | bytes 8388608 | tf_op jit(solution)/shard_map/all_to_all | solution.py:100
  39.3 2.2 %copy.68 = bf16[12,8,32,256]{3,1,2,0:T(8,128)(2,1)} copy(bf16[12,8,32,256]{3,2,1,0:T(8,128)(2,1)S(1)} %bitcast.129) | data formatting | bytes 3145728
  41.5 3.2 %collective-permute-start.2 = (bf16[96,8192]{1,0:T(8,128)(2,1)}, bf16[96,8192]{1,0:T(8,128)(2,1)}, u32[]{:S(2)}, u32[]{:S(2)}) collective-permute-start(bf16[96,8192]{1,0:T(8,128)(2,1)} %bitcast.64), channel_id=1, source_target_pairs={{0,8},{8,16},{16,24},{24,0},{1,9},{9,17},{17,25},{25,1},{2,10},{10... | collective-permute-start | bytes 4718600 | tf_op jit(solution)/shard_map/ppermute | solution.py:81
  44.6 3.3 %collective-permute-start.3 = (bf16[96,8192]{1,0:T(8,128)(2,1)}, bf16[96,8192]{1,0:T(8,128)(2,1)}, u32[]{:S(2)}, u32[]{:S(2)}) collective-permute-start(bf16[96,8192]{1,0:T(8,128)(2,1)} %bitcast.64), channel_id=1, source_target_pairs={{0,16},{24,8},{1,17},{25,9},{2,18},{26,10},{3,19},{27,11},{4,20},{... | collective-permute-start | bytes 4718600 | tf_op jit(solution)/shard_map/ppermute | solution.py:81
  53.0 2.8 %copy.67 = bf16[16,8,32,256]{3,1,2,0:T(8,128)(2,1)} copy(bf16[16,8,32,256]{3,2,1,0:T(8,128)(2,1)S(1)} %bitcast.121) | data formatting | bytes 4194304
  55.7 1.9 %constant_dynamic-update-slice_fusion.3 = bf16[256,8192]{1,0:T(8,128)(2,1)} fusion(bf16[32,8192]{1,0:T(8,128)(2,1)} %collective-permute-done), kind=kLoop, calls=%fused_computation.41 | loop fusion | bytes 1048576
  57.7 30.6 %all-to-all-done = bf16[256,2,32,128]{3,2,1,0:T(8,128)(2,1)} async-done(((bf16[256,2,32,128]{3,2,1,0:T(8,128)(2,1)}), bf16[256,2,32,128]{3,2,1,0:T(8,128)(2,1)}, u32[]{:S(2)}, u32[]{:S(2)}) %all-to-all-start) | async-done | bytes 4194336 | tf_op jit(solution)/shard_map/all_to_all | solution.py:100
  88.2 3.3 %copy.51 = bf16[32,2,8,32,128]{4,3,2,1,0:T(8,128)(2,1)S(1)} copy(bf16[32,2,8,32,128]{4,3,1,0,2:T(8,128)(2,1)} %bitcast.17) | data formatting | bytes 8388608 | tf_op jit(solution)/shard_map/all_to_all | solution.py:100
  91.5 0.8 fusion.5
  92.7 2.4 %copy.55 = bf16[32,256,2,128]{1,0,3,2:T(8,128)(2,1)S(1)} copy(bf16[32,256,2,128]{1,3,0,2:T(8,128)(2,1)S(1)} %maximum_bitcast_fusion.1) | data formatting | bytes 8388608 | tf_op jit(solution)/shard_map/transpose | solution.py:53
  95.1 4.3 %copy.66 = bf16[32,8,32,256]{3,1,2,0:T(8,128)(2,1)S(1)} copy(bf16[32,8,32,256]{3,2,1,0:T(8,128)(2,1)S(1)} %bitcast.126) | data formatting | bytes 8388608
  99.4 0.8 fusion.4
  100.6 2.7 %copy.53 = bf16[32,256,2,128]{1,0,3,2:T(8,128)(2,1)S(1)} copy(bf16[32,256,2,128]{1,3,0,2:T(8,128)(2,1)S(1)} %maximum_bitcast_fusion) | data formatting | bytes 8388608 | tf_op jit(solution)/shard_map/transpose | solution.py:53
  103.3 4.3 %copy.65 = bf16[32,8,32,256]{3,1,2,0:T(8,128)(2,1)S(1)} copy(bf16[32,8,32,256]{3,2,1,0:T(8,128)(2,1)S(1)} %bitcast.127) | data formatting | bytes 8388608
  107.6 1.5 %fusion.20 = f32[128,256]{1,0:T(8,128)S(1)} fusion(bf16[128,8192]{1,0:T(8,128)(2,1)S(1)} %bitcast.128, bf16[8192,256]{0,1:T(8,128)(2,1)S(1)} %bitcast.124), kind=kOutput, calls=%fused_computation.51 | convolution fusion | flops 536870912 | bytes 6422528 | tf_op jit(solution)/shard_map/dot_general | solution.py:57
  109.2 3.7 %collective-permute-done.3 = bf16[96,8192]{1,0:T(8,128)(2,1)} collective-permute-done((bf16[96,8192]{1,0:T(8,128)(2,1)}, bf16[96,8192]{1,0:T(8,128)(2,1)}, u32[]{:S(2)}, u32[]{:S(2)}) %collective-permute-start.3) | collective-permute-done | bytes 1572896 | tf_op jit(solution)/shard_map/ppermute | solution.py:81
  112.8 1.5 %constant_dynamic-update-slice_fusion.2 = bf16[256,8192]{1,0:T(8,128)(2,1)S(1)} fusion(bf16[256,8192]{1,0:T(8,128)(2,1)S(1)} %copy-done.1, bf16[96,8192]{1,0:T(8,128)(2,1)} %collective-permute-done.2), kind=kLoop, calls=%fused_computation.40 | loop fusion | bytes 3145728
  114.4 1.5 %constant_dynamic-update-slice_fusion = bf16[256,8192]{1,0:T(8,128)(2,1)S(1)} fusion(bf16[256,8192]{1,0:T(8,128)(2,1)S(1)} %constant_dynamic-update-slice_fusion.1, bf16[96,8192]{1,0:T(8,128)(2,1)} %collective-permute-done.3), kind=kLoop, calls=%fused_computation.38 | loop fusion | bytes 3145728 | tf_op jit(solution)/shard_map/concatenate | solution.py:112
  115.9 1.3 fusion.22
  117.9 1.3 fusion.21
  119.3 1.3 collective-permute-start.5
  120.7 0.8 collective-permute-done.4
  121.6 4.8 %collective-permute-done.5 = f32[128,128]{0,1:T(8,128)S(1)} collective-permute-done((f32[128,128]{0,1:T(8,128)S(1)}, f32[128,128]{0,1:T(8,128)S(1)}, u32[]{:S(2)}, u32[]{:S(2)}) %collective-permute-start.5) | collective-permute-done | bytes 65568 | tf_op jit(solution)/shard_map/ppermute | solution.py:123
  126.4 10.6 %all_to_all.23 = f32[8,128,64]{1,2,0:T(8,128)S(1)} all-to-all(f32[8,128,64]{1,2,0:T(8,128)S(1)} %bitcast.131), channel_id=1, replica_groups=mesh['ri'=4,'ao'=8] {'ao'}, dimensions={0} | all-to-all | bytes 524288 | tf_op jit(solution)/shard_map/all_to_all | solution.py:128
  (66 shorter events, 7.3 us)
Async XLA Ops:
  0.0 11.6 %copy-start.4 = (s32[1,8]{1,0:T(1,128)S(1)}, s32[1,8]{1,0:T(1,128)}, u32[]{:S(2)}) copy-start(s32[1,8]{1,0:T(1,128)} %param.15) | copy-start | bytes 100
  0.0 11.8 %copy-start.5 = (s32[1,8]{1,0:T(1,128)S(1)}, s32[1,8]{1,0:T(1,128)}, u32[]{:S(2)}) copy-start(s32[1,8]{1,0:T(1,128)} %param.16) | copy-start | bytes 100
  0.0 12.0 %copy-start.3 = (bf16[32,256]{1,0:T(8,128)(2,1)S(1)}, bf16[32,256]{1,0:T(8,128)(2,1)}, u32[]{:S(2)}) copy-start(bf16[32,256]{1,0:T(8,128)(2,1)} %param.13) | copy-start | bytes 49156
  0.0 12.0 %copy-start.2 = (bf16[32,256]{1,0:T(8,128)(2,1)S(1)}, bf16[32,256]{1,0:T(8,128)(2,1)}, u32[]{:S(2)}) copy-start(bf16[32,256]{1,0:T(8,128)(2,1)} %param.14) | copy-start | bytes 49156
  0.0 21.3 %copy-start.6 = (s32[1,8]{1,0:T(1,128)S(1)}, s32[1,8]{1,0:T(1,128)}, u32[]{:S(2)}) copy-start(s32[1,8]{1,0:T(1,128)} %param.17) | copy-start | bytes 100
  4.1 21.2 %collective-permute-start = (bf16[32,8192]{1,0:T(8,128)(2,1)}, bf16[32,8192]{1,0:T(8,128)(2,1)}, u32[]{:S(2)}, u32[]{:S(2)}) collective-permute-start(bf16[32,8192]{1,0:T(8,128)(2,1)} %bitcast.50), channel_id=1, source_target_pairs={{0,8},{8,16},{16,24},{24,0},{1,9},{9,17},{17,25},{25,1},{2,10},{10... | collective-permute-start | bytes 1572872 | tf_op jit(solution)/shard_map/ppermute | solution.py:80
  7.1 22.8 %collective-permute-start.1 = (bf16[32,8192]{1,0:T(8,128)(2,1)}, bf16[32,8192]{1,0:T(8,128)(2,1)S(1)}, u32[]{:S(2)}, u32[]{:S(2)}) collective-permute-start(bf16[32,8192]{1,0:T(8,128)(2,1)} %bitcast.50), channel_id=1, source_target_pairs={{0,16},{24,8},{1,17},{25,9},{2,18},{26,10},{3,19},{27,11},{4,20},{... | collective-permute-start | bytes 1572872 | tf_op jit(solution)/shard_map/ppermute | solution.py:80
  34.6 53.7 %all-to-all-start = ((bf16[256,2,32,128]{3,2,1,0:T(8,128)(2,1)}), bf16[256,2,32,128]{3,2,1,0:T(8,128)(2,1)}, u32[]{:S(2)}, u32[]{:S(2)}) async-start(bf16[256,2,32,128]{3,2,1,0:T(8,128)(2,1)} %copy.50), calls=%async_computation | async-start | bytes 8388608 | tf_op jit(solution)/shard_map/all_to_all | solution.py:100
  39.1 8.9 %copy-start.10 = (s32[4]{0:T(128)S(1)}, s32[4]{0:T(128)}, u32[]{:S(2)}) copy-start(s32[4]{0:T(128)} %constant.32.clone) | copy-start | bytes 52
  39.1 10.1 %copy-start.9 = (s32[4]{0:T(128)S(1)}, s32[4]{0:T(128)}, u32[]{:S(2)}) copy-start(s32[4]{0:T(128)} %constant.33.clone) | copy-start | bytes 52
  39.2 11.4 %copy-start.8 = (s32[4]{0:T(128)S(1)}, s32[4]{0:T(128)}, u32[]{:S(2)}) copy-start(s32[4]{0:T(128)} %constant.34.clone) | copy-start | bytes 52
  39.2 12.6 %copy-start.7 = (s32[4]{0:T(128)S(1)}, s32[4]{0:T(128)}, u32[]{:S(2)}) copy-start(s32[4]{0:T(128)} %constant.35.clone) | copy-start | bytes 52
  41.5 67.7 %collective-permute-start.2 = (bf16[96,8192]{1,0:T(8,128)(2,1)}, bf16[96,8192]{1,0:T(8,128)(2,1)}, u32[]{:S(2)}, u32[]{:S(2)}) collective-permute-start(bf16[96,8192]{1,0:T(8,128)(2,1)} %bitcast.64), channel_id=1, source_target_pairs={{0,8},{8,16},{16,24},{24,0},{1,9},{9,17},{17,25},{25,1},{2,10},{10... | collective-permute-start | bytes 4718600 | tf_op jit(solution)/shard_map/ppermute | solution.py:81
  44.6 68.2 %collective-permute-start.3 = (bf16[96,8192]{1,0:T(8,128)(2,1)}, bf16[96,8192]{1,0:T(8,128)(2,1)}, u32[]{:S(2)}, u32[]{:S(2)}) collective-permute-start(bf16[96,8192]{1,0:T(8,128)(2,1)} %bitcast.64), channel_id=1, source_target_pairs={{0,16},{24,8},{1,17},{25,9},{2,18},{26,10},{3,19},{27,11},{4,20},{... | collective-permute-start | bytes 4718600 | tf_op jit(solution)/shard_map/ppermute | solution.py:81
  103.3 4.3 %copy-start = (bf16[16,8,32,256]{3,1,2,0:T(8,128)(2,1)S(1)}, bf16[16,8,32,256]{3,1,2,0:T(8,128)(2,1)}, u32[]{:S(2)}) copy-start(bf16[16,8,32,256]{3,1,2,0:T(8,128)(2,1)} %copy.67) | copy-start | bytes 6291460
  107.6 5.2 %copy-start.1 = (bf16[256,8192]{1,0:T(8,128)(2,1)S(1)}, bf16[256,8192]{1,0:T(8,128)(2,1)}, u32[]{:S(2)}) copy-start(bf16[256,8192]{1,0:T(8,128)(2,1)} %constant_dynamic-update-slice_fusion.3) | copy-start | bytes 12582916
  117.2 4.3 %collective-permute-start.4 = (f32[128,128]{0,1:T(8,128)S(1)}, f32[128,128]{0,1:T(8,128)S(1)}, u32[]{:S(2)}, u32[]{:S(2)}) collective-permute-start(f32[128,128]{0,1:T(8,128)S(1)} %get-tuple-element.28), channel_id=1, source_target_pairs={{8,0},{16,8},{24,16},{0,24},{9,1},{17,9},{25,17},{1,25},{10,2},{18... | collective-permute-start | bytes 196616 | tf_op jit(solution)/shard_map/ppermute | solution.py:123
  119.3 7.1 %collective-permute-start.5 = (f32[128,128]{0,1:T(8,128)S(1)}, f32[128,128]{0,1:T(8,128)S(1)}, u32[]{:S(2)}, u32[]{:S(2)}) collective-permute-start(f32[128,128]{0,1:T(8,128)S(1)} %get-tuple-element.27), channel_id=1, source_target_pairs={{16,0},{8,24},{17,1},{9,25},{18,2},{10,26},{19,3},{11,27},{20,4},{... | collective-permute-start | bytes 196616 | tf_op jit(solution)/shard_map/ppermute | solution.py:123

commit v12 on v11

--- a/solution.py
+++ b/solution.py
@@ -105,13 +105,27 @@
     v_weights = weight_pair(v_part)
     w_weights = weight_pair(w_part)
     diag = slab_product(own_flat, w_weights)
+    early_stack = jnp.concatenate(early)
+    early_mine = slab_product(early_stack, v_weights)
+    early_theirs = slab_product(early_stack, w_weights)
 
-    v_weights, w_weights, diag, late = lax.optimization_barrier(
-        (v_weights, w_weights, diag, late)
+    v_weights, w_weights, diag, early_mine, early_theirs, late = lax.optimization_barrier(
+        (v_weights, w_weights, diag, early_mine, early_theirs, late)
     )
-    stacked_slabs = jnp.concatenate([part for pair in zip(early, late) for part in pair])
-    mine_all = slab_product(stacked_slabs, v_weights)
-    theirs_all = slab_product(stacked_slabs, w_weights)
+    late_stack = jnp.concatenate(late)
+    late_mine = slab_product(late_stack, v_weights)
+    late_theirs = slab_product(late_stack, w_weights)
+    count = len(routes)
+    lead = rows // 4
+    rest = rows - lead
+
+    def slab_rows(early_part, late_part, index):
+        return jnp.concatenate(
+            [early_part[index * lead:(index + 1) * lead], late_part[index * rest:(index + 1) * rest]]
+        )
+
+    mine_all = jnp.concatenate([slab_rows(early_mine, late_mine, i) for i in range(count)])
+    theirs_all = jnp.concatenate([slab_rows(early_theirs, late_theirs, i) for i in range(count)])
     total = jnp.zeros((rows, planes * rows), jnp.float32)
     total = add_cols(total, diag, plane)
     for index, (route, recv_from, send_to) in enumerate(routes):

time: 138 us -> 137 us (level)
  waiting for transfers between devices: 44.4 us -> 35.1 us
  matrix products: 8.78 us -> 14.3 us
  starting transfers between devices: 20.6 us -> 22.9 us
    ppermute x2, waiting for transfers between devices: 5.64 us -> 0.01 us  [per_device(): back = lax.ppermute(theirs, 'ri', [(d, s) for s, d in route])]
    dot_general x3 -> x5, matrix products: 4.09 us -> 9.56 us  [slab_product(): out = jnp.dot(flat, weights, preferred_element_type=jnp.float32)]
    ppermute x2, waiting for transfers between devices: 3.66 us -> 0.01 us  [per_device(): lax.ppermute(own_flat[lead:], 'ri', route)]
    ppermute x2, starting transfers between devices: 1.99 us -> 3.55 us  [per_device(): back = lax.ppermute(theirs, 'ri', [(d, s) for s, d in route])]
    unnamed x30 -> x29, local copies, waits for them, and re-layouts: 18.1 us -> 17.9 us
  transfers between devices with their start and end apart: 7 -> 7, of which waited for: 5 -> 2; matrix products, arithmetic and copies ran while one was open for 26% -> 30% of each run, Pallas kernels for 0% -> 0%
where the time goes in v12:
time: 137 us
  local copies, waits for them, and re-layouts  37.8 us (28%)
  waiting for transfers between devices  35.1 us (26%)
  starting transfers between devices  22.9 us (17%)
  blocking collectives  18.7 us (14%)
  matrix products  14.3 us (10%)
  other arithmetic  4.82 us (4%)
  between operations  3.06 us (2%)
    all_to_all x1, waiting for transfers between devices, per_device(): swapped = lax.all_to_all(halves, 'ao', 0, 2, tiled=True)  31.3 us
    unnamed x29, local copies, waits for them, and re-layouts  17.9 us
    dot_general x5, matrix products, slab_product(): out = jnp.dot(flat, weights, preferred_element_type=jnp.float32)  9.56 us
    all_to_all x1, blocking collectives, per_device(): got = lax.all_to_all(sent, 'ao', 0, 0, tiled=True)  9.35 us
    all_gather x1, blocking collectives, per_device(): full = lax.all_gather(stacked, 'ao', axis=1, tiled=True)  9.32 us
    ppermute x2, starting transfers between devices, per_device(): lax.ppermute(own_flat[:lead], 'ri', route)  8.33 us
    ppermute x2, starting transfers between devices, per_device(): lax.ppermute(own_flat[lead:], 'ri', route)  6.48 us
    transpose x2, local copies, waits for them, and re-layouts, weight_pair(): both.transpose(2, 3, 0, 1).reshape(values.shape[1] * values.shape[2], -1)  4.86 us
  transfers between devices with their start and end apart: 7, of which 2 were waited for; matrix products, arithmetic and copies ran while one was open for 30% of the time, Pallas kernels for 0%

profile of v12, /device:TPU:0, one launch (start us, length us, event | category | flops | bytes accessed | tf_op | source)
XLA Modules:
  0.0 136.7 jit_solution(16196486188761319060)
XLA Ops:
  1.1 1.8 %broadcast_multiply_fusion = bf16[128,32,256]{2,1,0:T(8,128)(2,1)S(1)} fusion(bf16[128,32,256]{2,1,0:T(8,128)(2,1)} %param.11, bf16[128,256]{1,0:T(8,128)(2,1)S(1)} %copy.54), kind=kLoop, calls=%fused_computation.20 | loop fusion | flops 1048576 | bytes 4259840 | tf_op jit(solution)/shard_map/mul | solution.py:42
  3.0 1.1 copy.72
  4.1 3.0 %collective-permute-start = (bf16[32,8192]{1,0:T(8,128)(2,1)}, bf16[32,8192]{1,0:T(8,128)(2,1)S(1)}, u32[]{:S(2)}, u32[]{:S(2)}) collective-permute-start(bf16[32,8192]{1,0:T(8,128)(2,1)} %bitcast.50), channel_id=1, source_target_pairs={{0,8},{8,16},{16,24},{24,0},{1,9},{9,17},{17,25},{25,1},{2,10},{10... | collective-permute-start | bytes 1572872 | tf_op jit(solution)/shard_map/ppermute | solution.py:80
  7.1 5.3 %collective-permute-start.1 = (bf16[32,8192]{1,0:T(8,128)(2,1)}, bf16[32,8192]{1,0:T(8,128)(2,1)}, u32[]{:S(2)}, u32[]{:S(2)}) collective-permute-start(bf16[32,8192]{1,0:T(8,128)(2,1)} %bitcast.50), channel_id=1, source_target_pairs={{0,16},{24,8},{1,17},{25,9},{2,18},{26,10},{3,19},{27,11},{4,20},{... | collective-permute-start | bytes 1572872 | tf_op jit(solution)/shard_map/ppermute | solution.py:80
  12.8 9.3 %all_gather.3 = bf16[2,256,256]{2,1,0:T(8,128)(2,1)S(1)} all-gather(bf16[2,32,256]{2,1,0:T(8,128)(2,1)S(1)} %pad_maximum_fusion.2), channel_id=1, replica_groups=mesh['ri'=4,'ao'=8] {'ao'}, dimensions={1}, use_global_device_ids=true | all-gather | bytes 294912 | tf_op jit(solution)/shard_map/all_gather | solution.py:86
  22.9 3.2 %convert_bitcast_fusion = bf16[256,2,32,128]{3,0,2,1:T(8,128)(2,1)S(1)} fusion(bf16[128,32,256]{2,1,0:T(8,128)(2,1)S(1)} %broadcast_multiply_fusion, bf16[1,256,256]{1,2,0:T(8,128)(2,1)S(1)} %copy.52, bf16[1,256,256]{1,2,0:T(8,128)(2,1)S(1)} %copy.51), kind=kOutput, calls=%fused_computation.9 | convolution fusion | flops 1076363264 | bytes 6553600 | tf_op jit(solution)/shard_map/prk,dkc->cdrp/dot_general | solution.py:93
  26.1 3.8 %collective-permute-done.1 = bf16[32,8192]{1,0:T(8,128)(2,1)} collective-permute-done((bf16[32,8192]{1,0:T(8,128)(2,1)}, bf16[32,8192]{1,0:T(8,128)(2,1)}, u32[]{:S(2)}, u32[]{:S(2)}) %collective-permute-start.1) | collective-permute-done | bytes 524320 | tf_op jit(solution)/shard_map/ppermute | solution.py:80
  29.9 4.7 %copy.56 = bf16[256,2,32,128]{3,2,1,0:T(8,128)(2,1)} copy(bf16[256,2,32,128]{3,0,2,1:T(8,128)(2,1)S(1)} %convert_bitcast_fusion) | data formatting | bytes 8388608 | tf_op jit(solution)/shard_map/optimization_barrier | solution.py:99
  34.6 4.6 %all-to-all-start = ((bf16[256,2,32,128]{3,2,1,0:T(8,128)(2,1)}), bf16[256,2,32,128]{3,2,1,0:T(8,128)(2,1)}, u32[]{:S(2)}, u32[]{:S(2)}) async-start(bf16[256,2,32,128]{3,2,1,0:T(8,128)(2,1)} %copy.56), calls=%async_computation | async-start | bytes 8388608 | tf_op jit(solution)/shard_map/all_to_all | solution.py:100
  39.3 2.2 %copy.76 = bf16[12,8,32,256]{3,1,2,0:T(8,128)(2,1)} copy(bf16[12,8,32,256]{3,2,1,0:T(8,128)(2,1)S(1)} %bitcast.136) | data formatting | bytes 3145728
  41.5 3.3 %collective-permute-start.2 = (bf16[96,8192]{1,0:T(8,128)(2,1)}, bf16[96,8192]{1,0:T(8,128)(2,1)}, u32[]{:S(2)}, u32[]{:S(2)}) collective-permute-start(bf16[96,8192]{1,0:T(8,128)(2,1)} %bitcast.64), channel_id=1, source_target_pairs={{0,8},{8,16},{16,24},{24,0},{1,9},{9,17},{17,25},{25,1},{2,10},{10... | collective-permute-start | bytes 4718600 | tf_op jit(solution)/shard_map/ppermute | solution.py:81
  44.8 3.2 %collective-permute-start.3 = (bf16[96,8192]{1,0:T(8,128)(2,1)}, bf16[96,8192]{1,0:T(8,128)(2,1)}, u32[]{:S(2)}, u32[]{:S(2)}) collective-permute-start(bf16[96,8192]{1,0:T(8,128)(2,1)} %bitcast.64), channel_id=1, source_target_pairs={{0,16},{24,8},{1,17},{25,9},{2,18},{26,10},{3,19},{27,11},{4,20},{... | collective-permute-start | bytes 4718600 | tf_op jit(solution)/shard_map/ppermute | solution.py:81
  53.0 2.8 %copy.75 = bf16[16,8,32,256]{3,1,2,0:T(8,128)(2,1)} copy(bf16[16,8,32,256]{3,2,1,0:T(8,128)(2,1)S(1)} %bitcast.125) | data formatting | bytes 4194304
  55.8 1.1 constant_dynamic-update-slice_fusion
  56.9 31.3 %all-to-all-done = bf16[256,2,32,128]{3,2,1,0:T(8,128)(2,1)} async-done(((bf16[256,2,32,128]{3,2,1,0:T(8,128)(2,1)}), bf16[256,2,32,128]{3,2,1,0:T(8,128)(2,1)}, u32[]{:S(2)}, u32[]{:S(2)}) %all-to-all-start) | async-done | bytes 4194336 | tf_op jit(solution)/shard_map/all_to_all | solution.py:100
  88.3 3.3 %copy.57 = bf16[32,2,8,32,128]{4,3,2,1,0:T(8,128)(2,1)S(1)} copy(bf16[32,2,8,32,128]{4,3,1,0,2:T(8,128)(2,1)} %bitcast.17) | data formatting | bytes 8388608 | tf_op jit(solution)/shard_map/all_to_all | solution.py:100
  91.5 0.8 fusion.5
  92.7 2.4 %copy.61 = bf16[32,256,2,128]{1,0,3,2:T(8,128)(2,1)S(1)} copy(bf16[32,256,2,128]{1,3,0,2:T(8,128)(2,1)S(1)} %maximum_bitcast_fusion.1) | data formatting | bytes 8388608 | tf_op jit(solution)/shard_map/transpose | solution.py:53
  95.1 4.3 %copy.74 = bf16[32,8,32,256]{3,1,2,0:T(8,128)(2,1)S(1)} copy(bf16[32,8,32,256]{3,2,1,0:T(8,128)(2,1)S(1)} %bitcast.133) | data formatting | bytes 8388608
  100.2 1.6 %fusion.25 = f32[64,256]{1,0:T(8,128)S(1)} fusion(bf16[64,8192]{1,0:T(8,128)(2,1)S(1)} %constant_dynamic-update-slice_fusion, bf16[8192,256]{0,1:T(8,128)(2,1)S(1)} %bitcast.126), kind=kOutput, calls=%fused_computation.60 | convolution fusion | flops 268435456 | bytes 5308416 | tf_op jit(solution)/shard_map/dot_general | solution.py:57
  102.2 2.4 %copy.59 = bf16[32,256,2,128]{1,0,3,2:T(8,128)(2,1)S(1)} copy(bf16[32,256,2,128]{1,3,0,2:T(8,128)(2,1)S(1)} %maximum_bitcast_fusion) | data formatting | bytes 8388608 | tf_op jit(solution)/shard_map/transpose | solution.py:53
  104.7 4.3 %copy.73 = bf16[32,8,32,256]{3,1,2,0:T(8,128)(2,1)S(1)} copy(bf16[32,8,32,256]{3,2,1,0:T(8,128)(2,1)S(1)} %bitcast.134) | data formatting | bytes 8388608
  109.0 1.4 %fusion.24 = f32[64,256]{1,0:T(8,128)S(1)} fusion(bf16[64,8192]{1,0:T(8,128)(2,1)S(1)} %constant_dynamic-update-slice_fusion, bf16[8192,256]{0,1:T(8,128)(2,1)S(1)} %bitcast.131), kind=kOutput, calls=%fused_computation.59 | convolution fusion | flops 268435456 | bytes 5308416 | tf_op jit(solution)/shard_map/dot_general | solution.py:57
  110.4 1.7 %copy-done.1 = bf16[16,8,32,256]{3,1,2,0:T(8,128)(2,1)S(1)} copy-done((bf16[16,8,32,256]{3,1,2,0:T(8,128)(2,1)S(1)}, bf16[16,8,32,256]{3,1,2,0:T(8,128)(2,1)}, u32[]{:S(2)}) %copy-start.1) | copy-done | bytes 2097176
  112.1 1.5 %fusion.23 = f32[128,256]{1,0:T(8,128)S(1)} fusion(bf16[128,8192]{1,0:T(8,128)(2,1)S(1)} %bitcast.135, bf16[8192,256]{0,1:T(8,128)(2,1)S(1)} %bitcast.127), kind=kOutput, calls=%fused_computation.58 | convolution fusion | flops 536870912 | bytes 6422528 | tf_op jit(solution)/shard_map/dot_general | solution.py:57
  113.7 1.5 %constant_dynamic-update-slice_fusion.3 = bf16[192,8192]{1,0:T(8,128)(2,1)S(1)} fusion(bf16[96,8192]{1,0:T(8,128)(2,1)} %collective-permute-done.2), kind=kLoop, calls=%fused_computation.45 | loop fusion | bytes 3145728
  115.2 1.5 %constant_dynamic-update-slice_fusion.2 = bf16[192,8192]{1,0:T(8,128)(2,1)S(1)} fusion(bf16[192,8192]{1,0:T(8,128)(2,1)S(1)} %constant_dynamic-update-slice_fusion.3, bf16[96,8192]{1,0:T(8,128)(2,1)} %collective-permute-done.3), kind=kLoop, calls=%fused_computation.44 | loop fusion | bytes 3145728 | tf_op jit(solution)/shard_map/concatenate | solution.py:115
  116.7 1.3 fusion.27
  118.3 1.3 collective-permute-start.5
  120.4 2.3 %collective-permute-start.4 = (f32[128,128]{0,1:T(8,128)}, f32[128,128]{0,1:T(8,128)S(1)}, u32[]{:S(2)}, u32[]{:S(2)}) collective-permute-start(f32[128,128]{0,1:T(8,128)} %pad_maximum_fusion), channel_id=1, source_target_pairs={{8,0},{16,8},{24,16},{0,24},{9,1},{17,9},{25,17},{1,25},{10,2},{18... | collective-permute-start | bytes 196616 | tf_op jit(solution)/shard_map/ppermute | solution.py:137
  122.7 3.7 %fusion.26 = f32[192,256]{1,0:T(8,128)S(1)} fusion(bf16[192,8192]{1,0:T(8,128)(2,1)S(1)} %constant_dynamic-update-slice_fusion.2, bf16[8192,256]{0,1:T(8,128)(2,1)} %bitcast.132), kind=kOutput, calls=%fused_computation.61 | convolution fusion | flops 805306368 | bytes 7536640 | tf_op jit(solution)/shard_map/dot_general | solution.py:57
  126.7 9.3 %all_to_all.23 = f32[8,128,64]{1,2,0:T(8,128)S(1)} all-to-all(f32[8,128,64]{1,2,0:T(8,128)S(1)} %bitcast.137), channel_id=1, replica_groups=mesh['ri'=4,'ao'=8] {'ao'}, dimensions={0} | all-to-all | bytes 524288 | tf_op jit(solution)/shard_map/all_to_all | solution.py:142
  (77 shorter events, 8.4 us)
Async XLA Ops:
  1.1 11.3 %copy-start.4 = (s32[1,8]{1,0:T(1,128)S(1)}, s32[1,8]{1,0:T(1,128)}, u32[]{:S(2)}) copy-start(s32[1,8]{1,0:T(1,128)} %param.15) | copy-start | bytes 100
  1.1 11.5 %copy-start.5 = (s32[1,8]{1,0:T(1,128)S(1)}, s32[1,8]{1,0:T(1,128)}, u32[]{:S(2)}) copy-start(s32[1,8]{1,0:T(1,128)} %param.16) | copy-start | bytes 100
  1.1 11.6 %copy-start.2 = (bf16[32,256]{1,0:T(8,128)(2,1)S(1)}, bf16[32,256]{1,0:T(8,128)(2,1)}, u32[]{:S(2)}) copy-start(bf16[32,256]{1,0:T(8,128)(2,1)} %param.14) | copy-start | bytes 49156
  1.1 11.6 %copy-start.3 = (bf16[32,256]{1,0:T(8,128)(2,1)S(1)}, bf16[32,256]{1,0:T(8,128)(2,1)}, u32[]{:S(2)}) copy-start(bf16[32,256]{1,0:T(8,128)(2,1)} %param.13) | copy-start | bytes 49156
  1.1 21.0 %copy-start.6 = (s32[1,8]{1,0:T(1,128)S(1)}, s32[1,8]{1,0:T(1,128)}, u32[]{:S(2)}) copy-start(s32[1,8]{1,0:T(1,128)} %param.17) | copy-start | bytes 100
  4.1 22.0 %collective-permute-start = (bf16[32,8192]{1,0:T(8,128)(2,1)}, bf16[32,8192]{1,0:T(8,128)(2,1)S(1)}, u32[]{:S(2)}, u32[]{:S(2)}) collective-permute-start(bf16[32,8192]{1,0:T(8,128)(2,1)} %bitcast.50), channel_id=1, source_target_pairs={{0,8},{8,16},{16,24},{24,0},{1,9},{9,17},{17,25},{25,1},{2,10},{10... | collective-permute-start | bytes 1572872 | tf_op jit(solution)/shard_map/ppermute | solution.py:80
  7.1 22.8 %collective-permute-start.1 = (bf16[32,8192]{1,0:T(8,128)(2,1)}, bf16[32,8192]{1,0:T(8,128)(2,1)}, u32[]{:S(2)}, u32[]{:S(2)}) collective-permute-start(bf16[32,8192]{1,0:T(8,128)(2,1)} %bitcast.50), channel_id=1, source_target_pairs={{0,16},{24,8},{1,17},{25,9},{2,18},{26,10},{3,19},{27,11},{4,20},{... | collective-permute-start | bytes 1572872 | tf_op jit(solution)/shard_map/ppermute | solution.py:80
  34.6 53.7 %all-to-all-start = ((bf16[256,2,32,128]{3,2,1,0:T(8,128)(2,1)}), bf16[256,2,32,128]{3,2,1,0:T(8,128)(2,1)}, u32[]{:S(2)}, u32[]{:S(2)}) async-start(bf16[256,2,32,128]{3,2,1,0:T(8,128)(2,1)} %copy.56), calls=%async_computation | async-start | bytes 8388608 | tf_op jit(solution)/shard_map/all_to_all | solution.py:100
  39.1 8.8 %copy-start.10 = (s32[4]{0:T(128)S(1)}, s32[4]{0:T(128)}, u32[]{:S(2)}) copy-start(s32[4]{0:T(128)} %constant.32.clone) | copy-start | bytes 52
  39.1 10.1 %copy-start.9 = (s32[4]{0:T(128)S(1)}, s32[4]{0:T(128)}, u32[]{:S(2)}) copy-start(s32[4]{0:T(128)} %constant.33.clone) | copy-start | bytes 52
  39.2 11.2 %copy-start.8 = (s32[4]{0:T(128)S(1)}, s32[4]{0:T(128)}, u32[]{:S(2)}) copy-start(s32[4]{0:T(128)} %constant.34.clone) | copy-start | bytes 52
  39.2 12.6 %copy-start.7 = (s32[4]{0:T(128)S(1)}, s32[4]{0:T(128)}, u32[]{:S(2)}) copy-start(s32[4]{0:T(128)} %constant.35.clone) | copy-start | bytes 52
  41.5 72.2 %collective-permute-start.2 = (bf16[96,8192]{1,0:T(8,128)(2,1)}, bf16[96,8192]{1,0:T(8,128)(2,1)}, u32[]{:S(2)}, u32[]{:S(2)}) collective-permute-start(bf16[96,8192]{1,0:T(8,128)(2,1)} %bitcast.64), channel_id=1, source_target_pairs={{0,8},{8,16},{16,24},{24,0},{1,9},{9,17},{17,25},{25,1},{2,10},{10... | collective-permute-start | bytes 4718600 | tf_op jit(solution)/shard_map/ppermute | solution.py:81
  44.8 68.9 %collective-permute-start.3 = (bf16[96,8192]{1,0:T(8,128)(2,1)}, bf16[96,8192]{1,0:T(8,128)(2,1)}, u32[]{:S(2)}, u32[]{:S(2)}) collective-permute-start(bf16[96,8192]{1,0:T(8,128)(2,1)} %bitcast.64), channel_id=1, source_target_pairs={{0,16},{24,8},{1,17},{25,9},{2,18},{26,10},{3,19},{27,11},{4,20},{... | collective-permute-start | bytes 4718600 | tf_op jit(solution)/shard_map/ppermute | solution.py:81
  108.9 4.7 %copy-start = (bf16[32,8,32,256]{3,1,2,0:T(8,128)(2,1)}, bf16[32,8,32,256]{3,1,2,0:T(8,128)(2,1)S(1)}, u32[]{:S(2)}) copy-start(bf16[32,8,32,256]{3,1,2,0:T(8,128)(2,1)S(1)} %copy.73) | copy-start | bytes 12582916
  109.0 3.1 %copy-start.1 = (bf16[16,8,32,256]{3,1,2,0:T(8,128)(2,1)S(1)}, bf16[16,8,32,256]{3,1,2,0:T(8,128)(2,1)}, u32[]{:S(2)}) copy-start(bf16[16,8,32,256]{3,1,2,0:T(8,128)(2,1)} %copy.75) | copy-start | bytes 6291460
  118.3 8.4 %collective-permute-start.5 = (f32[128,128]{0,1:T(8,128)S(1)}, f32[128,128]{0,1:T(8,128)S(1)}, u32[]{:S(2)}, u32[]{:S(2)}) collective-permute-start(f32[128,128]{0,1:T(8,128)S(1)} %pad_maximum_fusion.1), channel_id=1, source_target_pairs={{16,0},{8,24},{17,1},{9,25},{18,2},{10,26},{19,3},{11,27},{20,4},{... | collective-permute-start | bytes 196616 | tf_op jit(solution)/shard_map/ppermute | solution.py:137
  120.4 6.2 %collective-permute-start.4 = (f32[128,128]{0,1:T(8,128)}, f32[128,128]{0,1:T(8,128)S(1)}, u32[]{:S(2)}, u32[]{:S(2)}) collective-permute-start(f32[128,128]{0,1:T(8,128)} %pad_maximum_fusion), channel_id=1, source_target_pairs={{8,0},{16,8},{24,16},{0,24},{9,1},{17,9},{25,17},{1,25},{10,2},{18... | collective-permute-start | bytes 196616 | tf_op jit(solution)/shard_map/ppermute | solution.py:137

commit v13 on v12

--- a/solution.py
+++ b/solution.py
@@ -104,10 +104,11 @@
     w_part = jnp.einsum("kl,nlq->qnk", occ_rows, virt_t, preferred_element_type=jnp.float32)
     v_weights = weight_pair(v_part)
     w_weights = weight_pair(w_part)
-    diag = slab_product(own_flat, w_weights)
     early_stack = jnp.concatenate(early)
     early_mine = slab_product(early_stack, v_weights)
-    early_theirs = slab_product(early_stack, w_weights)
+    with_own = slab_product(jnp.concatenate([own_flat, early_stack]), w_weights)
+    diag = with_own[:rows]
+    early_theirs = with_own[rows:]
 
     v_weights, w_weights, diag, early_mine, early_theirs, late = lax.optimization_barrier(
         (v_weights, w_weights, diag, early_mine, early_theirs, late)

time: 137 us -> 136 us (level)
  local copies, waits for them, and re-layouts: 37.8 us -> 34.2 us
  matrix products: 14.3 us -> 16.1 us
    unnamed x29 -> x30, local copies, waits for them, and re-layouts: 17.9 us -> 15.4 us
    dot_general x5 -> x4, matrix products: 9.56 us -> 11.1 us  [slab_product(): out = jnp.dot(flat, weights, preferred_element_type=jnp.float32)]
where the time goes in v13:
time: 136 us; the launch traced here: 135 us
  waiting for transfers between devices  36.1 us (27%)
  local copies, waits for them, and re-layouts  34.2 us (25%)
  starting transfers between devices  23.1 us (17%)
  blocking collectives  18.7 us (14%)
  matrix products  16.1 us (12%)
  other arithmetic  4.18 us (3%)
  between operations  2.99 us (2%)
    all_to_all x1, waiting for transfers between devices, per_device(): swapped = lax.all_to_all(halves, 'ao', 0, 2, tiled=True)  32.6 us
    unnamed x30, local copies, waits for them, and re-layouts  15.4 us
    dot_general x4, matrix products, slab_product(): out = jnp.dot(flat, weights, preferred_element_type=jnp.float32)  11.1 us
    all_to_all x1, blocking collectives, per_device(): got = lax.all_to_all(sent, 'ao', 0, 0, tiled=True)  9.35 us
    all_gather x1, blocking collectives, per_device(): full = lax.all_gather(stacked, 'ao', axis=1, tiled=True)  9.32 us
    ppermute x2, starting transfers between devices, per_device(): lax.ppermute(own_flat[:lead], 'ri', route)  8.36 us
    ppermute x2, starting transfers between devices, per_device(): lax.ppermute(own_flat[lead:], 'ri', route)  6.59 us
    transpose x2, local copies, waits for them, and re-layouts, weight_pair(): both.transpose(2, 3, 0, 1).reshape(values.shape[1] * values.shape[2], -1)  4.86 us
  transfers between devices with their start and end apart: 7, of which 2 were waited for; matrix products, arithmetic and copies ran while one was open for 30% of the time, Pallas kernels for 0%

profile of v13, /device:TPU:0, one launch (start us, length us, event | category | flops | bytes accessed | tf_op | source)
XLA Modules:
  0.0 135.3 jit_solution(7689708857152782875)
XLA Ops:
  0.0 0.7 convert_element_type.32
  1.1 1.8 %broadcast_multiply_fusion = bf16[128,32,256]{2,1,0:T(8,128)(2,1)S(1)} fusion(bf16[128,32,256]{2,1,0:T(8,128)(2,1)} %param.11, bf16[128,256]{1,0:T(8,128)(2,1)S(1)} %copy.54), kind=kLoop, calls=%fused_computation.30 | loop fusion | flops 1048576 | bytes 4259840 | tf_op jit(solution)/shard_map/mul | solution.py:42
  3.3 3.1 %collective-permute-start = (bf16[32,8192]{1,0:T(8,128)(2,1)S(1)}, bf16[32,8192]{1,0:T(8,128)(2,1)}, u32[]{:S(2)}, u32[]{:S(2)}) collective-permute-start(bf16[32,8192]{1,0:T(8,128)(2,1)S(1)} %bitcast.140), channel_id=1, source_target_pairs={{0,8},{8,16},{16,24},{24,0},{1,9},{9,17},{17,25},{25,1},{2,10},{10... | collective-permute-start | bytes 1572872 | tf_op jit(solution)/shard_map/ppermute | solution.py:80
  6.3 5.3 %collective-permute-start.1 = (bf16[32,8192]{1,0:T(8,128)(2,1)S(1)}, bf16[32,8192]{1,0:T(8,128)(2,1)}, u32[]{:S(2)}, u32[]{:S(2)}) collective-permute-start(bf16[32,8192]{1,0:T(8,128)(2,1)S(1)} %bitcast.141), channel_id=1, source_target_pairs={{0,16},{24,8},{1,17},{25,9},{2,18},{26,10},{3,19},{27,11},{4,20},{... | collective-permute-start | bytes 1572872 | tf_op jit(solution)/shard_map/ppermute | solution.py:80
  12.0 9.3 %all_gather.3 = bf16[2,256,256]{2,1,0:T(8,128)(2,1)S(1)} all-gather(bf16[2,32,256]{2,1,0:T(8,128)(2,1)S(1)} %pad_maximum_fusion.2), channel_id=1, replica_groups=mesh['ri'=4,'ao'=8] {'ao'}, dimensions={1}, use_global_device_ids=true | all-gather | bytes 294912 | tf_op jit(solution)/shard_map/all_gather | solution.py:86
  22.1 3.2 %convert_bitcast_fusion = bf16[256,2,32,128]{3,0,2,1:T(8,128)(2,1)S(1)} fusion(bf16[128,32,256]{2,1,0:T(8,128)(2,1)S(1)} %broadcast_multiply_fusion, bf16[1,256,256]{1,2,0:T(8,128)(2,1)S(1)} %copy.52, bf16[1,256,256]{1,2,0:T(8,128)(2,1)S(1)} %copy.51), kind=kOutput, calls=%fused_computation.9 | convolution fusion | flops 1076363264 | bytes 6553600 | tf_op jit(solution)/shard_map/prk,dkc->cdrp/dot_general | solution.py:93
  25.3 3.5 %collective-permute-done.1 = bf16[32,8192]{1,0:T(8,128)(2,1)} collective-permute-done((bf16[32,8192]{1,0:T(8,128)(2,1)S(1)}, bf16[32,8192]{1,0:T(8,128)(2,1)}, u32[]{:S(2)}, u32[]{:S(2)}) %collective-permute-start.1) | collective-permute-done | bytes 524320 | tf_op jit(solution)/shard_map/ppermute | solution.py:80
  28.8 4.7 %copy.56 = bf16[256,2,32,128]{3,2,1,0:T(8,128)(2,1)} copy(bf16[256,2,32,128]{3,0,2,1:T(8,128)(2,1)S(1)} %convert_bitcast_fusion) | data formatting | bytes 8388608 | tf_op jit(solution)/shard_map/optimization_barrier | solution.py:99
  33.5 4.6 %all-to-all-start = ((bf16[256,2,32,128]{3,2,1,0:T(8,128)(2,1)}), bf16[256,2,32,128]{3,2,1,0:T(8,128)(2,1)}, u32[]{:S(2)}, u32[]{:S(2)}) async-start(bf16[256,2,32,128]{3,2,1,0:T(8,128)(2,1)} %copy.56), calls=%async_computation | async-start | bytes 8388608 | tf_op jit(solution)/shard_map/all_to_all | solution.py:100
  38.3 2.2 %copy.76 = bf16[12,8,32,256]{3,1,2,0:T(8,128)(2,1)} copy(bf16[12,8,32,256]{3,2,1,0:T(8,128)(2,1)S(1)} %bitcast.128) | data formatting | bytes 3145728
  40.4 3.4 %collective-permute-start.2 = (bf16[96,8192]{1,0:T(8,128)(2,1)}, bf16[96,8192]{1,0:T(8,128)(2,1)}, u32[]{:S(2)}, u32[]{:S(2)}) collective-permute-start(bf16[96,8192]{1,0:T(8,128)(2,1)} %bitcast.64), channel_id=1, source_target_pairs={{0,8},{8,16},{16,24},{24,0},{1,9},{9,17},{17,25},{25,1},{2,10},{10... | collective-permute-start | bytes 4718600 | tf_op jit(solution)/shard_map/ppermute | solution.py:81
  43.8 3.2 %collective-permute-start.3 = (bf16[96,8192]{1,0:T(8,128)(2,1)}, bf16[96,8192]{1,0:T(8,128)(2,1)}, u32[]{:S(2)}, u32[]{:S(2)}) collective-permute-start(bf16[96,8192]{1,0:T(8,128)(2,1)} %bitcast.64), channel_id=1, source_target_pairs={{0,16},{24,8},{1,17},{25,9},{2,18},{26,10},{3,19},{27,11},{4,20},{... | collective-permute-start | bytes 4718600 | tf_op jit(solution)/shard_map/ppermute | solution.py:81
  48.3 0.6 dynamic_slice.26
  51.9 2.8 %copy.75 = bf16[16,8,32,256]{3,1,2,0:T(8,128)(2,1)} copy(bf16[16,8,32,256]{3,2,1,0:T(8,128)(2,1)S(1)} %bitcast.121) | data formatting | bytes 4194304
  54.7 32.6 %all-to-all-done = bf16[256,2,32,128]{3,2,1,0:T(8,128)(2,1)} async-done(((bf16[256,2,32,128]{3,2,1,0:T(8,128)(2,1)}), bf16[256,2,32,128]{3,2,1,0:T(8,128)(2,1)}, u32[]{:S(2)}, u32[]{:S(2)}) %all-to-all-start) | async-done | bytes 4194336 | tf_op jit(solution)/shard_map/all_to_all | solution.py:100
  87.2 3.3 %copy.57 = bf16[32,2,8,32,128]{4,3,2,1,0:T(8,128)(2,1)S(1)} copy(bf16[32,2,8,32,128]{4,3,1,0,2:T(8,128)(2,1)} %bitcast.17) | data formatting | bytes 8388608 | tf_op jit(solution)/shard_map/all_to_all | solution.py:100
  90.5 0.8 fusion.11
  91.7 2.4 %copy.61 = bf16[32,256,2,128]{1,0,3,2:T(8,128)(2,1)S(1)} copy(bf16[32,256,2,128]{1,3,0,2:T(8,128)(2,1)S(1)} %maximum_bitcast_fusion.1) | data formatting | bytes 8388608 | tf_op jit(solution)/shard_map/transpose | solution.py:53
  94.1 4.3 %copy.74 = bf16[32,8,32,256]{3,1,2,0:T(8,128)(2,1)S(1)} copy(bf16[32,8,32,256]{3,2,1,0:T(8,128)(2,1)S(1)} %bitcast.126) | data formatting | bytes 8388608
  98.5 2.7 %fusion.2 = f32[192,256]{1,0:T(8,128)S(1)} fusion(bf16[8192,256]{0,1:T(8,128)(2,1)S(1)} %bitcast.129, bf16[32,8192]{1,0:T(8,128)(2,1)} %collective-permute-done.1, bf16[32,8192]{1,0:T(8,128)(2,1)} %collective-permute-done, bf16[128,8192]{1,0:T(8,128)(2,1)S(1)} %bitcast.132), kind=kOutput, calls=%fused_computation.10 | convolution fusion | flops 814743552 | bytes 7536640 | tf_op jit(solution)/shard_map/dot_general | solution.py:57
  101.2 1.0 fusion.10
  102.7 2.4 %copy.59 = bf16[32,256,2,128]{1,0,3,2:T(8,128)(2,1)S(1)} copy(bf16[32,256,2,128]{1,3,0,2:T(8,128)(2,1)S(1)} %maximum_bitcast_fusion) | data formatting | bytes 8388608 | tf_op jit(solution)/shard_map/transpose | solution.py:53
  105.1 4.3 %copy.73 = bf16[32,8,32,256]{3,1,2,0:T(8,128)(2,1)S(1)} copy(bf16[32,8,32,256]{3,2,1,0:T(8,128)(2,1)S(1)} %bitcast.127) | data formatting | bytes 8388608
  109.4 3.4 %fusion.16 = f32[64,256]{1,0:T(8,128)S(1)} fusion(bf16[8192,256]{0,1:T(8,128)(2,1)S(1)} %bitcast.124, bf16[32,8192]{1,0:T(8,128)(2,1)} %collective-permute-done.1, bf16[32,8192]{1,0:T(8,128)(2,1)} %collective-permute-done), kind=kOutput, calls=%fused_computation.26 | convolution fusion | flops 270532608 | bytes 5308416 | tf_op jit(solution)/shard_map/dot_general | solution.py:57
  112.8 1.5 %constant_dynamic-update-slice_fusion.1 = bf16[192,8192]{1,0:T(8,128)(2,1)S(1)} fusion(bf16[96,8192]{1,0:T(8,128)(2,1)} %collective-permute-done.2), kind=kLoop, calls=%fused_computation.53 | loop fusion | bytes 3145728
  114.3 1.5 %constant_dynamic-update-slice_fusion = bf16[192,8192]{1,0:T(8,128)(2,1)S(1)} fusion(bf16[192,8192]{1,0:T(8,128)(2,1)S(1)} %constant_dynamic-update-slice_fusion.1, bf16[96,8192]{1,0:T(8,128)(2,1)} %collective-permute-done.3), kind=kLoop, calls=%fused_computation.52 | loop fusion | bytes 3145728 | tf_op jit(solution)/shard_map/concatenate | solution.py:116
  115.9 1.3 fusion.36
  117.5 1.3 collective-permute-start.5
  119.0 2.3 %collective-permute-start.4 = (f32[128,128]{0,1:T(8,128)S(1)}, f32[128,128]{0,1:T(8,128)S(1)}, u32[]{:S(2)}, u32[]{:S(2)}) collective-permute-start(f32[128,128]{0,1:T(8,128)S(1)} %pad_maximum_fusion), channel_id=1, source_target_pairs={{8,0},{16,8},{24,16},{0,24},{9,1},{17,9},{25,17},{1,25},{10,2},{18... | collective-permute-start | bytes 196616 | tf_op jit(solution)/shard_map/ppermute | solution.py:138
  121.3 3.7 %fusion.35 = f32[192,256]{1,0:T(8,128)S(1)} fusion(bf16[192,8192]{1,0:T(8,128)(2,1)S(1)} %constant_dynamic-update-slice_fusion, bf16[8192,256]{0,1:T(8,128)(2,1)} %bitcast.125), kind=kOutput, calls=%fused_computation.67 | convolution fusion | flops 805306368 | bytes 7536640 | tf_op jit(solution)/shard_map/dot_general | solution.py:57
  125.4 9.3 %all_to_all.23 = f32[8,128,64]{1,2,0:T(8,128)S(1)} all-to-all(f32[8,128,64]{1,2,0:T(8,128)S(1)} %bitcast.131), channel_id=1, replica_groups=mesh['ri'=4,'ao'=8] {'ao'}, dimensions={0} | all-to-all | bytes 524288 | tf_op jit(solution)/shard_map/all_to_all | solution.py:143
  134.7 0.6 reduce_sum.9
  (79 shorter events, 5.3 us)
Async XLA Ops:
  1.1 10.5 %copy-start.5 = (s32[1,8]{1,0:T(1,128)S(1)}, s32[1,8]{1,0:T(1,128)}, u32[]{:S(2)}) copy-start(s32[1,8]{1,0:T(1,128)} %param.15) | copy-start | bytes 100
  1.1 10.7 %copy-start.6 = (s32[1,8]{1,0:T(1,128)S(1)}, s32[1,8]{1,0:T(1,128)}, u32[]{:S(2)}) copy-start(s32[1,8]{1,0:T(1,128)} %param.16) | copy-start | bytes 100
  1.1 10.9 %copy-start.3 = (bf16[32,256]{1,0:T(8,128)(2,1)S(1)}, bf16[32,256]{1,0:T(8,128)(2,1)}, u32[]{:S(2)}) copy-start(bf16[32,256]{1,0:T(8,128)(2,1)} %param.14) | copy-start | bytes 49156
  1.1 10.8 %copy-start.4 = (bf16[32,256]{1,0:T(8,128)(2,1)S(1)}, bf16[32,256]{1,0:T(8,128)(2,1)}, u32[]{:S(2)}) copy-start(bf16[32,256]{1,0:T(8,128)(2,1)} %param.13) | copy-start | bytes 49156
  1.1 20.2 %copy-start.7 = (s32[1,8]{1,0:T(1,128)S(1)}, s32[1,8]{1,0:T(1,128)}, u32[]{:S(2)}) copy-start(s32[1,8]{1,0:T(1,128)} %param.17) | copy-start | bytes 100
  3.3 22.0 %collective-permute-start = (bf16[32,8192]{1,0:T(8,128)(2,1)S(1)}, bf16[32,8192]{1,0:T(8,128)(2,1)}, u32[]{:S(2)}, u32[]{:S(2)}) collective-permute-start(bf16[32,8192]{1,0:T(8,128)(2,1)S(1)} %bitcast.140), channel_id=1, source_target_pairs={{0,8},{8,16},{16,24},{24,0},{1,9},{9,17},{17,25},{25,1},{2,10},{10... | collective-permute-start | bytes 1572872 | tf_op jit(solution)/shard_map/ppermute | solution.py:80
  6.3 22.5 %collective-permute-start.1 = (bf16[32,8192]{1,0:T(8,128)(2,1)S(1)}, bf16[32,8192]{1,0:T(8,128)(2,1)}, u32[]{:S(2)}, u32[]{:S(2)}) collective-permute-start(bf16[32,8192]{1,0:T(8,128)(2,1)S(1)} %bitcast.141), channel_id=1, source_target_pairs={{0,16},{24,8},{1,17},{25,9},{2,18},{26,10},{3,19},{27,11},{4,20},{... | collective-permute-start | bytes 1572872 | tf_op jit(solution)/shard_map/ppermute | solution.py:80
  33.5 53.7 %all-to-all-start = ((bf16[256,2,32,128]{3,2,1,0:T(8,128)(2,1)}), bf16[256,2,32,128]{3,2,1,0:T(8,128)(2,1)}, u32[]{:S(2)}, u32[]{:S(2)}) async-start(bf16[256,2,32,128]{3,2,1,0:T(8,128)(2,1)} %copy.56), calls=%async_computation | async-start | bytes 8388608 | tf_op jit(solution)/shard_map/all_to_all | solution.py:100
  38.1 8.9 %copy-start.11 = (s32[4]{0:T(128)S(1)}, s32[4]{0:T(128)}, u32[]{:S(2)}) copy-start(s32[4]{0:T(128)} %constant.32.clone) | copy-start | bytes 52
  38.1 10.2 %copy-start.10 = (s32[4]{0:T(128)S(1)}, s32[4]{0:T(128)}, u32[]{:S(2)}) copy-start(s32[4]{0:T(128)} %constant.33.clone) | copy-start | bytes 52
  38.1 11.4 %copy-start.9 = (s32[4]{0:T(128)S(1)}, s32[4]{0:T(128)}, u32[]{:S(2)}) copy-start(s32[4]{0:T(128)} %constant.34.clone) | copy-start | bytes 52
  38.1 12.6 %copy-start.8 = (s32[4]{0:T(128)S(1)}, s32[4]{0:T(128)}, u32[]{:S(2)}) copy-start(s32[4]{0:T(128)} %constant.35.clone) | copy-start | bytes 52
  40.4 72.3 %collective-permute-start.2 = (bf16[96,8192]{1,0:T(8,128)(2,1)}, bf16[96,8192]{1,0:T(8,128)(2,1)}, u32[]{:S(2)}, u32[]{:S(2)}) collective-permute-start(bf16[96,8192]{1,0:T(8,128)(2,1)} %bitcast.64), channel_id=1, source_target_pairs={{0,8},{8,16},{16,24},{24,0},{1,9},{9,17},{17,25},{25,1},{2,10},{10... | collective-permute-start | bytes 4718600 | tf_op jit(solution)/shard_map/ppermute | solution.py:81
  43.8 69.0 %collective-permute-start.3 = (bf16[96,8192]{1,0:T(8,128)(2,1)}, bf16[96,8192]{1,0:T(8,128)(2,1)}, u32[]{:S(2)}, u32[]{:S(2)}) collective-permute-start(bf16[96,8192]{1,0:T(8,128)(2,1)} %bitcast.64), channel_id=1, source_target_pairs={{0,16},{24,8},{1,17},{25,9},{2,18},{26,10},{3,19},{27,11},{4,20},{... | collective-permute-start | bytes 4718600 | tf_op jit(solution)/shard_map/ppermute | solution.py:81
  94.1 4.3 %copy-start.1 = (bf16[16,8,32,256]{3,1,2,0:T(8,128)(2,1)S(1)}, bf16[16,8,32,256]{3,1,2,0:T(8,128)(2,1)}, u32[]{:S(2)}) copy-start(bf16[16,8,32,256]{3,1,2,0:T(8,128)(2,1)} %copy.75) | copy-start | bytes 6291460
  101.2 1.0 copy-start.2
  109.4 4.9 %copy-start = (bf16[32,8,32,256]{3,1,2,0:T(8,128)(2,1)}, bf16[32,8,32,256]{3,1,2,0:T(8,128)(2,1)S(1)}, u32[]{:S(2)}) copy-start(bf16[32,8,32,256]{3,1,2,0:T(8,128)(2,1)S(1)} %copy.73) | copy-start | bytes 12582916
  115.8 1.4 %slice-start.1 = ((f32[192,128]{1,0:T(8,128)}), f32[64,128]{1,0:T(8,128)S(1)}, s32[]{:S(2)}) async-start(f32[192,128]{1,0:T(8,128)} %copy-done.2), calls=%async_computation.3 | async-start | bytes 65536 | tf_op jit(solution)/shard_map/slice | solution.py:111
  117.5 7.8 %collective-permute-start.5 = (f32[128,128]{0,1:T(8,128)S(1)}, f32[128,128]{0,1:T(8,128)S(1)}, u32[]{:S(2)}, u32[]{:S(2)}) collective-permute-start(f32[128,128]{0,1:T(8,128)S(1)} %pad_maximum_fusion.1), channel_id=1, source_target_pairs={{16,0},{8,24},{17,1},{9,25},{18,2},{10,26},{19,3},{11,27},{20,4},{... | collective-permute-start | bytes 196616 | tf_op jit(solution)/shard_map/ppermute | solution.py:138
  119.0 6.1 %slice-start = ((f32[192,128]{1,0:T(8,128)}), f32[128,128]{1,0:T(8,128)S(1)}, s32[]{:S(2)}) async-start(f32[192,128]{1,0:T(8,128)} %copy-done.2), calls=%async_computation.2 | async-start | bytes 131072 | tf_op jit(solution)/shard_map/slice | solution.py:110
  119.0 6.3 %collective-permute-start.4 = (f32[128,128]{0,1:T(8,128)S(1)}, f32[128,128]{0,1:T(8,128)S(1)}, u32[]{:S(2)}, u32[]{:S(2)}) collective-permute-start(f32[128,128]{0,1:T(8,128)S(1)} %pad_maximum_fusion), channel_id=1, source_target_pairs={{8,0},{16,8},{24,16},{0,24},{9,1},{17,9},{25,17},{1,25},{10,2},{18... | collective-permute-start | bytes 196616 | tf_op jit(solution)/shard_map/ppermute | solution.py:138

commit v14 on v13

--- a/solution.py
+++ b/solution.py
@@ -78,7 +78,7 @@
     own_flat = own.reshape(rows, -1)
     lead = rows // 4
     early = [lax.ppermute(own_flat[:lead], "ri", route) for route, _, _ in routes]
-    late = [lax.ppermute(own_flat[lead:], "ri", route) for route, _, _ in routes]
+    late_source = own_flat[lead:]
 
     stacked = jnp.stack(
         [screen_density(occ_density, occ_mask), screen_density(virt_density, virt_mask)]
@@ -96,7 +96,8 @@
         jnp.stack([occ_rows, virt_rows]),
         preferred_element_type=jnp.float32,
     ).astype(jnp.bfloat16)
-    halves, early = lax.optimization_barrier((halves, early))
+    halves, early, late_source = lax.optimization_barrier((halves, early, late_source))
+    late = [lax.ppermute(late_source, "ri", route) for route, _, _ in routes]
     swapped = lax.all_to_all(halves, "ao", 0, 2, tiled=True)
     occ_t = swapped[:, 0]
     virt_t = swapped[:, 1]

time: 136 us -> 140 us (1.029)
  waiting for transfers between devices: 36.1 us -> 40.3 us
  starting transfers between devices: 23.1 us -> 20.6 us
    all_to_all x1, waiting for transfers between devices: 32.6 us -> 37.3 us  [per_device(): swapped = lax.all_to_all(halves, 'ao', 0, 2, tiled=True)]
    ppermute x2, waiting for transfers between devices: 3.49 us -> 0.01 us  [per_device(): lax.ppermute(own_flat[:lead], 'ri', route)]
    ppermute x2, waiting for transfers between devices: 0.01 us -> 3.04 us  [per_device(): late = [lax.ppermute(late_source, 'ri', route) for route, _, _ in routes]]
    ppermute x2, starting transfers between devices: 6.59 us -> 4.3 us  [per_device(): late = [lax.ppermute(late_source, 'ri', route) for route, _, _ in routes]]
    concatenate x1, local copies, waits for them, and re-layouts: 1.51 us -> 0.11 us  [per_device(): late_stack = jnp.concatenate(late)]
    unnamed x30 -> x32, local copies, waits for them, and re-layouts: 15.4 us -> 15.8 us
  transfers between devices with their start and end apart: 7 -> 7, of which waited for: 2 -> 2; matrix products, arithmetic and copies ran while one was open for 30% -> 32% of each run, Pallas kernels for 0% -> 0%
where the time goes in v14:
time: 140 us; the launch traced here: 139 us
  waiting for transfers between devices  40.3 us (29%)
  local copies, waits for them, and re-layouts  34.6 us (25%)
  starting transfers between devices  20.6 us (15%)
  blocking collectives  19.9 us (14%)
  matrix products  16.7 us (12%)
  other arithmetic  4.16 us (3%)
  between operations  2.93 us (2%)
    all_to_all x1, waiting for transfers between devices, per_device(): swapped = lax.all_to_all(halves, 'ao', 0, 2, tiled=True)  37.3 us
    unnamed x32, local copies, waits for them, and re-layouts  15.8 us
    dot_general x4, matrix products, slab_product(): out = jnp.dot(flat, weights, preferred_element_type=jnp.float32)  12.1 us
    all_to_all x1, blocking collectives, per_device(): got = lax.all_to_all(sent, 'ao', 0, 0, tiled=True)  10.6 us
    all_gather x1, blocking collectives, per_device(): full = lax.all_gather(stacked, 'ao', axis=1, tiled=True)  9.32 us
    ppermute x2, starting transfers between devices, per_device(): lax.ppermute(own_flat[:lead], 'ri', route)  8.39 us
    transpose x2, local copies, waits for them, and re-layouts, weight_pair(): both.transpose(2, 3, 0, 1).reshape(values.shape[1] * values.shape[2], -1)  5.08 us
    all_to_all x1, starting transfers between devices, per_device(): swapped = lax.all_to_all(halves, 'ao', 0, 2, tiled=True)  4.72 us
  transfers between devices with their start and end apart: 7, of which 2 were waited for; matrix products, arithmetic and copies ran while one was open for 32% of the time, Pallas kernels for 0%

profile of v14, /device:TPU:0, one launch (start us, length us, event | category | flops | bytes accessed | tf_op | source)
XLA Modules:
  0.0 139.3 jit_solution(8879152093955182784)
XLA Ops:
  0.0 0.7 convert_element_type.32
  1.1 1.8 %broadcast_multiply_fusion = bf16[128,32,256]{2,1,0:T(8,128)(2,1)S(1)} fusion(bf16[128,32,256]{2,1,0:T(8,128)(2,1)} %param.11, bf16[128,256]{1,0:T(8,128)(2,1)S(1)} %copy.54), kind=kLoop, calls=%fused_computation.30 | loop fusion | flops 1048576 | bytes 4259840 | tf_op jit(solution)/shard_map/mul | solution.py:42
  3.2 3.1 %collective-permute-start = (bf16[32,8192]{1,0:T(8,128)(2,1)S(1)}, bf16[32,8192]{1,0:T(8,128)(2,1)}, u32[]{:S(2)}, u32[]{:S(2)}) collective-permute-start(bf16[32,8192]{1,0:T(8,128)(2,1)S(1)} %bitcast.142), channel_id=1, source_target_pairs={{0,8},{8,16},{16,24},{24,0},{1,9},{9,17},{17,25},{25,1},{2,10},{10... | collective-permute-start | bytes 1572872 | tf_op jit(solution)/shard_map/ppermute | solution.py:80
  6.3 5.3 %collective-permute-start.1 = (bf16[32,8192]{1,0:T(8,128)(2,1)S(1)}, bf16[32,8192]{1,0:T(8,128)(2,1)}, u32[]{:S(2)}, u32[]{:S(2)}) collective-permute-start(bf16[32,8192]{1,0:T(8,128)(2,1)S(1)} %bitcast.143), channel_id=1, source_target_pairs={{0,16},{24,8},{1,17},{25,9},{2,18},{26,10},{3,19},{27,11},{4,20},{... | collective-permute-start | bytes 1572872 | tf_op jit(solution)/shard_map/ppermute | solution.py:80
  11.6 1.3 slice.110
  13.3 9.3 %all_gather.3 = bf16[2,256,256]{2,1,0:T(8,128)(2,1)S(1)} all-gather(bf16[2,32,256]{2,1,0:T(8,128)(2,1)S(1)} %pad_maximum_fusion.2), channel_id=1, replica_groups=mesh['ri'=4,'ao'=8] {'ao'}, dimensions={1}, use_global_device_ids=true | all-gather | bytes 294912 | tf_op jit(solution)/shard_map/all_gather | solution.py:86
  23.5 3.6 %copy.73 = bf16[12,8,32,256]{3,1,2,0:T(8,128)(2,1)} copy(bf16[12,8,32,256]{3,2,1,0:T(8,128)(2,1)} %bitcast.128) | data formatting | bytes 3145728
  27.0 3.1 %convert_bitcast_fusion = bf16[256,2,32,128]{3,0,2,1:T(8,128)(2,1)S(1)} fusion(bf16[128,32,256]{2,1,0:T(8,128)(2,1)S(1)} %broadcast_multiply_fusion, bf16[1,256,256]{1,2,0:T(8,128)(2,1)S(1)} %copy.52, bf16[1,256,256]{1,2,0:T(8,128)(2,1)S(1)} %copy.51), kind=kOutput, calls=%fused_computation.9 | convolution fusion | flops 1076363264 | bytes 6553600 | tf_op jit(solution)/shard_map/prk,dkc->cdrp/dot_general | solution.py:93
  30.2 4.7 %copy.56 = bf16[256,2,32,128]{3,2,1,0:T(8,128)(2,1)} copy(bf16[256,2,32,128]{3,0,2,1:T(8,128)(2,1)S(1)} %convert_bitcast_fusion) | data formatting | bytes 8388608 | tf_op jit(solution)/shard_map/optimization_barrier | solution.py:99
  35.0 4.7 %all-to-all-start = ((bf16[256,2,32,128]{3,2,1,0:T(8,128)(2,1)}), bf16[256,2,32,128]{3,2,1,0:T(8,128)(2,1)}, u32[]{:S(2)}, u32[]{:S(2)}) async-start(bf16[256,2,32,128]{3,2,1,0:T(8,128)(2,1)} %copy.56), calls=%async_computation | async-start | bytes 8388608 | tf_op jit(solution)/shard_map/all_to_all | solution.py:101
  39.7 0.6 dynamic_slice.24
  42.1 0.6 dynamic_slice.28
  44.4 2.8 %copy.76 = bf16[16,8,32,256]{3,1,2,0:T(8,128)(2,1)} copy(bf16[16,8,32,256]{3,2,1,0:T(8,128)(2,1)S(1)} %bitcast.121) | data formatting | bytes 4194304
  47.2 2.0 %collective-permute-start.2 = (bf16[96,8192]{1,0:T(8,128)(2,1)}, bf16[96,8192]{1,0:T(8,128)(2,1)S(1)}, u32[]{:S(2)}, u32[]{:S(2)}) collective-permute-start(bf16[96,8192]{1,0:T(8,128)(2,1)} %bitcast.134), channel_id=1, source_target_pairs={{0,8},{8,16},{16,24},{24,0},{1,9},{9,17},{17,25},{25,1},{2,10},{10... | collective-permute-start | bytes 4718600 | tf_op jit(solution)/shard_map/ppermute | solution.py:100
  49.2 2.3 %collective-permute-start.3 = (bf16[96,8192]{1,0:T(8,128)(2,1)}, bf16[96,8192]{1,0:T(8,128)(2,1)S(1)}, u32[]{:S(2)}, u32[]{:S(2)}) collective-permute-start(bf16[96,8192]{1,0:T(8,128)(2,1)} %bitcast.135), channel_id=1, source_target_pairs={{0,16},{24,8},{1,17},{25,9},{2,18},{26,10},{3,19},{27,11},{4,20},{... | collective-permute-start | bytes 4718600 | tf_op jit(solution)/shard_map/ppermute | solution.py:100
  51.6 37.3 %all-to-all-done = bf16[256,2,32,128]{3,2,1,0:T(8,128)(2,1)} async-done(((bf16[256,2,32,128]{3,2,1,0:T(8,128)(2,1)}), bf16[256,2,32,128]{3,2,1,0:T(8,128)(2,1)}, u32[]{:S(2)}, u32[]{:S(2)}) %all-to-all-start) | async-done | bytes 4194336 | tf_op jit(solution)/shard_map/all_to_all | solution.py:101
  88.8 3.3 %copy.57 = bf16[32,2,8,32,128]{4,3,2,1,0:T(8,128)(2,1)S(1)} copy(bf16[32,2,8,32,128]{4,3,1,0,2:T(8,128)(2,1)} %bitcast.17) | data formatting | bytes 8388608 | tf_op jit(solution)/shard_map/all_to_all | solution.py:101
  92.1 0.8 fusion.11
  93.3 2.4 %copy.61 = bf16[32,256,2,128]{1,0,3,2:T(8,128)(2,1)S(1)} copy(bf16[32,256,2,128]{1,3,0,2:T(8,128)(2,1)S(1)} %maximum_bitcast_fusion.1) | data formatting | bytes 8388608 | tf_op jit(solution)/shard_map/transpose | solution.py:53
  95.7 4.3 %copy.75 = bf16[32,8,32,256]{3,1,2,0:T(8,128)(2,1)S(1)} copy(bf16[32,8,32,256]{3,2,1,0:T(8,128)(2,1)S(1)} %bitcast.126) | data formatting | bytes 8388608
  100.0 2.7 %fusion.2 = f32[192,256]{1,0:T(8,128)S(1)} fusion(bf16[8192,256]{0,1:T(8,128)(2,1)S(1)} %bitcast.129, bf16[32,8192]{1,0:T(8,128)(2,1)} %collective-permute-done.1, bf16[32,8192]{1,0:T(8,128)(2,1)} %collective-permute-done, bf16[128,8192]{1,0:T(8,128)(2,1)S(1)} %bitcast.132), kind=kOutput, calls=%fused_computation.10 | convolution fusion | flops 814743552 | bytes 7536640 | tf_op jit(solution)/shard_map/dot_general | solution.py:57
  102.8 0.8 fusion.10
  104.0 2.6 %copy.59 = bf16[32,256,2,128]{1,0,3,2:T(8,128)(2,1)S(1)} copy(bf16[32,256,2,128]{1,3,0,2:T(8,128)(2,1)S(1)} %maximum_bitcast_fusion) | data formatting | bytes 8388608 | tf_op jit(solution)/shard_map/transpose | solution.py:53
  106.7 4.3 %copy.74 = bf16[32,8,32,256]{3,1,2,0:T(8,128)(2,1)S(1)} copy(bf16[32,8,32,256]{3,2,1,0:T(8,128)(2,1)S(1)} %bitcast.127) | data formatting | bytes 8388608
  111.0 3.4 %fusion.16 = f32[64,256]{1,0:T(8,128)S(1)} fusion(bf16[8192,256]{0,1:T(8,128)(2,1)S(1)} %bitcast.124, bf16[32,8192]{1,0:T(8,128)(2,1)} %collective-permute-done.1, bf16[32,8192]{1,0:T(8,128)(2,1)} %collective-permute-done), kind=kOutput, calls=%fused_computation.26 | convolution fusion | flops 270532608 | bytes 5308416 | tf_op jit(solution)/shard_map/dot_general | solution.py:57
  114.4 3.0 %collective-permute-done.3 = bf16[96,8192]{1,0:T(8,128)(2,1)S(1)} collective-permute-done((bf16[96,8192]{1,0:T(8,128)(2,1)}, bf16[96,8192]{1,0:T(8,128)(2,1)S(1)}, u32[]{:S(2)}, u32[]{:S(2)}) %collective-permute-start.3) | collective-permute-done | bytes 1572896 | tf_op jit(solution)/shard_map/ppermute | solution.py:100
  117.7 1.3 fusion.36
  119.6 1.3 collective-permute-start.5
  121.1 1.9 %collective-permute-start.4 = (f32[128,128]{0,1:T(8,128)S(1)}, f32[128,128]{0,1:T(8,128)S(1)}, u32[]{:S(2)}, u32[]{:S(2)}) collective-permute-start(f32[128,128]{0,1:T(8,128)S(1)} %pad_maximum_fusion), channel_id=1, source_target_pairs={{8,0},{16,8},{24,16},{0,24},{9,1},{17,9},{25,17},{1,25},{10,2},{18... | collective-permute-start | bytes 196616 | tf_op jit(solution)/shard_map/ppermute | solution.py:139
  123.0 4.7 %fusion.35 = f32[192,256]{1,0:T(8,128)S(1)} fusion(bf16[192,8192]{1,0:T(8,128)(2,1)} %copy-done.2, bf16[8192,256]{0,1:T(8,128)(2,1)} %bitcast.125), kind=kOutput, calls=%fused_computation.67 | convolution fusion | flops 805306368 | bytes 7536640 | tf_op jit(solution)/shard_map/dot_general | solution.py:57
  128.1 10.6 %all_to_all.23 = f32[8,128,64]{1,2,0:T(8,128)S(1)} all-to-all(f32[8,128,64]{1,2,0:T(8,128)S(1)} %bitcast.131), channel_id=1, replica_groups=mesh['ri'=4,'ao'=8] {'ao'}, dimensions={0} | all-to-all | bytes 524288 | tf_op jit(solution)/shard_map/all_to_all | solution.py:144
  138.7 0.6 reduce_sum.9
  (81 shorter events, 5.2 us)
Async XLA Ops:
  2.8 10.1 %copy-start.6 = (s32[1,8]{1,0:T(1,128)S(1)}, s32[1,8]{1,0:T(1,128)}, u32[]{:S(2)}) copy-start(s32[1,8]{1,0:T(1,128)} %param.15) | copy-start | bytes 100
  2.9 10.3 %copy-start.7 = (s32[1,8]{1,0:T(1,128)S(1)}, s32[1,8]{1,0:T(1,128)}, u32[]{:S(2)}) copy-start(s32[1,8]{1,0:T(1,128)} %param.16) | copy-start | bytes 100
  2.9 10.4 %copy-start.4 = (bf16[32,256]{1,0:T(8,128)(2,1)S(1)}, bf16[32,256]{1,0:T(8,128)(2,1)}, u32[]{:S(2)}) copy-start(bf16[32,256]{1,0:T(8,128)(2,1)} %param.14) | copy-start | bytes 49156
  2.9 10.4 %copy-start.5 = (bf16[32,256]{1,0:T(8,128)(2,1)S(1)}, bf16[32,256]{1,0:T(8,128)(2,1)}, u32[]{:S(2)}) copy-start(bf16[32,256]{1,0:T(8,128)(2,1)} %param.13) | copy-start | bytes 49156
  2.9 19.8 %copy-start.8 = (s32[1,8]{1,0:T(1,128)S(1)}, s32[1,8]{1,0:T(1,128)}, u32[]{:S(2)}) copy-start(s32[1,8]{1,0:T(1,128)} %param.17) | copy-start | bytes 100
  3.2 27.0 %collective-permute-start = (bf16[32,8192]{1,0:T(8,128)(2,1)S(1)}, bf16[32,8192]{1,0:T(8,128)(2,1)}, u32[]{:S(2)}, u32[]{:S(2)}) collective-permute-start(bf16[32,8192]{1,0:T(8,128)(2,1)S(1)} %bitcast.142), channel_id=1, source_target_pairs={{0,8},{8,16},{16,24},{24,0},{1,9},{9,17},{17,25},{25,1},{2,10},{10... | collective-permute-start | bytes 1572872 | tf_op jit(solution)/shard_map/ppermute | solution.py:80
  6.3 23.9 %collective-permute-start.1 = (bf16[32,8192]{1,0:T(8,128)(2,1)S(1)}, bf16[32,8192]{1,0:T(8,128)(2,1)}, u32[]{:S(2)}, u32[]{:S(2)}) collective-permute-start(bf16[32,8192]{1,0:T(8,128)(2,1)S(1)} %bitcast.143), channel_id=1, source_target_pairs={{0,16},{24,8},{1,17},{25,9},{2,18},{26,10},{3,19},{27,11},{4,20},{... | collective-permute-start | bytes 1572872 | tf_op jit(solution)/shard_map/ppermute | solution.py:80
  35.0 4.7 %copy-start.12 = (s32[4]{0:T(128)S(1)}, s32[4]{0:T(128)}, u32[]{:S(2)}) copy-start(s32[4]{0:T(128)} %constant.32.clone) | copy-start | bytes 52
  35.0 6.0 %copy-start.11 = (s32[4]{0:T(128)S(1)}, s32[4]{0:T(128)}, u32[]{:S(2)}) copy-start(s32[4]{0:T(128)} %constant.33.clone) | copy-start | bytes 52
  35.0 7.2 %copy-start.10 = (s32[4]{0:T(128)S(1)}, s32[4]{0:T(128)}, u32[]{:S(2)}) copy-start(s32[4]{0:T(128)} %constant.34.clone) | copy-start | bytes 52
  35.0 8.3 %copy-start.9 = (s32[4]{0:T(128)S(1)}, s32[4]{0:T(128)}, u32[]{:S(2)}) copy-start(s32[4]{0:T(128)} %constant.35.clone) | copy-start | bytes 52
  35.0 53.9 %all-to-all-start = ((bf16[256,2,32,128]{3,2,1,0:T(8,128)(2,1)}), bf16[256,2,32,128]{3,2,1,0:T(8,128)(2,1)}, u32[]{:S(2)}, u32[]{:S(2)}) async-start(bf16[256,2,32,128]{3,2,1,0:T(8,128)(2,1)} %copy.56), calls=%async_computation | async-start | bytes 8388608 | tf_op jit(solution)/shard_map/all_to_all | solution.py:101
  47.2 67.1 %collective-permute-start.2 = (bf16[96,8192]{1,0:T(8,128)(2,1)}, bf16[96,8192]{1,0:T(8,128)(2,1)S(1)}, u32[]{:S(2)}, u32[]{:S(2)}) collective-permute-start(bf16[96,8192]{1,0:T(8,128)(2,1)} %bitcast.134), channel_id=1, source_target_pairs={{0,8},{8,16},{16,24},{24,0},{1,9},{9,17},{17,25},{25,1},{2,10},{10... | collective-permute-start | bytes 4718600 | tf_op jit(solution)/shard_map/ppermute | solution.py:100
  49.2 68.2 %collective-permute-start.3 = (bf16[96,8192]{1,0:T(8,128)(2,1)}, bf16[96,8192]{1,0:T(8,128)(2,1)S(1)}, u32[]{:S(2)}, u32[]{:S(2)}) collective-permute-start(bf16[96,8192]{1,0:T(8,128)(2,1)} %bitcast.135), channel_id=1, source_target_pairs={{0,16},{24,8},{1,17},{25,9},{2,18},{26,10},{3,19},{27,11},{4,20},{... | collective-permute-start | bytes 4718600 | tf_op jit(solution)/shard_map/ppermute | solution.py:100
  95.7 4.3 %copy-start.1 = (bf16[16,8,32,256]{3,1,2,0:T(8,128)(2,1)S(1)}, bf16[16,8,32,256]{3,1,2,0:T(8,128)(2,1)}, u32[]{:S(2)}) copy-start(bf16[16,8,32,256]{3,1,2,0:T(8,128)(2,1)} %copy.76) | copy-start | bytes 6291460
  102.8 0.8 copy-start.3
  110.9 6.6 %copy-start = (bf16[32,8,32,256]{3,1,2,0:T(8,128)(2,1)}, bf16[32,8,32,256]{3,1,2,0:T(8,128)(2,1)S(1)}, u32[]{:S(2)}) copy-start(bf16[32,8,32,256]{3,1,2,0:T(8,128)(2,1)S(1)} %copy.74) | copy-start | bytes 12582916
  117.6 1.7 %copy-start.2 = (bf16[192,8192]{1,0:T(8,128)(2,1)}, bf16[192,8192]{1,0:T(8,128)(2,1)S(1)}, u32[]{:S(2)}) copy-start(bf16[192,8192]{1,0:T(8,128)(2,1)S(1)} %constant_dynamic-update-slice_fusion) | copy-start | bytes 9437188
  117.6 1.8 %slice-start.1 = ((f32[192,128]{1,0:T(8,128)}), f32[64,128]{1,0:T(8,128)S(1)}, s32[]{:S(2)}) async-start(f32[192,128]{1,0:T(8,128)} %copy-done.3), calls=%async_computation.3 | async-start | bytes 65536 | tf_op jit(solution)/shard_map/slice | solution.py:112
  119.6 8.4 %collective-permute-start.5 = (f32[128,128]{0,1:T(8,128)S(1)}, f32[128,128]{0,1:T(8,128)S(1)}, u32[]{:S(2)}, u32[]{:S(2)}) collective-permute-start(f32[128,128]{0,1:T(8,128)S(1)} %pad_maximum_fusion.1), channel_id=1, source_target_pairs={{16,0},{8,24},{17,1},{9,25},{18,2},{10,26},{19,3},{11,27},{20,4},{... | collective-permute-start | bytes 196616 | tf_op jit(solution)/shard_map/ppermute | solution.py:139
  121.1 6.7 %slice-start = ((f32[192,128]{1,0:T(8,128)}), f32[128,128]{1,0:T(8,128)S(1)}, s32[]{:S(2)}) async-start(f32[192,128]{1,0:T(8,128)} %copy-done.3), calls=%async_computation.2 | async-start | bytes 131072 | tf_op jit(solution)/shard_map/slice | solution.py:111
  121.1 6.8 %collective-permute-start.4 = (f32[128,128]{0,1:T(8,128)S(1)}, f32[128,128]{0,1:T(8,128)S(1)}, u32[]{:S(2)}, u32[]{:S(2)}) collective-permute-start(f32[128,128]{0,1:T(8,128)S(1)} %pad_maximum_fusion), channel_id=1, source_target_pairs={{8,0},{16,8},{24,16},{0,24},{9,1},{17,9},{25,17},{1,25},{10,2},{18... | collective-permute-start | bytes 196616 | tf_op jit(solution)/shard_map/ppermute | solution.py:139

commit v15 on v13

--- a/solution.py
+++ b/solution.py
@@ -129,14 +129,18 @@
     theirs_all = jnp.concatenate([slab_rows(early_theirs, late_theirs, i) for i in range(count)])
     total = jnp.zeros((rows, planes * rows), jnp.float32)
     total = add_cols(total, diag, plane)
+    total_t = jnp.zeros((planes * rows, rows), jnp.float32)
     for index, (route, recv_from, send_to) in enumerate(routes):
         source = jnp.array(recv_from, jnp.int32)[plane]
         target = jnp.array(send_to, jnp.int32)[plane]
         mine = mine_all[index * rows:(index + 1) * rows]
         theirs = theirs_all[index * rows:(index + 1) * rows]
-        total = add_cols(total, mine.T, source)
+        at = (source * rows, jnp.int32(0))
+        here = lax.dynamic_slice(total_t, at, mine.shape)
+        total_t = lax.dynamic_update_slice(total_t, here + mine, at)
         back = lax.ppermute(theirs, "ri", [(d, s) for s, d in route])
         total = add_cols(total, back, target)
+    total = total + total_t.T
 
     width = total.shape[1] // cycle_size
     sent = total.reshape(rows, cycle_size, width).transpose(1, 0, 2)

time: 136 us -> 140 us (1.029)
  waiting for transfers between devices: 36.1 us -> 39.8 us
    ppermute x2, waiting for transfers between devices: 0.01 us -> 3.86 us  [per_device(): back = lax.ppermute(theirs, 'ri', [(d, s) for s, d in route])]
  transfers between devices with their start and end apart: 7 -> 7, of which waited for: 2 -> 3; matrix products, arithmetic and copies ran while one was open for 30% -> 27% of each run, Pallas kernels for 0% -> 0%
where the time goes in v15:
time: 140 us; the launch traced here: 139 us
  waiting for transfers between devices  39.8 us (28%)
  local copies, waits for them, and re-layouts  34.3 us (24%)
  starting transfers between devices  23.1 us (16%)
  blocking collectives  18.7 us (13%)
  matrix products  16.1 us (12%)
  other arithmetic  4.21 us (3%)
  between operations  3.09 us (2%)
    all_to_all x1, waiting for transfers between devices, per_device(): swapped = lax.all_to_all(halves, 'ao', 0, 2, tiled=True)  32.5 us
    unnamed x30, local copies, waits for them, and re-layouts  15.4 us
    dot_general x4, matrix products, slab_product(): out = jnp.dot(flat, weights, preferred_element_type=jnp.float32)  11.2 us
    all_to_all x1, blocking collectives, per_device(): got = lax.all_to_all(sent, 'ao', 0, 0, tiled=True)  9.35 us
    all_gather x1, blocking collectives, per_device(): full = lax.all_gather(stacked, 'ao', axis=1, tiled=True)  9.32 us
    ppermute x2, starting transfers between devices, per_device(): lax.ppermute(own_flat[:lead], 'ri', route)  8.36 us
    ppermute x2, starting transfers between devices, per_device(): lax.ppermute(own_flat[lead:], 'ri', route)  6.59 us
    transpose x2, local copies, waits for them, and re-layouts, weight_pair(): both.transpose(2, 3, 0, 1).reshape(values.shape[1] * values.shape[2], -1)  4.86 us
  transfers between devices with their start and end apart: 7, of which 3 were waited for; matrix products, arithmetic and copies ran while one was open for 27% of the time, Pallas kernels for 0%

profile of v15, /device:TPU:0, one launch (start us, length us, event | category | flops | bytes accessed | tf_op | source)
XLA Modules:
  0.0 139.3 jit_solution(4190327677884002617)
XLA Ops:
  0.0 0.7 convert_element_type.32
  1.1 1.8 %broadcast_multiply_fusion = bf16[128,32,256]{2,1,0:T(8,128)(2,1)S(1)} fusion(bf16[128,32,256]{2,1,0:T(8,128)(2,1)} %param.11, bf16[128,256]{1,0:T(8,128)(2,1)S(1)} %copy.53), kind=kLoop, calls=%fused_computation.30 | loop fusion | flops 1048576 | bytes 4259840 | tf_op jit(solution)/shard_map/mul | solution.py:42
  3.3 3.1 %collective-permute-start = (bf16[32,8192]{1,0:T(8,128)(2,1)S(1)}, bf16[32,8192]{1,0:T(8,128)(2,1)}, u32[]{:S(2)}, u32[]{:S(2)}) collective-permute-start(bf16[32,8192]{1,0:T(8,128)(2,1)S(1)} %bitcast.130), channel_id=1, source_target_pairs={{0,8},{8,16},{16,24},{24,0},{1,9},{9,17},{17,25},{25,1},{2,10},{10... | collective-permute-start | bytes 1572872 | tf_op jit(solution)/shard_map/ppermute | solution.py:80
  6.3 5.3 %collective-permute-start.1 = (bf16[32,8192]{1,0:T(8,128)(2,1)S(1)}, bf16[32,8192]{1,0:T(8,128)(2,1)}, u32[]{:S(2)}, u32[]{:S(2)}) collective-permute-start(bf16[32,8192]{1,0:T(8,128)(2,1)S(1)} %bitcast.131), channel_id=1, source_target_pairs={{0,16},{24,8},{1,17},{25,9},{2,18},{26,10},{3,19},{27,11},{4,20},{... | collective-permute-start | bytes 1572872 | tf_op jit(solution)/shard_map/ppermute | solution.py:80
  12.0 9.3 %all_gather.3 = bf16[2,256,256]{2,1,0:T(8,128)(2,1)S(1)} all-gather(bf16[2,32,256]{2,1,0:T(8,128)(2,1)S(1)} %pad_maximum_fusion.2), channel_id=1, replica_groups=mesh['ri'=4,'ao'=8] {'ao'}, dimensions={1}, use_global_device_ids=true | all-gather | bytes 294912 | tf_op jit(solution)/shard_map/all_gather | solution.py:86
  22.1 3.2 %convert_bitcast_fusion = bf16[256,2,32,128]{3,0,2,1:T(8,128)(2,1)S(1)} fusion(bf16[128,32,256]{2,1,0:T(8,128)(2,1)S(1)} %broadcast_multiply_fusion, bf16[1,256,256]{1,2,0:T(8,128)(2,1)S(1)} %copy.51, bf16[1,256,256]{1,2,0:T(8,128)(2,1)S(1)} %copy.50), kind=kOutput, calls=%fused_computation.9 | convolution fusion | flops 1076363264 | bytes 6553600 | tf_op jit(solution)/shard_map/prk,dkc->cdrp/dot_general | solution.py:93
  25.3 3.5 %collective-permute-done.1 = bf16[32,8192]{1,0:T(8,128)(2,1)} collective-permute-done((bf16[32,8192]{1,0:T(8,128)(2,1)S(1)}, bf16[32,8192]{1,0:T(8,128)(2,1)}, u32[]{:S(2)}, u32[]{:S(2)}) %collective-permute-start.1) | collective-permute-done | bytes 524320 | tf_op jit(solution)/shard_map/ppermute | solution.py:80
  28.8 4.7 %copy.55 = bf16[256,2,32,128]{3,2,1,0:T(8,128)(2,1)} copy(bf16[256,2,32,128]{3,0,2,1:T(8,128)(2,1)S(1)} %convert_bitcast_fusion) | data formatting | bytes 8388608 | tf_op jit(solution)/shard_map/optimization_barrier | solution.py:99
  33.5 4.6 %all-to-all-start = ((bf16[256,2,32,128]{3,2,1,0:T(8,128)(2,1)}), bf16[256,2,32,128]{3,2,1,0:T(8,128)(2,1)}, u32[]{:S(2)}, u32[]{:S(2)}) async-start(bf16[256,2,32,128]{3,2,1,0:T(8,128)(2,1)} %copy.55), calls=%async_computation | async-start | bytes 8388608 | tf_op jit(solution)/shard_map/all_to_all | solution.py:100
  38.3 2.2 %copy.75 = bf16[12,8,32,256]{3,1,2,0:T(8,128)(2,1)} copy(bf16[12,8,32,256]{3,2,1,0:T(8,128)(2,1)S(1)} %bitcast.118) | data formatting | bytes 3145728
  40.4 3.4 %collective-permute-start.2 = (bf16[96,8192]{1,0:T(8,128)(2,1)}, bf16[96,8192]{1,0:T(8,128)(2,1)}, u32[]{:S(2)}, u32[]{:S(2)}) collective-permute-start(bf16[96,8192]{1,0:T(8,128)(2,1)} %bitcast.63), channel_id=1, source_target_pairs={{0,8},{8,16},{16,24},{24,0},{1,9},{9,17},{17,25},{25,1},{2,10},{10... | collective-permute-start | bytes 4718600 | tf_op jit(solution)/shard_map/ppermute | solution.py:81
  43.8 3.2 %collective-permute-start.3 = (bf16[96,8192]{1,0:T(8,128)(2,1)}, bf16[96,8192]{1,0:T(8,128)(2,1)}, u32[]{:S(2)}, u32[]{:S(2)}) collective-permute-start(bf16[96,8192]{1,0:T(8,128)(2,1)} %bitcast.63), channel_id=1, source_target_pairs={{0,16},{24,8},{1,17},{25,9},{2,18},{26,10},{3,19},{27,11},{4,20},{... | collective-permute-start | bytes 4718600 | tf_op jit(solution)/shard_map/ppermute | solution.py:81
  52.0 2.8 %copy.74 = bf16[16,8,32,256]{3,1,2,0:T(8,128)(2,1)} copy(bf16[16,8,32,256]{3,2,1,0:T(8,128)(2,1)S(1)} %bitcast.111) | data formatting | bytes 4194304
  54.7 32.5 %all-to-all-done = bf16[256,2,32,128]{3,2,1,0:T(8,128)(2,1)} async-done(((bf16[256,2,32,128]{3,2,1,0:T(8,128)(2,1)}), bf16[256,2,32,128]{3,2,1,0:T(8,128)(2,1)}, u32[]{:S(2)}, u32[]{:S(2)}) %all-to-all-start) | async-done | bytes 4194336 | tf_op jit(solution)/shard_map/all_to_all | solution.py:100
  87.2 3.3 %copy.56 = bf16[32,2,8,32,128]{4,3,2,1,0:T(8,128)(2,1)S(1)} copy(bf16[32,2,8,32,128]{4,3,1,0,2:T(8,128)(2,1)} %bitcast.17) | data formatting | bytes 8388608 | tf_op jit(solution)/shard_map/all_to_all | solution.py:100
  90.5 0.8 fusion.11
  91.7 2.4 %copy.60 = bf16[32,256,2,128]{1,0,3,2:T(8,128)(2,1)S(1)} copy(bf16[32,256,2,128]{1,3,0,2:T(8,128)(2,1)S(1)} %maximum_bitcast_fusion.1) | data formatting | bytes 8388608 | tf_op jit(solution)/shard_map/transpose | solution.py:53
  94.1 4.3 %copy.73 = bf16[32,8,32,256]{3,1,2,0:T(8,128)(2,1)S(1)} copy(bf16[32,8,32,256]{3,2,1,0:T(8,128)(2,1)S(1)} %bitcast.116) | data formatting | bytes 8388608
  98.5 3.5 %fusion.2 = f32[192,256]{1,0:T(8,128)S(1)} fusion(bf16[8192,256]{0,1:T(8,128)(2,1)S(1)} %bitcast.119, bf16[32,8192]{1,0:T(8,128)(2,1)} %collective-permute-done.1, bf16[32,8192]{1,0:T(8,128)(2,1)} %collective-permute-done, bf16[128,8192]{1,0:T(8,128)(2,1)S(1)} %bitcast.121), kind=kOutput, calls=%fused_computation.10 | convolution fusion | flops 814743552 | bytes 7536640 | tf_op jit(solution)/shard_map/dot_general | solution.py:57
  102.1 1.0 fusion.10
  103.5 2.4 %copy.58 = bf16[32,256,2,128]{1,0,3,2:T(8,128)(2,1)S(1)} copy(bf16[32,256,2,128]{1,3,0,2:T(8,128)(2,1)S(1)} %maximum_bitcast_fusion) | data formatting | bytes 8388608 | tf_op jit(solution)/shard_map/transpose | solution.py:53
  105.9 4.3 %copy.72 = bf16[32,8,32,256]{3,1,2,0:T(8,128)(2,1)S(1)} copy(bf16[32,8,32,256]{3,2,1,0:T(8,128)(2,1)S(1)} %bitcast.117) | data formatting | bytes 8388608
  110.2 2.6 %fusion.16 = f32[64,256]{1,0:T(8,128)S(1)} fusion(bf16[8192,256]{0,1:T(8,128)(2,1)S(1)} %bitcast.114, bf16[32,8192]{1,0:T(8,128)(2,1)} %collective-permute-done.1, bf16[32,8192]{1,0:T(8,128)(2,1)} %collective-permute-done), kind=kOutput, calls=%fused_computation.26 | convolution fusion | flops 270532608 | bytes 5308416 | tf_op jit(solution)/shard_map/dot_general | solution.py:57
  112.8 1.5 %constant_dynamic-update-slice_fusion.1 = bf16[192,8192]{1,0:T(8,128)(2,1)S(1)} fusion(bf16[96,8192]{1,0:T(8,128)(2,1)} %collective-permute-done.2), kind=kLoop, calls=%fused_computation.51 | loop fusion | bytes 3145728
  114.3 1.5 %constant_dynamic-update-slice_fusion = bf16[192,8192]{1,0:T(8,128)(2,1)S(1)} fusion(bf16[192,8192]{1,0:T(8,128)(2,1)S(1)} %constant_dynamic-update-slice_fusion.1, bf16[96,8192]{1,0:T(8,128)(2,1)} %collective-permute-done.3), kind=kLoop, calls=%fused_computation.50 | loop fusion | bytes 3145728 | tf_op jit(solution)/shard_map/concatenate | solution.py:116
  115.9 1.3 fusion.33
  117.5 3.8 %fusion.32 = f32[192,256]{1,0:T(8,128)S(1)} fusion(bf16[192,8192]{1,0:T(8,128)(2,1)S(1)} %constant_dynamic-update-slice_fusion, bf16[8192,256]{0,1:T(8,128)(2,1)} %bitcast.120), kind=kOutput, calls=%fused_computation.65 | convolution fusion | flops 805306368 | bytes 7536640 | tf_op jit(solution)/shard_map/dot_general | solution.py:57
  121.3 1.3 collective-permute-start.5
  122.7 2.3 %collective-permute-start.4 = (f32[128,128]{1,0:T(8,128)S(1)}, f32[128,128]{1,0:T(8,128)S(1)}, u32[]{:S(2)}, u32[]{:S(2)}) collective-permute-start(f32[128,128]{1,0:T(8,128)S(1)} %pad_maximum_fusion), channel_id=1, source_target_pairs={{8,0},{16,8},{24,16},{0,24},{9,1},{17,9},{25,17},{1,25},{10,2},{18... | collective-permute-start | bytes 196616 | tf_op jit(solution)/shard_map/ppermute | solution.py:141
  125.3 3.9 %collective-permute-done.4 = f32[128,128]{1,0:T(8,128)S(1)} collective-permute-done((f32[128,128]{1,0:T(8,128)S(1)}, f32[128,128]{1,0:T(8,128)S(1)}, u32[]{:S(2)}, u32[]{:S(2)}) %collective-permute-start.4) | collective-permute-done | bytes 65568 | tf_op jit(solution)/shard_map/ppermute | solution.py:141
  129.3 9.3 %all_to_all.23 = f32[8,128,64]{1,2,0:T(8,128)S(1)} all-to-all(f32[8,128,64]{1,2,0:T(8,128)S(1)} %bitcast.129), channel_id=1, replica_groups=mesh['ri'=4,'ao'=8] {'ao'}, dimensions={0} | all-to-all | bytes 524288 | tf_op jit(solution)/shard_map/all_to_all | solution.py:147
  138.7 0.6 reduce_sum.9
  (81 shorter events, 6.0 us)
Async XLA Ops:
  1.1 10.5 %copy-start.5 = (s32[1,8]{1,0:T(1,128)S(1)}, s32[1,8]{1,0:T(1,128)}, u32[]{:S(2)}) copy-start(s32[1,8]{1,0:T(1,128)} %param.15) | copy-start | bytes 100
  1.1 10.7 %copy-start.6 = (s32[1,8]{1,0:T(1,128)S(1)}, s32[1,8]{1,0:T(1,128)}, u32[]{:S(2)}) copy-start(s32[1,8]{1,0:T(1,128)} %param.16) | copy-start | bytes 100
  1.1 10.9 %copy-start.3 = (bf16[32,256]{1,0:T(8,128)(2,1)S(1)}, bf16[32,256]{1,0:T(8,128)(2,1)}, u32[]{:S(2)}) copy-start(bf16[32,256]{1,0:T(8,128)(2,1)} %param.14) | copy-start | bytes 49156
  1.1 10.8 %copy-start.4 = (bf16[32,256]{1,0:T(8,128)(2,1)S(1)}, bf16[32,256]{1,0:T(8,128)(2,1)}, u32[]{:S(2)}) copy-start(bf16[32,256]{1,0:T(8,128)(2,1)} %param.13) | copy-start | bytes 49156
  1.1 20.2 %copy-start.7 = (s32[1,8]{1,0:T(1,128)S(1)}, s32[1,8]{1,0:T(1,128)}, u32[]{:S(2)}) copy-start(s32[1,8]{1,0:T(1,128)} %param.17) | copy-start | bytes 100
  3.3 22.0 %collective-permute-start = (bf16[32,8192]{1,0:T(8,128)(2,1)S(1)}, bf16[32,8192]{1,0:T(8,128)(2,1)}, u32[]{:S(2)}, u32[]{:S(2)}) collective-permute-start(bf16[32,8192]{1,0:T(8,128)(2,1)S(1)} %bitcast.130), channel_id=1, source_target_pairs={{0,8},{8,16},{16,24},{24,0},{1,9},{9,17},{17,25},{25,1},{2,10},{10... | collective-permute-start | bytes 1572872 | tf_op jit(solution)/shard_map/ppermute | solution.py:80
  6.3 22.5 %collective-permute-start.1 = (bf16[32,8192]{1,0:T(8,128)(2,1)S(1)}, bf16[32,8192]{1,0:T(8,128)(2,1)}, u32[]{:S(2)}, u32[]{:S(2)}) collective-permute-start(bf16[32,8192]{1,0:T(8,128)(2,1)S(1)} %bitcast.131), channel_id=1, source_target_pairs={{0,16},{24,8},{1,17},{25,9},{2,18},{26,10},{3,19},{27,11},{4,20},{... | collective-permute-start | bytes 1572872 | tf_op jit(solution)/shard_map/ppermute | solution.py:80
  33.5 53.7 %all-to-all-start = ((bf16[256,2,32,128]{3,2,1,0:T(8,128)(2,1)}), bf16[256,2,32,128]{3,2,1,0:T(8,128)(2,1)}, u32[]{:S(2)}, u32[]{:S(2)}) async-start(bf16[256,2,32,128]{3,2,1,0:T(8,128)(2,1)} %copy.55), calls=%async_computation | async-start | bytes 8388608 | tf_op jit(solution)/shard_map/all_to_all | solution.py:100
  38.1 8.9 %copy-start.11 = (s32[4]{0:T(128)S(1)}, s32[4]{0:T(128)}, u32[]{:S(2)}) copy-start(s32[4]{0:T(128)} %constant.33.clone) | copy-start | bytes 52
  38.1 10.2 %copy-start.10 = (s32[4]{0:T(128)S(1)}, s32[4]{0:T(128)}, u32[]{:S(2)}) copy-start(s32[4]{0:T(128)} %constant.35.clone) | copy-start | bytes 52
  38.1 11.4 %copy-start.9 = (s32[4]{0:T(128)S(1)}, s32[4]{0:T(128)}, u32[]{:S(2)}) copy-start(s32[4]{0:T(128)} %constant.34.clone) | copy-start | bytes 52
  38.1 12.7 %copy-start.8 = (s32[4]{0:T(128)S(1)}, s32[4]{0:T(128)}, u32[]{:S(2)}) copy-start(s32[4]{0:T(128)} %constant.36.clone) | copy-start | bytes 52
  40.4 72.4 %collective-permute-start.2 = (bf16[96,8192]{1,0:T(8,128)(2,1)}, bf16[96,8192]{1,0:T(8,128)(2,1)}, u32[]{:S(2)}, u32[]{:S(2)}) collective-permute-start(bf16[96,8192]{1,0:T(8,128)(2,1)} %bitcast.63), channel_id=1, source_target_pairs={{0,8},{8,16},{16,24},{24,0},{1,9},{9,17},{17,25},{25,1},{2,10},{10... | collective-permute-start | bytes 4718600 | tf_op jit(solution)/shard_map/ppermute | solution.py:81
  43.8 69.0 %collective-permute-start.3 = (bf16[96,8192]{1,0:T(8,128)(2,1)}, bf16[96,8192]{1,0:T(8,128)(2,1)}, u32[]{:S(2)}, u32[]{:S(2)}) collective-permute-start(bf16[96,8192]{1,0:T(8,128)(2,1)} %bitcast.63), channel_id=1, source_target_pairs={{0,16},{24,8},{1,17},{25,9},{2,18},{26,10},{3,19},{27,11},{4,20},{... | collective-permute-start | bytes 4718600 | tf_op jit(solution)/shard_map/ppermute | solution.py:81
  94.1 4.3 %copy-start.1 = (bf16[16,8,32,256]{3,1,2,0:T(8,128)(2,1)S(1)}, bf16[16,8,32,256]{3,1,2,0:T(8,128)(2,1)}, u32[]{:S(2)}) copy-start(bf16[16,8,32,256]{3,1,2,0:T(8,128)(2,1)} %copy.74) | copy-start | bytes 6291460
  98.4 3.6 %copy-start = (bf16[32,8,32,256]{3,1,2,0:T(8,128)(2,1)}, bf16[32,8,32,256]{3,1,2,0:T(8,128)(2,1)S(1)}, u32[]{:S(2)}) copy-start(bf16[32,8,32,256]{3,1,2,0:T(8,128)(2,1)S(1)} %copy.73) | copy-start | bytes 12582916
  102.0 1.0 copy-start.2
  117.5 3.8 %slice-start.1 = ((f32[192,128]{1,0:T(8,128)}), f32[64,128]{1,0:T(8,128)S(1)}, s32[]{:S(2)}) async-start(f32[192,128]{1,0:T(8,128)} %copy-done.2), calls=%async_computation.3 | async-start | bytes 65536 | tf_op jit(solution)/shard_map/slice | solution.py:111
  117.5 7.5 %slice-start = ((f32[192,128]{1,0:T(8,128)}), f32[128,128]{1,0:T(8,128)S(1)}, s32[]{:S(2)}) async-start(f32[192,128]{1,0:T(8,128)} %copy-done.2), calls=%async_computation.2 | async-start | bytes 131072 | tf_op jit(solution)/shard_map/slice | solution.py:110
  121.3 7.8 %collective-permute-start.5 = (f32[128,128]{1,0:T(8,128)S(1)}, f32[128,128]{1,0:T(8,128)S(1)}, u32[]{:S(2)}, u32[]{:S(2)}) collective-permute-start(f32[128,128]{1,0:T(8,128)S(1)} %pad_maximum_fusion.1), channel_id=1, source_target_pairs={{16,0},{8,24},{17,1},{9,25},{18,2},{10,26},{19,3},{11,27},{20,4},{... | collective-permute-start | bytes 196616 | tf_op jit(solution)/shard_map/ppermute | solution.py:141
  122.7 6.4 %collective-permute-start.4 = (f32[128,128]{1,0:T(8,128)S(1)}, f32[128,128]{1,0:T(8,128)S(1)}, u32[]{:S(2)}, u32[]{:S(2)}) collective-permute-start(f32[128,128]{1,0:T(8,128)S(1)} %pad_maximum_fusion), channel_id=1, source_target_pairs={{8,0},{16,8},{24,16},{0,24},{9,1},{17,9},{25,17},{1,25},{10,2},{18... | collective-permute-start | bytes 196616 | tf_op jit(solution)/shard_map/ppermute | solution.py:141

commit v16 on v13

--- a/solution.py
+++ b/solution.py
@@ -1,6 +1,7 @@
 import jax
 import jax.numpy as jnp
 from jax import lax
+from jax.experimental.layout import Layout, with_layout_constraint
 from jax.sharding import PartitionSpec as P
 
 BS = 32
@@ -96,6 +97,7 @@
         jnp.stack([occ_rows, virt_rows]),
         preferred_element_type=jnp.float32,
     ).astype(jnp.bfloat16)
+    halves = with_layout_constraint(halves, Layout(major_to_minor=(0, 1, 2, 3)))
     halves, early = lax.optimization_barrier((halves, early))
     swapped = lax.all_to_all(halves, "ao", 0, 2, tiled=True)
     occ_t = swapped[:, 0]

time: 136 us -> 132 us (0.971)
  waiting for transfers between devices: 36.1 us -> 33.9 us
  starting transfers between devices: 23.1 us -> 21 us
    dot_general x0 -> x1, local copies, waits for them, and re-layouts: none -> 4.73 us  [per_device(): jnp.einsum('prk,dkc->cdrp', own, jnp.stack([occ_rows, virt_rows]), prefer...]
    optimization_barrier x1 -> x0, local copies, waits for them, and re-layouts: 4.73 us -> none  [per_device(): halves, early = lax.optimization_barrier((halves, early))]
    ppermute x2, waiting for transfers between devices: 3.49 us -> 0.01 us  [per_device(): lax.ppermute(own_flat[:lead], 'ri', route)]
  transfers between devices with their start and end apart: 7 -> 7, of which waited for: 2 -> 2; matrix products, arithmetic and copies ran while one was open for 30% -> 35% of each run, Pallas kernels for 0% -> 0%
where the time goes in v16:
time: 132 us; the launch traced here: 131 us
  local copies, waits for them, and re-layouts  34.2 us (26%)
  waiting for transfers between devices  33.9 us (26%)
  starting transfers between devices  21 us (16%)
  blocking collectives  18.7 us (14%)
  matrix products  16.1 us (12%)
  other arithmetic  4.17 us (3%)
  between operations  2.98 us (2%)
    all_to_all x1, waiting for transfers between devices, per_device(): swapped = lax.all_to_all(halves, 'ao', 0, 2, tiled=True)  33.8 us
    unnamed x30, local copies, waits for them, and re-layouts  15.4 us
    dot_general x4, matrix products, slab_product(): out = jnp.dot(flat, weights, preferred_element_type=jnp.float32)  11.1 us
    all_to_all x1, blocking collectives, per_device(): got = lax.all_to_all(sent, 'ao', 0, 0, tiled=True)  9.35 us
    all_gather x1, blocking collectives, per_device(): full = lax.all_gather(stacked, 'ao', axis=1, tiled=True)  9.32 us
    ppermute x2, starting transfers between devices, per_device(): lax.ppermute(own_flat[:lead], 'ri', route)  8.36 us
    ppermute x2, starting transfers between devices, per_device(): lax.ppermute(own_flat[lead:], 'ri', route)  5.36 us
    transpose x2, local copies, waits for them, and re-layouts, weight_pair(): both.transpose(2, 3, 0, 1).reshape(values.shape[1] * values.shape[2], -1)  4.86 us
  transfers between devices with their start and end apart: 7, of which 2 were waited for; matrix products, arithmetic and copies ran while one was open for 35% of the time, Pallas kernels for 0%

profile of v16, /device:TPU:0, one launch (start us, length us, event | category | flops | bytes accessed | tf_op | source)
XLA Modules:
  0.0 131.0 jit_solution(13696888787203270410)
XLA Ops:
  0.0 0.7 convert_element_type.32
  1.1 1.8 %broadcast_multiply_fusion = bf16[128,32,256]{2,1,0:T(8,128)(2,1)S(1)} fusion(bf16[128,32,256]{2,1,0:T(8,128)(2,1)} %param.11, bf16[128,256]{1,0:T(8,128)(2,1)S(1)} %copy.25), kind=kLoop, calls=%fused_computation.32 | loop fusion | flops 1048576 | bytes 4259840 | tf_op jit(solution)/shard_map/mul | solution.py:43
  3.3 3.1 %collective-permute-start = (bf16[32,8192]{1,0:T(8,128)(2,1)S(1)}, bf16[32,8192]{1,0:T(8,128)(2,1)}, u32[]{:S(2)}, u32[]{:S(2)}) collective-permute-start(bf16[32,8192]{1,0:T(8,128)(2,1)S(1)} %bitcast.142), channel_id=1, source_target_pairs={{0,8},{8,16},{16,24},{24,0},{1,9},{9,17},{17,25},{25,1},{2,10},{10... | collective-permute-start | bytes 1572872 | tf_op jit(solution)/shard_map/ppermute | solution.py:81
  6.3 5.3 %collective-permute-start.1 = (bf16[32,8192]{1,0:T(8,128)(2,1)S(1)}, bf16[32,8192]{1,0:T(8,128)(2,1)}, u32[]{:S(2)}, u32[]{:S(2)}) collective-permute-start(bf16[32,8192]{1,0:T(8,128)(2,1)S(1)} %bitcast.143), channel_id=1, source_target_pairs={{0,16},{24,8},{1,17},{25,9},{2,18},{26,10},{3,19},{27,11},{4,20},{... | collective-permute-start | bytes 1572872 | tf_op jit(solution)/shard_map/ppermute | solution.py:81
  12.0 9.3 %all_gather.3 = bf16[2,256,256]{2,1,0:T(8,128)(2,1)S(1)} all-gather(bf16[2,32,256]{2,1,0:T(8,128)(2,1)S(1)} %pad_maximum_fusion.2), channel_id=1, replica_groups=mesh['ri'=4,'ao'=8] {'ao'}, dimensions={1}, use_global_device_ids=true | all-gather | bytes 294912 | tf_op jit(solution)/shard_map/all_gather | solution.py:87
  22.1 3.2 %fusion.15 = bf16[2,256,128,32]{2,1,3,0:T(8,128)(2,1)S(1)} fusion(bf16[128,32,256]{2,1,0:T(8,128)(2,1)S(1)} %broadcast_multiply_fusion, bf16[1,256,256]{1,2,0:T(8,128)(2,1)S(1)} %copy.23, bf16[1,256,256]{1,2,0:T(8,128)(2,1)S(1)} %copy.22), kind=kOutput, calls=%fused_computation.25 | convolution fusion | flops 1074266112 | bytes 6553600 | tf_op jit(solution)/shard_map/prk,dkc->cdrp/dot_general | solution.py:94
  25.3 4.7 %copy.55 = bf16[2,256,128,32]{2,3,0,1:T(8,128)(2,1)} copy(bf16[2,256,128,32]{2,1,3,0:T(8,128)(2,1)S(1)} %fusion.15) | data formatting | bytes 8388608 | tf_op jit(solution)/shard_map/prk,dkc->cdrp/dot_general | solution.py:94
  30.0 4.6 %all-to-all-start = ((bf16[256,2,32,128]{3,2,1,0:T(8,128)(2,1)}), bf16[256,2,32,128]{3,2,1,0:T(8,128)(2,1)}, u32[]{:S(2)}, u32[]{:S(2)}) async-start(bf16[256,2,32,128]{3,2,1,0:T(8,128)(2,1)} %bitcast.125), calls=%async_computation | async-start | bytes 8388608 | tf_op jit(solution)/shard_map/all_to_all | solution.py:102
  34.8 2.2 %copy.47 = bf16[12,8,32,256]{3,1,2,0:T(8,128)(2,1)} copy(bf16[12,8,32,256]{3,2,1,0:T(8,128)(2,1)S(1)} %bitcast.130) | data formatting | bytes 3145728
  37.0 2.2 %collective-permute-start.2 = (bf16[96,8192]{1,0:T(8,128)(2,1)}, bf16[96,8192]{1,0:T(8,128)(2,1)}, u32[]{:S(2)}, u32[]{:S(2)}) collective-permute-start(bf16[96,8192]{1,0:T(8,128)(2,1)} %bitcast.64), channel_id=1, source_target_pairs={{0,8},{8,16},{16,24},{24,0},{1,9},{9,17},{17,25},{25,1},{2,10},{10... | collective-permute-start | bytes 4718600 | tf_op jit(solution)/shard_map/ppermute | solution.py:82
  39.1 3.2 %collective-permute-start.3 = (bf16[96,8192]{1,0:T(8,128)(2,1)}, bf16[96,8192]{1,0:T(8,128)(2,1)}, u32[]{:S(2)}, u32[]{:S(2)}) collective-permute-start(bf16[96,8192]{1,0:T(8,128)(2,1)} %bitcast.64), channel_id=1, source_target_pairs={{0,16},{24,8},{1,17},{25,9},{2,18},{26,10},{3,19},{27,11},{4,20},{... | collective-permute-start | bytes 4718600 | tf_op jit(solution)/shard_map/ppermute | solution.py:82
  43.6 0.6 dynamic_slice.26
  46.0 0.6 dynamic_slice.30
  47.2 2.8 %copy.46 = bf16[16,8,32,256]{3,1,2,0:T(8,128)(2,1)} copy(bf16[16,8,32,256]{3,2,1,0:T(8,128)(2,1)S(1)} %bitcast.122) | data formatting | bytes 4194304
  49.9 33.8 %all-to-all-done = bf16[256,2,32,128]{3,2,1,0:T(8,128)(2,1)} async-done(((bf16[256,2,32,128]{3,2,1,0:T(8,128)(2,1)}), bf16[256,2,32,128]{3,2,1,0:T(8,128)(2,1)}, u32[]{:S(2)}, u32[]{:S(2)}) %all-to-all-start) | async-done | bytes 4194336 | tf_op jit(solution)/shard_map/all_to_all | solution.py:102
  83.7 3.3 %copy.28 = bf16[8,32,2,32,128]{4,3,0,2,1:T(8,128)(2,1)S(1)} copy(bf16[8,32,2,32,128]{4,3,2,1,0:T(8,128)(2,1)} %bitcast.16) | data formatting | bytes 8388608 | tf_op jit(solution)/shard_map/all_to_all | solution.py:102
  87.0 0.8 fusion.12
  88.2 2.4 %copy.32 = bf16[32,256,2,128]{1,0,3,2:T(8,128)(2,1)S(1)} copy(bf16[32,256,2,128]{1,3,0,2:T(8,128)(2,1)S(1)} %maximum_bitcast_fusion.1) | data formatting | bytes 8388608 | tf_op jit(solution)/shard_map/transpose | solution.py:54
  90.6 4.3 %copy.45 = bf16[32,8,32,256]{3,1,2,0:T(8,128)(2,1)S(1)} copy(bf16[32,8,32,256]{3,2,1,0:T(8,128)(2,1)S(1)} %bitcast.128) | data formatting | bytes 8388608
  95.0 2.7 %fusion.3 = f32[192,256]{1,0:T(8,128)S(1)} fusion(bf16[8192,256]{0,1:T(8,128)(2,1)S(1)} %bitcast.131, bf16[32,8192]{1,0:T(8,128)(2,1)} %collective-permute-done.1, bf16[32,8192]{1,0:T(8,128)(2,1)} %collective-permute-done, bf16[128,8192]{1,0:T(8,128)(2,1)S(1)} %bitcast.134), kind=kOutput, calls=%fused_computation.11 | convolution fusion | flops 814743552 | bytes 7536640 | tf_op jit(solution)/shard_map/dot_general | solution.py:58
  97.7 1.0 fusion.11
  99.2 2.4 %copy.30 = bf16[32,256,2,128]{1,0,3,2:T(8,128)(2,1)S(1)} copy(bf16[32,256,2,128]{1,3,0,2:T(8,128)(2,1)S(1)} %maximum_bitcast_fusion) | data formatting | bytes 8388608 | tf_op jit(solution)/shard_map/transpose | solution.py:54
  101.6 4.3 %copy.44 = bf16[32,8,32,256]{3,1,2,0:T(8,128)(2,1)S(1)} copy(bf16[32,8,32,256]{3,2,1,0:T(8,128)(2,1)S(1)} %bitcast.129) | data formatting | bytes 8388608
  105.9 3.4 %fusion.18 = f32[64,256]{1,0:T(8,128)S(1)} fusion(bf16[8192,256]{0,1:T(8,128)(2,1)S(1)} %bitcast.126, bf16[32,8192]{1,0:T(8,128)(2,1)} %collective-permute-done.1, bf16[32,8192]{1,0:T(8,128)(2,1)} %collective-permute-done), kind=kOutput, calls=%fused_computation.28 | convolution fusion | flops 270532608 | bytes 5308416 | tf_op jit(solution)/shard_map/dot_general | solution.py:58
  109.3 1.5 %constant_dynamic-update-slice_fusion.1 = bf16[192,8192]{1,0:T(8,128)(2,1)S(1)} fusion(bf16[96,8192]{1,0:T(8,128)(2,1)} %collective-permute-done.2), kind=kLoop, calls=%fused_computation.55 | loop fusion | bytes 3145728
  110.8 1.5 %constant_dynamic-update-slice_fusion = bf16[192,8192]{1,0:T(8,128)(2,1)S(1)} fusion(bf16[192,8192]{1,0:T(8,128)(2,1)S(1)} %constant_dynamic-update-slice_fusion.1, bf16[96,8192]{1,0:T(8,128)(2,1)} %collective-permute-done.3), kind=kLoop, calls=%fused_computation.54 | loop fusion | bytes 3145728 | tf_op jit(solution)/shard_map/concatenate | solution.py:118
  112.4 1.3 fusion.38
  114.0 1.3 collective-permute-start.5
  115.5 1.4 %collective-permute-start.4 = (f32[128,128]{0,1:T(8,128)S(1)}, f32[128,128]{0,1:T(8,128)S(1)}, u32[]{:S(2)}, u32[]{:S(2)}) collective-permute-start(f32[128,128]{0,1:T(8,128)S(1)} %pad_maximum_fusion), channel_id=1, source_target_pairs={{8,0},{16,8},{24,16},{0,24},{9,1},{17,9},{25,17},{1,25},{10,2},{18... | collective-permute-start | bytes 196616 | tf_op jit(solution)/shard_map/ppermute | solution.py:140
  116.9 3.7 %fusion.37 = f32[192,256]{1,0:T(8,128)S(1)} fusion(bf16[192,8192]{1,0:T(8,128)(2,1)S(1)} %constant_dynamic-update-slice_fusion, bf16[8192,256]{0,1:T(8,128)(2,1)} %bitcast.127), kind=kOutput, calls=%fused_computation.69 | convolution fusion | flops 805306368 | bytes 7536640 | tf_op jit(solution)/shard_map/dot_general | solution.py:58
  121.1 9.3 %all_to_all.23 = f32[8,128,64]{1,2,0:T(8,128)S(1)} all-to-all(f32[8,128,64]{1,2,0:T(8,128)S(1)} %bitcast.133), channel_id=1, replica_groups=mesh['ri'=4,'ao'=8] {'ao'}, dimensions={0} | all-to-all | bytes 524288 | tf_op jit(solution)/shard_map/all_to_all | solution.py:145
  130.4 0.6 reduce_sum.9
  (79 shorter events, 4.8 us)
Async XLA Ops:
  1.1 10.5 %copy-start.5 = (s32[1,8]{1,0:T(1,128)S(1)}, s32[1,8]{1,0:T(1,128)}, u32[]{:S(2)}) copy-start(s32[1,8]{1,0:T(1,128)} %param.15) | copy-start | bytes 100
  1.1 10.7 %copy-start.6 = (s32[1,8]{1,0:T(1,128)S(1)}, s32[1,8]{1,0:T(1,128)}, u32[]{:S(2)}) copy-start(s32[1,8]{1,0:T(1,128)} %param.16) | copy-start | bytes 100
  1.1 10.9 %copy-start.3 = (bf16[32,256]{1,0:T(8,128)(2,1)S(1)}, bf16[32,256]{1,0:T(8,128)(2,1)}, u32[]{:S(2)}) copy-start(bf16[32,256]{1,0:T(8,128)(2,1)} %param.14) | copy-start | bytes 49156
  1.1 10.8 %copy-start.4 = (bf16[32,256]{1,0:T(8,128)(2,1)S(1)}, bf16[32,256]{1,0:T(8,128)(2,1)}, u32[]{:S(2)}) copy-start(bf16[32,256]{1,0:T(8,128)(2,1)} %param.13) | copy-start | bytes 49156
  1.1 20.2 %copy-start.7 = (s32[1,8]{1,0:T(1,128)S(1)}, s32[1,8]{1,0:T(1,128)}, u32[]{:S(2)}) copy-start(s32[1,8]{1,0:T(1,128)} %param.17) | copy-start | bytes 100
  3.3 26.8 %collective-permute-start = (bf16[32,8192]{1,0:T(8,128)(2,1)S(1)}, bf16[32,8192]{1,0:T(8,128)(2,1)}, u32[]{:S(2)}, u32[]{:S(2)}) collective-permute-start(bf16[32,8192]{1,0:T(8,128)(2,1)S(1)} %bitcast.142), channel_id=1, source_target_pairs={{0,8},{8,16},{16,24},{24,0},{1,9},{9,17},{17,25},{25,1},{2,10},{10... | collective-permute-start | bytes 1572872 | tf_op jit(solution)/shard_map/ppermute | solution.py:81
  6.3 23.7 %collective-permute-start.1 = (bf16[32,8192]{1,0:T(8,128)(2,1)S(1)}, bf16[32,8192]{1,0:T(8,128)(2,1)}, u32[]{:S(2)}, u32[]{:S(2)}) collective-permute-start(bf16[32,8192]{1,0:T(8,128)(2,1)S(1)} %bitcast.143), channel_id=1, source_target_pairs={{0,16},{24,8},{1,17},{25,9},{2,18},{26,10},{3,19},{27,11},{4,20},{... | collective-permute-start | bytes 1572872 | tf_op jit(solution)/shard_map/ppermute | solution.py:81
  30.0 53.7 %all-to-all-start = ((bf16[256,2,32,128]{3,2,1,0:T(8,128)(2,1)}), bf16[256,2,32,128]{3,2,1,0:T(8,128)(2,1)}, u32[]{:S(2)}, u32[]{:S(2)}) async-start(bf16[256,2,32,128]{3,2,1,0:T(8,128)(2,1)} %bitcast.125), calls=%async_computation | async-start | bytes 8388608 | tf_op jit(solution)/shard_map/all_to_all | solution.py:102
  34.6 7.7 %copy-start.11 = (s32[4]{0:T(128)S(1)}, s32[4]{0:T(128)}, u32[]{:S(2)}) copy-start(s32[4]{0:T(128)} %constant.32.clone) | copy-start | bytes 52
  34.6 8.9 %copy-start.10 = (s32[4]{0:T(128)S(1)}, s32[4]{0:T(128)}, u32[]{:S(2)}) copy-start(s32[4]{0:T(128)} %constant.33.clone) | copy-start | bytes 52
  34.6 10.2 %copy-start.9 = (s32[4]{0:T(128)S(1)}, s32[4]{0:T(128)}, u32[]{:S(2)}) copy-start(s32[4]{0:T(128)} %constant.34.clone) | copy-start | bytes 52
  34.7 11.3 %copy-start.8 = (s32[4]{0:T(128)S(1)}, s32[4]{0:T(128)}, u32[]{:S(2)}) copy-start(s32[4]{0:T(128)} %constant.35.clone) | copy-start | bytes 52
  37.0 72.3 %collective-permute-start.2 = (bf16[96,8192]{1,0:T(8,128)(2,1)}, bf16[96,8192]{1,0:T(8,128)(2,1)}, u32[]{:S(2)}, u32[]{:S(2)}) collective-permute-start(bf16[96,8192]{1,0:T(8,128)(2,1)} %bitcast.64), channel_id=1, source_target_pairs={{0,8},{8,16},{16,24},{24,0},{1,9},{9,17},{17,25},{25,1},{2,10},{10... | collective-permute-start | bytes 4718600 | tf_op jit(solution)/shard_map/ppermute | solution.py:82
  39.1 70.2 %collective-permute-start.3 = (bf16[96,8192]{1,0:T(8,128)(2,1)}, bf16[96,8192]{1,0:T(8,128)(2,1)}, u32[]{:S(2)}, u32[]{:S(2)}) collective-permute-start(bf16[96,8192]{1,0:T(8,128)(2,1)} %bitcast.64), channel_id=1, source_target_pairs={{0,16},{24,8},{1,17},{25,9},{2,18},{26,10},{3,19},{27,11},{4,20},{... | collective-permute-start | bytes 4718600 | tf_op jit(solution)/shard_map/ppermute | solution.py:82
  90.6 4.3 %copy-start.1 = (bf16[16,8,32,256]{3,1,2,0:T(8,128)(2,1)S(1)}, bf16[16,8,32,256]{3,1,2,0:T(8,128)(2,1)}, u32[]{:S(2)}) copy-start(bf16[16,8,32,256]{3,1,2,0:T(8,128)(2,1)} %copy.46) | copy-start | bytes 6291460
  97.7 1.0 copy-start.2
  105.9 4.9 %copy-start = (bf16[32,8,32,256]{3,1,2,0:T(8,128)(2,1)}, bf16[32,8,32,256]{3,1,2,0:T(8,128)(2,1)S(1)}, u32[]{:S(2)}) copy-start(bf16[32,8,32,256]{3,1,2,0:T(8,128)(2,1)S(1)} %copy.44) | copy-start | bytes 12582916
  112.4 1.4 %slice-start.1 = ((f32[192,128]{1,0:T(8,128)}), f32[64,128]{1,0:T(8,128)S(1)}, s32[]{:S(2)}) async-start(f32[192,128]{1,0:T(8,128)} %copy-done.2), calls=%async_computation.3 | async-start | bytes 65536 | tf_op jit(solution)/shard_map/slice | solution.py:113
  114.0 7.1 %collective-permute-start.5 = (f32[128,128]{0,1:T(8,128)S(1)}, f32[128,128]{0,1:T(8,128)S(1)}, u32[]{:S(2)}, u32[]{:S(2)}) collective-permute-start(f32[128,128]{0,1:T(8,128)S(1)} %pad_maximum_fusion.1), channel_id=1, source_target_pairs={{16,0},{8,24},{17,1},{9,25},{18,2},{10,26},{19,3},{11,27},{20,4},{... | collective-permute-start | bytes 196616 | tf_op jit(solution)/shard_map/ppermute | solution.py:140
  115.5 5.2 %slice-start = ((f32[192,128]{1,0:T(8,128)}), f32[128,128]{1,0:T(8,128)S(1)}, s32[]{:S(2)}) async-start(f32[192,128]{1,0:T(8,128)} %copy-done.2), calls=%async_computation.2 | async-start | bytes 131072 | tf_op jit(solution)/shard_map/slice | solution.py:112
  115.5 5.4 %collective-permute-start.4 = (f32[128,128]{0,1:T(8,128)S(1)}, f32[128,128]{0,1:T(8,128)S(1)}, u32[]{:S(2)}, u32[]{:S(2)}) collective-permute-start(f32[128,128]{0,1:T(8,128)S(1)} %pad_maximum_fusion), channel_id=1, source_target_pairs={{8,0},{16,8},{24,16},{0,24},{9,1},{17,9},{25,17},{1,25},{10,2},{18... | collective-permute-start | bytes 196616 | tf_op jit(solution)/shard_map/ppermute | solution.py:140

commit v17 on v16

--- a/solution.py
+++ b/solution.py
@@ -51,7 +51,8 @@
 def weight_pair(values):
     hi, lo = split_hi_lo(values)
     both = jnp.stack([hi, lo])
-    return both.transpose(2, 3, 0, 1).reshape(values.shape[1] * values.shape[2], -1)
+    flat = both.transpose(2, 3, 0, 1).reshape(values.shape[1] * values.shape[2], -1)
+    return with_layout_constraint(flat, Layout(major_to_minor=(0, 1)))
 
 
 def slab_product(flat, weights):

time: 132 us -> 155 us (1.17)
  local copies, waits for them, and re-layouts: 34.2 us -> 53.4 us
  other arithmetic: 4.17 us -> 8.15 us
    transpose x2, local copies, waits for them, and re-layouts: 4.86 us -> 22.5 us  [weight_pair(): both.transpose(2, 3, 0, 1).reshape(values.shape[1] * values.shape[2], -1)]
    transpose x2, other arithmetic: 0.77 us -> 4.75 us  [weight_pair(): both.transpose(2, 3, 0, 1).reshape(values.shape[1] * values.shape[2], -1)]
    unnamed x30 -> x38, local copies, waits for them, and re-layouts: 15.4 us -> 16.9 us
  transfers between devices with their start and end apart: 7 -> 7, of which waited for: 2 -> 2; matrix products, arithmetic and copies ran while one was open for 35% -> 42% of each run, Pallas kernels for 0% -> 0%
where the time goes in v17:
time: 155 us; the launch traced here: 154 us
  local copies, waits for them, and re-layouts  53.4 us (34%)
  waiting for transfers between devices  34.4 us (22%)
  starting transfers between devices  21 us (14%)
  blocking collectives  18.7 us (12%)
  matrix products  15.4 us (10%)
  other arithmetic  8.15 us (5%)
  between operations  3.01 us (2%)
    all_to_all x1, waiting for transfers between devices, per_device(): swapped = lax.all_to_all(halves, 'ao', 0, 2, tiled=True)  33.7 us
    transpose x2, local copies, waits for them, and re-layouts, weight_pair(): both.transpose(2, 3, 0, 1).reshape(values.shape[1] * values.shape[2], -1)  22.5 us
    unnamed x38, local copies, waits for them, and re-layouts  16.9 us
    dot_general x4, matrix products, slab_product(): out = jnp.dot(flat, weights, preferred_element_type=jnp.float32)  10.7 us
    all_to_all x1, blocking collectives, per_device(): got = lax.all_to_all(sent, 'ao', 0, 0, tiled=True)  9.35 us
    all_gather x1, blocking collectives, per_device(): full = lax.all_gather(stacked, 'ao', axis=1, tiled=True)  9.32 us
    ppermute x2, starting transfers between devices, per_device(): lax.ppermute(own_flat[:lead], 'ri', route)  8.35 us
    ppermute x2, starting transfers between devices, per_device(): lax.ppermute(own_flat[lead:], 'ri', route)  5.38 us
  transfers between devices with their start and end apart: 7, of which 2 were waited for; matrix products, arithmetic and copies ran while one was open for 42% of the time, Pallas kernels for 0%

profile of v17, /device:TPU:0, one launch (start us, length us, event | category | flops | bytes accessed | tf_op | source)
XLA Modules:
  0.0 154.0 jit_solution(13691628615702287928)
XLA Ops:
  1.1 1.8 %broadcast_multiply_fusion = bf16[128,32,256]{2,1,0:T(8,128)(2,1)S(1)} fusion(bf16[128,32,256]{2,1,0:T(8,128)(2,1)} %param.11, bf16[128,256]{1,0:T(8,128)(2,1)S(1)} %copy.27), kind=kLoop, calls=%fused_computation.34 | loop fusion | flops 1048576 | bytes 4259840 | tf_op jit(solution)/shard_map/mul | solution.py:43
  3.3 3.1 %collective-permute-start = (bf16[32,8192]{1,0:T(8,128)(2,1)S(1)}, bf16[32,8192]{1,0:T(8,128)(2,1)}, u32[]{:S(2)}, u32[]{:S(2)}) collective-permute-start(bf16[32,8192]{1,0:T(8,128)(2,1)S(1)} %bitcast.142), channel_id=1, source_target_pairs={{0,8},{8,16},{16,24},{24,0},{1,9},{9,17},{17,25},{25,1},{2,10},{10... | collective-permute-start | bytes 1572872 | tf_op jit(solution)/shard_map/ppermute | solution.py:82
  6.3 5.3 %collective-permute-start.1 = (bf16[32,8192]{1,0:T(8,128)(2,1)S(1)}, bf16[32,8192]{1,0:T(8,128)(2,1)}, u32[]{:S(2)}, u32[]{:S(2)}) collective-permute-start(bf16[32,8192]{1,0:T(8,128)(2,1)S(1)} %bitcast.143), channel_id=1, source_target_pairs={{0,16},{24,8},{1,17},{25,9},{2,18},{26,10},{3,19},{27,11},{4,20},{... | collective-permute-start | bytes 1572872 | tf_op jit(solution)/shard_map/ppermute | solution.py:82
  12.0 9.3 %all_gather.3 = bf16[2,256,256]{2,1,0:T(8,128)(2,1)S(1)} all-gather(bf16[2,32,256]{2,1,0:T(8,128)(2,1)S(1)} %pad_maximum_fusion.2), channel_id=1, replica_groups=mesh['ri'=4,'ao'=8] {'ao'}, dimensions={1}, use_global_device_ids=true | all-gather | bytes 294912 | tf_op jit(solution)/shard_map/all_gather | solution.py:88
  22.1 3.2 %fusion.15 = bf16[2,256,128,32]{2,1,3,0:T(8,128)(2,1)S(1)} fusion(bf16[128,32,256]{2,1,0:T(8,128)(2,1)S(1)} %broadcast_multiply_fusion, bf16[1,256,256]{1,2,0:T(8,128)(2,1)S(1)} %copy.25, bf16[1,256,256]{1,2,0:T(8,128)(2,1)S(1)} %copy.24), kind=kOutput, calls=%fused_computation.27 | convolution fusion | flops 1074266112 | bytes 6553600 | tf_op jit(solution)/shard_map/prk,dkc->cdrp/dot_general | solution.py:95
  25.3 4.7 %copy.61 = bf16[2,256,128,32]{2,3,0,1:T(8,128)(2,1)} copy(bf16[2,256,128,32]{2,1,3,0:T(8,128)(2,1)S(1)} %fusion.15) | data formatting | bytes 8388608 | tf_op jit(solution)/shard_map/prk,dkc->cdrp/dot_general | solution.py:95
  30.0 4.5 %all-to-all-start = ((bf16[256,2,32,128]{3,2,1,0:T(8,128)(2,1)}), bf16[256,2,32,128]{3,2,1,0:T(8,128)(2,1)}, u32[]{:S(2)}, u32[]{:S(2)}) async-start(bf16[256,2,32,128]{3,2,1,0:T(8,128)(2,1)} %bitcast.126), calls=%async_computation | async-start | bytes 8388608 | tf_op jit(solution)/shard_map/all_to_all | solution.py:103
  34.8 2.2 %copy.49 = bf16[12,8,32,256]{3,1,2,0:T(8,128)(2,1)} copy(bf16[12,8,32,256]{3,2,1,0:T(8,128)(2,1)S(1)} %bitcast.132) | data formatting | bytes 3145728
  37.0 2.2 %collective-permute-start.2 = (bf16[96,8192]{1,0:T(8,128)(2,1)}, bf16[96,8192]{1,0:T(8,128)(2,1)}, u32[]{:S(2)}, u32[]{:S(2)}) collective-permute-start(bf16[96,8192]{1,0:T(8,128)(2,1)} %bitcast.60), channel_id=1, source_target_pairs={{0,8},{8,16},{16,24},{24,0},{1,9},{9,17},{17,25},{25,1},{2,10},{10... | collective-permute-start | bytes 4718600 | tf_op jit(solution)/shard_map/ppermute | solution.py:83
  39.1 3.2 %collective-permute-start.3 = (bf16[96,8192]{1,0:T(8,128)(2,1)}, bf16[96,8192]{1,0:T(8,128)(2,1)}, u32[]{:S(2)}, u32[]{:S(2)}) collective-permute-start(bf16[96,8192]{1,0:T(8,128)(2,1)} %bitcast.60), channel_id=1, source_target_pairs={{0,16},{24,8},{1,17},{25,9},{2,18},{26,10},{3,19},{27,11},{4,20},{... | collective-permute-start | bytes 4718600 | tf_op jit(solution)/shard_map/ppermute | solution.py:83
  47.3 2.7 %copy.48 = bf16[16,8,32,256]{3,1,2,0:T(8,128)(2,1)} copy(bf16[16,8,32,256]{3,2,1,0:T(8,128)(2,1)S(1)} %bitcast.122) | data formatting | bytes 4194304
  50.0 33.7 %all-to-all-done = bf16[256,2,32,128]{3,2,1,0:T(8,128)(2,1)} async-done(((bf16[256,2,32,128]{3,2,1,0:T(8,128)(2,1)}), bf16[256,2,32,128]{3,2,1,0:T(8,128)(2,1)}, u32[]{:S(2)}, u32[]{:S(2)}) %all-to-all-start) | async-done | bytes 4194336 | tf_op jit(solution)/shard_map/all_to_all | solution.py:103
  83.7 3.3 %copy.30 = bf16[8,32,2,32,128]{4,3,0,2,1:T(8,128)(2,1)S(1)} copy(bf16[8,32,2,32,128]{4,3,2,1,0:T(8,128)(2,1)} %bitcast.16) | data formatting | bytes 8388608 | tf_op jit(solution)/shard_map/all_to_all | solution.py:103
  87.0 0.8 fusion.12
  87.8 1.2 copy-done
  89.0 2.4 %maximum_bitcast_fusion.1 = bf16[32,256,2,128]{1,3,0,2:T(8,128)(2,1)} fusion(bf16[1,128,32,256]{3,1,2,0:T(8,128)(2,1)S(1)} %get-tuple-element.26, bf16[1,128,32,256]{3,1,2,0:T(8,128)(2,1)S(1)} %get-tuple-element.25), kind=kLoop, calls=%fused_computation.12 | loop fusion | flops 2097152 | bytes 8388608 | tf_op jit(solution)/shard_map/transpose | solution.py:54
  91.4 11.3 %copy.34 = bf16[32,256,2,128]{3,2,1,0:T(2,128)(2,1)} copy(bf16[32,256,2,128]{1,3,0,2:T(8,128)(2,1)} %maximum_bitcast_fusion.1) | data formatting | bytes 8388608 | tf_op jit(solution)/shard_map/transpose | solution.py:54
  102.7 3.6 %fusion.3 = f32[192,256]{1,0:T(8,128)S(1)} fusion(bf16[32,8192]{1,0:T(8,128)(2,1)} %collective-permute-done.1, bf16[32,8192]{1,0:T(8,128)(2,1)} %collective-permute-done, bf16[128,8192]{1,0:T(8,128)(2,1)S(1)} %bitcast.134, bf16[1024,8,2,128]{3,2,1,0:T(2,128)(2,1)} %bitcast.128), kind=kOutput, calls=%fused_computation.13 | convolution fusion | flops 814743552 | bytes 7536640 | tf_op jit(solution)/shard_map/dot_general | solution.py:59
  106.4 2.7 %copy.62 = bf16[1024,8,2,128]{3,1,2,0:T(8,128)(2,1)} copy(bf16[1024,8,2,128]{3,2,1,0:T(2,128)(2,1)S(1)} %bitcast.129) | data formatting | bytes 8388608
  109.1 1.0 copy-done.1
  110.1 0.8 fusion.11
  110.9 2.4 %maximum_bitcast_fusion = bf16[32,256,2,128]{1,3,0,2:T(8,128)(2,1)} fusion(bf16[1,128,32,256]{3,1,2,0:T(8,128)(2,1)S(1)} %get-tuple-element.28, bf16[1,128,32,256]{3,1,2,0:T(8,128)(2,1)S(1)} %get-tuple-element.27), kind=kLoop, calls=%fused_computation.11 | loop fusion | flops 2097152 | bytes 8388608 | tf_op jit(solution)/shard_map/transpose | solution.py:54
  113.3 11.2 %copy.32 = bf16[32,256,2,128]{3,2,1,0:T(2,128)(2,1)} copy(bf16[32,256,2,128]{1,3,0,2:T(8,128)(2,1)} %maximum_bitcast_fusion) | data formatting | bytes 8388608 | tf_op jit(solution)/shard_map/transpose | solution.py:54
  124.5 4.9 %copy.63 = bf16[1024,8,2,128]{3,1,2,0:T(8,128)(2,1)} copy(bf16[1024,8,2,128]{3,2,1,0:T(2,128)(2,1)} %bitcast.130) | data formatting | bytes 8388608
  129.4 2.1 %fusion.18 = f32[64,256]{1,0:T(8,128)S(1)} fusion(bf16[32,8192]{1,0:T(8,128)(2,1)} %collective-permute-done.1, bf16[32,8192]{1,0:T(8,128)(2,1)} %collective-permute-done, bf16[1024,8,2,128]{3,2,1,0:T(2,128)(2,1)S(1)} %bitcast.131), kind=kOutput, calls=%fused_computation.30 | convolution fusion | flops 270532608 | bytes 5308416 | tf_op jit(solution)/shard_map/dot_general | solution.py:59
  131.5 1.7 %constant_dynamic-update-slice_fusion.1 = bf16[192,8192]{1,0:T(8,128)(2,1)S(1)} fusion(bf16[96,8192]{1,0:T(8,128)(2,1)} %collective-permute-done.2), kind=kLoop, calls=%fused_computation.57 | loop fusion | bytes 3145728
  133.2 1.6 %constant_dynamic-update-slice_fusion = bf16[192,8192]{1,0:T(8,128)(2,1)S(1)} fusion(bf16[192,8192]{1,0:T(8,128)(2,1)S(1)} %constant_dynamic-update-slice_fusion.1, bf16[96,8192]{1,0:T(8,128)(2,1)} %collective-permute-done.3), kind=kLoop, calls=%fused_computation.56 | loop fusion | bytes 3145728 | tf_op jit(solution)/shard_map/concatenate | solution.py:119
  134.8 1.8 %fusion.38 = f32[192,256]{0,1:T(8,128)S(1)} fusion(bf16[192,8192]{1,0:T(8,128)(2,1)S(1)} %constant_dynamic-update-slice_fusion, bf16[8192,256]{1,0:T(8,128)(2,1)S(1)} %bitcast.127), kind=kOutput, calls=%fused_computation.72 | convolution fusion | flops 805306368 | bytes 7536640 | tf_op jit(solution)/shard_map/dot_general | solution.py:59
  136.9 1.3 collective-permute-start.5
  138.4 1.4 collective-permute-start.4
  139.8 3.2 %fusion.37 = f32[192,256]{1,0:T(8,128)S(1)} fusion(bf16[192,8192]{1,0:T(8,128)(2,1)S(1)} %constant_dynamic-update-slice_fusion, bf16[8192,256]{1,0:T(8,128)(2,1)} %bitcast.123), kind=kOutput, calls=%fused_computation.71 | convolution fusion | flops 805306368 | bytes 7536640 | tf_op jit(solution)/shard_map/dot_general | solution.py:59
  144.0 9.3 %all_to_all.23 = f32[8,128,64]{1,2,0:T(8,128)S(1)} all-to-all(f32[8,128,64]{1,2,0:T(8,128)S(1)} %bitcast.133), channel_id=1, replica_groups=mesh['ri'=4,'ao'=8] {'ao'}, dimensions={0} | all-to-all | bytes 524288 | tf_op jit(solution)/shard_map/all_to_all | solution.py:146
  (87 shorter events, 7.3 us)
Async XLA Ops:
  1.1 10.5 %copy-start.9 = (s32[1,8]{1,0:T(1,128)S(1)}, s32[1,8]{1,0:T(1,128)}, u32[]{:S(2)}) copy-start(s32[1,8]{1,0:T(1,128)} %param.15) | copy-start | bytes 100
  1.1 10.7 %copy-start.10 = (s32[1,8]{1,0:T(1,128)S(1)}, s32[1,8]{1,0:T(1,128)}, u32[]{:S(2)}) copy-start(s32[1,8]{1,0:T(1,128)} %param.16) | copy-start | bytes 100
  1.1 10.9 %copy-start.7 = (bf16[32,256]{1,0:T(8,128)(2,1)S(1)}, bf16[32,256]{1,0:T(8,128)(2,1)}, u32[]{:S(2)}) copy-start(bf16[32,256]{1,0:T(8,128)(2,1)} %param.14) | copy-start | bytes 49156
  1.1 10.8 %copy-start.8 = (bf16[32,256]{1,0:T(8,128)(2,1)S(1)}, bf16[32,256]{1,0:T(8,128)(2,1)}, u32[]{:S(2)}) copy-start(bf16[32,256]{1,0:T(8,128)(2,1)} %param.13) | copy-start | bytes 49156
  1.1 20.2 %copy-start.11 = (s32[1,8]{1,0:T(1,128)S(1)}, s32[1,8]{1,0:T(1,128)}, u32[]{:S(2)}) copy-start(s32[1,8]{1,0:T(1,128)} %param.17) | copy-start | bytes 100
  3.3 26.8 %collective-permute-start = (bf16[32,8192]{1,0:T(8,128)(2,1)S(1)}, bf16[32,8192]{1,0:T(8,128)(2,1)}, u32[]{:S(2)}, u32[]{:S(2)}) collective-permute-start(bf16[32,8192]{1,0:T(8,128)(2,1)S(1)} %bitcast.142), channel_id=1, source_target_pairs={{0,8},{8,16},{16,24},{24,0},{1,9},{9,17},{17,25},{25,1},{2,10},{10... | collective-permute-start | bytes 1572872 | tf_op jit(solution)/shard_map/ppermute | solution.py:82
  6.3 23.7 %collective-permute-start.1 = (bf16[32,8192]{1,0:T(8,128)(2,1)S(1)}, bf16[32,8192]{1,0:T(8,128)(2,1)}, u32[]{:S(2)}, u32[]{:S(2)}) collective-permute-start(bf16[32,8192]{1,0:T(8,128)(2,1)S(1)} %bitcast.143), channel_id=1, source_target_pairs={{0,16},{24,8},{1,17},{25,9},{2,18},{26,10},{3,19},{27,11},{4,20},{... | collective-permute-start | bytes 1572872 | tf_op jit(solution)/shard_map/ppermute | solution.py:82
  30.0 53.7 %all-to-all-start = ((bf16[256,2,32,128]{3,2,1,0:T(8,128)(2,1)}), bf16[256,2,32,128]{3,2,1,0:T(8,128)(2,1)}, u32[]{:S(2)}, u32[]{:S(2)}) async-start(bf16[256,2,32,128]{3,2,1,0:T(8,128)(2,1)} %bitcast.126), calls=%async_computation | async-start | bytes 8388608 | tf_op jit(solution)/shard_map/all_to_all | solution.py:103
  34.6 7.8 %copy-start.15 = (s32[4]{0:T(128)S(1)}, s32[4]{0:T(128)}, u32[]{:S(2)}) copy-start(s32[4]{0:T(128)} %constant.32.clone) | copy-start | bytes 52
  34.6 9.0 %copy-start.14 = (s32[4]{0:T(128)S(1)}, s32[4]{0:T(128)}, u32[]{:S(2)}) copy-start(s32[4]{0:T(128)} %constant.33.clone) | copy-start | bytes 52
  34.6 10.2 %copy-start.13 = (s32[4]{0:T(128)S(1)}, s32[4]{0:T(128)}, u32[]{:S(2)}) copy-start(s32[4]{0:T(128)} %constant.34.clone) | copy-start | bytes 52
  34.6 11.4 %copy-start.12 = (s32[4]{0:T(128)S(1)}, s32[4]{0:T(128)}, u32[]{:S(2)}) copy-start(s32[4]{0:T(128)} %constant.35.clone) | copy-start | bytes 52
  37.0 94.5 %collective-permute-start.2 = (bf16[96,8192]{1,0:T(8,128)(2,1)}, bf16[96,8192]{1,0:T(8,128)(2,1)}, u32[]{:S(2)}, u32[]{:S(2)}) collective-permute-start(bf16[96,8192]{1,0:T(8,128)(2,1)} %bitcast.60), channel_id=1, source_target_pairs={{0,8},{8,16},{16,24},{24,0},{1,9},{9,17},{17,25},{25,1},{2,10},{10... | collective-permute-start | bytes 4718600 | tf_op jit(solution)/shard_map/ppermute | solution.py:83
  39.1 92.4 %collective-permute-start.3 = (bf16[96,8192]{1,0:T(8,128)(2,1)}, bf16[96,8192]{1,0:T(8,128)(2,1)}, u32[]{:S(2)}, u32[]{:S(2)}) collective-permute-start(bf16[96,8192]{1,0:T(8,128)(2,1)} %bitcast.60), channel_id=1, source_target_pairs={{0,16},{24,8},{1,17},{25,9},{2,18},{26,10},{3,19},{27,11},{4,20},{... | collective-permute-start | bytes 4718600 | tf_op jit(solution)/shard_map/ppermute | solution.py:83
  87.0 2.0 %copy-start = (bf16[8,32,2,32,128]{4,3,0,2,1:T(8,128)(2,1)}, bf16[8,32,2,32,128]{4,3,0,2,1:T(8,128)(2,1)S(1)}, u32[]{:S(2)}) copy-start(bf16[8,32,2,32,128]{4,3,0,2,1:T(8,128)(2,1)S(1)} %copy.30) | copy-start | bytes 12582916
  91.4 11.3 %copy-start.5 = (bf16[16,8,32,256]{3,1,2,0:T(8,128)(2,1)S(1)}, bf16[16,8,32,256]{3,1,2,0:T(8,128)(2,1)}, u32[]{:S(2)}) copy-start(bf16[16,8,32,256]{3,1,2,0:T(8,128)(2,1)} %copy.48) | copy-start | bytes 6291460
  102.7 3.7 %copy-start.3 = (bf16[32,256,2,128]{3,2,1,0:T(2,128)(2,1)S(1)}, bf16[32,256,2,128]{3,2,1,0:T(2,128)(2,1)}, u32[]{:S(2)}) copy-start(bf16[32,256,2,128]{3,2,1,0:T(2,128)(2,1)} %copy.34) | copy-start | bytes 12582916
  106.3 2.8 %copy-start.6 = (f32[192,128]{1,0:T(8,128)}, f32[192,128]{1,0:T(8,128)S(1)}, u32[]{:S(2)}) copy-start(f32[192,128]{1,0:T(8,128)S(1)} %slice_add_fusion.2) | copy-start | bytes 294916
  106.4 3.7 %copy-start.1 = (bf16[8,32,2,32,128]{4,3,0,2,1:T(8,128)(2,1)S(1)}, bf16[8,32,2,32,128]{4,3,0,2,1:T(8,128)(2,1)}, u32[]{:S(2)}) copy-start(bf16[8,32,2,32,128]{4,3,0,2,1:T(8,128)(2,1)} %copy-done) | copy-start | bytes 12582916
  124.5 4.9 %copy-start.4 = (bf16[32,256,2,128]{3,2,1,0:T(2,128)(2,1)S(1)}, bf16[32,256,2,128]{3,2,1,0:T(2,128)(2,1)}, u32[]{:S(2)}) copy-start(bf16[32,256,2,128]{3,2,1,0:T(2,128)(2,1)} %copy.32) | copy-start | bytes 12582916
  131.5 3.2 %copy-start.2 = (bf16[1024,8,2,128]{3,1,2,0:T(8,128)(2,1)S(1)}, bf16[1024,8,2,128]{3,1,2,0:T(8,128)(2,1)}, u32[]{:S(2)}) copy-start(bf16[1024,8,2,128]{3,1,2,0:T(8,128)(2,1)} %copy.62) | copy-start | bytes 12582916
  134.7 2.0 %slice-start.1 = ((f32[192,128]{1,0:T(8,128)}), f32[64,128]{1,0:T(8,128)S(1)}, s32[]{:S(2)}) async-start(f32[192,128]{1,0:T(8,128)} %copy-done.6), calls=%async_computation.3 | async-start | bytes 65536 | tf_op jit(solution)/shard_map/slice | solution.py:114
  136.9 7.1 %collective-permute-start.5 = (f32[128,128]{0,1:T(8,128)S(1)}, f32[128,128]{0,1:T(8,128)S(1)}, u32[]{:S(2)}, u32[]{:S(2)}) collective-permute-start(f32[128,128]{0,1:T(8,128)S(1)} %pad_maximum_fusion.1), channel_id=1, source_target_pairs={{16,0},{8,24},{17,1},{9,25},{18,2},{10,26},{19,3},{11,27},{20,4},{... | collective-permute-start | bytes 196616 | tf_op jit(solution)/shard_map/ppermute | solution.py:141
  138.4 4.6 %slice-start = ((f32[192,128]{1,0:T(8,128)}), f32[128,128]{1,0:T(8,128)S(1)}, s32[]{:S(2)}) async-start(f32[192,128]{1,0:T(8,128)} %copy-done.6), calls=%async_computation.2 | async-start | bytes 131072 | tf_op jit(solution)/shard_map/slice | solution.py:113
  138.4 4.8 %collective-permute-start.4 = (f32[128,128]{0,1:T(8,128)S(1)}, f32[128,128]{0,1:T(8,128)S(1)}, u32[]{:S(2)}, u32[]{:S(2)}) collective-permute-start(f32[128,128]{0,1:T(8,128)S(1)} %pad_maximum_fusion), channel_id=1, source_target_pairs={{8,0},{16,8},{24,16},{0,24},{9,1},{17,9},{25,17},{1,25},{10,2},{18... | collective-permute-start | bytes 196616 | tf_op jit(solution)/shard_map/ppermute | solution.py:141

commit v18 on v16

--- a/solution.py
+++ b/solution.py
@@ -77,7 +77,7 @@
     routes = pair_routes(planes)
     own = mask_slab(tensor, live_blocks)
     own_flat = own.reshape(rows, -1)
-    lead = rows // 4
+    lead = rows * 5 // 16
     early = [lax.ppermute(own_flat[:lead], "ri", route) for route, _, _ in routes]
     late = [lax.ppermute(own_flat[lead:], "ri", route) for route, _, _ in routes]
 
@@ -119,7 +119,7 @@
     late_mine = slab_product(late_stack, v_weights)
     late_theirs = slab_product(late_stack, w_weights)
     count = len(routes)
-    lead = rows // 4
+    lead = rows * 5 // 16
     rest = rows - lead
 
     def slab_rows(early_part, late_part, index):

time: 132 us -> 139 us (1.053)
  waiting for transfers between devices: 33.9 us -> 37.7 us
  starting transfers between devices: 21 us -> 23.3 us
    ppermute x2, waiting for transfers between devices: 0.01 us -> 4.29 us  [per_device(): lax.ppermute(own_flat[:lead], 'ri', route)]
    dot_general x4, matrix products: 11.1 us -> 12.6 us  [slab_product(): out = jnp.dot(flat, weights, preferred_element_type=jnp.float32)]
    unnamed x30 -> x40, local copies, waits for them, and re-layouts: 15.4 us -> 14.2 us
  transfers between devices with their start and end apart: 7 -> 7, of which waited for: 2 -> 2; matrix products, arithmetic and copies ran while one was open for 35% -> 34% of each run, Pallas kernels for 0% -> 0%
where the time goes in v18:
time: 139 us; the launch traced here: 138 us
  waiting for transfers between devices  37.7 us (27%)
  local copies, waits for them, and re-layouts  33.1 us (24%)
  starting transfers between devices  23.3 us (17%)
  blocking collectives  18.7 us (13%)
  matrix products  17.3 us (12%)
  other arithmetic  4.8 us (3%)
  between operations  3.19 us (2%)
    all_to_all x1, waiting for transfers between devices, per_device(): swapped = lax.all_to_all(halves, 'ao', 0, 2, tiled=True)  33.4 us
    unnamed x40, local copies, waits for them, and re-layouts  14.2 us
    dot_general x4, matrix products, slab_product(): out = jnp.dot(flat, weights, preferred_element_type=jnp.float32)  12.6 us
    all_to_all x1, blocking collectives, per_device(): got = lax.all_to_all(sent, 'ao', 0, 0, tiled=True)  9.35 us
    all_gather x1, blocking collectives, per_device(): full = lax.all_gather(stacked, 'ao', axis=1, tiled=True)  9.32 us
    ppermute x2, starting transfers between devices, per_device(): lax.ppermute(own_flat[:lead], 'ri', route)  8.4 us
    ppermute x2, starting transfers between devices, per_device(): lax.ppermute(own_flat[lead:], 'ri', route)  6.73 us
    transpose x2, local copies, waits for them, and re-layouts, weight_pair(): both.transpose(2, 3, 0, 1).reshape(values.shape[1] * values.shape[2], -1)  4.86 us
  transfers between devices with their start and end apart: 7, of which 2 were waited for; matrix products, arithmetic and copies ran while one was open for 34% of the time, Pallas kernels for 0%

profile of v18, /device:TPU:0, one launch (start us, length us, event | category | flops | bytes accessed | tf_op | source)
XLA Modules:
  0.0 138.1 jit_solution(5294753799942190753)
XLA Ops:
  0.0 0.7 convert_element_type.32
  1.1 1.8 %broadcast_multiply_fusion = bf16[128,32,256]{2,1,0:T(8,128)(2,1)S(1)} fusion(bf16[128,32,256]{2,1,0:T(8,128)(2,1)} %param.11, bf16[128,256]{1,0:T(8,128)(2,1)S(1)} %copy.25), kind=kLoop, calls=%fused_computation.32 | loop fusion | flops 1048576 | bytes 4259840 | tf_op jit(solution)/shard_map/mul | solution.py:43
  3.4 3.1 %collective-permute-start = (bf16[40,8192]{1,0:T(8,128)(2,1)S(1)}, bf16[40,8192]{1,0:T(8,128)(2,1)}, u32[]{:S(2)}, u32[]{:S(2)}) collective-permute-start(bf16[40,8192]{1,0:T(8,128)(2,1)S(1)} %bitcast.144), channel_id=1, source_target_pairs={{0,8},{8,16},{16,24},{24,0},{1,9},{9,17},{17,25},{25,1},{2,10},{10... | collective-permute-start | bytes 1966088 | tf_op jit(solution)/shard_map/ppermute | solution.py:81
  6.4 5.3 %collective-permute-start.1 = (bf16[40,8192]{1,0:T(8,128)(2,1)S(1)}, bf16[40,8192]{1,0:T(8,128)(2,1)}, u32[]{:S(2)}, u32[]{:S(2)}) collective-permute-start(bf16[40,8192]{1,0:T(8,128)(2,1)S(1)} %bitcast.145), channel_id=1, source_target_pairs={{0,16},{24,8},{1,17},{25,9},{2,18},{26,10},{3,19},{27,11},{4,20},{... | collective-permute-start | bytes 1966088 | tf_op jit(solution)/shard_map/ppermute | solution.py:81
  12.2 9.3 %all_gather.3 = bf16[2,256,256]{2,1,0:T(8,128)(2,1)S(1)} all-gather(bf16[2,32,256]{2,1,0:T(8,128)(2,1)S(1)} %pad_maximum_fusion.2), channel_id=1, replica_groups=mesh['ri'=4,'ao'=8] {'ao'}, dimensions={1}, use_global_device_ids=true | all-gather | bytes 294912 | tf_op jit(solution)/shard_map/all_gather | solution.py:87
  22.3 3.2 %fusion.15 = bf16[2,256,128,32]{2,1,3,0:T(8,128)(2,1)S(1)} fusion(bf16[128,32,256]{2,1,0:T(8,128)(2,1)S(1)} %broadcast_multiply_fusion, bf16[1,256,256]{1,2,0:T(8,128)(2,1)S(1)} %copy.23, bf16[1,256,256]{1,2,0:T(8,128)(2,1)S(1)} %copy.22), kind=kOutput, calls=%fused_computation.25 | convolution fusion | flops 1074266112 | bytes 6553600 | tf_op jit(solution)/shard_map/prk,dkc->cdrp/dot_general | solution.py:94
  25.5 4.7 %copy.55 = bf16[2,256,128,32]{2,3,0,1:T(8,128)(2,1)} copy(bf16[2,256,128,32]{2,1,3,0:T(8,128)(2,1)S(1)} %fusion.15) | data formatting | bytes 8388608 | tf_op jit(solution)/shard_map/prk,dkc->cdrp/dot_general | solution.py:94
  30.2 4.3 %collective-permute-done.1 = bf16[40,8192]{1,0:T(8,128)(2,1)} collective-permute-done((bf16[40,8192]{1,0:T(8,128)(2,1)S(1)}, bf16[40,8192]{1,0:T(8,128)(2,1)}, u32[]{:S(2)}, u32[]{:S(2)}) %collective-permute-start.1) | collective-permute-done | bytes 655392 | tf_op jit(solution)/shard_map/ppermute | solution.py:81
  34.5 4.5 %all-to-all-start = ((bf16[256,2,32,128]{3,2,1,0:T(8,128)(2,1)}), bf16[256,2,32,128]{3,2,1,0:T(8,128)(2,1)}, u32[]{:S(2)}, u32[]{:S(2)}) async-start(bf16[256,2,32,128]{3,2,1,0:T(8,128)(2,1)} %bitcast.125), calls=%async_computation | async-start | bytes 8388608 | tf_op jit(solution)/shard_map/all_to_all | solution.py:102
  39.2 0.9 copy.47
  40.2 3.4 %collective-permute-start.2 = (bf16[88,8192]{1,0:T(8,128)(2,1)S(1)}, bf16[88,8192]{1,0:T(8,128)(2,1)}, u32[]{:S(2)}, u32[]{:S(2)}) collective-permute-start(bf16[88,8192]{1,0:T(8,128)(2,1)S(1)} %bitcast.136), channel_id=1, source_target_pairs={{0,8},{8,16},{16,24},{24,0},{1,9},{9,17},{17,25},{25,1},{2,10},{10... | collective-permute-start | bytes 4325384 | tf_op jit(solution)/shard_map/ppermute | solution.py:82
  43.6 3.3 %collective-permute-start.3 = (bf16[88,8192]{1,0:T(8,128)(2,1)S(1)}, bf16[88,8192]{1,0:T(8,128)(2,1)}, u32[]{:S(2)}, u32[]{:S(2)}) collective-permute-start(bf16[88,8192]{1,0:T(8,128)(2,1)S(1)} %bitcast.137), channel_id=1, source_target_pairs={{0,16},{24,8},{1,17},{25,9},{2,18},{26,10},{3,19},{27,11},{4,20},{... | collective-permute-start | bytes 4325384 | tf_op jit(solution)/shard_map/ppermute | solution.py:82
  48.1 0.7 dynamic_slice.26
  52.0 2.8 %copy.46 = bf16[16,8,32,256]{3,1,2,0:T(8,128)(2,1)} copy(bf16[16,8,32,256]{3,2,1,0:T(8,128)(2,1)S(1)} %bitcast.122) | data formatting | bytes 4194304
  54.7 33.4 %all-to-all-done = bf16[256,2,32,128]{3,2,1,0:T(8,128)(2,1)} async-done(((bf16[256,2,32,128]{3,2,1,0:T(8,128)(2,1)}), bf16[256,2,32,128]{3,2,1,0:T(8,128)(2,1)}, u32[]{:S(2)}, u32[]{:S(2)}) %all-to-all-start) | async-done | bytes 4194336 | tf_op jit(solution)/shard_map/all_to_all | solution.py:102
  88.2 3.3 %copy.28 = bf16[8,32,2,32,128]{4,3,0,2,1:T(8,128)(2,1)S(1)} copy(bf16[8,32,2,32,128]{4,3,2,1,0:T(8,128)(2,1)} %bitcast.16) | data formatting | bytes 8388608 | tf_op jit(solution)/shard_map/all_to_all | solution.py:102
  91.5 0.8 fusion.12
  92.7 2.4 %copy.32 = bf16[32,256,2,128]{1,0,3,2:T(8,128)(2,1)S(1)} copy(bf16[32,256,2,128]{1,3,0,2:T(8,128)(2,1)S(1)} %maximum_bitcast_fusion.1) | data formatting | bytes 8388608 | tf_op jit(solution)/shard_map/transpose | solution.py:54
  95.1 4.3 %copy.45 = bf16[32,8,32,256]{3,1,2,0:T(8,128)(2,1)S(1)} copy(bf16[32,8,32,256]{3,2,1,0:T(8,128)(2,1)S(1)} %bitcast.128) | data formatting | bytes 8388608
  99.5 3.9 %fusion.3 = f32[208,256]{1,0:T(8,128)S(1)} fusion(bf16[8192,256]{0,1:T(8,128)(2,1)S(1)} %bitcast.131, bf16[40,8192]{1,0:T(8,128)(2,1)} %collective-permute-done.1, bf16[40,8192]{1,0:T(8,128)(2,1)} %collective-permute-done, bf16[128,8192]{1,0:T(8,128)(2,1)S(1)} %bitcast.135), kind=kOutput, calls=%fused_computation.11 | convolution fusion | flops 882638848 | bytes 7815168 | tf_op jit(solution)/shard_map/dot_general | solution.py:58
  103.5 0.8 fusion.11
  104.6 2.4 %copy.30 = bf16[32,256,2,128]{1,0,3,2:T(8,128)(2,1)S(1)} copy(bf16[32,256,2,128]{1,3,0,2:T(8,128)(2,1)S(1)} %maximum_bitcast_fusion) | data formatting | bytes 8388608 | tf_op jit(solution)/shard_map/transpose | solution.py:54
  107.1 4.3 %copy.44 = bf16[32,8,32,256]{3,1,2,0:T(8,128)(2,1)S(1)} copy(bf16[32,8,32,256]{3,2,1,0:T(8,128)(2,1)S(1)} %bitcast.129) | data formatting | bytes 8388608
  111.4 3.7 %fusion.18 = f32[80,256]{1,0:T(8,128)S(1)} fusion(bf16[8192,256]{0,1:T(8,128)(2,1)S(1)} %bitcast.126, bf16[40,8192]{1,0:T(8,128)(2,1)} %collective-permute-done.1, bf16[40,8192]{1,0:T(8,128)(2,1)} %collective-permute-done), kind=kOutput, calls=%fused_computation.28 | convolution fusion | flops 338165760 | bytes 5586944 | tf_op jit(solution)/shard_map/dot_general | solution.py:58
  115.7 1.5 %constant_dynamic-update-slice_fusion.1 = bf16[176,8192]{1,0:T(8,128)(2,1)S(1)} fusion(bf16[88,8192]{1,0:T(8,128)(2,1)} %collective-permute-done.2), kind=kLoop, calls=%fused_computation.55 | loop fusion | bytes 2883584
  117.1 1.5 %constant_dynamic-update-slice_fusion = bf16[176,8192]{1,0:T(8,128)(2,1)S(1)} fusion(bf16[176,8192]{1,0:T(8,128)(2,1)S(1)} %constant_dynamic-update-slice_fusion.1, bf16[88,8192]{1,0:T(8,128)(2,1)} %collective-permute-done.3), kind=kLoop, calls=%fused_computation.54 | loop fusion | bytes 2883584 | tf_op jit(solution)/shard_map/concatenate | solution.py:118
  118.6 1.3 fusion.38
  120.2 1.3 collective-permute-start.5
  121.8 2.3 %collective-permute-start.4 = (f32[128,128]{0,1:T(8,128)S(1)}, f32[128,128]{0,1:T(8,128)S(1)}, u32[]{:S(2)}, u32[]{:S(2)}) collective-permute-start(f32[128,128]{0,1:T(8,128)S(1)} %pad_maximum_fusion), channel_id=1, source_target_pairs={{8,0},{16,8},{24,16},{0,24},{9,1},{17,9},{25,17},{1,25},{10,2},{18... | collective-permute-start | bytes 196616 | tf_op jit(solution)/shard_map/ppermute | solution.py:140
  124.1 3.7 %fusion.37 = f32[176,256]{1,0:T(8,128)S(1)} fusion(bf16[176,8192]{1,0:T(8,128)(2,1)S(1)} %constant_dynamic-update-slice_fusion, bf16[8192,256]{0,1:T(8,128)(2,1)} %bitcast.127), kind=kOutput, calls=%fused_computation.69 | convolution fusion | flops 738197504 | bytes 7258112 | tf_op jit(solution)/shard_map/dot_general | solution.py:58
  128.1 9.3 %all_to_all.23 = f32[8,128,64]{1,2,0:T(8,128)S(1)} all-to-all(f32[8,128,64]{1,2,0:T(8,128)S(1)} %bitcast.134), channel_id=1, replica_groups=mesh['ri'=4,'ao'=8] {'ao'}, dimensions={0} | all-to-all | bytes 524288 | tf_op jit(solution)/shard_map/all_to_all | solution.py:145
  137.5 0.6 reduce_sum.9
  (89 shorter events, 6.1 us)
Async XLA Ops:
  1.1 10.7 %copy-start.10 = (s32[1,8]{1,0:T(1,128)S(1)}, s32[1,8]{1,0:T(1,128)}, u32[]{:S(2)}) copy-start(s32[1,8]{1,0:T(1,128)} %param.15) | copy-start | bytes 100
  1.1 10.8 %copy-start.11 = (s32[1,8]{1,0:T(1,128)S(1)}, s32[1,8]{1,0:T(1,128)}, u32[]{:S(2)}) copy-start(s32[1,8]{1,0:T(1,128)} %param.16) | copy-start | bytes 100
  1.1 11.0 %copy-start.12 = (s32[1,8]{1,0:T(1,128)S(1)}, s32[1,8]{1,0:T(1,128)}, u32[]{:S(2)}) copy-start(s32[1,8]{1,0:T(1,128)} %param.17) | copy-start | bytes 100
  1.1 11.0 %copy-start.8 = (bf16[32,256]{1,0:T(8,128)(2,1)S(1)}, bf16[32,256]{1,0:T(8,128)(2,1)}, u32[]{:S(2)}) copy-start(bf16[32,256]{1,0:T(8,128)(2,1)} %param.14) | copy-start | bytes 49156
  1.1 11.0 %copy-start.9 = (bf16[32,256]{1,0:T(8,128)(2,1)S(1)}, bf16[32,256]{1,0:T(8,128)(2,1)}, u32[]{:S(2)}) copy-start(bf16[32,256]{1,0:T(8,128)(2,1)} %param.13) | copy-start | bytes 49156
  3.4 26.9 %collective-permute-start = (bf16[40,8192]{1,0:T(8,128)(2,1)S(1)}, bf16[40,8192]{1,0:T(8,128)(2,1)}, u32[]{:S(2)}, u32[]{:S(2)}) collective-permute-start(bf16[40,8192]{1,0:T(8,128)(2,1)S(1)} %bitcast.144), channel_id=1, source_target_pairs={{0,8},{8,16},{16,24},{24,0},{1,9},{9,17},{17,25},{25,1},{2,10},{10... | collective-permute-start | bytes 1966088 | tf_op jit(solution)/shard_map/ppermute | solution.py:81
  6.4 28.1 %collective-permute-start.1 = (bf16[40,8192]{1,0:T(8,128)(2,1)S(1)}, bf16[40,8192]{1,0:T(8,128)(2,1)}, u32[]{:S(2)}, u32[]{:S(2)}) collective-permute-start(bf16[40,8192]{1,0:T(8,128)(2,1)S(1)} %bitcast.145), channel_id=1, source_target_pairs={{0,16},{24,8},{1,17},{25,9},{2,18},{26,10},{3,19},{27,11},{4,20},{... | collective-permute-start | bytes 1966088 | tf_op jit(solution)/shard_map/ppermute | solution.py:81
  22.1 3.4 %copy-start.2 = (bf16[1,8,32,256]{3,2,0,1:T(8,128)(2,1)}, bf16[1,8,32,256]{3,2,0,1:T(8,128)(2,1)S(1)}, u32[]{:S(2)}) copy-start(bf16[1,8,32,256]{3,2,0,1:T(8,128)(2,1)S(1)} %get-tuple-element.30) | copy-start | bytes 393220
  22.1 3.4 %copy-start.4 = (bf16[1,8,32,256]{3,2,0,1:T(8,128)(2,1)}, bf16[1,8,32,256]{3,2,0,1:T(8,128)(2,1)S(1)}, u32[]{:S(2)}) copy-start(bf16[1,8,32,256]{3,2,0,1:T(8,128)(2,1)S(1)} %get-tuple-element.29) | copy-start | bytes 393220
  34.5 53.7 %all-to-all-start = ((bf16[256,2,32,128]{3,2,1,0:T(8,128)(2,1)}), bf16[256,2,32,128]{3,2,1,0:T(8,128)(2,1)}, u32[]{:S(2)}, u32[]{:S(2)}) async-start(bf16[256,2,32,128]{3,2,1,0:T(8,128)(2,1)} %bitcast.125), calls=%async_computation | async-start | bytes 8388608 | tf_op jit(solution)/shard_map/all_to_all | solution.py:102
  39.1 7.8 %copy-start.16 = (s32[4]{0:T(128)S(1)}, s32[4]{0:T(128)}, u32[]{:S(2)}) copy-start(s32[4]{0:T(128)} %constant.32.clone) | copy-start | bytes 52
  39.1 9.1 %copy-start.15 = (s32[4]{0:T(128)S(1)}, s32[4]{0:T(128)}, u32[]{:S(2)}) copy-start(s32[4]{0:T(128)} %constant.33.clone) | copy-start | bytes 52
  39.1 10.4 %copy-start.14 = (s32[4]{0:T(128)S(1)}, s32[4]{0:T(128)}, u32[]{:S(2)}) copy-start(s32[4]{0:T(128)} %constant.34.clone) | copy-start | bytes 52
  39.1 11.6 %copy-start.13 = (s32[4]{0:T(128)S(1)}, s32[4]{0:T(128)}, u32[]{:S(2)}) copy-start(s32[4]{0:T(128)} %constant.35.clone) | copy-start | bytes 52
  40.2 75.5 %collective-permute-start.2 = (bf16[88,8192]{1,0:T(8,128)(2,1)S(1)}, bf16[88,8192]{1,0:T(8,128)(2,1)}, u32[]{:S(2)}, u32[]{:S(2)}) collective-permute-start(bf16[88,8192]{1,0:T(8,128)(2,1)S(1)} %bitcast.136), channel_id=1, source_target_pairs={{0,8},{8,16},{16,24},{24,0},{1,9},{9,17},{17,25},{25,1},{2,10},{10... | collective-permute-start | bytes 4325384 | tf_op jit(solution)/shard_map/ppermute | solution.py:82
  43.6 72.0 %collective-permute-start.3 = (bf16[88,8192]{1,0:T(8,128)(2,1)S(1)}, bf16[88,8192]{1,0:T(8,128)(2,1)}, u32[]{:S(2)}, u32[]{:S(2)}) collective-permute-start(bf16[88,8192]{1,0:T(8,128)(2,1)S(1)} %bitcast.137), channel_id=1, source_target_pairs={{0,16},{24,8},{1,17},{25,9},{2,18},{26,10},{3,19},{27,11},{4,20},{... | collective-permute-start | bytes 4325384 | tf_op jit(solution)/shard_map/ppermute | solution.py:82
  88.2 3.3 %copy-start.5 = (bf16[1,8,32,256]{3,2,0,1:T(8,128)(2,1)S(1)}, bf16[1,8,32,256]{3,2,0,1:T(8,128)(2,1)}, u32[]{:S(2)}) copy-start(bf16[1,8,32,256]{3,2,0,1:T(8,128)(2,1)} %copy-done.4) | copy-start | bytes 393220
  95.1 4.3 %copy-start.1 = (bf16[16,8,32,256]{3,1,2,0:T(8,128)(2,1)S(1)}, bf16[16,8,32,256]{3,1,2,0:T(8,128)(2,1)}, u32[]{:S(2)}) copy-start(bf16[16,8,32,256]{3,1,2,0:T(8,128)(2,1)} %copy.46) | copy-start | bytes 6291460
  99.5 4.0 %copy-start.3 = (bf16[1,8,32,256]{3,2,0,1:T(8,128)(2,1)S(1)}, bf16[1,8,32,256]{3,2,0,1:T(8,128)(2,1)}, u32[]{:S(2)}) copy-start(bf16[1,8,32,256]{3,2,0,1:T(8,128)(2,1)} %copy-done.2) | copy-start | bytes 393220
  103.4 0.8 copy-start.6
  111.4 5.8 %copy-start = (bf16[32,8,32,256]{3,1,2,0:T(8,128)(2,1)}, bf16[32,8,32,256]{3,1,2,0:T(8,128)(2,1)S(1)}, u32[]{:S(2)}) copy-start(bf16[32,8,32,256]{3,1,2,0:T(8,128)(2,1)S(1)} %copy.44) | copy-start | bytes 12582916
  118.6 1.5 %slice-start.1 = ((f32[208,128]{1,0:T(8,128)}), f32[80,128]{1,0:T(8,128)S(1)}, s32[]{:S(2)}) async-start(f32[208,128]{1,0:T(8,128)} %copy-done.6), calls=%async_computation.3 | async-start | bytes 81920 | tf_op jit(solution)/shard_map/slice | solution.py:113
  120.2 7.9 %collective-permute-start.5 = (f32[128,128]{0,1:T(8,128)S(1)}, f32[128,128]{0,1:T(8,128)S(1)}, u32[]{:S(2)}, u32[]{:S(2)}) collective-permute-start(f32[128,128]{0,1:T(8,128)S(1)} %pad_maximum_fusion.1), channel_id=1, source_target_pairs={{16,0},{8,24},{17,1},{9,25},{18,2},{10,26},{19,3},{11,27},{20,4},{... | collective-permute-start | bytes 196616 | tf_op jit(solution)/shard_map/ppermute | solution.py:140
  121.7 6.1 %slice-start = ((f32[208,128]{1,0:T(8,128)}), f32[128,128]{1,0:T(8,128)S(1)}, s32[]{:S(2)}) async-start(f32[208,128]{1,0:T(8,128)} %copy-done.6), calls=%async_computation.2 | async-start | bytes 131072 | tf_op jit(solution)/shard_map/slice | solution.py:112
  121.7 6.2 %copy-start.7 = (f32[80,128]{1,0:T(8,128)S(1)}, f32[80,128]{1,0:T(8,128)}, u32[]{:S(2)}) copy-start(f32[80,128]{1,0:T(8,128)} %slice_add_fusion.3) | copy-start | bytes 122884
  121.8 6.3 %collective-permute-start.4 = (f32[128,128]{0,1:T(8,128)S(1)}, f32[128,128]{0,1:T(8,128)S(1)}, u32[]{:S(2)}, u32[]{:S(2)}) collective-permute-start(f32[128,128]{0,1:T(8,128)S(1)} %pad_maximum_fusion), channel_id=1, source_target_pairs={{8,0},{16,8},{24,16},{0,24},{9,1},{17,9},{25,17},{1,25},{10,2},{18... | collective-permute-start | bytes 196616 | tf_op jit(solution)/shard_map/ppermute | solution.py:140
